TPU v7x, 128 devices: a whole 4x4x4 slice. The times are simulated.
128 devices in a mesh: tok: 16 (over x, y), voc: 8 (over z, core).
Axes of the slice: x: 4, y: 4, z: 4, core: 2. Of those that a mesh axis runs over, the one named last changes fastest.
Arguments:
- hidden_rows: bfloat16 [512, 3584], P(('tok', 'voc')), may hold values from -40 to 40
- head_weight: bfloat16 [147456, 3584], P(('tok', 'voc')), may hold values from -0.09375 to 0.09375
- teacher_index: int32 [512, 64], replicated, may hold values from 0 to 147455, as said below
- teacher_logprob: float32 [512, 64], replicated, may hold values from -10 to -4.2
Outputs:
- row_loss: float32 [512], P(('tok', 'voc'))
- head_grad: bfloat16 [147456, 3584], P(('tok', 'voc'))
- input_grad: bfloat16 [512, 3584], P(('tok', 'voc'))
Inputs may be any that keep to these rules, and one draw needn't show every extreme that they name: `teacher_index`: the 64 entries of one token are distinct.
All inputs are finite; a program needn't handle non-finite values.
Results may differ from a plain program's by a relative error of at most 0.015.
Values may be sent and summed in bfloat16 or wider, within the bound.
No kernel may reach another device: no remote copies, remote signals or barrier semaphores. Data moves between devices by JAX's collectives and lax.ppermute only.
A program may use at most 128 MiB of HBM per device.

v0:
```python
import jax
import jax.numpy as jnp
from jax import lax
from jax.sharding import PartitionSpec as P

loss_scale = 256.0
RING = 4


def coords():
    tok = lax.axis_index("tok")
    voc = lax.axis_index("voc")
    return {"x": tok // RING, "y": tok % RING, "z": voc // 2, "c": voc % 2}


def stage_pairs(stage, shift, tok_n, voc_n):
    if stage == "c":
        return "voc", [(v, v ^ 1) for v in range(voc_n)]
    if stage == "z":
        return "voc", [(v, ((v // 2 + shift) % RING) * 2 + v % 2) for v in range(voc_n)]
    if stage == "y":
        return "tok", [(t, (t // RING) * RING + (t % RING + shift) % RING) for t in range(tok_n)]
    return "tok", [(t, ((t // RING + shift) % RING) * RING + t % RING) for t in range(tok_n)]


def exchange(block_for, stage, tok_n, voc_n):
    n = 2 if stage == "c" else RING
    got = [block_for(0)]
    for shift in range(1, n):
        axis, pairs = stage_pairs(stage, shift, tok_n, voc_n)
        got.append(lax.ppermute(block_for(shift), axis, pairs))
    return jnp.stack(got)


def ring_order(me, n):
    if n == 2:
        return jnp.arange(2, dtype=jnp.int32) ^ me
    return (me - jnp.arange(n, dtype=jnp.int32)) % n


def to_arrival(nat, at):
    rest = nat.shape[1:]
    a = nat.reshape((RING, RING, RING, 2, -1) + rest)
    for axis, stage, n in ((0, "x", RING), (1, "y", RING), (2, "z", RING), (3, "c", 2)):
        a = jnp.take(a, ring_order(at[stage], n), axis=axis)
    a = jnp.transpose(a, (3, 2, 1, 0) + tuple(range(4, a.ndim)))
    return a.reshape(nat.shape)


def to_natural(arr, at):
    lead = arr.shape[:-1]
    k = len(lead)
    a = arr.reshape(lead + (2, RING, RING, RING, -1))
    for axis, stage, n in ((k, "c", 2), (k + 1, "z", RING), (k + 2, "y", RING), (k + 3, "x", RING)):
        a = jnp.take(a, ring_order(at[stage], n), axis=axis)
    perm = tuple(range(k)) + (k + 3, k + 2, k + 1, k, k + 4)
    return jnp.transpose(a, perm).reshape(arr.shape)


def per_device(hidden_rows, head_weight, teacher_index, teacher_logprob, tok_n, voc_n):
    voc_dev = head_weight.shape[0]
    tok_dev = hidden_rows.shape[0]
    width = hidden_rows.shape[1]
    at = coords()

    every = hidden_rows
    for stage in ("x", "y", "z", "c"):
        got = exchange(lambda s: every, stage, tok_n, voc_n)
        every = got.reshape(-1, width)

    logits = lax.dot_general(
        every, head_weight, (((1,), (1,)), ((), ())), preferred_element_type=jnp.float32
    )
    position = lax.axis_index(("tok", "voc"))
    offset = position * voc_dev
    index_arr = to_arrival(teacher_index, at)
    logprob_arr = to_arrival(teacher_logprob, at)
    local = index_arr - offset
    probs_arr = jnp.exp(logprob_arr)
    columns = jnp.arange(voc_dev, dtype=jnp.int32)[None, None, :]
    target = jnp.sum(jnp.where(local[:, :, None] == columns, probs_arr[:, :, None], 0.0), axis=1)
    part_dot = jnp.sum(logits * target, axis=1)
    local_peak = jnp.max(logits, axis=1)
    local_sum = jnp.sum(jnp.exp(logits - local_peak[:, None]), axis=1)

    stats = to_natural(jnp.stack([local_peak, local_sum, part_dot]), at)
    for stage in ("c", "z", "y", "x"):
        n = 2 if stage == "c" else RING
        got = exchange(lambda s: stats, stage, tok_n, voc_n)
        got = jnp.take(got, ring_order(at[stage], n), axis=0)
        peak = jnp.max(got[:, 0], axis=0)
        summed = jnp.sum(got[:, 1] * jnp.exp(got[:, 0] - peak[None]), axis=0)
        dotted = jnp.sum(got[:, 2], axis=0)
        stats = jnp.stack([peak, summed, dotted])
    peak, summed, dotted = stats[0], stats[1], stats[2]

    lse = peak + jnp.log(summed)
    probs = jnp.exp(teacher_logprob)
    total_p = jnp.sum(probs, axis=1)
    own_term = jnp.sum(probs * teacher_logprob, axis=1)
    loss_all = own_term - dotted + total_p * lse
    row_loss = lax.dynamic_slice_in_dim(loss_all, position * tok_dev, tok_dev, 0)
    lse_arr = to_arrival(lse, at)
    total_arr = jnp.sum(probs_arr, axis=1)
    grad = (loss_scale * (total_arr[:, None] * jnp.exp(logits - lse_arr[:, None]) - target)).astype(
        jnp.bfloat16
    )
    partial = jnp.dot(grad, head_weight, preferred_element_type=jnp.float32)
    head_grad = lax.dot_general(
        grad, every, (((0,), (0,)), ((), ())), preferred_element_type=jnp.float32
    ).astype(jnp.bfloat16)

    acc = partial.reshape(2, -1, width)
    for stage in ("c", "z", "y", "x"):
        n = acc.shape[0]
        got = exchange(lambda s: acc[(-s) % n].astype(jnp.bfloat16), stage, tok_n, voc_n)
        acc = acc[0] + jnp.sum(got[1:].astype(jnp.float32), axis=0)
        if stage != "x":
            acc = acc.reshape(RING, -1, width)
    return (row_loss, head_grad, acc.astype(jnp.bfloat16))


def solution(mesh):
    tok_n = mesh.shape["tok"]
    voc_n = mesh.shape["voc"]
    placed = (P(("tok", "voc"), None), P(("tok", "voc"), None), P(), P())

    def body(h, w, ti, tl):
        return per_device(h, w, ti, tl, tok_n, voc_n)

    return jax.shard_map(
        body,
        mesh=mesh,
        in_specs=placed,
        out_specs=(P(("tok", "voc")), P(("tok", "voc"), None), P(("tok", "voc"), None)),
        check_vma=False,
    )
```

profile of v0, /device:TPU:0, one launch (start us, length us, event | category | flops | bytes accessed | tf_op | source)
XLA Modules:
  0.0 249.9 jit_solution(16422556272069394367)
XLA Ops:
  0.6 1.6 collective-permute-start
  2.3 2.7 %collective-permute-start.1 = (bf16[4,3584]{1,0:T(4,128)(2,1)}, bf16[4,3584]{1,0:T(4,128)(2,1)S(1)}, u32[]{:S(2)}, u32[]{:S(2)}) collective-permute-start(bf16[4,3584]{1,0:T(4,128)(2,1)} %param.6), channel_id=1, source_target_pairs={{0,64},{8,72},{16,80},{24,88},{32,96},{40,104},{48,112},{56,120},{... | collective-permute-start | bytes 86024 | tf_op jit(solution)/shard_map/ppermute | solution.py:31
  5.0 1.4 collective-permute-start.2
  6.6 1.0 copy.115
  7.6 0.7 gather_fusion
  8.5 0.7 gather_fusion.1
  9.6 0.7 gather_fusion.4
  11.3 0.7 gather_fusion.2
  12.2 0.7 gather_fusion.3
  13.1 1.6 collective-permute-start.3
  14.7 2.9 %collective-permute-start.4 = (bf16[16,3584]{1,0:T(8,128)(2,1)S(1)}, bf16[16,3584]{1,0:T(8,128)(2,1)S(1)}, u32[]{:S(2)}, u32[]{:S(2)}) collective-permute-start(bf16[16,3584]{1,0:T(8,128)(2,1)S(1)} %reshape.286), channel_id=1, source_target_pairs={{0,16},{8,24},{16,0},{24,8},{32,48},{40,56},{48,32},{56,40},{64,80... | collective-permute-start | bytes 344072 | tf_op jit(solution)/shard_map/ppermute | solution.py:31
  17.6 1.3 collective-permute-start.5
  19.2 0.7 gather_fusion.6
  20.4 1.7 collective-permute-done.4
  22.5 4.0 %collective-permute-start.7 = (bf16[64,3584]{1,0:T(8,128)(2,1)S(1)}, bf16[64,3584]{1,0:T(8,128)(2,1)S(1)}, u32[]{:S(2)}, u32[]{:S(2)}) collective-permute-start(bf16[64,3584]{1,0:T(8,128)(2,1)S(1)} %bitcast.150), channel_id=1, source_target_pairs={{0,4},{1,5},{2,6},{3,7},{4,0},{5,1},{6,2},{7,3},{8,12},{9,13},{10,... | collective-permute-start | bytes 1376264 | tf_op jit(solution)/shard_map/ppermute | solution.py:31
  26.4 0.7 collective-permute-start.8
  27.2 1.3 collective-permute-start.6
  28.7 0.7 gather_fusion.7
  29.8 8.1 %collective-permute-done.7 = bf16[64,3584]{1,0:T(8,128)(2,1)S(1)} collective-permute-done((bf16[64,3584]{1,0:T(8,128)(2,1)S(1)}, bf16[64,3584]{1,0:T(8,128)(2,1)S(1)}, u32[]{:S(2)}, u32[]{:S(2)}) %collective-permute-start.7) | collective-permute-done | bytes 458784 | tf_op jit(solution)/shard_map/ppermute | solution.py:31
  37.9 8.5 %collective-permute-done.8 = bf16[64,3584]{1,0:T(8,128)(2,1)S(1)} collective-permute-done((bf16[64,3584]{1,0:T(8,128)(2,1)S(1)}, bf16[64,3584]{1,0:T(8,128)(2,1)S(1)}, u32[]{:S(2)}, u32[]{:S(2)}) %collective-permute-start.8) | collective-permute-done | bytes 458784 | tf_op jit(solution)/shard_map/ppermute | solution.py:31
  46.9 94.7 %select_reduce_fusion = f32[512,1152]{1,0:T(8,128)S(1)} fusion(f32[512,64]{1,0:T(8,128)S(1)} %bitcast.157, s32[512,64]{1,0:T(8,128)S(1)} %bitcast.156), kind=kLoop, calls=%fused_computation.20 | loop fusion | flops 112656384 | bytes 2621440 | tf_op jit(solution)/shard_map/reduce_sum | solution.py:81
  142.0 10.2 %fusion.41 = (f32[512]{0:T(512)S(1)}, f32[512,1152]{1,0:T(8,128)}) fusion(bf16[512,3584]{1,0:T(8,128)(2,1)S(1)} %bitcast.147, bf16[1152,3584]{1,0:T(8,128)(2,1)} %param.7), kind=kOutput, calls=%fused_computation.160 | convolution fusion | flops 4228447744 | bytes 14288896 | tf_op jit(solution)/shard_map/dot_general | solution.py:71
  152.4 2.3 exponential_reduce_fusion
  160.9 1.1 collective-permute-start.11
  162.0 3.1 %collective-permute-start.12 = (f32[3,512]{1,0:T(4,128)S(1)}, f32[3,512]{1,0:T(4,128)S(1)}, u32[]{:S(2)}, u32[]{:S(2)}) collective-permute-start(f32[3,512]{1,0:T(4,128)S(1)} %get-tuple-element.50), channel_id=1, source_target_pairs={{0,4},{1,5},{2,6},{3,7},{4,0},{5,1},{6,2},{7,3},{8,12},{9,13},{10,... | collective-permute-start | bytes 18440 | tf_op jit(solution)/shard_map/ppermute | solution.py:31
  165.1 1.0 collective-permute-start.13
  166.1 1.1 collective-permute-done.12
  167.2 1.6 collective-permute-done.13
  169.6 3.9 %collective-permute-start.15 = (f32[3,512]{1,0:T(4,128)S(1)}, f32[3,512]{1,0:T(4,128)S(1)}, u32[]{:S(2)}, u32[]{:S(2)}) collective-permute-start(f32[3,512]{1,0:T(4,128)S(1)} %get-tuple-element.48), channel_id=1, source_target_pairs={{0,16},{8,24},{16,0},{24,8},{32,48},{40,56},{48,32},{56,40},{64,80... | collective-permute-start | bytes 18440 | tf_op jit(solution)/shard_map/ppermute | solution.py:31
  173.6 0.8 collective-permute-done.14
  174.4 0.8 collective-permute-done.15
  175.2 1.9 collective-permute-done.16
  178.5 1.4 collective-permute-start.18
  180.0 1.3 collective-permute-start.19
  181.4 1.3 collective-permute-done.17
  182.8 0.9 collective-permute-done.18
  187.7 2.3 multiply_convert_fusion
  189.9 7.3 %fusion.42 = f32[512,3584]{1,0:T(8,128)S(1)} fusion(bf16[512,1152]{1,0:T(8,128)(2,1)S(1)} %multiply_convert_fusion, bf16[1152,3584]{1,0:T(8,128)(2,1)} %param.7), kind=kOutput, calls=%fused_computation.161 | convolution fusion | flops 4227858432 | bytes 16777216 | tf_op jit(solution)/shard_map/dot_general | solution.py:108
  197.5 3.8 %collective-permute-done.20 = bf16[256,3584]{1,0:T(8,128)(2,1)S(1)} collective-permute-done((bf16[256,3584]{1,0:T(8,128)(2,1)S(1)}, bf16[256,3584]{1,0:T(8,128)(2,1)S(1)}, u32[]{:S(2)}, u32[]{:S(2)}) %collective-permute-start.20) | collective-permute-done | bytes 1835040 | tf_op jit(solution)/shard_map/ppermute | solution.py:31
  202.1 3.7 %collective-permute-start.22 = (bf16[64,3584]{1,0:T(8,128)(2,1)S(1)}, bf16[64,3584]{1,0:T(8,128)(2,1)S(1)}, u32[]{:S(2)}, u32[]{:S(2)}) collective-permute-start(bf16[64,3584]{1,0:T(8,128)(2,1)S(1)} %get-tuple-element.26), channel_id=1, source_target_pairs={{0,4},{1,5},{2,6},{3,7},{4,0},{5,1},{6,2},{7,3},{8,12},{9,13},{10,... | collective-permute-start | bytes 1376264 | tf_op jit(solution)/shard_map/ppermute | solution.py:31
  206.3 10.0 %collective-permute-done.21 = bf16[64,3584]{1,0:T(8,128)(2,1)S(1)} collective-permute-done((bf16[64,3584]{1,0:T(8,128)(2,1)S(1)}, bf16[64,3584]{1,0:T(8,128)(2,1)S(1)}, u32[]{:S(2)}, u32[]{:S(2)}) %collective-permute-start.21) | collective-permute-done | bytes 458784 | tf_op jit(solution)/shard_map/ppermute | solution.py:31
  216.2 10.0 %collective-permute-done.22 = bf16[64,3584]{1,0:T(8,128)(2,1)S(1)} collective-permute-done((bf16[64,3584]{1,0:T(8,128)(2,1)S(1)}, bf16[64,3584]{1,0:T(8,128)(2,1)S(1)}, u32[]{:S(2)}, u32[]{:S(2)}) %collective-permute-start.22) | collective-permute-done | bytes 458784 | tf_op jit(solution)/shard_map/ppermute | solution.py:31
  227.0 2.6 %collective-permute-start.25 = (bf16[16,3584]{1,0:T(8,128)(2,1)S(1)}, bf16[16,3584]{1,0:T(8,128)(2,1)S(1)}, u32[]{:S(2)}, u32[]{:S(2)}) collective-permute-start(bf16[16,3584]{1,0:T(8,128)(2,1)S(1)} %get-tuple-element.29), channel_id=1, source_target_pairs={{0,16},{8,24},{16,0},{24,8},{32,48},{40,56},{48,32},{56,40},{64,80... | collective-permute-start | bytes 344072 | tf_op jit(solution)/shard_map/ppermute | solution.py:31
  229.6 1.4 collective-permute-start.26
  230.9 3.7 %collective-permute-done.24 = bf16[16,3584]{1,0:T(8,128)(2,1)S(1)} collective-permute-done((bf16[16,3584]{1,0:T(8,128)(2,1)S(1)}, bf16[16,3584]{1,0:T(8,128)(2,1)S(1)}, u32[]{:S(2)}, u32[]{:S(2)}) %collective-permute-start.24) | collective-permute-done | bytes 114720 | tf_op jit(solution)/shard_map/ppermute | solution.py:31
  235.4 2.0 collective-permute-start.27
  237.4 2.1 collective-permute-start.28
  240.1 8.5 %convolution_convert_fusion = bf16[1152,3584]{1,0:T(8,128)(2,1)} fusion(bf16[512,1152]{1,0:T(8,128)(2,1)S(1)} %multiply_convert_fusion, bf16[512,3584]{1,0:T(8,128)(2,1)} %bitcast.148), kind=kOutput, calls=%fused_computation.22 | convolution fusion | flops 4231987200 | bytes 13107200 | tf_op jit(solution)/shard_map/dot_general | solution.py:109
  (142 shorter events, 21.9 us)
Async XLA Ops:
  0.6 8.8 %copy-start.1 = (f32[512,64]{0,1:T(8,128)S(1)}, f32[512,64]{0,1:T(8,128)}, u32[]{:S(2)}) copy-start(f32[512,64]{0,1:T(8,128)} %param.9) | copy-start | bytes 393220
  0.6 12.3 %collective-permute-start = (bf16[4,3584]{1,0:T(4,128)(2,1)}, bf16[4,3584]{1,0:T(4,128)(2,1)S(1)}, u32[]{:S(2)}, u32[]{:S(2)}) collective-permute-start(bf16[4,3584]{1,0:T(4,128)(2,1)} %param.6), channel_id=1, source_target_pairs={{0,32},{8,40},{16,48},{24,56},{32,64},{40,72},{48,80},{56,88},{64,... | collective-permute-start | bytes 86024 | tf_op jit(solution)/shard_map/ppermute | solution.py:31
  2.3 10.6 %collective-permute-start.1 = (bf16[4,3584]{1,0:T(4,128)(2,1)}, bf16[4,3584]{1,0:T(4,128)(2,1)S(1)}, u32[]{:S(2)}, u32[]{:S(2)}) collective-permute-start(bf16[4,3584]{1,0:T(4,128)(2,1)} %param.6), channel_id=1, source_target_pairs={{0,64},{8,72},{16,80},{24,88},{32,96},{40,104},{48,112},{56,120},{... | collective-permute-start | bytes 86024 | tf_op jit(solution)/shard_map/ppermute | solution.py:31
  5.0 7.9 %collective-permute-start.2 = (bf16[4,3584]{1,0:T(4,128)(2,1)}, bf16[4,3584]{1,0:T(4,128)(2,1)S(1)}, u32[]{:S(2)}, u32[]{:S(2)}) collective-permute-start(bf16[4,3584]{1,0:T(4,128)(2,1)} %param.6), channel_id=1, source_target_pairs={{0,96},{8,104},{16,112},{24,120},{32,0},{40,8},{48,16},{56,24},{64... | collective-permute-start | bytes 86024 | tf_op jit(solution)/shard_map/ppermute | solution.py:31
  9.4 3.6 %copy-start.2 = (bf16[4,3584]{1,0:T(4,128)(2,1)S(1)}, bf16[4,3584]{1,0:T(4,128)(2,1)}, u32[]{:S(2)}) copy-start(bf16[4,3584]{1,0:T(4,128)(2,1)} %param.6) | copy-start | bytes 86020
  13.1 7.3 %collective-permute-start.3 = (bf16[16,3584]{1,0:T(8,128)(2,1)S(1)}, bf16[16,3584]{1,0:T(8,128)(2,1)S(1)}, u32[]{:S(2)}, u32[]{:S(2)}) collective-permute-start(bf16[16,3584]{1,0:T(8,128)(2,1)S(1)} %reshape.286), channel_id=1, source_target_pairs={{0,8},{8,16},{16,24},{24,0},{32,40},{40,48},{48,56},{56,32},{64,72... | collective-permute-start | bytes 344072 | tf_op jit(solution)/shard_map/ppermute | solution.py:31
  14.7 7.4 %collective-permute-start.4 = (bf16[16,3584]{1,0:T(8,128)(2,1)S(1)}, bf16[16,3584]{1,0:T(8,128)(2,1)S(1)}, u32[]{:S(2)}, u32[]{:S(2)}) collective-permute-start(bf16[16,3584]{1,0:T(8,128)(2,1)S(1)} %reshape.286), channel_id=1, source_target_pairs={{0,16},{8,24},{16,0},{24,8},{32,48},{40,56},{48,32},{56,40},{64,80... | collective-permute-start | bytes 344072 | tf_op jit(solution)/shard_map/ppermute | solution.py:31
  17.6 4.8 %collective-permute-start.5 = (bf16[16,3584]{1,0:T(8,128)(2,1)S(1)}, bf16[16,3584]{1,0:T(8,128)(2,1)S(1)}, u32[]{:S(2)}, u32[]{:S(2)}) collective-permute-start(bf16[16,3584]{1,0:T(8,128)(2,1)S(1)} %reshape.286), channel_id=1, source_target_pairs={{0,24},{8,0},{16,8},{24,16},{32,56},{40,32},{48,40},{56,48},{64,88... | collective-permute-start | bytes 344072 | tf_op jit(solution)/shard_map/ppermute | solution.py:31
  22.5 15.4 %collective-permute-start.7 = (bf16[64,3584]{1,0:T(8,128)(2,1)S(1)}, bf16[64,3584]{1,0:T(8,128)(2,1)S(1)}, u32[]{:S(2)}, u32[]{:S(2)}) collective-permute-start(bf16[64,3584]{1,0:T(8,128)(2,1)S(1)} %bitcast.150), channel_id=1, source_target_pairs={{0,4},{1,5},{2,6},{3,7},{4,0},{5,1},{6,2},{7,3},{8,12},{9,13},{10,... | collective-permute-start | bytes 1376264 | tf_op jit(solution)/shard_map/ppermute | solution.py:31
  26.4 20.0 %collective-permute-start.8 = (bf16[64,3584]{1,0:T(8,128)(2,1)S(1)}, bf16[64,3584]{1,0:T(8,128)(2,1)S(1)}, u32[]{:S(2)}, u32[]{:S(2)}) collective-permute-start(bf16[64,3584]{1,0:T(8,128)(2,1)S(1)} %bitcast.151), channel_id=1, source_target_pairs={{0,6},{1,7},{2,0},{3,1},{4,2},{5,3},{6,4},{7,5},{8,14},{9,15},{10,... | collective-permute-start | bytes 1376264 | tf_op jit(solution)/shard_map/ppermute | solution.py:31
  27.2 19.3 %collective-permute-start.6 = (bf16[64,3584]{1,0:T(8,128)(2,1)S(1)}, bf16[64,3584]{1,0:T(8,128)(2,1)S(1)}, u32[]{:S(2)}, u32[]{:S(2)}) collective-permute-start(bf16[64,3584]{1,0:T(8,128)(2,1)S(1)} %bitcast.152), channel_id=1, source_target_pairs={{0,2},{1,3},{2,4},{3,5},{4,6},{5,7},{6,0},{7,1},{8,10},{9,11},{10,... | collective-permute-start | bytes 1376264 | tf_op jit(solution)/shard_map/ppermute | solution.py:31
  46.6 95.0 %collective-permute-start.9 = (bf16[256,3584]{1,0:T(8,128)(2,1)S(1)}, bf16[256,3584]{1,0:T(8,128)(2,1)S(1)}, u32[]{:S(2)}, u32[]{:S(2)}) collective-permute-start(bf16[256,3584]{1,0:T(8,128)(2,1)S(1)} %bitcast.145), channel_id=1, source_target_pairs={{0,1},{1,0},{2,3},{3,2},{4,5},{5,4},{6,7},{7,6},{8,9},{9,8},{10,11... | collective-permute-start | bytes 5505032 | tf_op jit(solution)/shard_map/ppermute | solution.py:31
  142.0 10.3 %copy-start = (bf16[2,256,3584]{2,1,0:T(8,128)(2,1)}, bf16[2,256,3584]{2,1,0:T(8,128)(2,1)S(1)}, u32[]{:S(2)}) copy-start(bf16[2,256,3584]{2,1,0:T(8,128)(2,1)S(1)} %pad_maximum_fusion) | copy-start | bytes 11010052
  158.8 1.4 collective-permute-start.10
  160.9 5.2 %collective-permute-start.11 = (f32[3,512]{1,0:T(4,128)S(1)}, f32[3,512]{1,0:T(4,128)S(1)}, u32[]{:S(2)}, u32[]{:S(2)}) collective-permute-start(f32[3,512]{1,0:T(4,128)S(1)} %get-tuple-element.50), channel_id=1, source_target_pairs={{0,2},{1,3},{2,4},{3,5},{4,6},{5,7},{6,0},{7,1},{8,10},{9,11},{10,... | collective-permute-start | bytes 18440 | tf_op jit(solution)/shard_map/ppermute | solution.py:31
  162.0 5.2 %collective-permute-start.12 = (f32[3,512]{1,0:T(4,128)S(1)}, f32[3,512]{1,0:T(4,128)S(1)}, u32[]{:S(2)}, u32[]{:S(2)}) collective-permute-start(f32[3,512]{1,0:T(4,128)S(1)} %get-tuple-element.50), channel_id=1, source_target_pairs={{0,4},{1,5},{2,6},{3,7},{4,0},{5,1},{6,2},{7,3},{8,12},{9,13},{10,... | collective-permute-start | bytes 18440 | tf_op jit(solution)/shard_map/ppermute | solution.py:31
  165.1 3.7 %collective-permute-start.13 = (f32[3,512]{1,0:T(4,128)S(1)}, f32[3,512]{1,0:T(4,128)S(1)}, u32[]{:S(2)}, u32[]{:S(2)}) collective-permute-start(f32[3,512]{1,0:T(4,128)S(1)} %get-tuple-element.50), channel_id=1, source_target_pairs={{0,6},{1,7},{2,0},{3,1},{4,2},{5,3},{6,4},{7,5},{8,14},{9,15},{10,... | collective-permute-start | bytes 18440 | tf_op jit(solution)/shard_map/ppermute | solution.py:31
  169.5 4.9 %collective-permute-start.14 = (f32[3,512]{1,0:T(4,128)S(1)}, f32[3,512]{1,0:T(4,128)S(1)}, u32[]{:S(2)}, u32[]{:S(2)}) collective-permute-start(f32[3,512]{1,0:T(4,128)S(1)} %get-tuple-element.48), channel_id=1, source_target_pairs={{0,8},{8,16},{16,24},{24,0},{32,40},{40,48},{48,56},{56,32},{64,72... | collective-permute-start | bytes 18440 | tf_op jit(solution)/shard_map/ppermute | solution.py:31
  169.6 5.6 %collective-permute-start.15 = (f32[3,512]{1,0:T(4,128)S(1)}, f32[3,512]{1,0:T(4,128)S(1)}, u32[]{:S(2)}, u32[]{:S(2)}) collective-permute-start(f32[3,512]{1,0:T(4,128)S(1)} %get-tuple-element.48), channel_id=1, source_target_pairs={{0,16},{8,24},{16,0},{24,8},{32,48},{40,56},{48,32},{56,40},{64,80... | collective-permute-start | bytes 18440 | tf_op jit(solution)/shard_map/ppermute | solution.py:31
  173.5 3.7 %collective-permute-start.16 = (f32[3,512]{1,0:T(4,128)S(1)}, f32[3,512]{1,0:T(4,128)S(1)}, u32[]{:S(2)}, u32[]{:S(2)}) collective-permute-start(f32[3,512]{1,0:T(4,128)S(1)} %get-tuple-element.48), channel_id=1, source_target_pairs={{0,24},{8,0},{16,8},{24,16},{32,56},{40,32},{48,40},{56,48},{64,88... | collective-permute-start | bytes 18440 | tf_op jit(solution)/shard_map/ppermute | solution.py:31
  177.9 4.9 %collective-permute-start.17 = (f32[3,512]{1,0:T(4,128)S(1)}, f32[3,512]{1,0:T(4,128)S(1)}, u32[]{:S(2)}, u32[]{:S(2)}) collective-permute-start(f32[3,512]{1,0:T(4,128)S(1)} %get-tuple-element.46), channel_id=1, source_target_pairs={{0,32},{8,40},{16,48},{24,56},{32,64},{40,72},{48,80},{56,88},{64,... | collective-permute-start | bytes 18440 | tf_op jit(solution)/shard_map/ppermute | solution.py:31
  178.5 5.2 %collective-permute-start.18 = (f32[3,512]{1,0:T(4,128)S(1)}, f32[3,512]{1,0:T(4,128)S(1)}, u32[]{:S(2)}, u32[]{:S(2)}) collective-permute-start(f32[3,512]{1,0:T(4,128)S(1)} %get-tuple-element.46), channel_id=1, source_target_pairs={{0,64},{8,72},{16,80},{24,88},{32,96},{40,104},{48,112},{56,120},{... | collective-permute-start | bytes 18440 | tf_op jit(solution)/shard_map/ppermute | solution.py:31
  180.0 3.8 %collective-permute-start.19 = (f32[3,512]{1,0:T(4,128)S(1)}, f32[3,512]{1,0:T(4,128)S(1)}, u32[]{:S(2)}, u32[]{:S(2)}) collective-permute-start(f32[3,512]{1,0:T(4,128)S(1)} %get-tuple-element.46), channel_id=1, source_target_pairs={{0,96},{8,104},{16,112},{24,120},{32,0},{40,8},{48,16},{56,24},{64... | collective-permute-start | bytes 18440 | tf_op jit(solution)/shard_map/ppermute | solution.py:31
  197.4 3.9 %collective-permute-start.20 = (bf16[256,3584]{1,0:T(8,128)(2,1)S(1)}, bf16[256,3584]{1,0:T(8,128)(2,1)S(1)}, u32[]{:S(2)}, u32[]{:S(2)}) collective-permute-start(bf16[256,3584]{1,0:T(8,128)(2,1)S(1)} %slice.213), channel_id=1, source_target_pairs={{0,1},{1,0},{2,3},{3,2},{4,5},{5,4},{6,7},{7,6},{8,9},{9,8},{10,11... | collective-permute-start | bytes 5505032 | tf_op jit(solution)/shard_map/ppermute | solution.py:31
  202.1 14.2 %collective-permute-start.21 = (bf16[64,3584]{1,0:T(8,128)(2,1)S(1)}, bf16[64,3584]{1,0:T(8,128)(2,1)S(1)}, u32[]{:S(2)}, u32[]{:S(2)}) collective-permute-start(bf16[64,3584]{1,0:T(8,128)(2,1)S(1)} %get-tuple-element.24), channel_id=1, source_target_pairs={{0,2},{1,3},{2,4},{3,5},{4,6},{5,7},{6,0},{7,1},{8,10},{9,11},{10,... | collective-permute-start | bytes 1376264 | tf_op jit(solution)/shard_map/ppermute | solution.py:31
  202.1 24.0 %collective-permute-start.22 = (bf16[64,3584]{1,0:T(8,128)(2,1)S(1)}, bf16[64,3584]{1,0:T(8,128)(2,1)S(1)}, u32[]{:S(2)}, u32[]{:S(2)}) collective-permute-start(bf16[64,3584]{1,0:T(8,128)(2,1)S(1)} %get-tuple-element.26), channel_id=1, source_target_pairs={{0,4},{1,5},{2,6},{3,7},{4,0},{5,1},{6,2},{7,3},{8,12},{9,13},{10,... | collective-permute-start | bytes 1376264 | tf_op jit(solution)/shard_map/ppermute | solution.py:31
  205.8 20.5 %collective-permute-start.23 = (bf16[64,3584]{1,0:T(8,128)(2,1)S(1)}, bf16[64,3584]{1,0:T(8,128)(2,1)S(1)}, u32[]{:S(2)}, u32[]{:S(2)}) collective-permute-start(bf16[64,3584]{1,0:T(8,128)(2,1)S(1)} %get-tuple-element.25), channel_id=1, source_target_pairs={{0,6},{1,7},{2,0},{3,1},{4,2},{5,3},{6,4},{7,5},{8,14},{9,15},{10,... | collective-permute-start | bytes 1376264 | tf_op jit(solution)/shard_map/ppermute | solution.py:31
  226.7 7.9 %collective-permute-start.24 = (bf16[16,3584]{1,0:T(8,128)(2,1)S(1)}, bf16[16,3584]{1,0:T(8,128)(2,1)S(1)}, u32[]{:S(2)}, u32[]{:S(2)}) collective-permute-start(bf16[16,3584]{1,0:T(8,128)(2,1)S(1)} %get-tuple-element.27), channel_id=1, source_target_pairs={{0,8},{8,16},{16,24},{24,0},{32,40},{40,48},{48,56},{56,32},{64,72... | collective-permute-start | bytes 344072 | tf_op jit(solution)/shard_map/ppermute | solution.py:31
  227.0 7.7 %collective-permute-start.25 = (bf16[16,3584]{1,0:T(8,128)(2,1)S(1)}, bf16[16,3584]{1,0:T(8,128)(2,1)S(1)}, u32[]{:S(2)}, u32[]{:S(2)}) collective-permute-start(bf16[16,3584]{1,0:T(8,128)(2,1)S(1)} %get-tuple-element.29), channel_id=1, source_target_pairs={{0,16},{8,24},{16,0},{24,8},{32,48},{40,56},{48,32},{56,40},{64,80... | collective-permute-start | bytes 344072 | tf_op jit(solution)/shard_map/ppermute | solution.py:31
  229.6 5.7 %collective-permute-start.26 = (bf16[16,3584]{1,0:T(8,128)(2,1)S(1)}, bf16[16,3584]{1,0:T(8,128)(2,1)S(1)}, u32[]{:S(2)}, u32[]{:S(2)}) collective-permute-start(bf16[16,3584]{1,0:T(8,128)(2,1)S(1)} %get-tuple-element.28), channel_id=1, source_target_pairs={{0,24},{8,0},{16,8},{24,16},{32,56},{40,32},{48,40},{56,48},{64,88... | collective-permute-start | bytes 344072 | tf_op jit(solution)/shard_map/ppermute | solution.py:31
  235.4 13.8 %collective-permute-start.27 = (bf16[4,3584]{1,0:T(4,128)(2,1)S(1)}, bf16[4,3584]{1,0:T(4,128)(2,1)S(1)}, u32[]{:S(2)}, u32[]{:S(2)}) collective-permute-start(bf16[4,3584]{1,0:T(4,128)(2,1)S(1)} %get-tuple-element.32), channel_id=1, source_target_pairs={{0,32},{8,40},{16,48},{24,56},{32,64},{40,72},{48,80},{56,88},{64,... | collective-permute-start | bytes 86024 | tf_op jit(solution)/shard_map/ppermute | solution.py:31
  237.4 11.8 %collective-permute-start.28 = (bf16[4,3584]{1,0:T(4,128)(2,1)S(1)}, bf16[4,3584]{1,0:T(4,128)(2,1)S(1)}, u32[]{:S(2)}, u32[]{:S(2)}) collective-permute-start(bf16[4,3584]{1,0:T(4,128)(2,1)S(1)} %get-tuple-element.34), channel_id=1, source_target_pairs={{0,64},{8,72},{16,80},{24,88},{32,96},{40,104},{48,112},{56,120},{... | collective-permute-start | bytes 86024 | tf_op jit(solution)/shard_map/ppermute | solution.py:31
  239.5 9.7 %collective-permute-start.29 = (bf16[4,3584]{1,0:T(4,128)(2,1)S(1)}, bf16[4,3584]{1,0:T(4,128)(2,1)S(1)}, u32[]{:S(2)}, u32[]{:S(2)}) collective-permute-start(bf16[4,3584]{1,0:T(4,128)(2,1)S(1)} %get-tuple-element.33), channel_id=1, source_target_pairs={{0,96},{8,104},{16,112},{24,120},{32,0},{40,8},{48,16},{56,24},{64... | collective-permute-start | bytes 86024 | tf_op jit(solution)/shard_map/ppermute | solution.py:31
where the time goes:
time: 250 us
  other arithmetic  105 us (42%)
  waiting for transfers between devices  56.3 us (23%)
  starting transfers between devices  44.5 us (18%)
  matrix products  26 us (10%)
  local copies, waits for them, and re-layouts  17.1 us (7%)
    reduce_sum x1, other arithmetic, per_device(): jnp.sum(jnp.where(local[:, :, None] == columns, probs_arr[:, :, None], 0....  94.7 us
    ppermute x30, waiting for transfers between devices, exchange(): got.append(lax.ppermute(block_for(shift), axis, pairs))  56.3 us
    ppermute x30, starting transfers between devices, exchange(): got.append(lax.ppermute(block_for(shift), axis, pairs))  44.5 us
    dot_general x1, matrix products, per_device(): lax.dot_general(every, head_weight, (((1,), (1,)), ((), ())), preferred_e...  10.2 us
    dot_general x1, matrix products, per_device(): lax.dot_general(grad, every, (((0,), (0,)), ((), ())), preferred_element_...  8.47 us
    gather x12, local copies, waits for them, and re-layouts, to_arrival(): a = jnp.take(a, ring_order(at[stage], n), axis=axis)  8.02 us
    dot_general x1, matrix products, per_device(): partial = jnp.dot(grad, head_weight, preferred_element_type=jnp.float32)  7.3 us
  transfers between devices with their start and end apart: 30, of which 20 were waited for; matrix products, arithmetic and copies ran while one was open for 45% of the time, Pallas kernels for 0%

commit v1 on v0

--- a/solution.py
+++ b/solution.py
@@ -5,6 +5,47 @@
 
 loss_scale = 256.0
 RING = 4
+
+
+HITS = 8
+
+
+def dense_target(local, probs, voc_dev):
+    blocks = local.shape[0] // 64
+    local_b = local.reshape(blocks, 64, local.shape[1])
+    probs_b = probs.reshape(blocks, 64, probs.shape[1])
+    columns = jnp.arange(voc_dev, dtype=jnp.int32)[None, None, :]
+
+    def one_block(args):
+        block_local, block_probs = args
+        equal = block_local[:, :, None] == columns
+        return jnp.sum(jnp.where(equal, block_probs[:, :, None], 0.0), axis=1)
+
+    return lax.map(one_block, (local_b, probs_b)).reshape(local.shape[0], voc_dev)
+
+
+def compact_target(local, probs, voc_dev):
+    valid = (local >= 0) & (local < voc_dev)
+    rank = jnp.cumsum(valid.astype(jnp.int32), axis=1) - 1
+    slot = jnp.arange(HITS, dtype=jnp.int32)[None, None, :]
+    chosen = valid[:, :, None] & (rank[:, :, None] == slot)
+    slot_local = jnp.sum(jnp.where(chosen, local[:, :, None], 0), axis=1)
+    slot_probs = jnp.sum(jnp.where(chosen, probs[:, :, None], 0.0), axis=1)
+    columns = jnp.arange(voc_dev, dtype=jnp.int32)[None, :]
+    target = jnp.zeros((local.shape[0], voc_dev), jnp.float32)
+    for j in range(HITS):
+        target = target + jnp.where(slot_local[:, j : j + 1] == columns, slot_probs[:, j : j + 1], 0.0)
+    return target
+
+
+def teacher_target(local, probs, voc_dev):
+    valid = (local >= 0) & (local < voc_dev)
+    crowded = jnp.any(jnp.sum(valid.astype(jnp.int32), axis=1) > HITS)
+    return lax.cond(
+        crowded,
+        lambda: dense_target(local, probs, voc_dev),
+        lambda: compact_target(local, probs, voc_dev),
+    )
 
 
 def coords():
@@ -77,8 +118,7 @@
     logprob_arr = to_arrival(teacher_logprob, at)
     local = index_arr - offset
     probs_arr = jnp.exp(logprob_arr)
-    columns = jnp.arange(voc_dev, dtype=jnp.int32)[None, None, :]
-    target = jnp.sum(jnp.where(local[:, :, None] == columns, probs_arr[:, :, None], 0.0), axis=1)
+    target = teacher_target(local, probs_arr, voc_dev)
     part_dot = jnp.sum(logits * target, axis=1)
     local_peak = jnp.max(logits, axis=1)
     local_sum = jnp.sum(jnp.exp(logits - local_peak[:, None]), axis=1)

time: 250 us -> 167 us (0.67)
  other arithmetic: 105 us -> 19.8 us
    reduce_sum x1 -> x2, other arithmetic: 94.7 us -> 0.53 us  [the longest x1 0.26 us: compact_target(): slot_local = jnp.sum(jnp.where(chosen, local[:, :, None], 0), axis=1)]
    add x0 -> x1, other arithmetic: none -> 3.57 us  [compact_target(): target + jnp.where(slot_local[:, j:j + 1] == columns, slot_probs[:, j:j +...]
    another operation x11, other arithmetic: 0.8 us -> 3.49 us  [exchange(): return jnp.stack(got)]
  transfers between devices with their start and end apart: 30 -> 30, of which waited for: 20 -> 21; matrix products, arithmetic and copies ran while one was open for 45% -> 15% of each run, Pallas kernels for 0% -> 0%
where the time goes in v1:
time: 167 us
  waiting for transfers between devices  57.5 us (34%)
  starting transfers between devices  44.7 us (27%)
  matrix products  24.6 us (15%)
  other arithmetic  19.8 us (12%)
  local copies, waits for them, and re-layouts  18.3 us (11%)
  between operations  2.04 us (1%)
    ppermute x30, waiting for transfers between devices, exchange(): got.append(lax.ppermute(block_for(shift), axis, pairs))  57.5 us
    ppermute x30, starting transfers between devices, exchange(): got.append(lax.ppermute(block_for(shift), axis, pairs))  44.7 us
    dot_general x1, matrix products, per_device(): lax.dot_general(every, head_weight, (((1,), (1,)), ((), ())), preferred_e...  8.83 us
    dot_general x1, matrix products, per_device(): lax.dot_general(grad, every, (((0,), (0,)), ((), ())), preferred_element_...  8.47 us
    gather x12, local copies, waits for them, and re-layouts, to_arrival(): a = jnp.take(a, ring_order(at[stage], n), axis=axis)  8.02 us
    dot_general x1, matrix products, per_device(): partial = jnp.dot(grad, head_weight, preferred_element_type=jnp.float32)  7.3 us
    add x1, other arithmetic, compact_target(): target + jnp.where(slot_local[:, j:j + 1] == columns, slot_probs[:, j:j +...  3.57 us
    another operation x11, other arithmetic, exchange(): return jnp.stack(got)  3.49 us
  transfers between devices with their start and end apart: 30, of which 21 were waited for; matrix products, arithmetic and copies ran while one was open for 15% of the time, Pallas kernels for 0%

profile of v1, /device:TPU:0, one launch (start us, length us, event | category | flops | bytes accessed | tf_op | source)
XLA Modules:
  0.0 167.0 jit_solution(17543754009931605993)
XLA Ops:
  0.6 1.6 collective-permute-start
  2.3 2.7 %collective-permute-start.1 = (bf16[4,3584]{1,0:T(4,128)(2,1)}, bf16[4,3584]{1,0:T(4,128)(2,1)S(1)}, u32[]{:S(2)}, u32[]{:S(2)}) collective-permute-start(bf16[4,3584]{1,0:T(4,128)(2,1)} %param.10), channel_id=1, source_target_pairs={{0,64},{8,72},{16,80},{24,88},{32,96},{40,104},{48,112},{56,120},{... | collective-permute-start | bytes 86024 | tf_op jit(solution)/shard_map/ppermute | solution.py:72
  5.0 1.4 collective-permute-start.2
  6.5 1.0 copy.135
  9.5 1.6 collective-permute-start.3
  11.1 2.9 %collective-permute-start.4 = (bf16[16,3584]{1,0:T(8,128)(2,1)S(1)}, bf16[16,3584]{1,0:T(8,128)(2,1)S(1)}, u32[]{:S(2)}, u32[]{:S(2)}) collective-permute-start(bf16[16,3584]{1,0:T(8,128)(2,1)S(1)} %reshape.300), channel_id=1, source_target_pairs={{0,16},{8,24},{16,0},{24,8},{32,48},{40,56},{48,32},{56,40},{64,80... | collective-permute-start | bytes 344072 | tf_op jit(solution)/shard_map/ppermute | solution.py:72
  14.0 1.3 collective-permute-start.5
  15.4 0.7 gather_fusion.2
  16.8 1.7 %collective-permute-done.4 = bf16[16,3584]{1,0:T(8,128)(2,1)S(1)} collective-permute-done((bf16[16,3584]{1,0:T(8,128)(2,1)S(1)}, bf16[16,3584]{1,0:T(8,128)(2,1)S(1)}, u32[]{:S(2)}, u32[]{:S(2)}) %collective-permute-start.4) | collective-permute-done | bytes 114720 | tf_op jit(solution)/shard_map/ppermute | solution.py:72
  18.9 2.0 %collective-permute-start.6 = (bf16[64,3584]{1,0:T(8,128)(2,1)S(1)}, bf16[64,3584]{1,0:T(8,128)(2,1)S(1)}, u32[]{:S(2)}, u32[]{:S(2)}) collective-permute-start(bf16[64,3584]{1,0:T(8,128)(2,1)S(1)} %bitcast.180), channel_id=1, source_target_pairs={{0,2},{1,3},{2,4},{3,5},{4,6},{5,7},{6,0},{7,1},{8,10},{9,11},{10,... | collective-permute-start | bytes 1376264 | tf_op jit(solution)/shard_map/ppermute | solution.py:72
  20.9 3.6 %collective-permute-start.7 = (bf16[64,3584]{1,0:T(8,128)(2,1)S(1)}, bf16[64,3584]{1,0:T(8,128)(2,1)S(1)}, u32[]{:S(2)}, u32[]{:S(2)}) collective-permute-start(bf16[64,3584]{1,0:T(8,128)(2,1)S(1)} %bitcast.181), channel_id=1, source_target_pairs={{0,4},{1,5},{2,6},{3,7},{4,0},{5,1},{6,2},{7,3},{8,12},{9,13},{10,... | collective-permute-start | bytes 1376264 | tf_op jit(solution)/shard_map/ppermute | solution.py:72
  24.4 1.0 collective-permute-start.8
  25.7 7.8 %collective-permute-done.6 = bf16[64,3584]{1,0:T(8,128)(2,1)S(1)} collective-permute-done((bf16[64,3584]{1,0:T(8,128)(2,1)S(1)}, bf16[64,3584]{1,0:T(8,128)(2,1)S(1)}, u32[]{:S(2)}, u32[]{:S(2)}) %collective-permute-start.6) | collective-permute-done | bytes 458784 | tf_op jit(solution)/shard_map/ppermute | solution.py:72
  33.5 9.8 %collective-permute-done.7 = bf16[64,3584]{1,0:T(8,128)(2,1)S(1)} collective-permute-done((bf16[64,3584]{1,0:T(8,128)(2,1)S(1)}, bf16[64,3584]{1,0:T(8,128)(2,1)S(1)}, u32[]{:S(2)}, u32[]{:S(2)}) %collective-permute-start.7) | collective-permute-done | bytes 458784 | tf_op jit(solution)/shard_map/ppermute | solution.py:72
  43.4 0.8 copy-done.2
  44.3 1.4 pad_maximum_fusion.1
  46.5 2.4 %fusion.4 = (s32[2,4,4,4,4,64]{5,4,1,2,3,0:T(4,128)S(1)}, s32[2,4,4,4,4]{4,3,2,1,0:T(4,128)S(1)}) fusion(s32[2,4,4,4,4,64]{5,4,3,2,1,0:T(4,128)S(1)} %gather_fusion.3, s32[]{:T(128)S(6)} %mul.48, pred[2]{0:T(512)(128)(4,1)S(1)} %compare_and_fusion.4), kind=kLoop, calls=%fused_computation.62 | loop fusion | flops 228864 | bytes 264198 | tf_op jit(solution)/shard_map/sub | solution.py:119
  50.8 0.7 gather_fusion.6
  54.1 4.6 %conditional.1 = (f32[512,1152]{1,0:T(8,128)}) conditional(s32[]{:T(128)} %convert_element_type.43, (s32[512,64]{1,0:T(8,128)S(1)}, f32[512,64]{1,0:T(8,128)S(1)}) %tuple.93, (s32[512,64]{1,0:T(8,128)S(1)}, f32[512,64]{1,0:T(8,128)S(1)}) %tuple.94), branch_computations={%region_5.9_spmd, %region_9.13_spmd} | conditional | flops 17883136 | bytes 4423692 | solution.py:44
  55.2 3.6 %select_add_fusion = f32[512,1152]{1,0:T(8,128)} fusion(f32[512]{0:T(512)S(1)} %bitcast.224, s32[512]{0:T(512)S(1)} %bitcast.216, f32[512]{0:T(512)S(1)} %bitcast.225, s32[512]{0:T(512)S(1)} %bitcast.217, f32[512]{0:T(512)S(1)} %bitcast.226, s32[512]{0:T(512)S(1)} %bitcast.218, f32[512]{0:T(512)S(1)} %bitcast.227, s32[512]{0:T(512)S(1)} %bitcast.219, ...), kind=kLoop, calls=%fused_computation.21 | loop fusion | flops 13565952 | bytes 2392064 | tf_op jit(solution)/shard_map/cond/branch_0_fun/add | solution.py:37
  58.8 1.8 %pad_maximum_fusion = bf16[2,256,3584]{2,1,0:T(8,128)(2,1)S(1)} fusion(bf16[1,256,3584]{2,1,0:T(8,128)(2,1)} %bitcast.33, bf16[1,256,3584]{2,1,0:T(8,128)(2,1)S(1)} %bitcast.177), kind=kLoop, calls=%fused_computation.44 | loop fusion | flops 1835008 | bytes 7340032 | tf_op jit(solution)/shard_map/stack | solution.py:73
  60.7 8.8 %fusion.48 = (f32[512]{0:T(512)S(1)}, f32[512,1152]{1,0:T(8,128)S(1)}) fusion(bf16[512,3584]{1,0:T(8,128)(2,1)S(1)} %bitcast.178, bf16[1152,3584]{1,0:T(8,128)(2,1)} %param.11), kind=kOutput, calls=%fused_computation.185 | convolution fusion | flops 4228447744 | bytes 14288896 | tf_op jit(solution)/shard_map/dot_general | solution.py:112
  69.7 2.3 %exponential_reduce_fusion = (f32[512]{0:T(512)S(1)}, f32[512]{0:T(512)S(1)}) fusion(f32[512,1152]{1,0:T(8,128)S(1)} %get-tuple-element.146, f32[512]{0:T(512)S(1)} %get-tuple-element.145, f32[512,1152]{1,0:T(8,128)} %get-tuple-element.187), kind=kLoop, calls=%fused_computation.48 | loop fusion | flops 2358272 | bytes 4724736 | tf_op jit(solution)/shard_map/reduce_sum | solution.py:124
  78.2 1.1 collective-permute-start.11
  79.3 2.4 %collective-permute-start.12 = (f32[3,512]{1,0:T(4,128)S(1)}, f32[3,512]{1,0:T(4,128)S(1)}, u32[]{:S(2)}, u32[]{:S(2)}) collective-permute-start(f32[3,512]{1,0:T(4,128)S(1)} %get-tuple-element.144), channel_id=1, source_target_pairs={{0,4},{1,5},{2,6},{3,7},{4,0},{5,1},{6,2},{7,3},{8,12},{9,13},{10,... | collective-permute-start | bytes 18440 | tf_op jit(solution)/shard_map/ppermute | solution.py:72
  81.7 1.3 collective-permute-start.13
  83.1 1.4 collective-permute-done.12
  84.5 0.9 collective-permute-done.13
  86.2 3.9 %collective-permute-start.15 = (f32[3,512]{1,0:T(4,128)S(1)}, f32[3,512]{1,0:T(4,128)S(1)}, u32[]{:S(2)}, u32[]{:S(2)}) collective-permute-start(f32[3,512]{1,0:T(4,128)S(1)} %get-tuple-element.142), channel_id=1, source_target_pairs={{0,16},{8,24},{16,0},{24,8},{32,48},{40,56},{48,32},{56,40},{64,80... | collective-permute-start | bytes 18440 | tf_op jit(solution)/shard_map/ppermute | solution.py:72
  90.2 0.8 collective-permute-done.14
  91.1 0.8 collective-permute-done.15
  91.8 1.9 %collective-permute-done.16 = f32[3,512]{1,0:T(4,128)S(1)} collective-permute-done((f32[3,512]{1,0:T(4,128)S(1)}, f32[3,512]{1,0:T(4,128)S(1)}, u32[]{:S(2)}, u32[]{:S(2)}) %collective-permute-start.16) | collective-permute-done | bytes 6176 | tf_op jit(solution)/shard_map/ppermute | solution.py:72
  95.2 1.5 collective-permute-start.18
  96.7 1.2 collective-permute-start.19
  98.1 1.3 collective-permute-done.17
  99.4 0.9 collective-permute-done.18
  104.3 2.3 %multiply_convert_fusion = bf16[512,1152]{1,0:T(8,128)(2,1)S(1)} fusion(f32[512,1152]{1,0:T(8,128)} %get-tuple-element.187, f32[512,1152]{1,0:T(8,128)S(1)} %get-tuple-element.146, f32[512]{0:T(512)S(1)} %sub.190, f32[512]{0:T(512)S(1)} %mul.56), kind=kLoop, calls=%fused_computation.46 | loop fusion | flops 2949120 | bytes 5902336 | tf_op jit(solution)/shard_map/convert_element_type | solution.py:145
  106.6 7.3 %fusion.49 = f32[512,3584]{1,0:T(8,128)S(1)} fusion(bf16[512,1152]{1,0:T(8,128)(2,1)S(1)} %multiply_convert_fusion, bf16[1152,3584]{1,0:T(8,128)(2,1)} %param.11), kind=kOutput, calls=%fused_computation.186 | convolution fusion | flops 4227858432 | bytes 16777216 | tf_op jit(solution)/shard_map/dot_general | solution.py:148
  114.4 3.8 %collective-permute-done.20 = bf16[256,3584]{1,0:T(8,128)(2,1)S(1)} collective-permute-done((bf16[256,3584]{1,0:T(8,128)(2,1)S(1)}, bf16[256,3584]{1,0:T(8,128)(2,1)S(1)}, u32[]{:S(2)}, u32[]{:S(2)}) %collective-permute-start.20) | collective-permute-done | bytes 1835040 | tf_op jit(solution)/shard_map/ppermute | solution.py:72
  119.6 3.3 %collective-permute-start.22 = (bf16[64,3584]{1,0:T(8,128)(2,1)S(1)}, bf16[64,3584]{1,0:T(8,128)(2,1)S(1)}, u32[]{:S(2)}, u32[]{:S(2)}) collective-permute-start(bf16[64,3584]{1,0:T(8,128)(2,1)S(1)} %get-tuple-element.118), channel_id=1, source_target_pairs={{0,4},{1,5},{2,6},{3,7},{4,0},{5,1},{6,2},{7,3},{8,12},{9,13},{10,... | collective-permute-start | bytes 1376264 | tf_op jit(solution)/shard_map/ppermute | solution.py:72
  123.1 9.7 %collective-permute-done.21 = bf16[64,3584]{1,0:T(8,128)(2,1)S(1)} collective-permute-done((bf16[64,3584]{1,0:T(8,128)(2,1)S(1)}, bf16[64,3584]{1,0:T(8,128)(2,1)S(1)}, u32[]{:S(2)}, u32[]{:S(2)}) %collective-permute-start.21) | collective-permute-done | bytes 458784 | tf_op jit(solution)/shard_map/ppermute | solution.py:72
  132.9 10.4 %collective-permute-done.22 = bf16[64,3584]{1,0:T(8,128)(2,1)S(1)} collective-permute-done((bf16[64,3584]{1,0:T(8,128)(2,1)S(1)}, bf16[64,3584]{1,0:T(8,128)(2,1)S(1)}, u32[]{:S(2)}, u32[]{:S(2)}) %collective-permute-start.22) | collective-permute-done | bytes 458784 | tf_op jit(solution)/shard_map/ppermute | solution.py:72
  143.9 3.5 %collective-permute-start.25 = (bf16[16,3584]{1,0:T(8,128)(2,1)S(1)}, bf16[16,3584]{1,0:T(8,128)(2,1)S(1)}, u32[]{:S(2)}, u32[]{:S(2)}) collective-permute-start(bf16[16,3584]{1,0:T(8,128)(2,1)S(1)} %get-tuple-element.121), channel_id=1, source_target_pairs={{0,16},{8,24},{16,0},{24,8},{32,48},{40,56},{48,32},{56,40},{64,80... | collective-permute-start | bytes 344072 | tf_op jit(solution)/shard_map/ppermute | solution.py:72
  147.9 3.1 %collective-permute-done.24 = bf16[16,3584]{1,0:T(8,128)(2,1)S(1)} collective-permute-done((bf16[16,3584]{1,0:T(8,128)(2,1)S(1)}, bf16[16,3584]{1,0:T(8,128)(2,1)S(1)}, u32[]{:S(2)}, u32[]{:S(2)}) %collective-permute-start.24) | collective-permute-done | bytes 114720 | tf_op jit(solution)/shard_map/ppermute | solution.py:72
  151.0 1.2 collective-permute-done.25
  152.6 1.9 %collective-permute-start.27 = (bf16[4,3584]{1,0:T(4,128)(2,1)S(1)}, bf16[4,3584]{1,0:T(4,128)(2,1)S(1)}, u32[]{:S(2)}, u32[]{:S(2)}) collective-permute-start(bf16[4,3584]{1,0:T(4,128)(2,1)S(1)} %get-tuple-element.126), channel_id=1, source_target_pairs={{0,32},{8,40},{16,48},{24,56},{32,64},{40,72},{48,80},{56,88},{64,... | collective-permute-start | bytes 86024 | tf_op jit(solution)/shard_map/ppermute | solution.py:72
  154.5 2.1 %collective-permute-start.28 = (bf16[4,3584]{1,0:T(4,128)(2,1)S(1)}, bf16[4,3584]{1,0:T(4,128)(2,1)S(1)}, u32[]{:S(2)}, u32[]{:S(2)}) collective-permute-start(bf16[4,3584]{1,0:T(4,128)(2,1)S(1)} %get-tuple-element.128), channel_id=1, source_target_pairs={{0,64},{8,72},{16,80},{24,88},{32,96},{40,104},{48,112},{56,120},{... | collective-permute-start | bytes 86024 | tf_op jit(solution)/shard_map/ppermute | solution.py:72
  157.3 8.5 %convolution_convert_fusion = bf16[1152,3584]{1,0:T(8,128)(2,1)} fusion(bf16[512,1152]{1,0:T(8,128)(2,1)S(1)} %multiply_convert_fusion, bf16[512,3584]{1,0:T(8,128)(2,1)} %bitcast.179), kind=kOutput, calls=%fused_computation.41 | convolution fusion | flops 4231987200 | bytes 13107200 | tf_op jit(solution)/shard_map/dot_general | solution.py:149
  (157 shorter events, 27.2 us)
Async XLA Ops:
  0.6 8.7 %copy-start.4 = (bf16[4,3584]{1,0:T(4,128)(2,1)S(1)}, bf16[4,3584]{1,0:T(4,128)(2,1)}, u32[]{:S(2)}) copy-start(bf16[4,3584]{1,0:T(4,128)(2,1)} %param.10) | copy-start | bytes 86020
  0.6 8.7 %collective-permute-start = (bf16[4,3584]{1,0:T(4,128)(2,1)}, bf16[4,3584]{1,0:T(4,128)(2,1)S(1)}, u32[]{:S(2)}, u32[]{:S(2)}) collective-permute-start(bf16[4,3584]{1,0:T(4,128)(2,1)} %param.10), channel_id=1, source_target_pairs={{0,32},{8,40},{16,48},{24,56},{32,64},{40,72},{48,80},{56,88},{64,... | collective-permute-start | bytes 86024 | tf_op jit(solution)/shard_map/ppermute | solution.py:72
  2.3 7.0 %collective-permute-start.1 = (bf16[4,3584]{1,0:T(4,128)(2,1)}, bf16[4,3584]{1,0:T(4,128)(2,1)S(1)}, u32[]{:S(2)}, u32[]{:S(2)}) collective-permute-start(bf16[4,3584]{1,0:T(4,128)(2,1)} %param.10), channel_id=1, source_target_pairs={{0,64},{8,72},{16,80},{24,88},{32,96},{40,104},{48,112},{56,120},{... | collective-permute-start | bytes 86024 | tf_op jit(solution)/shard_map/ppermute | solution.py:72
  5.0 4.3 %collective-permute-start.2 = (bf16[4,3584]{1,0:T(4,128)(2,1)}, bf16[4,3584]{1,0:T(4,128)(2,1)S(1)}, u32[]{:S(2)}, u32[]{:S(2)}) collective-permute-start(bf16[4,3584]{1,0:T(4,128)(2,1)} %param.10), channel_id=1, source_target_pairs={{0,96},{8,104},{16,112},{24,120},{32,0},{40,8},{48,16},{56,24},{64... | collective-permute-start | bytes 86024 | tf_op jit(solution)/shard_map/ppermute | solution.py:72
  9.5 7.3 %collective-permute-start.3 = (bf16[16,3584]{1,0:T(8,128)(2,1)S(1)}, bf16[16,3584]{1,0:T(8,128)(2,1)S(1)}, u32[]{:S(2)}, u32[]{:S(2)}) collective-permute-start(bf16[16,3584]{1,0:T(8,128)(2,1)S(1)} %reshape.300), channel_id=1, source_target_pairs={{0,8},{8,16},{16,24},{24,0},{32,40},{40,48},{48,56},{56,32},{64,72... | collective-permute-start | bytes 344072 | tf_op jit(solution)/shard_map/ppermute | solution.py:72
  11.1 7.4 %collective-permute-start.4 = (bf16[16,3584]{1,0:T(8,128)(2,1)S(1)}, bf16[16,3584]{1,0:T(8,128)(2,1)S(1)}, u32[]{:S(2)}, u32[]{:S(2)}) collective-permute-start(bf16[16,3584]{1,0:T(8,128)(2,1)S(1)} %reshape.300), channel_id=1, source_target_pairs={{0,16},{8,24},{16,0},{24,8},{32,48},{40,56},{48,32},{56,40},{64,80... | collective-permute-start | bytes 344072 | tf_op jit(solution)/shard_map/ppermute | solution.py:72
  14.0 4.8 %collective-permute-start.5 = (bf16[16,3584]{1,0:T(8,128)(2,1)S(1)}, bf16[16,3584]{1,0:T(8,128)(2,1)S(1)}, u32[]{:S(2)}, u32[]{:S(2)}) collective-permute-start(bf16[16,3584]{1,0:T(8,128)(2,1)S(1)} %reshape.300), channel_id=1, source_target_pairs={{0,24},{8,0},{16,8},{24,16},{32,56},{40,32},{48,40},{56,48},{64,88... | collective-permute-start | bytes 344072 | tf_op jit(solution)/shard_map/ppermute | solution.py:72
  18.9 14.6 %collective-permute-start.6 = (bf16[64,3584]{1,0:T(8,128)(2,1)S(1)}, bf16[64,3584]{1,0:T(8,128)(2,1)S(1)}, u32[]{:S(2)}, u32[]{:S(2)}) collective-permute-start(bf16[64,3584]{1,0:T(8,128)(2,1)S(1)} %bitcast.180), channel_id=1, source_target_pairs={{0,2},{1,3},{2,4},{3,5},{4,6},{5,7},{6,0},{7,1},{8,10},{9,11},{10,... | collective-permute-start | bytes 1376264 | tf_op jit(solution)/shard_map/ppermute | solution.py:72
  20.9 22.5 %collective-permute-start.7 = (bf16[64,3584]{1,0:T(8,128)(2,1)S(1)}, bf16[64,3584]{1,0:T(8,128)(2,1)S(1)}, u32[]{:S(2)}, u32[]{:S(2)}) collective-permute-start(bf16[64,3584]{1,0:T(8,128)(2,1)S(1)} %bitcast.181), channel_id=1, source_target_pairs={{0,4},{1,5},{2,6},{3,7},{4,0},{5,1},{6,2},{7,3},{8,12},{9,13},{10,... | collective-permute-start | bytes 1376264 | tf_op jit(solution)/shard_map/ppermute | solution.py:72
  24.4 18.9 %collective-permute-start.8 = (bf16[64,3584]{1,0:T(8,128)(2,1)S(1)}, bf16[64,3584]{1,0:T(8,128)(2,1)S(1)}, u32[]{:S(2)}, u32[]{:S(2)}) collective-permute-start(bf16[64,3584]{1,0:T(8,128)(2,1)S(1)} %bitcast.182), channel_id=1, source_target_pairs={{0,6},{1,7},{2,0},{3,1},{4,2},{5,3},{6,4},{7,5},{8,14},{9,15},{10,... | collective-permute-start | bytes 1376264 | tf_op jit(solution)/shard_map/ppermute | solution.py:72
  43.4 0.8 copy-start.2
  43.4 0.9 copy-start.3
  44.3 4.7 %copy-start.1 = (f32[512,64]{0,1:T(8,128)S(1)}, f32[512,64]{0,1:T(8,128)}, u32[]{:S(2)}) copy-start(f32[512,64]{0,1:T(8,128)} %param.13) | copy-start | bytes 393220
  45.7 13.1 %collective-permute-start.9 = (bf16[256,3584]{1,0:T(8,128)(2,1)S(1)}, bf16[256,3584]{1,0:T(8,128)(2,1)}, u32[]{:S(2)}, u32[]{:S(2)}) collective-permute-start(bf16[256,3584]{1,0:T(8,128)(2,1)S(1)} %bitcast.176), channel_id=1, source_target_pairs={{0,1},{1,0},{2,3},{3,2},{4,5},{5,4},{6,7},{7,6},{8,9},{9,8},{10,11... | collective-permute-start | bytes 5505032 | tf_op jit(solution)/shard_map/ppermute | solution.py:72
  60.7 8.9 %copy-start = (bf16[2,256,3584]{2,1,0:T(8,128)(2,1)}, bf16[2,256,3584]{2,1,0:T(8,128)(2,1)S(1)}, u32[]{:S(2)}) copy-start(bf16[2,256,3584]{2,1,0:T(8,128)(2,1)S(1)} %pad_maximum_fusion) | copy-start | bytes 11010052
  76.1 1.4 collective-permute-start.10
  78.2 4.9 %collective-permute-start.11 = (f32[3,512]{1,0:T(4,128)S(1)}, f32[3,512]{1,0:T(4,128)S(1)}, u32[]{:S(2)}, u32[]{:S(2)}) collective-permute-start(f32[3,512]{1,0:T(4,128)S(1)} %get-tuple-element.144), channel_id=1, source_target_pairs={{0,2},{1,3},{2,4},{3,5},{4,6},{5,7},{6,0},{7,1},{8,10},{9,11},{10,... | collective-permute-start | bytes 18440 | tf_op jit(solution)/shard_map/ppermute | solution.py:72
  79.3 5.2 %collective-permute-start.12 = (f32[3,512]{1,0:T(4,128)S(1)}, f32[3,512]{1,0:T(4,128)S(1)}, u32[]{:S(2)}, u32[]{:S(2)}) collective-permute-start(f32[3,512]{1,0:T(4,128)S(1)} %get-tuple-element.144), channel_id=1, source_target_pairs={{0,4},{1,5},{2,6},{3,7},{4,0},{5,1},{6,2},{7,3},{8,12},{9,13},{10,... | collective-permute-start | bytes 18440 | tf_op jit(solution)/shard_map/ppermute | solution.py:72
  81.7 3.7 %collective-permute-start.13 = (f32[3,512]{1,0:T(4,128)S(1)}, f32[3,512]{1,0:T(4,128)S(1)}, u32[]{:S(2)}, u32[]{:S(2)}) collective-permute-start(f32[3,512]{1,0:T(4,128)S(1)} %get-tuple-element.144), channel_id=1, source_target_pairs={{0,6},{1,7},{2,0},{3,1},{4,2},{5,3},{6,4},{7,5},{8,14},{9,15},{10,... | collective-permute-start | bytes 18440 | tf_op jit(solution)/shard_map/ppermute | solution.py:72
  86.1 4.9 %collective-permute-start.14 = (f32[3,512]{1,0:T(4,128)S(1)}, f32[3,512]{1,0:T(4,128)S(1)}, u32[]{:S(2)}, u32[]{:S(2)}) collective-permute-start(f32[3,512]{1,0:T(4,128)S(1)} %get-tuple-element.142), channel_id=1, source_target_pairs={{0,8},{8,16},{16,24},{24,0},{32,40},{40,48},{48,56},{56,32},{64,72... | collective-permute-start | bytes 18440 | tf_op jit(solution)/shard_map/ppermute | solution.py:72
  86.2 5.6 %collective-permute-start.15 = (f32[3,512]{1,0:T(4,128)S(1)}, f32[3,512]{1,0:T(4,128)S(1)}, u32[]{:S(2)}, u32[]{:S(2)}) collective-permute-start(f32[3,512]{1,0:T(4,128)S(1)} %get-tuple-element.142), channel_id=1, source_target_pairs={{0,16},{8,24},{16,0},{24,8},{32,48},{40,56},{48,32},{56,40},{64,80... | collective-permute-start | bytes 18440 | tf_op jit(solution)/shard_map/ppermute | solution.py:72
  90.1 3.7 %collective-permute-start.16 = (f32[3,512]{1,0:T(4,128)S(1)}, f32[3,512]{1,0:T(4,128)S(1)}, u32[]{:S(2)}, u32[]{:S(2)}) collective-permute-start(f32[3,512]{1,0:T(4,128)S(1)} %get-tuple-element.142), channel_id=1, source_target_pairs={{0,24},{8,0},{16,8},{24,16},{32,56},{40,32},{48,40},{56,48},{64,88... | collective-permute-start | bytes 18440 | tf_op jit(solution)/shard_map/ppermute | solution.py:72
  94.5 4.9 %collective-permute-start.17 = (f32[3,512]{1,0:T(4,128)S(1)}, f32[3,512]{1,0:T(4,128)S(1)}, u32[]{:S(2)}, u32[]{:S(2)}) collective-permute-start(f32[3,512]{1,0:T(4,128)S(1)} %get-tuple-element.140), channel_id=1, source_target_pairs={{0,32},{8,40},{16,48},{24,56},{32,64},{40,72},{48,80},{56,88},{64,... | collective-permute-start | bytes 18440 | tf_op jit(solution)/shard_map/ppermute | solution.py:72
  95.2 5.2 %collective-permute-start.18 = (f32[3,512]{1,0:T(4,128)S(1)}, f32[3,512]{1,0:T(4,128)S(1)}, u32[]{:S(2)}, u32[]{:S(2)}) collective-permute-start(f32[3,512]{1,0:T(4,128)S(1)} %get-tuple-element.140), channel_id=1, source_target_pairs={{0,64},{8,72},{16,80},{24,88},{32,96},{40,104},{48,112},{56,120},{... | collective-permute-start | bytes 18440 | tf_op jit(solution)/shard_map/ppermute | solution.py:72
  96.7 3.7 %collective-permute-start.19 = (f32[3,512]{1,0:T(4,128)S(1)}, f32[3,512]{1,0:T(4,128)S(1)}, u32[]{:S(2)}, u32[]{:S(2)}) collective-permute-start(f32[3,512]{1,0:T(4,128)S(1)} %get-tuple-element.140), channel_id=1, source_target_pairs={{0,96},{8,104},{16,112},{24,120},{32,0},{40,8},{48,16},{56,24},{64... | collective-permute-start | bytes 18440 | tf_op jit(solution)/shard_map/ppermute | solution.py:72
  114.1 4.1 %collective-permute-start.20 = (bf16[256,3584]{1,0:T(8,128)(2,1)S(1)}, bf16[256,3584]{1,0:T(8,128)(2,1)S(1)}, u32[]{:S(2)}, u32[]{:S(2)}) collective-permute-start(bf16[256,3584]{1,0:T(8,128)(2,1)S(1)} %slice.277), channel_id=1, source_target_pairs={{0,1},{1,0},{2,3},{3,2},{4,5},{5,4},{6,7},{7,6},{8,9},{9,8},{10,11... | collective-permute-start | bytes 5505032 | tf_op jit(solution)/shard_map/ppermute | solution.py:72
  118.9 14.0 %collective-permute-start.21 = (bf16[64,3584]{1,0:T(8,128)(2,1)S(1)}, bf16[64,3584]{1,0:T(8,128)(2,1)S(1)}, u32[]{:S(2)}, u32[]{:S(2)}) collective-permute-start(bf16[64,3584]{1,0:T(8,128)(2,1)S(1)} %get-tuple-element.116), channel_id=1, source_target_pairs={{0,2},{1,3},{2,4},{3,5},{4,6},{5,7},{6,0},{7,1},{8,10},{9,11},{10,... | collective-permute-start | bytes 1376264 | tf_op jit(solution)/shard_map/ppermute | solution.py:72
  119.6 23.7 %collective-permute-start.22 = (bf16[64,3584]{1,0:T(8,128)(2,1)S(1)}, bf16[64,3584]{1,0:T(8,128)(2,1)S(1)}, u32[]{:S(2)}, u32[]{:S(2)}) collective-permute-start(bf16[64,3584]{1,0:T(8,128)(2,1)S(1)} %get-tuple-element.118), channel_id=1, source_target_pairs={{0,4},{1,5},{2,6},{3,7},{4,0},{5,1},{6,2},{7,3},{8,12},{9,13},{10,... | collective-permute-start | bytes 1376264 | tf_op jit(solution)/shard_map/ppermute | solution.py:72
  122.9 20.4 %collective-permute-start.23 = (bf16[64,3584]{1,0:T(8,128)(2,1)S(1)}, bf16[64,3584]{1,0:T(8,128)(2,1)S(1)}, u32[]{:S(2)}, u32[]{:S(2)}) collective-permute-start(bf16[64,3584]{1,0:T(8,128)(2,1)S(1)} %get-tuple-element.117), channel_id=1, source_target_pairs={{0,6},{1,7},{2,0},{3,1},{4,2},{5,3},{6,4},{7,5},{8,14},{9,15},{10,... | collective-permute-start | bytes 1376264 | tf_op jit(solution)/shard_map/ppermute | solution.py:72
  143.7 7.3 %collective-permute-start.24 = (bf16[16,3584]{1,0:T(8,128)(2,1)S(1)}, bf16[16,3584]{1,0:T(8,128)(2,1)S(1)}, u32[]{:S(2)}, u32[]{:S(2)}) collective-permute-start(bf16[16,3584]{1,0:T(8,128)(2,1)S(1)} %get-tuple-element.119), channel_id=1, source_target_pairs={{0,8},{8,16},{16,24},{24,0},{32,40},{40,48},{48,56},{56,32},{64,72... | collective-permute-start | bytes 344072 | tf_op jit(solution)/shard_map/ppermute | solution.py:72
  143.9 8.2 %collective-permute-start.25 = (bf16[16,3584]{1,0:T(8,128)(2,1)S(1)}, bf16[16,3584]{1,0:T(8,128)(2,1)S(1)}, u32[]{:S(2)}, u32[]{:S(2)}) collective-permute-start(bf16[16,3584]{1,0:T(8,128)(2,1)S(1)} %get-tuple-element.121), channel_id=1, source_target_pairs={{0,16},{8,24},{16,0},{24,8},{32,48},{40,56},{48,32},{56,40},{64,80... | collective-permute-start | bytes 344072 | tf_op jit(solution)/shard_map/ppermute | solution.py:72
  147.4 5.0 %collective-permute-start.26 = (bf16[16,3584]{1,0:T(8,128)(2,1)S(1)}, bf16[16,3584]{1,0:T(8,128)(2,1)S(1)}, u32[]{:S(2)}, u32[]{:S(2)}) collective-permute-start(bf16[16,3584]{1,0:T(8,128)(2,1)S(1)} %get-tuple-element.120), channel_id=1, source_target_pairs={{0,24},{8,0},{16,8},{24,16},{32,56},{40,32},{48,40},{56,48},{64,88... | collective-permute-start | bytes 344072 | tf_op jit(solution)/shard_map/ppermute | solution.py:72
  152.6 13.8 %collective-permute-start.27 = (bf16[4,3584]{1,0:T(4,128)(2,1)S(1)}, bf16[4,3584]{1,0:T(4,128)(2,1)S(1)}, u32[]{:S(2)}, u32[]{:S(2)}) collective-permute-start(bf16[4,3584]{1,0:T(4,128)(2,1)S(1)} %get-tuple-element.126), channel_id=1, source_target_pairs={{0,32},{8,40},{16,48},{24,56},{32,64},{40,72},{48,80},{56,88},{64,... | collective-permute-start | bytes 86024 | tf_op jit(solution)/shard_map/ppermute | solution.py:72
  154.5 11.8 %collective-permute-start.28 = (bf16[4,3584]{1,0:T(4,128)(2,1)S(1)}, bf16[4,3584]{1,0:T(4,128)(2,1)S(1)}, u32[]{:S(2)}, u32[]{:S(2)}) collective-permute-start(bf16[4,3584]{1,0:T(4,128)(2,1)S(1)} %get-tuple-element.128), channel_id=1, source_target_pairs={{0,64},{8,72},{16,80},{24,88},{32,96},{40,104},{48,112},{56,120},{... | collective-permute-start | bytes 86024 | tf_op jit(solution)/shard_map/ppermute | solution.py:72
  156.6 9.7 %collective-permute-start.29 = (bf16[4,3584]{1,0:T(4,128)(2,1)S(1)}, bf16[4,3584]{1,0:T(4,128)(2,1)S(1)}, u32[]{:S(2)}, u32[]{:S(2)}) collective-permute-start(bf16[4,3584]{1,0:T(4,128)(2,1)S(1)} %get-tuple-element.127), channel_id=1, source_target_pairs={{0,96},{8,104},{16,112},{24,120},{32,0},{40,8},{48,16},{56,24},{64... | collective-permute-start | bytes 86024 | tf_op jit(solution)/shard_map/ppermute | solution.py:72

commit v2 on v1

--- a/solution.py
+++ b/solution.py
@@ -73,29 +73,24 @@
     return jnp.stack(got)
 
 
-def ring_order(me, n):
-    if n == 2:
-        return jnp.arange(2, dtype=jnp.int32) ^ me
-    return (me - jnp.arange(n, dtype=jnp.int32)) % n
+def arrival_tokens(at):
+    r = jnp.arange(2 * RING ** 3 * 4, dtype=jnp.int32)
+    i = r % 4
+    x = (at["x"] - (r // 4) % RING) % RING
+    y = (at["y"] - (r // 16) % RING) % RING
+    z = (at["z"] - (r // 64) % RING) % RING
+    c = at["c"] ^ (r // 256)
+    return (((x * RING + y) * RING + z) * 2 + c) * 4 + i
 
 
-def to_arrival(nat, at):
-    rest = nat.shape[1:]
-    a = nat.reshape((RING, RING, RING, 2, -1) + rest)
-    for axis, stage, n in ((0, "x", RING), (1, "y", RING), (2, "z", RING), (3, "c", 2)):
-        a = jnp.take(a, ring_order(at[stage], n), axis=axis)
-    a = jnp.transpose(a, (3, 2, 1, 0) + tuple(range(4, a.ndim)))
-    return a.reshape(nat.shape)
-
-
-def to_natural(arr, at):
-    lead = arr.shape[:-1]
-    k = len(lead)
-    a = arr.reshape(lead + (2, RING, RING, RING, -1))
-    for axis, stage, n in ((k, "c", 2), (k + 1, "z", RING), (k + 2, "y", RING), (k + 3, "x", RING)):
-        a = jnp.take(a, ring_order(at[stage], n), axis=axis)
-    perm = tuple(range(k)) + (k + 3, k + 2, k + 1, k, k + 4)
-    return jnp.transpose(a, perm).reshape(arr.shape)
+def natural_rows(at):
+    t = jnp.arange(2 * RING ** 3 * 4, dtype=jnp.int32)
+    i = t % 4
+    s_c = at["c"] ^ ((t // 4) % 2)
+    s_z = (at["z"] - (t // 8) % RING) % RING
+    s_y = (at["y"] - (t // 32) % RING) % RING
+    s_x = (at["x"] - (t // 128) % RING) % RING
+    return (((s_c * RING + s_z) * RING + s_y) * RING + s_x) * 4 + i
 
 
 def per_device(hidden_rows, head_weight, teacher_index, teacher_logprob, tok_n, voc_n):
@@ -104,30 +99,32 @@
     width = hidden_rows.shape[1]
     at = coords()
 
+    position = lax.axis_index(("tok", "voc"))
+    offset = position * voc_dev
+    rows = arrival_tokens(at)
+    index_arr = jnp.take(teacher_index, rows, axis=0)
+    logprob_arr = jnp.take(teacher_logprob, rows, axis=0)
+    local = index_arr - offset
+    probs_arr = jnp.exp(logprob_arr)
+    target = teacher_target(local, probs_arr, voc_dev)
+
     every = hidden_rows
     for stage in ("x", "y", "z", "c"):
         got = exchange(lambda s: every, stage, tok_n, voc_n)
         every = got.reshape(-1, width)
+        if stage == "z":
+            every, target = lax.optimization_barrier((every, target))
 
     logits = lax.dot_general(
         every, head_weight, (((1,), (1,)), ((), ())), preferred_element_type=jnp.float32
     )
-    position = lax.axis_index(("tok", "voc"))
-    offset = position * voc_dev
-    index_arr = to_arrival(teacher_index, at)
-    logprob_arr = to_arrival(teacher_logprob, at)
-    local = index_arr - offset
-    probs_arr = jnp.exp(logprob_arr)
-    target = teacher_target(local, probs_arr, voc_dev)
     part_dot = jnp.sum(logits * target, axis=1)
     local_peak = jnp.max(logits, axis=1)
     local_sum = jnp.sum(jnp.exp(logits - local_peak[:, None]), axis=1)
 
-    stats = to_natural(jnp.stack([local_peak, local_sum, part_dot]), at)
+    stats = jnp.take(jnp.stack([local_peak, local_sum, part_dot]), natural_rows(at), axis=1)
     for stage in ("c", "z", "y", "x"):
-        n = 2 if stage == "c" else RING
         got = exchange(lambda s: stats, stage, tok_n, voc_n)
-        got = jnp.take(got, ring_order(at[stage], n), axis=0)
         peak = jnp.max(got[:, 0], axis=0)
         summed = jnp.sum(got[:, 1] * jnp.exp(got[:, 0] - peak[None]), axis=0)
         dotted = jnp.sum(got[:, 2], axis=0)
@@ -140,7 +137,7 @@
     own_term = jnp.sum(probs * teacher_logprob, axis=1)
     loss_all = own_term - dotted + total_p * lse
     row_loss = lax.dynamic_slice_in_dim(loss_all, position * tok_dev, tok_dev, 0)
-    lse_arr = to_arrival(lse, at)
+    lse_arr = jnp.take(lse, rows, axis=0)
     total_arr = jnp.sum(probs_arr, axis=1)
     grad = (loss_scale * (total_arr[:, None] * jnp.exp(logits - lse_arr[:, None]) - target)).astype(
         jnp.bfloat16
@@ -155,6 +152,8 @@
         n = acc.shape[0]
         got = exchange(lambda s: acc[(-s) % n].astype(jnp.bfloat16), stage, tok_n, voc_n)
         acc = acc[0] + jnp.sum(got[1:].astype(jnp.float32), axis=0)
+        if stage == "z":
+            acc, head_grad = lax.optimization_barrier((acc, head_grad))
         if stage != "x":
             acc = acc.reshape(RING, -1, width)
     return (row_loss, head_grad, acc.astype(jnp.bfloat16))

time: 167 us -> 148 us (0.89)
  local copies, waits for them, and re-layouts: 18.3 us -> 9.46 us
  starting transfers between devices: 44.7 us -> 37.4 us
  other arithmetic: 19.8 us -> 14.8 us
  waiting for transfers between devices: 57.5 us -> 61.8 us
  matrix products: 24.6 us -> 22.9 us
    ppermute x30, starting transfers between devices: 44.7 us -> 37.4 us  [exchange(): got.append(lax.ppermute(block_for(shift), axis, pairs))]
    gather x20 -> x4, local copies, waits for them, and re-layouts: 13 us -> 6.6 us  [the longest x1 3.49 us: per_device(): lse_arr = jnp.take(lse, rows, axis=0)]
    ppermute x30, waiting for transfers between devices: 57.5 us -> 61.8 us  [exchange(): got.append(lax.ppermute(block_for(shift), axis, pairs))]
    sub x1 -> x0, other arithmetic: 2.36 us -> none  [per_device(): local = index_arr - offset]
    another operation x11 -> x10, other arithmetic: 3.49 us -> 1.6 us  [exchange(): return jnp.stack(got)]
    dot_general x1, matrix products: 8.47 us -> 6.71 us  [per_device(): lax.dot_general(grad, every, (((0,), (0,)), ((), ())), preferred_element_...]
  transfers between devices with their start and end apart: 30 -> 30, of which waited for: 21 -> 23; matrix products, arithmetic and copies ran while one was open for 15% -> 12% of each run, Pallas kernels for 0% -> 0%
where the time goes in v2:
time: 148 us
  waiting for transfers between devices  61.8 us (42%)
  starting transfers between devices  37.4 us (25%)
  matrix products  22.9 us (15%)
  other arithmetic  14.8 us (10%)
  local copies, waits for them, and re-layouts  9.46 us (6%)
  between operations  1.7 us (1%)
    ppermute x30, waiting for transfers between devices, exchange(): got.append(lax.ppermute(block_for(shift), axis, pairs))  61.8 us
    ppermute x30, starting transfers between devices, exchange(): got.append(lax.ppermute(block_for(shift), axis, pairs))  37.4 us
    dot_general x1, matrix products, per_device(): lax.dot_general(every, head_weight, (((1,), (1,)), ((), ())), preferred_e...  8.86 us
    dot_general x1, matrix products, per_device(): partial = jnp.dot(grad, head_weight, preferred_element_type=jnp.float32)  7.3 us
    dot_general x1, matrix products, per_device(): lax.dot_general(grad, every, (((0,), (0,)), ((), ())), preferred_element_...  6.71 us
    add x1, other arithmetic, compact_target(): target + jnp.where(slot_local[:, j:j + 1] == columns, slot_probs[:, j:j +...  3.58 us
    gather x1, local copies, waits for them, and re-layouts, per_device(): lse_arr = jnp.take(lse, rows, axis=0)  3.49 us
  transfers between devices with their start and end apart: 30, of which 23 were waited for; matrix products, arithmetic and copies ran while one was open for 12% of the time, Pallas kernels for 0%

profile of v2, /device:TPU:0, one launch (start us, length us, event | category | flops | bytes accessed | tf_op | source)
XLA Modules:
  0.0 148.2 jit_solution(499552060713683915)
XLA Ops:
  0.6 2.9 %collective-permute-start.2 = (bf16[4,3584]{1,0:T(4,128)(2,1)}, bf16[4,3584]{1,0:T(4,128)(2,1)S(1)}, u32[]{:S(2)}, u32[]{:S(2)}) collective-permute-start(bf16[4,3584]{1,0:T(4,128)(2,1)} %param.8), channel_id=1, source_target_pairs={{0,96},{8,104},{16,112},{24,120},{32,0},{40,8},{48,16},{56,24},{64... | collective-permute-start | bytes 86024 | tf_op jit(solution)/shard_map/ppermute | solution.py:72
  3.5 0.8 collective-permute-start.1
  4.3 0.9 collective-permute-start
  5.3 3.8 %collective-permute-done.1 = bf16[4,3584]{1,0:T(4,128)(2,1)S(1)} collective-permute-done((bf16[4,3584]{1,0:T(4,128)(2,1)}, bf16[4,3584]{1,0:T(4,128)(2,1)S(1)}, u32[]{:S(2)}, u32[]{:S(2)}) %collective-permute-start.1) | collective-permute-done | bytes 28704 | tf_op jit(solution)/shard_map/ppermute | solution.py:72
  9.6 0.8 pad_maximum_fusion.3
  10.5 3.1 %collective-permute-start.5 = (bf16[16,3584]{1,0:T(8,128)(2,1)S(1)}, bf16[16,3584]{1,0:T(8,128)(2,1)S(1)}, u32[]{:S(2)}, u32[]{:S(2)}) collective-permute-start(bf16[16,3584]{1,0:T(8,128)(2,1)S(1)} %reshape.838), channel_id=1, source_target_pairs={{0,24},{8,0},{16,8},{24,16},{32,56},{40,32},{48,40},{56,48},{64,88... | collective-permute-start | bytes 344072 | tf_op jit(solution)/shard_map/ppermute | solution.py:72
  14.2 1.0 collective-permute-start.3
  15.2 1.0 copy.53
  16.3 1.0 gather_fusion
  17.4 2.6 %collective-permute-done.4 = bf16[16,3584]{1,0:T(8,128)(2,1)S(1)} collective-permute-done((bf16[16,3584]{1,0:T(8,128)(2,1)S(1)}, bf16[16,3584]{1,0:T(8,128)(2,1)S(1)}, u32[]{:S(2)}, u32[]{:S(2)}) %collective-permute-start.4) | collective-permute-done | bytes 114720 | tf_op jit(solution)/shard_map/ppermute | solution.py:72
  20.0 1.1 collective-permute-done.3
  21.2 4.1 %collective-permute-start.8 = (bf16[64,3584]{1,0:T(8,128)(2,1)S(1)}, bf16[64,3584]{1,0:T(8,128)(2,1)S(1)}, u32[]{:S(2)}, u32[]{:S(2)}) collective-permute-start(bf16[64,3584]{1,0:T(8,128)(2,1)S(1)} %bitcast.145), channel_id=1, source_target_pairs={{0,6},{1,7},{2,0},{3,1},{4,2},{5,3},{6,4},{7,5},{8,14},{9,15},{10,... | collective-permute-start | bytes 1376264 | tf_op jit(solution)/shard_map/ppermute | solution.py:72
  25.3 1.3 collective-permute-start.6
  28.2 1.0 gather_fusion.1
  29.5 4.6 %conditional.1 = (f32[512,1152]{1,0:T(8,128)}) conditional(s32[]{:T(128)} %convert_element_type.42, (s32[512,64]{1,0:T(8,128)S(1)}, f32[512,64]{1,0:T(8,128)S(1)}) %tuple.20, (s32[512,64]{1,0:T(8,128)S(1)}, f32[512,64]{1,0:T(8,128)S(1)}) %tuple.20), branch_computations={%region_3.7_spmd, %region_7.11_spmd} | conditional | flops 17883136 | bytes 4423692 | solution.py:44
  30.5 3.6 %select_add_fusion = f32[512,1152]{1,0:T(8,128)} fusion(f32[512]{0:T(512)S(1)} %bitcast.178, s32[512]{0:T(512)S(1)} %bitcast.186, f32[512]{0:T(512)S(1)} %bitcast.179, s32[512]{0:T(512)S(1)} %bitcast.187, f32[512]{0:T(512)S(1)} %bitcast.180, s32[512]{0:T(512)S(1)} %bitcast.188, f32[512]{0:T(512)S(1)} %bitcast.181, s32[512]{0:T(512)S(1)} %bitcast.189, ...), kind=kLoop, calls=%fused_computation.5 | loop fusion | flops 13565952 | bytes 2392064 | tf_op jit(solution)/shard_map/cond/branch_0_fun/add | solution.py:37
  34.1 7.7 %collective-permute-done.8 = bf16[64,3584]{1,0:T(8,128)(2,1)S(1)} collective-permute-done((bf16[64,3584]{1,0:T(8,128)(2,1)S(1)}, bf16[64,3584]{1,0:T(8,128)(2,1)S(1)}, u32[]{:S(2)}, u32[]{:S(2)}) %collective-permute-start.8) | collective-permute-done | bytes 458784 | tf_op jit(solution)/shard_map/ppermute | solution.py:72
  41.9 3.4 %collective-permute-done.6 = bf16[64,3584]{1,0:T(8,128)(2,1)S(1)} collective-permute-done((bf16[64,3584]{1,0:T(8,128)(2,1)S(1)}, bf16[64,3584]{1,0:T(8,128)(2,1)S(1)}, u32[]{:S(2)}, u32[]{:S(2)}) %collective-permute-start.6) | collective-permute-done | bytes 458784 | tf_op jit(solution)/shard_map/ppermute | solution.py:72
  45.6 3.8 %collective-permute-done.9 = bf16[256,3584]{1,0:T(8,128)(2,1)S(1)} collective-permute-done((bf16[256,3584]{1,0:T(8,128)(2,1)S(1)}, bf16[256,3584]{1,0:T(8,128)(2,1)S(1)}, u32[]{:S(2)}, u32[]{:S(2)}) %collective-permute-start.9) | collective-permute-done | bytes 1835040 | tf_op jit(solution)/shard_map/ppermute | solution.py:72
  49.7 8.9 %fusion.115 = (f32[512]{0:T(512)S(1)}, f32[512,1152]{1,0:T(8,128)S(1)}) fusion(bf16[512,3584]{1,0:T(8,128)(2,1)S(1)} %bitcast.142, bf16[1152,3584]{1,0:T(8,128)(2,1)} %param.9), kind=kOutput, calls=%fused_computation.317 | convolution fusion | flops 4228447744 | bytes 14288896 | tf_op jit(solution)/shard_map/dot_general | solution.py:118
  58.6 2.4 %exponential_reduce_fusion = (f32[512]{0:T(512)S(1)}, f32[512]{0:T(512)S(1)}) fusion(f32[512,1152]{1,0:T(8,128)S(1)} %get-tuple-element.138, f32[512]{0:T(512)S(1)} %get-tuple-element.137, f32[512,1152]{1,0:T(8,128)} %get-tuple-element.183), kind=kLoop, calls=%fused_computation.32 | loop fusion | flops 2358272 | bytes 4724736 | tf_op jit(solution)/shard_map/reduce_sum | solution.py:123
  61.2 1.0 gather_fusion.2
  64.9 1.2 collective-permute-start.11
  66.1 2.1 %collective-permute-start.13 = (f32[3,512]{1,0:T(4,128)S(1)}, f32[3,512]{1,0:T(4,128)S(1)}, u32[]{:S(2)}, u32[]{:S(2)}) collective-permute-start(f32[3,512]{1,0:T(4,128)S(1)} %get-tuple-element.136), channel_id=1, source_target_pairs={{0,6},{1,7},{2,0},{3,1},{4,2},{5,3},{6,4},{7,5},{8,14},{9,15},{10,... | collective-permute-start | bytes 18440 | tf_op jit(solution)/shard_map/ppermute | solution.py:72
  68.1 1.3 collective-permute-done.12
  69.9 0.9 collective-permute-start.15
  70.8 0.9 collective-permute-start.14
  71.7 2.3 %collective-permute-start.16 = (f32[3,512]{1,0:T(4,128)S(1)}, f32[3,512]{1,0:T(4,128)S(1)}, u32[]{:S(2)}, u32[]{:S(2)}) collective-permute-start(f32[3,512]{1,0:T(4,128)S(1)} %get-tuple-element.134), channel_id=1, source_target_pairs={{0,24},{8,0},{16,8},{24,16},{32,56},{40,32},{48,40},{56,48},{64,88... | collective-permute-start | bytes 18440 | tf_op jit(solution)/shard_map/ppermute | solution.py:72
  74.0 1.1 collective-permute-done.15
  75.8 0.8 collective-permute-start.19
  76.5 1.0 collective-permute-start.18
  77.6 1.2 collective-permute-start.17
  78.8 2.9 %collective-permute-done.18 = f32[3,512]{1,0:T(4,128)S(1)} collective-permute-done((f32[3,512]{1,0:T(4,128)S(1)}, f32[3,512]{1,0:T(4,128)S(1)}, u32[]{:S(2)}, u32[]{:S(2)}) %collective-permute-start.18) | collective-permute-done | bytes 6176 | tf_op jit(solution)/shard_map/ppermute | solution.py:72
  82.6 3.5 %gather_fusion.3 = f32[512]{0:T(512)S(1)} fusion(f32[512]{0:T(512)S(1)} %get-tuple-element.100, s32[1024]{0:T(1024)S(1)} %pad_clamp_fusion.1), kind=kCustom, calls=%fused_computation.3 | custom fusion | bytes 6144 | tf_op jit(solution)/shard_map/jit(_take)/gather | solution.py:140
  86.1 2.3 %multiply_convert_fusion = bf16[512,1152]{1,0:T(8,128)(2,1)S(1)} fusion(f32[512,1152]{1,0:T(8,128)} %get-tuple-element.183, f32[512,1152]{1,0:T(8,128)S(1)} %get-tuple-element.138, f32[512]{0:T(512)S(1)} %broadcast_select_fusion, f32[512]{0:T(512)S(1)} %get-tuple-element.97), kind=kLoop, calls=%fused_computation.30 | loop fusion | flops 2949120 | bytes 5902336 | tf_op jit(solution)/shard_map/convert_element_type | solution.py:142
  88.4 7.3 %fusion.116 = f32[512,3584]{1,0:T(8,128)S(1)} fusion(bf16[512,1152]{1,0:T(8,128)(2,1)S(1)} %multiply_convert_fusion, bf16[1152,3584]{1,0:T(8,128)(2,1)} %param.9), kind=kOutput, calls=%fused_computation.318 | convolution fusion | flops 4227858432 | bytes 16777216 | tf_op jit(solution)/shard_map/dot_general | solution.py:145
  96.0 3.8 %collective-permute-done.20 = bf16[256,3584]{1,0:T(8,128)(2,1)S(1)} collective-permute-done((bf16[256,3584]{1,0:T(8,128)(2,1)S(1)}, bf16[256,3584]{1,0:T(8,128)(2,1)S(1)}, u32[]{:S(2)}, u32[]{:S(2)}) %collective-permute-start.20) | collective-permute-done | bytes 1835040 | tf_op jit(solution)/shard_map/ppermute | solution.py:72
  100.5 3.3 %collective-permute-start.23 = (bf16[64,3584]{1,0:T(8,128)(2,1)S(1)}, bf16[64,3584]{1,0:T(8,128)(2,1)S(1)}, u32[]{:S(2)}, u32[]{:S(2)}) collective-permute-start(bf16[64,3584]{1,0:T(8,128)(2,1)S(1)} %get-tuple-element.122), channel_id=1, source_target_pairs={{0,6},{1,7},{2,0},{3,1},{4,2},{5,3},{6,4},{7,5},{8,14},{9,15},{10,... | collective-permute-start | bytes 1376264 | tf_op jit(solution)/shard_map/ppermute | solution.py:72
  104.7 6.7 %convolution_convert_fusion = bf16[1152,3584]{1,0:T(8,128)(2,1)} fusion(bf16[512,1152]{1,0:T(8,128)(2,1)S(1)} %multiply_convert_fusion, bf16[512,3584]{1,0:T(8,128)(2,1)S(1)} %bitcast.143), kind=kOutput, calls=%fused_computation.25 | convolution fusion | flops 4231987200 | bytes 13107200 | tf_op jit(solution)/shard_map/dot_general | solution.py:146
  111.4 12.2 %collective-permute-done.23 = bf16[64,3584]{1,0:T(8,128)(2,1)S(1)} collective-permute-done((bf16[64,3584]{1,0:T(8,128)(2,1)S(1)}, bf16[64,3584]{1,0:T(8,128)(2,1)S(1)}, u32[]{:S(2)}, u32[]{:S(2)}) %collective-permute-start.23) | collective-permute-done | bytes 458784 | tf_op jit(solution)/shard_map/ppermute | solution.py:72
  123.7 3.7 %collective-permute-done.21 = bf16[64,3584]{1,0:T(8,128)(2,1)S(1)} collective-permute-done((bf16[64,3584]{1,0:T(8,128)(2,1)S(1)}, bf16[64,3584]{1,0:T(8,128)(2,1)S(1)}, u32[]{:S(2)}, u32[]{:S(2)}) %collective-permute-start.21) | collective-permute-done | bytes 458784 | tf_op jit(solution)/shard_map/ppermute | solution.py:72
  127.8 3.3 %collective-permute-start.26 = (bf16[16,3584]{1,0:T(8,128)(2,1)S(1)}, bf16[16,3584]{1,0:T(8,128)(2,1)S(1)}, u32[]{:S(2)}, u32[]{:S(2)}) collective-permute-start(bf16[16,3584]{1,0:T(8,128)(2,1)S(1)} %get-tuple-element.125), channel_id=1, source_target_pairs={{0,24},{8,0},{16,8},{24,16},{32,56},{40,32},{48,40},{56,48},{64,88... | collective-permute-start | bytes 344072 | tf_op jit(solution)/shard_map/ppermute | solution.py:72
  132.0 4.1 %collective-permute-done.26 = bf16[16,3584]{1,0:T(8,128)(2,1)S(1)} collective-permute-done((bf16[16,3584]{1,0:T(8,128)(2,1)S(1)}, bf16[16,3584]{1,0:T(8,128)(2,1)S(1)}, u32[]{:S(2)}, u32[]{:S(2)}) %collective-permute-start.26) | collective-permute-done | bytes 114720 | tf_op jit(solution)/shard_map/ppermute | solution.py:72
  136.1 2.5 %collective-permute-done.25 = bf16[16,3584]{1,0:T(8,128)(2,1)S(1)} collective-permute-done((bf16[16,3584]{1,0:T(8,128)(2,1)S(1)}, bf16[16,3584]{1,0:T(8,128)(2,1)S(1)}, u32[]{:S(2)}, u32[]{:S(2)}) %collective-permute-start.25) | collective-permute-done | bytes 114720 | tf_op jit(solution)/shard_map/ppermute | solution.py:72
  138.6 0.9 collective-permute-done.24
  139.6 1.9 %collective-permute-start.29 = (bf16[4,3584]{1,0:T(4,128)(2,1)S(1)}, bf16[4,3584]{1,0:T(4,128)(2,1)S(1)}, u32[]{:S(2)}, u32[]{:S(2)}) collective-permute-start(bf16[4,3584]{1,0:T(4,128)(2,1)S(1)} %get-tuple-element.128), channel_id=1, source_target_pairs={{0,96},{8,104},{16,112},{24,120},{32,0},{40,8},{48,16},{56,24},{64... | collective-permute-start | bytes 86024 | tf_op jit(solution)/shard_map/ppermute | solution.py:72
  141.5 0.9 collective-permute-start.28
  143.6 3.3 %collective-permute-done.28 = bf16[4,3584]{1,0:T(4,128)(2,1)S(1)} collective-permute-done((bf16[4,3584]{1,0:T(4,128)(2,1)S(1)}, bf16[4,3584]{1,0:T(4,128)(2,1)S(1)}, u32[]{:S(2)}, u32[]{:S(2)}) %collective-permute-start.28) | collective-permute-done | bytes 28704 | tf_op jit(solution)/shard_map/ppermute | solution.py:72
  (103 shorter events, 14.8 us)
Async XLA Ops:
  0.6 4.7 %collective-permute-start.2 = (bf16[4,3584]{1,0:T(4,128)(2,1)}, bf16[4,3584]{1,0:T(4,128)(2,1)S(1)}, u32[]{:S(2)}, u32[]{:S(2)}) collective-permute-start(bf16[4,3584]{1,0:T(4,128)(2,1)} %param.8), channel_id=1, source_target_pairs={{0,96},{8,104},{16,112},{24,120},{32,0},{40,8},{48,16},{56,24},{64... | collective-permute-start | bytes 86024 | tf_op jit(solution)/shard_map/ppermute | solution.py:72
  3.5 5.6 %collective-permute-start.1 = (bf16[4,3584]{1,0:T(4,128)(2,1)}, bf16[4,3584]{1,0:T(4,128)(2,1)S(1)}, u32[]{:S(2)}, u32[]{:S(2)}) collective-permute-start(bf16[4,3584]{1,0:T(4,128)(2,1)} %param.8), channel_id=1, source_target_pairs={{0,64},{8,72},{16,80},{24,88},{32,96},{40,104},{48,112},{56,120},{... | collective-permute-start | bytes 86024 | tf_op jit(solution)/shard_map/ppermute | solution.py:72
  4.3 5.3 %collective-permute-start = (bf16[4,3584]{1,0:T(4,128)(2,1)}, bf16[4,3584]{1,0:T(4,128)(2,1)S(1)}, u32[]{:S(2)}, u32[]{:S(2)}) collective-permute-start(bf16[4,3584]{1,0:T(4,128)(2,1)} %param.8), channel_id=1, source_target_pairs={{0,32},{8,40},{16,48},{24,56},{32,64},{40,72},{48,80},{56,88},{64,... | collective-permute-start | bytes 86024 | tf_op jit(solution)/shard_map/ppermute | solution.py:72
  10.5 17.6 %copy-start.2 = (f32[512,64]{0,1:T(8,128)S(1)}, f32[512,64]{0,1:T(8,128)}, u32[]{:S(2)}) copy-start(f32[512,64]{0,1:T(8,128)} %param.11) | copy-start | bytes 393220
  10.5 6.9 %collective-permute-start.5 = (bf16[16,3584]{1,0:T(8,128)(2,1)S(1)}, bf16[16,3584]{1,0:T(8,128)(2,1)S(1)}, u32[]{:S(2)}, u32[]{:S(2)}) collective-permute-start(bf16[16,3584]{1,0:T(8,128)(2,1)S(1)} %reshape.838), channel_id=1, source_target_pairs={{0,24},{8,0},{16,8},{24,16},{32,56},{40,32},{48,40},{56,48},{64,88... | collective-permute-start | bytes 344072 | tf_op jit(solution)/shard_map/ppermute | solution.py:72
  13.6 6.4 %collective-permute-start.4 = (bf16[16,3584]{1,0:T(8,128)(2,1)S(1)}, bf16[16,3584]{1,0:T(8,128)(2,1)S(1)}, u32[]{:S(2)}, u32[]{:S(2)}) collective-permute-start(bf16[16,3584]{1,0:T(8,128)(2,1)S(1)} %reshape.838), channel_id=1, source_target_pairs={{0,16},{8,24},{16,0},{24,8},{32,48},{40,56},{48,32},{56,40},{64,80... | collective-permute-start | bytes 344072 | tf_op jit(solution)/shard_map/ppermute | solution.py:72
  14.2 6.9 %collective-permute-start.3 = (bf16[16,3584]{1,0:T(8,128)(2,1)S(1)}, bf16[16,3584]{1,0:T(8,128)(2,1)S(1)}, u32[]{:S(2)}, u32[]{:S(2)}) collective-permute-start(bf16[16,3584]{1,0:T(8,128)(2,1)S(1)} %reshape.838), channel_id=1, source_target_pairs={{0,8},{8,16},{16,24},{24,0},{32,40},{40,48},{48,56},{56,32},{64,72... | collective-permute-start | bytes 344072 | tf_op jit(solution)/shard_map/ppermute | solution.py:72
  17.3 44.9 %copy-start.3 = (pred[512]{0:T(512)(128)(4,1)}, pred[512]{0:T(512)(128)(4,1)S(1)}, u32[]{:S(2)}) copy-start(pred[512]{0:T(512)(128)(4,1)S(1)} %get-tuple-element.142) | copy-start | bytes 1540
  21.2 20.7 %collective-permute-start.8 = (bf16[64,3584]{1,0:T(8,128)(2,1)S(1)}, bf16[64,3584]{1,0:T(8,128)(2,1)S(1)}, u32[]{:S(2)}, u32[]{:S(2)}) collective-permute-start(bf16[64,3584]{1,0:T(8,128)(2,1)S(1)} %bitcast.145), channel_id=1, source_target_pairs={{0,6},{1,7},{2,0},{3,1},{4,2},{5,3},{6,4},{7,5},{8,14},{9,15},{10,... | collective-permute-start | bytes 1376264 | tf_op jit(solution)/shard_map/ppermute | solution.py:72
  25.3 16.6 %collective-permute-start.7 = (bf16[64,3584]{1,0:T(8,128)(2,1)S(1)}, bf16[64,3584]{1,0:T(8,128)(2,1)S(1)}, u32[]{:S(2)}, u32[]{:S(2)}) collective-permute-start(bf16[64,3584]{1,0:T(8,128)(2,1)S(1)} %bitcast.146), channel_id=1, source_target_pairs={{0,4},{1,5},{2,6},{3,7},{4,0},{5,1},{6,2},{7,3},{8,12},{9,13},{10,... | collective-permute-start | bytes 1376264 | tf_op jit(solution)/shard_map/ppermute | solution.py:72
  25.3 20.0 %collective-permute-start.6 = (bf16[64,3584]{1,0:T(8,128)(2,1)S(1)}, bf16[64,3584]{1,0:T(8,128)(2,1)S(1)}, u32[]{:S(2)}, u32[]{:S(2)}) collective-permute-start(bf16[64,3584]{1,0:T(8,128)(2,1)S(1)} %bitcast.147), channel_id=1, source_target_pairs={{0,2},{1,3},{2,4},{3,5},{4,6},{5,7},{6,0},{7,1},{8,10},{9,11},{10,... | collective-permute-start | bytes 1376264 | tf_op jit(solution)/shard_map/ppermute | solution.py:72
  45.5 3.9 %collective-permute-start.9 = (bf16[256,3584]{1,0:T(8,128)(2,1)S(1)}, bf16[256,3584]{1,0:T(8,128)(2,1)S(1)}, u32[]{:S(2)}, u32[]{:S(2)}) collective-permute-start(bf16[256,3584]{1,0:T(8,128)(2,1)S(1)} %bitcast.140), channel_id=1, source_target_pairs={{0,1},{1,0},{2,3},{3,2},{4,5},{5,4},{6,7},{7,6},{8,9},{9,8},{10,11... | collective-permute-start | bytes 5505032 | tf_op jit(solution)/shard_map/ppermute | solution.py:72
  49.7 8.9 %copy-start = (bf16[2,256,3584]{2,1,0:T(8,128)(2,1)}, bf16[2,256,3584]{2,1,0:T(8,128)(2,1)S(1)}, u32[]{:S(2)}) copy-start(bf16[2,256,3584]{2,1,0:T(8,128)(2,1)S(1)} %pad_maximum_fusion) | copy-start | bytes 11010052
  62.4 1.6 %collective-permute-start.10 = (f32[3,512]{0,1:T(8,128)S(1)}, f32[3,512]{0,1:T(8,128)S(1)}, u32[]{:S(2)}, u32[]{:S(2)}) collective-permute-start(f32[3,512]{0,1:T(8,128)S(1)} %bitcast_select_fusion.1), channel_id=1, source_target_pairs={{0,1},{1,0},{2,3},{3,2},{4,5},{5,4},{6,7},{7,6},{8,9},{9,8},{10,11... | collective-permute-start | bytes 18440 | tf_op jit(solution)/shard_map/ppermute | solution.py:72
  64.2 5.2 %collective-permute-start.12 = (f32[3,512]{1,0:T(4,128)S(1)}, f32[3,512]{1,0:T(4,128)S(1)}, u32[]{:S(2)}, u32[]{:S(2)}) collective-permute-start(f32[3,512]{1,0:T(4,128)S(1)} %get-tuple-element.136), channel_id=1, source_target_pairs={{0,4},{1,5},{2,6},{3,7},{4,0},{5,1},{6,2},{7,3},{8,12},{9,13},{10,... | collective-permute-start | bytes 18440 | tf_op jit(solution)/shard_map/ppermute | solution.py:72
  64.9 4.9 %collective-permute-start.11 = (f32[3,512]{1,0:T(4,128)S(1)}, f32[3,512]{1,0:T(4,128)S(1)}, u32[]{:S(2)}, u32[]{:S(2)}) collective-permute-start(f32[3,512]{1,0:T(4,128)S(1)} %get-tuple-element.136), channel_id=1, source_target_pairs={{0,2},{1,3},{2,4},{3,5},{4,6},{5,7},{6,0},{7,1},{8,10},{9,11},{10,... | collective-permute-start | bytes 18440 | tf_op jit(solution)/shard_map/ppermute | solution.py:72
  66.1 3.7 %collective-permute-start.13 = (f32[3,512]{1,0:T(4,128)S(1)}, f32[3,512]{1,0:T(4,128)S(1)}, u32[]{:S(2)}, u32[]{:S(2)}) collective-permute-start(f32[3,512]{1,0:T(4,128)S(1)} %get-tuple-element.136), channel_id=1, source_target_pairs={{0,6},{1,7},{2,0},{3,1},{4,2},{5,3},{6,4},{7,5},{8,14},{9,15},{10,... | collective-permute-start | bytes 18440 | tf_op jit(solution)/shard_map/ppermute | solution.py:72
  69.9 5.2 %collective-permute-start.15 = (f32[3,512]{1,0:T(4,128)S(1)}, f32[3,512]{1,0:T(4,128)S(1)}, u32[]{:S(2)}, u32[]{:S(2)}) collective-permute-start(f32[3,512]{1,0:T(4,128)S(1)} %get-tuple-element.134), channel_id=1, source_target_pairs={{0,16},{8,24},{16,0},{24,8},{32,48},{40,56},{48,32},{56,40},{64,80... | collective-permute-start | bytes 18440 | tf_op jit(solution)/shard_map/ppermute | solution.py:72
  70.8 4.9 %collective-permute-start.14 = (f32[3,512]{1,0:T(4,128)S(1)}, f32[3,512]{1,0:T(4,128)S(1)}, u32[]{:S(2)}, u32[]{:S(2)}) collective-permute-start(f32[3,512]{1,0:T(4,128)S(1)} %get-tuple-element.134), channel_id=1, source_target_pairs={{0,8},{8,16},{16,24},{24,0},{32,40},{40,48},{48,56},{56,32},{64,72... | collective-permute-start | bytes 18440 | tf_op jit(solution)/shard_map/ppermute | solution.py:72
  71.7 3.9 %collective-permute-start.16 = (f32[3,512]{1,0:T(4,128)S(1)}, f32[3,512]{1,0:T(4,128)S(1)}, u32[]{:S(2)}, u32[]{:S(2)}) collective-permute-start(f32[3,512]{1,0:T(4,128)S(1)} %get-tuple-element.134), channel_id=1, source_target_pairs={{0,24},{8,0},{16,8},{24,16},{32,56},{40,32},{48,40},{56,48},{64,88... | collective-permute-start | bytes 18440 | tf_op jit(solution)/shard_map/ppermute | solution.py:72
  75.8 6.7 %collective-permute-start.19 = (f32[3,512]{1,0:T(4,128)S(1)}, f32[3,512]{1,0:T(4,128)S(1)}, u32[]{:S(2)}, u32[]{:S(2)}) collective-permute-start(f32[3,512]{1,0:T(4,128)S(1)} %get-tuple-element.132), channel_id=1, source_target_pairs={{0,96},{8,104},{16,112},{24,120},{32,0},{40,8},{48,16},{56,24},{64... | collective-permute-start | bytes 18440 | tf_op jit(solution)/shard_map/ppermute | solution.py:72
  76.5 5.2 %collective-permute-start.18 = (f32[3,512]{1,0:T(4,128)S(1)}, f32[3,512]{1,0:T(4,128)S(1)}, u32[]{:S(2)}, u32[]{:S(2)}) collective-permute-start(f32[3,512]{1,0:T(4,128)S(1)} %get-tuple-element.132), channel_id=1, source_target_pairs={{0,64},{8,72},{16,80},{24,88},{32,96},{40,104},{48,112},{56,120},{... | collective-permute-start | bytes 18440 | tf_op jit(solution)/shard_map/ppermute | solution.py:72
  77.6 4.9 %collective-permute-start.17 = (f32[3,512]{1,0:T(4,128)S(1)}, f32[3,512]{1,0:T(4,128)S(1)}, u32[]{:S(2)}, u32[]{:S(2)}) collective-permute-start(f32[3,512]{1,0:T(4,128)S(1)} %get-tuple-element.132), channel_id=1, source_target_pairs={{0,32},{8,40},{16,48},{24,56},{32,64},{40,72},{48,80},{56,88},{64,... | collective-permute-start | bytes 18440 | tf_op jit(solution)/shard_map/ppermute | solution.py:72
  95.9 3.9 %collective-permute-start.20 = (bf16[256,3584]{1,0:T(8,128)(2,1)S(1)}, bf16[256,3584]{1,0:T(8,128)(2,1)S(1)}, u32[]{:S(2)}, u32[]{:S(2)}) collective-permute-start(bf16[256,3584]{1,0:T(8,128)(2,1)S(1)} %slice.277), channel_id=1, source_target_pairs={{0,1},{1,0},{2,3},{3,2},{4,5},{5,4},{6,7},{7,6},{8,9},{9,8},{10,11... | collective-permute-start | bytes 5505032 | tf_op jit(solution)/shard_map/ppermute | solution.py:72
  99.7 5.0 %copy-start.1 = (bf16[2,256,3584]{2,1,0:T(8,128)(2,1)S(1)}, bf16[2,256,3584]{2,1,0:T(8,128)(2,1)}, u32[]{:S(2)}) copy-start(bf16[2,256,3584]{2,1,0:T(8,128)(2,1)} %copy-done) | copy-start | bytes 11010052
  100.5 23.2 %collective-permute-start.23 = (bf16[64,3584]{1,0:T(8,128)(2,1)S(1)}, bf16[64,3584]{1,0:T(8,128)(2,1)S(1)}, u32[]{:S(2)}, u32[]{:S(2)}) collective-permute-start(bf16[64,3584]{1,0:T(8,128)(2,1)S(1)} %get-tuple-element.122), channel_id=1, source_target_pairs={{0,6},{1,7},{2,0},{3,1},{4,2},{5,3},{6,4},{7,5},{8,14},{9,15},{10,... | collective-permute-start | bytes 1376264 | tf_op jit(solution)/shard_map/ppermute | solution.py:72
  103.8 19.9 %collective-permute-start.22 = (bf16[64,3584]{1,0:T(8,128)(2,1)S(1)}, bf16[64,3584]{1,0:T(8,128)(2,1)S(1)}, u32[]{:S(2)}, u32[]{:S(2)}) collective-permute-start(bf16[64,3584]{1,0:T(8,128)(2,1)S(1)} %get-tuple-element.123), channel_id=1, source_target_pairs={{0,4},{1,5},{2,6},{3,7},{4,0},{5,1},{6,2},{7,3},{8,12},{9,13},{10,... | collective-permute-start | bytes 1376264 | tf_op jit(solution)/shard_map/ppermute | solution.py:72
  104.3 23.0 %collective-permute-start.21 = (bf16[64,3584]{1,0:T(8,128)(2,1)S(1)}, bf16[64,3584]{1,0:T(8,128)(2,1)S(1)}, u32[]{:S(2)}, u32[]{:S(2)}) collective-permute-start(bf16[64,3584]{1,0:T(8,128)(2,1)S(1)} %get-tuple-element.121), channel_id=1, source_target_pairs={{0,2},{1,3},{2,4},{3,5},{4,6},{5,7},{6,0},{7,1},{8,10},{9,11},{10,... | collective-permute-start | bytes 1376264 | tf_op jit(solution)/shard_map/ppermute | solution.py:72
  127.8 8.3 %collective-permute-start.26 = (bf16[16,3584]{1,0:T(8,128)(2,1)S(1)}, bf16[16,3584]{1,0:T(8,128)(2,1)S(1)}, u32[]{:S(2)}, u32[]{:S(2)}) collective-permute-start(bf16[16,3584]{1,0:T(8,128)(2,1)S(1)} %get-tuple-element.125), channel_id=1, source_target_pairs={{0,24},{8,0},{16,8},{24,16},{32,56},{40,32},{48,40},{56,48},{64,88... | collective-permute-start | bytes 344072 | tf_op jit(solution)/shard_map/ppermute | solution.py:72
  131.1 7.5 %collective-permute-start.25 = (bf16[16,3584]{1,0:T(8,128)(2,1)S(1)}, bf16[16,3584]{1,0:T(8,128)(2,1)S(1)}, u32[]{:S(2)}, u32[]{:S(2)}) collective-permute-start(bf16[16,3584]{1,0:T(8,128)(2,1)S(1)} %get-tuple-element.126), channel_id=1, source_target_pairs={{0,16},{8,24},{16,0},{24,8},{32,48},{40,56},{48,32},{56,40},{64,80... | collective-permute-start | bytes 344072 | tf_op jit(solution)/shard_map/ppermute | solution.py:72
  131.3 8.2 %collective-permute-start.24 = (bf16[16,3584]{1,0:T(8,128)(2,1)S(1)}, bf16[16,3584]{1,0:T(8,128)(2,1)S(1)}, u32[]{:S(2)}, u32[]{:S(2)}) collective-permute-start(bf16[16,3584]{1,0:T(8,128)(2,1)S(1)} %get-tuple-element.124), channel_id=1, source_target_pairs={{0,8},{8,16},{16,24},{24,0},{32,40},{40,48},{48,56},{56,32},{64,72... | collective-permute-start | bytes 344072 | tf_op jit(solution)/shard_map/ppermute | solution.py:72
  139.6 3.9 %collective-permute-start.29 = (bf16[4,3584]{1,0:T(4,128)(2,1)S(1)}, bf16[4,3584]{1,0:T(4,128)(2,1)S(1)}, u32[]{:S(2)}, u32[]{:S(2)}) collective-permute-start(bf16[4,3584]{1,0:T(4,128)(2,1)S(1)} %get-tuple-element.128), channel_id=1, source_target_pairs={{0,96},{8,104},{16,112},{24,120},{32,0},{40,8},{48,16},{56,24},{64... | collective-permute-start | bytes 86024 | tf_op jit(solution)/shard_map/ppermute | solution.py:72
  141.5 5.4 %collective-permute-start.28 = (bf16[4,3584]{1,0:T(4,128)(2,1)S(1)}, bf16[4,3584]{1,0:T(4,128)(2,1)S(1)}, u32[]{:S(2)}, u32[]{:S(2)}) collective-permute-start(bf16[4,3584]{1,0:T(4,128)(2,1)S(1)} %get-tuple-element.129), channel_id=1, source_target_pairs={{0,64},{8,72},{16,80},{24,88},{32,96},{40,104},{48,112},{56,120},{... | collective-permute-start | bytes 86024 | tf_op jit(solution)/shard_map/ppermute | solution.py:72
  142.4 5.1 %collective-permute-start.27 = (bf16[4,3584]{1,0:T(4,128)(2,1)S(1)}, bf16[4,3584]{1,0:T(4,128)(2,1)S(1)}, u32[]{:S(2)}, u32[]{:S(2)}) collective-permute-start(bf16[4,3584]{1,0:T(4,128)(2,1)S(1)} %get-tuple-element.127), channel_id=1, source_target_pairs={{0,32},{8,40},{16,48},{24,56},{32,64},{40,72},{48,80},{56,88},{64,... | collective-permute-start | bytes 86024 | tf_op jit(solution)/shard_map/ppermute | solution.py:72

commit v3 on v2

--- a/solution.py
+++ b/solution.py
@@ -54,46 +54,82 @@
     return {"x": tok // RING, "y": tok % RING, "z": voc // 2, "c": voc % 2}
 
 
-def stage_pairs(stage, shift, tok_n, voc_n):
-    if stage == "c":
-        return "voc", [(v, v ^ 1) for v in range(voc_n)]
-    if stage == "z":
-        return "voc", [(v, ((v // 2 + shift) % RING) * 2 + v % 2) for v in range(voc_n)]
-    if stage == "y":
-        return "tok", [(t, (t // RING) * RING + (t % RING + shift) % RING) for t in range(tok_n)]
-    return "tok", [(t, ((t // RING + shift) % RING) * RING + t % RING) for t in range(tok_n)]
-
-
-def exchange(block_for, stage, tok_n, voc_n):
+AXES = ("tok", "voc")
+
+
+def device_coords(d, voc_n):
+    tok, voc = divmod(d, voc_n)
+    return tok // RING, tok % RING, voc // 2, voc % 2
+
+
+def device_id(x, y, z, c, voc_n):
+    return (x * RING + y) * voc_n + z * 2 + c
+
+
+def ring_axis(stage, core):
+    if stage == "r1":
+        return "x" if core == 0 else "z"
+    if stage == "r3":
+        return "z" if core == 0 else "x"
+    if stage == "r2":
+        return "y"
+    return stage
+
+
+def stage_pairs(stage, shift, n_dev, voc_n):
+    pairs = []
+    for d in range(n_dev):
+        x, y, z, c = device_coords(d, voc_n)
+        axis = ring_axis(stage, c)
+        if axis == "c":
+            c = c ^ 1
+        elif axis == "x":
+            x = (x + shift) % RING
+        elif axis == "y":
+            y = (y + shift) % RING
+        else:
+            z = (z + shift) % RING
+        pairs.append((d, device_id(x, y, z, c, voc_n)))
+    return pairs
+
+
+def exchange(block_for, stage, n_dev, voc_n):
     n = 2 if stage == "c" else RING
     got = [block_for(0)]
     for shift in range(1, n):
-        axis, pairs = stage_pairs(stage, shift, tok_n, voc_n)
-        got.append(lax.ppermute(block_for(shift), axis, pairs))
+        got.append(lax.ppermute(block_for(shift), AXES, stage_pairs(stage, shift, n_dev, voc_n)))
     return jnp.stack(got)
 
 
 def arrival_tokens(at):
     r = jnp.arange(2 * RING ** 3 * 4, dtype=jnp.int32)
     i = r % 4
-    x = (at["x"] - (r // 4) % RING) % RING
-    y = (at["y"] - (r // 16) % RING) % RING
-    z = (at["z"] - (r // 64) % RING) % RING
+    s_r1 = (r // 4) % RING
+    s_r2 = (r // 16) % RING
+    s_r3 = (r // 64) % RING
     c = at["c"] ^ (r // 256)
+    s_x = jnp.where(c == 0, s_r1, s_r3)
+    s_z = jnp.where(c == 0, s_r3, s_r1)
+    x = (at["x"] - s_x) % RING
+    y = (at["y"] - s_r2) % RING
+    z = (at["z"] - s_z) % RING
     return (((x * RING + y) * RING + z) * 2 + c) * 4 + i
 
 
 def natural_rows(at):
     t = jnp.arange(2 * RING ** 3 * 4, dtype=jnp.int32)
     i = t % 4
-    s_c = at["c"] ^ ((t // 4) % 2)
+    c = (t // 4) % 2
+    s_c = at["c"] ^ c
     s_z = (at["z"] - (t // 8) % RING) % RING
     s_y = (at["y"] - (t // 32) % RING) % RING
     s_x = (at["x"] - (t // 128) % RING) % RING
-    return (((s_c * RING + s_z) * RING + s_y) * RING + s_x) * 4 + i
-
-
-def per_device(hidden_rows, head_weight, teacher_index, teacher_logprob, tok_n, voc_n):
+    s_r1 = jnp.where(c == 0, s_x, s_z)
+    s_r3 = jnp.where(c == 0, s_z, s_x)
+    return (((s_c * RING + s_r3) * RING + s_y) * RING + s_r1) * 4 + i
+
+
+def per_device(hidden_rows, head_weight, teacher_index, teacher_logprob, n_dev, voc_n):
     voc_dev = head_weight.shape[0]
     tok_dev = hidden_rows.shape[0]
     width = hidden_rows.shape[1]
@@ -109,10 +145,10 @@
     target = teacher_target(local, probs_arr, voc_dev)
 
     every = hidden_rows
-    for stage in ("x", "y", "z", "c"):
-        got = exchange(lambda s: every, stage, tok_n, voc_n)
+    for stage in ("r1", "r2", "r3", "c"):
+        got = exchange(lambda s: every, stage, n_dev, voc_n)
         every = got.reshape(-1, width)
-        if stage == "z":
+        if stage == "r3":
             every, target = lax.optimization_barrier((every, target))
 
     logits = lax.dot_general(
@@ -124,7 +160,7 @@
 
     stats = jnp.take(jnp.stack([local_peak, local_sum, part_dot]), natural_rows(at), axis=1)
     for stage in ("c", "z", "y", "x"):
-        got = exchange(lambda s: stats, stage, tok_n, voc_n)
+        got = exchange(lambda s: stats, stage, n_dev, voc_n)
         peak = jnp.max(got[:, 0], axis=0)
         summed = jnp.sum(got[:, 1] * jnp.exp(got[:, 0] - peak[None]), axis=0)
         dotted = jnp.sum(got[:, 2], axis=0)
@@ -148,24 +184,24 @@
     ).astype(jnp.bfloat16)
 
     acc = partial.reshape(2, -1, width)
-    for stage in ("c", "z", "y", "x"):
+    for stage in ("c", "r3", "r2", "r1"):
         n = acc.shape[0]
-        got = exchange(lambda s: acc[(-s) % n].astype(jnp.bfloat16), stage, tok_n, voc_n)
+        got = exchange(lambda s: acc[(-s) % n].astype(jnp.bfloat16), stage, n_dev, voc_n)
         acc = acc[0] + jnp.sum(got[1:].astype(jnp.float32), axis=0)
-        if stage == "z":
+        if stage == "r3":
             acc, head_grad = lax.optimization_barrier((acc, head_grad))
-        if stage != "x":
+        if stage != "r1":
             acc = acc.reshape(RING, -1, width)
     return (row_loss, head_grad, acc.astype(jnp.bfloat16))
 
 
 def solution(mesh):
-    tok_n = mesh.shape["tok"]
     voc_n = mesh.shape["voc"]
+    n_dev = mesh.shape["tok"] * voc_n
     placed = (P(("tok", "voc"), None), P(("tok", "voc"), None), P(), P())
 
     def body(h, w, ti, tl):
-        return per_device(h, w, ti, tl, tok_n, voc_n)
+        return per_device(h, w, ti, tl, n_dev, voc_n)
 
     return jax.shard_map(
         body,

time: 148 us -> 133 us (0.90)
  waiting for transfers between devices: 61.8 us -> 47.6 us
    ppermute x30, waiting for transfers between devices: 61.8 us -> 47.6 us  [exchange(): lax.ppermute(block_for(shift), AXES, stage_pairs(stage, shift, n_dev, voc...]
  transfers between devices with their start and end apart: 30 -> 30, of which waited for: 23 -> 25; matrix products, arithmetic and copies ran while one was open for 12% -> 13% of each run, Pallas kernels for 0% -> 0%
where the time goes in v3:
time: 133 us
  waiting for transfers between devices  47.6 us (36%)
  starting transfers between devices  36.5 us (27%)
  matrix products  22.9 us (17%)
  other arithmetic  14.8 us (11%)
  local copies, waits for them, and re-layouts  9.46 us (7%)
  between operations  1.68 us (1%)
    ppermute x30, waiting for transfers between devices, exchange(): lax.ppermute(block_for(shift), AXES, stage_pairs(stage, shift, n_dev, voc...  47.6 us
    ppermute x30, starting transfers between devices, exchange(): lax.ppermute(block_for(shift), AXES, stage_pairs(stage, shift, n_dev, voc...  36.5 us
    dot_general x1, matrix products, per_device(): lax.dot_general(every, head_weight, (((1,), (1,)), ((), ())), preferred_e...  8.86 us
    dot_general x1, matrix products, per_device(): partial = jnp.dot(grad, head_weight, preferred_element_type=jnp.float32)  7.3 us
    dot_general x1, matrix products, per_device(): lax.dot_general(grad, every, (((0,), (0,)), ((), ())), preferred_element_...  6.71 us
    add x1, other arithmetic, compact_target(): target + jnp.where(slot_local[:, j:j + 1] == columns, slot_probs[:, j:j +...  3.58 us
    gather x1, local copies, waits for them, and re-layouts, per_device(): lse_arr = jnp.take(lse, rows, axis=0)  3.49 us
  transfers between devices with their start and end apart: 30, of which 25 were waited for; matrix products, arithmetic and copies ran while one was open for 13% of the time, Pallas kernels for 0%

profile of v3, /device:TPU:0, one launch (start us, length us, event | category | flops | bytes accessed | tf_op | source)
XLA Modules:
  0.0 132.9 jit_solution(870818600840624506)
XLA Ops:
  0.6 2.9 %collective-permute-start.2 = (bf16[4,3584]{1,0:T(4,128)(2,1)}, bf16[4,3584]{1,0:T(4,128)(2,1)S(1)}, u32[]{:S(2)}, u32[]{:S(2)}) collective-permute-start(bf16[4,3584]{1,0:T(4,128)(2,1)} %param.8), channel_id=1, source_target_pairs={{0,96},{1,7},{2,98},{3,1},{4,100},{5,3},{6,102},{7,5},{8,104},{9,1... | collective-permute-start | bytes 86024 | tf_op jit(solution)/shard_map/ppermute | solution.py:100
  3.5 0.8 collective-permute-start.1
  4.3 0.9 collective-permute-start
  5.3 3.8 %collective-permute-done.1 = bf16[4,3584]{1,0:T(4,128)(2,1)S(1)} collective-permute-done((bf16[4,3584]{1,0:T(4,128)(2,1)}, bf16[4,3584]{1,0:T(4,128)(2,1)S(1)}, u32[]{:S(2)}, u32[]{:S(2)}) %collective-permute-start.1) | collective-permute-done | bytes 28704 | tf_op jit(solution)/shard_map/ppermute | solution.py:100
  9.6 0.8 pad_maximum_fusion.3
  10.5 3.1 %collective-permute-start.5 = (bf16[16,3584]{1,0:T(8,128)(2,1)S(1)}, bf16[16,3584]{1,0:T(8,128)(2,1)S(1)}, u32[]{:S(2)}, u32[]{:S(2)}) collective-permute-start(bf16[16,3584]{1,0:T(8,128)(2,1)S(1)} %reshape.856), channel_id=1, source_target_pairs={{0,24},{1,25},{2,26},{3,27},{4,28},{5,29},{6,30},{7,31},{8,0},{9,1... | collective-permute-start | bytes 344072 | tf_op jit(solution)/shard_map/ppermute | solution.py:100
  14.2 1.0 collective-permute-start.3
  15.2 1.0 copy.53
  16.3 1.0 gather_fusion
  18.2 2.5 %collective-permute-done.4 = bf16[16,3584]{1,0:T(8,128)(2,1)S(1)} collective-permute-done((bf16[16,3584]{1,0:T(8,128)(2,1)S(1)}, bf16[16,3584]{1,0:T(8,128)(2,1)S(1)}, u32[]{:S(2)}, u32[]{:S(2)}) %collective-permute-start.4) | collective-permute-done | bytes 114720 | tf_op jit(solution)/shard_map/ppermute | solution.py:100
  20.7 1.2 collective-permute-done.3
  21.9 3.4 %collective-permute-start.8 = (bf16[64,3584]{1,0:T(8,128)(2,1)S(1)}, bf16[64,3584]{1,0:T(8,128)(2,1)S(1)}, u32[]{:S(2)}, u32[]{:S(2)}) collective-permute-start(bf16[64,3584]{1,0:T(8,128)(2,1)S(1)} %bitcast.145), channel_id=1, source_target_pairs={{0,6},{1,97},{2,0},{3,99},{4,2},{5,101},{6,4},{7,103},{8,14},{9,10... | collective-permute-start | bytes 1376264 | tf_op jit(solution)/shard_map/ppermute | solution.py:100
  25.3 1.3 collective-permute-start.6
  28.2 1.0 gather_fusion.1
  29.5 4.6 %conditional.1 = (f32[512,1152]{1,0:T(8,128)}) conditional(s32[]{:T(128)} %convert_element_type.42, (s32[512,64]{1,0:T(8,128)S(1)}, f32[512,64]{1,0:T(8,128)S(1)}) %tuple.20, (s32[512,64]{1,0:T(8,128)S(1)}, f32[512,64]{1,0:T(8,128)S(1)}) %tuple.20), branch_computations={%region_3.7_spmd, %region_7.11_spmd} | conditional | flops 17883136 | bytes 4423692 | solution.py:44
  30.5 3.6 %select_add_fusion = f32[512,1152]{1,0:T(8,128)} fusion(f32[512]{0:T(512)S(1)} %bitcast.178, s32[512]{0:T(512)S(1)} %bitcast.186, f32[512]{0:T(512)S(1)} %bitcast.179, s32[512]{0:T(512)S(1)} %bitcast.187, f32[512]{0:T(512)S(1)} %bitcast.180, s32[512]{0:T(512)S(1)} %bitcast.188, f32[512]{0:T(512)S(1)} %bitcast.181, s32[512]{0:T(512)S(1)} %bitcast.189, ...), kind=kLoop, calls=%fused_computation.5 | loop fusion | flops 13565952 | bytes 2392064 | tf_op jit(solution)/shard_map/cond/branch_0_fun/add | solution.py:37
  34.1 2.1 %collective-permute-done.8 = bf16[64,3584]{1,0:T(8,128)(2,1)S(1)} collective-permute-done((bf16[64,3584]{1,0:T(8,128)(2,1)S(1)}, bf16[64,3584]{1,0:T(8,128)(2,1)S(1)}, u32[]{:S(2)}, u32[]{:S(2)}) %collective-permute-start.8) | collective-permute-done | bytes 458784 | tf_op jit(solution)/shard_map/ppermute | solution.py:100
  36.2 3.7 %collective-permute-done.6 = bf16[64,3584]{1,0:T(8,128)(2,1)S(1)} collective-permute-done((bf16[64,3584]{1,0:T(8,128)(2,1)S(1)}, bf16[64,3584]{1,0:T(8,128)(2,1)S(1)}, u32[]{:S(2)}, u32[]{:S(2)}) %collective-permute-start.6) | collective-permute-done | bytes 458784 | tf_op jit(solution)/shard_map/ppermute | solution.py:100
  40.3 3.8 %collective-permute-done.9 = bf16[256,3584]{1,0:T(8,128)(2,1)S(1)} collective-permute-done((bf16[256,3584]{1,0:T(8,128)(2,1)S(1)}, bf16[256,3584]{1,0:T(8,128)(2,1)S(1)}, u32[]{:S(2)}, u32[]{:S(2)}) %collective-permute-start.9) | collective-permute-done | bytes 1835040 | tf_op jit(solution)/shard_map/ppermute | solution.py:100
  44.4 8.9 %fusion.107 = (f32[512]{0:T(512)S(1)}, f32[512,1152]{1,0:T(8,128)S(1)}) fusion(bf16[512,3584]{1,0:T(8,128)(2,1)S(1)} %bitcast.142, bf16[1152,3584]{1,0:T(8,128)(2,1)} %param.9), kind=kOutput, calls=%fused_computation.313 | convolution fusion | flops 4228447744 | bytes 14288896 | tf_op jit(solution)/shard_map/dot_general | solution.py:154
  53.2 2.4 %exponential_reduce_fusion = (f32[512]{0:T(512)S(1)}, f32[512]{0:T(512)S(1)}) fusion(f32[512,1152]{1,0:T(8,128)S(1)} %get-tuple-element.138, f32[512]{0:T(512)S(1)} %get-tuple-element.137, f32[512,1152]{1,0:T(8,128)} %get-tuple-element.183), kind=kLoop, calls=%fused_computation.32 | loop fusion | flops 2358272 | bytes 4724736 | tf_op jit(solution)/shard_map/reduce_sum | solution.py:159
  55.9 1.0 gather_fusion.2
  59.3 1.5 %collective-permute-start.11 = (f32[3,512]{1,0:T(4,128)S(1)}, f32[3,512]{1,0:T(4,128)S(1)}, u32[]{:S(2)}, u32[]{:S(2)}) collective-permute-start(f32[3,512]{1,0:T(4,128)S(1)} %get-tuple-element.136), channel_id=1, source_target_pairs={{0,2},{1,3},{2,4},{3,5},{4,6},{5,7},{6,0},{7,1},{8,10},{9,11},{10,... | collective-permute-start | bytes 18440 | tf_op jit(solution)/shard_map/ppermute | solution.py:100
  60.7 1.8 %collective-permute-start.13 = (f32[3,512]{1,0:T(4,128)S(1)}, f32[3,512]{1,0:T(4,128)S(1)}, u32[]{:S(2)}, u32[]{:S(2)}) collective-permute-start(f32[3,512]{1,0:T(4,128)S(1)} %get-tuple-element.136), channel_id=1, source_target_pairs={{0,6},{1,7},{2,0},{3,1},{4,2},{5,3},{6,4},{7,5},{8,14},{9,15},{10,... | collective-permute-start | bytes 18440 | tf_op jit(solution)/shard_map/ppermute | solution.py:100
  62.5 1.6 %collective-permute-done.12 = f32[3,512]{1,0:T(4,128)S(1)} collective-permute-done((f32[3,512]{1,0:T(4,128)S(1)}, f32[3,512]{1,0:T(4,128)S(1)}, u32[]{:S(2)}, u32[]{:S(2)}) %collective-permute-start.12) | collective-permute-done | bytes 6176 | tf_op jit(solution)/shard_map/ppermute | solution.py:100
  64.5 0.9 collective-permute-start.15
  66.0 2.6 %collective-permute-start.16 = (f32[3,512]{1,0:T(4,128)S(1)}, f32[3,512]{1,0:T(4,128)S(1)}, u32[]{:S(2)}, u32[]{:S(2)}) collective-permute-start(f32[3,512]{1,0:T(4,128)S(1)} %get-tuple-element.134), channel_id=1, source_target_pairs={{0,24},{1,25},{2,26},{3,27},{4,28},{5,29},{6,30},{7,31},{8,0},{9,1... | collective-permute-start | bytes 18440 | tf_op jit(solution)/shard_map/ppermute | solution.py:100
  68.6 1.1 collective-permute-done.15
  70.3 0.9 collective-permute-start.19
  71.3 0.9 collective-permute-start.18
  72.2 1.2 collective-permute-start.17
  73.4 3.0 %collective-permute-done.18 = f32[3,512]{1,0:T(4,128)S(1)} collective-permute-done((f32[3,512]{1,0:T(4,128)S(1)}, f32[3,512]{1,0:T(4,128)S(1)}, u32[]{:S(2)}, u32[]{:S(2)}) %collective-permute-start.18) | collective-permute-done | bytes 6176 | tf_op jit(solution)/shard_map/ppermute | solution.py:100
  77.2 3.5 %gather_fusion.3 = f32[512]{0:T(512)S(1)} fusion(f32[512]{0:T(512)S(1)} %get-tuple-element.100, s32[1024]{0:T(1024)S(1)} %pad_clamp_fusion.1), kind=kCustom, calls=%fused_computation.3 | custom fusion | bytes 6144 | tf_op jit(solution)/shard_map/jit(_take)/gather | solution.py:176
  80.7 2.3 %multiply_convert_fusion = bf16[512,1152]{1,0:T(8,128)(2,1)S(1)} fusion(f32[512,1152]{1,0:T(8,128)} %get-tuple-element.183, f32[512,1152]{1,0:T(8,128)S(1)} %get-tuple-element.138, f32[512]{0:T(512)S(1)} %broadcast_select_fusion, f32[512]{0:T(512)S(1)} %get-tuple-element.97), kind=kLoop, calls=%fused_computation.30 | loop fusion | flops 2949120 | bytes 5902336 | tf_op jit(solution)/shard_map/convert_element_type | solution.py:178
  83.0 7.3 %fusion.108 = f32[512,3584]{1,0:T(8,128)S(1)} fusion(bf16[512,1152]{1,0:T(8,128)(2,1)S(1)} %multiply_convert_fusion, bf16[1152,3584]{1,0:T(8,128)(2,1)} %param.9), kind=kOutput, calls=%fused_computation.314 | convolution fusion | flops 4227858432 | bytes 16777216 | tf_op jit(solution)/shard_map/dot_general | solution.py:181
  90.6 3.8 %collective-permute-done.20 = bf16[256,3584]{1,0:T(8,128)(2,1)S(1)} collective-permute-done((bf16[256,3584]{1,0:T(8,128)(2,1)S(1)}, bf16[256,3584]{1,0:T(8,128)(2,1)S(1)}, u32[]{:S(2)}, u32[]{:S(2)}) %collective-permute-start.20) | collective-permute-done | bytes 1835040 | tf_op jit(solution)/shard_map/ppermute | solution.py:100
  95.1 3.2 %collective-permute-start.23 = (bf16[64,3584]{1,0:T(8,128)(2,1)S(1)}, bf16[64,3584]{1,0:T(8,128)(2,1)S(1)}, u32[]{:S(2)}, u32[]{:S(2)}) collective-permute-start(bf16[64,3584]{1,0:T(8,128)(2,1)S(1)} %get-tuple-element.122), channel_id=1, source_target_pairs={{0,6},{1,97},{2,0},{3,99},{4,2},{5,101},{6,4},{7,103},{8,14},{9,10... | collective-permute-start | bytes 1376264 | tf_op jit(solution)/shard_map/ppermute | solution.py:100
  98.3 0.8 collective-permute-start.22
  99.2 6.7 %convolution_convert_fusion = bf16[1152,3584]{1,0:T(8,128)(2,1)} fusion(bf16[512,1152]{1,0:T(8,128)(2,1)S(1)} %multiply_convert_fusion, bf16[512,3584]{1,0:T(8,128)(2,1)S(1)} %bitcast.143), kind=kOutput, calls=%fused_computation.25 | convolution fusion | flops 4231987200 | bytes 13107200 | tf_op jit(solution)/shard_map/dot_general | solution.py:182
  105.9 3.3 %collective-permute-done.23 = bf16[64,3584]{1,0:T(8,128)(2,1)S(1)} collective-permute-done((bf16[64,3584]{1,0:T(8,128)(2,1)S(1)}, bf16[64,3584]{1,0:T(8,128)(2,1)S(1)}, u32[]{:S(2)}, u32[]{:S(2)}) %collective-permute-start.23) | collective-permute-done | bytes 458784 | tf_op jit(solution)/shard_map/ppermute | solution.py:100
  109.2 4.0 %collective-permute-done.21 = bf16[64,3584]{1,0:T(8,128)(2,1)S(1)} collective-permute-done((bf16[64,3584]{1,0:T(8,128)(2,1)S(1)}, bf16[64,3584]{1,0:T(8,128)(2,1)S(1)}, u32[]{:S(2)}, u32[]{:S(2)}) %collective-permute-start.21) | collective-permute-done | bytes 458784 | tf_op jit(solution)/shard_map/ppermute | solution.py:100
  113.6 3.3 %collective-permute-start.26 = (bf16[16,3584]{1,0:T(8,128)(2,1)S(1)}, bf16[16,3584]{1,0:T(8,128)(2,1)S(1)}, u32[]{:S(2)}, u32[]{:S(2)}) collective-permute-start(bf16[16,3584]{1,0:T(8,128)(2,1)S(1)} %get-tuple-element.125), channel_id=1, source_target_pairs={{0,24},{1,25},{2,26},{3,27},{4,28},{5,29},{6,30},{7,31},{8,0},{9,1... | collective-permute-start | bytes 344072 | tf_op jit(solution)/shard_map/ppermute | solution.py:100
  117.8 2.6 %collective-permute-done.26 = bf16[16,3584]{1,0:T(8,128)(2,1)S(1)} collective-permute-done((bf16[16,3584]{1,0:T(8,128)(2,1)S(1)}, bf16[16,3584]{1,0:T(8,128)(2,1)S(1)}, u32[]{:S(2)}, u32[]{:S(2)}) %collective-permute-start.26) | collective-permute-done | bytes 114720 | tf_op jit(solution)/shard_map/ppermute | solution.py:100
  120.5 2.8 %collective-permute-done.25 = bf16[16,3584]{1,0:T(8,128)(2,1)S(1)} collective-permute-done((bf16[16,3584]{1,0:T(8,128)(2,1)S(1)}, bf16[16,3584]{1,0:T(8,128)(2,1)S(1)}, u32[]{:S(2)}, u32[]{:S(2)}) %collective-permute-start.25) | collective-permute-done | bytes 114720 | tf_op jit(solution)/shard_map/ppermute | solution.py:100
  123.3 1.1 collective-permute-done.24
  124.5 1.7 %collective-permute-start.29 = (bf16[4,3584]{1,0:T(4,128)(2,1)S(1)}, bf16[4,3584]{1,0:T(4,128)(2,1)S(1)}, u32[]{:S(2)}, u32[]{:S(2)}) collective-permute-start(bf16[4,3584]{1,0:T(4,128)(2,1)S(1)} %get-tuple-element.128), channel_id=1, source_target_pairs={{0,96},{1,7},{2,98},{3,1},{4,100},{5,3},{6,102},{7,5},{8,104},{9,1... | collective-permute-start | bytes 86024 | tf_op jit(solution)/shard_map/ppermute | solution.py:100
  126.2 0.9 collective-permute-start.28
  128.5 3.1 %collective-permute-done.28 = bf16[4,3584]{1,0:T(4,128)(2,1)S(1)} collective-permute-done((bf16[4,3584]{1,0:T(4,128)(2,1)S(1)}, bf16[4,3584]{1,0:T(4,128)(2,1)S(1)}, u32[]{:S(2)}, u32[]{:S(2)}) %collective-permute-start.28) | collective-permute-done | bytes 28704 | tf_op jit(solution)/shard_map/ppermute | solution.py:100
  (103 shorter events, 15.1 us)
Async XLA Ops:
  0.6 4.7 %collective-permute-start.2 = (bf16[4,3584]{1,0:T(4,128)(2,1)}, bf16[4,3584]{1,0:T(4,128)(2,1)S(1)}, u32[]{:S(2)}, u32[]{:S(2)}) collective-permute-start(bf16[4,3584]{1,0:T(4,128)(2,1)} %param.8), channel_id=1, source_target_pairs={{0,96},{1,7},{2,98},{3,1},{4,100},{5,3},{6,102},{7,5},{8,104},{9,1... | collective-permute-start | bytes 86024 | tf_op jit(solution)/shard_map/ppermute | solution.py:100
  3.5 5.6 %collective-permute-start.1 = (bf16[4,3584]{1,0:T(4,128)(2,1)}, bf16[4,3584]{1,0:T(4,128)(2,1)S(1)}, u32[]{:S(2)}, u32[]{:S(2)}) collective-permute-start(bf16[4,3584]{1,0:T(4,128)(2,1)} %param.8), channel_id=1, source_target_pairs={{0,64},{1,5},{2,66},{3,7},{4,68},{5,1},{6,70},{7,3},{8,72},{9,13},... | collective-permute-start | bytes 86024 | tf_op jit(solution)/shard_map/ppermute | solution.py:100
  4.3 5.3 %collective-permute-start = (bf16[4,3584]{1,0:T(4,128)(2,1)}, bf16[4,3584]{1,0:T(4,128)(2,1)S(1)}, u32[]{:S(2)}, u32[]{:S(2)}) collective-permute-start(bf16[4,3584]{1,0:T(4,128)(2,1)} %param.8), channel_id=1, source_target_pairs={{0,32},{1,3},{2,34},{3,5},{4,36},{5,7},{6,38},{7,1},{8,40},{9,11},... | collective-permute-start | bytes 86024 | tf_op jit(solution)/shard_map/ppermute | solution.py:100
  10.5 17.6 %copy-start.2 = (f32[512,64]{0,1:T(8,128)S(1)}, f32[512,64]{0,1:T(8,128)}, u32[]{:S(2)}) copy-start(f32[512,64]{0,1:T(8,128)} %param.11) | copy-start | bytes 393220
  10.5 7.6 %collective-permute-start.5 = (bf16[16,3584]{1,0:T(8,128)(2,1)S(1)}, bf16[16,3584]{1,0:T(8,128)(2,1)S(1)}, u32[]{:S(2)}, u32[]{:S(2)}) collective-permute-start(bf16[16,3584]{1,0:T(8,128)(2,1)S(1)} %reshape.856), channel_id=1, source_target_pairs={{0,24},{1,25},{2,26},{3,27},{4,28},{5,29},{6,30},{7,31},{8,0},{9,1... | collective-permute-start | bytes 344072 | tf_op jit(solution)/shard_map/ppermute | solution.py:100
  13.6 7.0 %collective-permute-start.4 = (bf16[16,3584]{1,0:T(8,128)(2,1)S(1)}, bf16[16,3584]{1,0:T(8,128)(2,1)S(1)}, u32[]{:S(2)}, u32[]{:S(2)}) collective-permute-start(bf16[16,3584]{1,0:T(8,128)(2,1)S(1)} %reshape.856), channel_id=1, source_target_pairs={{0,16},{1,17},{2,18},{3,19},{4,20},{5,21},{6,22},{7,23},{8,24},{9,... | collective-permute-start | bytes 344072 | tf_op jit(solution)/shard_map/ppermute | solution.py:100
  14.2 7.6 %collective-permute-start.3 = (bf16[16,3584]{1,0:T(8,128)(2,1)S(1)}, bf16[16,3584]{1,0:T(8,128)(2,1)S(1)}, u32[]{:S(2)}, u32[]{:S(2)}) collective-permute-start(bf16[16,3584]{1,0:T(8,128)(2,1)S(1)} %reshape.856), channel_id=1, source_target_pairs={{0,8},{1,9},{2,10},{3,11},{4,12},{5,13},{6,14},{7,15},{8,16},{9,17... | collective-permute-start | bytes 344072 | tf_op jit(solution)/shard_map/ppermute | solution.py:100
  17.3 39.6 %copy-start.3 = (pred[512]{0:T(512)(128)(4,1)}, pred[512]{0:T(512)(128)(4,1)S(1)}, u32[]{:S(2)}) copy-start(pred[512]{0:T(512)(128)(4,1)S(1)} %get-tuple-element.142) | copy-start | bytes 1540
  21.9 14.3 %collective-permute-start.8 = (bf16[64,3584]{1,0:T(8,128)(2,1)S(1)}, bf16[64,3584]{1,0:T(8,128)(2,1)S(1)}, u32[]{:S(2)}, u32[]{:S(2)}) collective-permute-start(bf16[64,3584]{1,0:T(8,128)(2,1)S(1)} %bitcast.145), channel_id=1, source_target_pairs={{0,6},{1,97},{2,0},{3,99},{4,2},{5,101},{6,4},{7,103},{8,14},{9,10... | collective-permute-start | bytes 1376264 | tf_op jit(solution)/shard_map/ppermute | solution.py:100
  25.3 10.9 %collective-permute-start.7 = (bf16[64,3584]{1,0:T(8,128)(2,1)S(1)}, bf16[64,3584]{1,0:T(8,128)(2,1)S(1)}, u32[]{:S(2)}, u32[]{:S(2)}) collective-permute-start(bf16[64,3584]{1,0:T(8,128)(2,1)S(1)} %bitcast.146), channel_id=1, source_target_pairs={{0,4},{1,65},{2,6},{3,67},{4,0},{5,69},{6,2},{7,71},{8,12},{9,73},... | collective-permute-start | bytes 1376264 | tf_op jit(solution)/shard_map/ppermute | solution.py:100
  25.3 14.6 %collective-permute-start.6 = (bf16[64,3584]{1,0:T(8,128)(2,1)S(1)}, bf16[64,3584]{1,0:T(8,128)(2,1)S(1)}, u32[]{:S(2)}, u32[]{:S(2)}) collective-permute-start(bf16[64,3584]{1,0:T(8,128)(2,1)S(1)} %bitcast.147), channel_id=1, source_target_pairs={{0,2},{1,33},{2,4},{3,35},{4,6},{5,37},{6,0},{7,39},{8,10},{9,41},... | collective-permute-start | bytes 1376264 | tf_op jit(solution)/shard_map/ppermute | solution.py:100
  40.1 3.9 %collective-permute-start.9 = (bf16[256,3584]{1,0:T(8,128)(2,1)S(1)}, bf16[256,3584]{1,0:T(8,128)(2,1)S(1)}, u32[]{:S(2)}, u32[]{:S(2)}) collective-permute-start(bf16[256,3584]{1,0:T(8,128)(2,1)S(1)} %bitcast.140), channel_id=1, source_target_pairs={{0,1},{1,0},{2,3},{3,2},{4,5},{5,4},{6,7},{7,6},{8,9},{9,8},{10,11... | collective-permute-start | bytes 5505032 | tf_op jit(solution)/shard_map/ppermute | solution.py:100
  44.4 8.9 %copy-start = (bf16[2,256,3584]{2,1,0:T(8,128)(2,1)}, bf16[2,256,3584]{2,1,0:T(8,128)(2,1)S(1)}, u32[]{:S(2)}) copy-start(bf16[2,256,3584]{2,1,0:T(8,128)(2,1)S(1)} %pad_maximum_fusion) | copy-start | bytes 11010052
  57.1 1.6 %collective-permute-start.10 = (f32[3,512]{0,1:T(8,128)S(1)}, f32[3,512]{0,1:T(8,128)S(1)}, u32[]{:S(2)}, u32[]{:S(2)}) collective-permute-start(f32[3,512]{0,1:T(8,128)S(1)} %bitcast_select_fusion.1), channel_id=1, source_target_pairs={{0,1},{1,0},{2,3},{3,2},{4,5},{5,4},{6,7},{7,6},{8,9},{9,8},{10,11... | collective-permute-start | bytes 18440 | tf_op jit(solution)/shard_map/ppermute | solution.py:100
  58.9 5.2 %collective-permute-start.12 = (f32[3,512]{1,0:T(4,128)S(1)}, f32[3,512]{1,0:T(4,128)S(1)}, u32[]{:S(2)}, u32[]{:S(2)}) collective-permute-start(f32[3,512]{1,0:T(4,128)S(1)} %get-tuple-element.136), channel_id=1, source_target_pairs={{0,4},{1,5},{2,6},{3,7},{4,0},{5,1},{6,2},{7,3},{8,12},{9,13},{10,... | collective-permute-start | bytes 18440 | tf_op jit(solution)/shard_map/ppermute | solution.py:100
  59.3 4.9 %collective-permute-start.11 = (f32[3,512]{1,0:T(4,128)S(1)}, f32[3,512]{1,0:T(4,128)S(1)}, u32[]{:S(2)}, u32[]{:S(2)}) collective-permute-start(f32[3,512]{1,0:T(4,128)S(1)} %get-tuple-element.136), channel_id=1, source_target_pairs={{0,2},{1,3},{2,4},{3,5},{4,6},{5,7},{6,0},{7,1},{8,10},{9,11},{10,... | collective-permute-start | bytes 18440 | tf_op jit(solution)/shard_map/ppermute | solution.py:100
  60.7 3.7 %collective-permute-start.13 = (f32[3,512]{1,0:T(4,128)S(1)}, f32[3,512]{1,0:T(4,128)S(1)}, u32[]{:S(2)}, u32[]{:S(2)}) collective-permute-start(f32[3,512]{1,0:T(4,128)S(1)} %get-tuple-element.136), channel_id=1, source_target_pairs={{0,6},{1,7},{2,0},{3,1},{4,2},{5,3},{6,4},{7,5},{8,14},{9,15},{10,... | collective-permute-start | bytes 18440 | tf_op jit(solution)/shard_map/ppermute | solution.py:100
  64.5 5.2 %collective-permute-start.15 = (f32[3,512]{1,0:T(4,128)S(1)}, f32[3,512]{1,0:T(4,128)S(1)}, u32[]{:S(2)}, u32[]{:S(2)}) collective-permute-start(f32[3,512]{1,0:T(4,128)S(1)} %get-tuple-element.134), channel_id=1, source_target_pairs={{0,16},{1,17},{2,18},{3,19},{4,20},{5,21},{6,22},{7,23},{8,24},{9,... | collective-permute-start | bytes 18440 | tf_op jit(solution)/shard_map/ppermute | solution.py:100
  65.4 4.9 %collective-permute-start.14 = (f32[3,512]{1,0:T(4,128)S(1)}, f32[3,512]{1,0:T(4,128)S(1)}, u32[]{:S(2)}, u32[]{:S(2)}) collective-permute-start(f32[3,512]{1,0:T(4,128)S(1)} %get-tuple-element.134), channel_id=1, source_target_pairs={{0,8},{1,9},{2,10},{3,11},{4,12},{5,13},{6,14},{7,15},{8,16},{9,17... | collective-permute-start | bytes 18440 | tf_op jit(solution)/shard_map/ppermute | solution.py:100
  66.0 4.3 %collective-permute-start.16 = (f32[3,512]{1,0:T(4,128)S(1)}, f32[3,512]{1,0:T(4,128)S(1)}, u32[]{:S(2)}, u32[]{:S(2)}) collective-permute-start(f32[3,512]{1,0:T(4,128)S(1)} %get-tuple-element.134), channel_id=1, source_target_pairs={{0,24},{1,25},{2,26},{3,27},{4,28},{5,29},{6,30},{7,31},{8,0},{9,1... | collective-permute-start | bytes 18440 | tf_op jit(solution)/shard_map/ppermute | solution.py:100
  70.3 6.7 %collective-permute-start.19 = (f32[3,512]{1,0:T(4,128)S(1)}, f32[3,512]{1,0:T(4,128)S(1)}, u32[]{:S(2)}, u32[]{:S(2)}) collective-permute-start(f32[3,512]{1,0:T(4,128)S(1)} %get-tuple-element.132), channel_id=1, source_target_pairs={{0,96},{1,97},{2,98},{3,99},{4,100},{5,101},{6,102},{7,103},{8,104... | collective-permute-start | bytes 18440 | tf_op jit(solution)/shard_map/ppermute | solution.py:100
  71.3 5.2 %collective-permute-start.18 = (f32[3,512]{1,0:T(4,128)S(1)}, f32[3,512]{1,0:T(4,128)S(1)}, u32[]{:S(2)}, u32[]{:S(2)}) collective-permute-start(f32[3,512]{1,0:T(4,128)S(1)} %get-tuple-element.132), channel_id=1, source_target_pairs={{0,64},{1,65},{2,66},{3,67},{4,68},{5,69},{6,70},{7,71},{8,72},{9,... | collective-permute-start | bytes 18440 | tf_op jit(solution)/shard_map/ppermute | solution.py:100
  72.2 4.9 %collective-permute-start.17 = (f32[3,512]{1,0:T(4,128)S(1)}, f32[3,512]{1,0:T(4,128)S(1)}, u32[]{:S(2)}, u32[]{:S(2)}) collective-permute-start(f32[3,512]{1,0:T(4,128)S(1)} %get-tuple-element.132), channel_id=1, source_target_pairs={{0,32},{1,33},{2,34},{3,35},{4,36},{5,37},{6,38},{7,39},{8,40},{9,... | collective-permute-start | bytes 18440 | tf_op jit(solution)/shard_map/ppermute | solution.py:100
  90.5 3.9 %collective-permute-start.20 = (bf16[256,3584]{1,0:T(8,128)(2,1)S(1)}, bf16[256,3584]{1,0:T(8,128)(2,1)S(1)}, u32[]{:S(2)}, u32[]{:S(2)}) collective-permute-start(bf16[256,3584]{1,0:T(8,128)(2,1)S(1)} %slice.277), channel_id=1, source_target_pairs={{0,1},{1,0},{2,3},{3,2},{4,5},{5,4},{6,7},{7,6},{8,9},{9,8},{10,11... | collective-permute-start | bytes 5505032 | tf_op jit(solution)/shard_map/ppermute | solution.py:100
  94.3 4.9 %copy-start.1 = (bf16[2,256,3584]{2,1,0:T(8,128)(2,1)S(1)}, bf16[2,256,3584]{2,1,0:T(8,128)(2,1)}, u32[]{:S(2)}) copy-start(bf16[2,256,3584]{2,1,0:T(8,128)(2,1)} %copy-done) | copy-start | bytes 11010052
  95.1 14.1 %collective-permute-start.23 = (bf16[64,3584]{1,0:T(8,128)(2,1)S(1)}, bf16[64,3584]{1,0:T(8,128)(2,1)S(1)}, u32[]{:S(2)}, u32[]{:S(2)}) collective-permute-start(bf16[64,3584]{1,0:T(8,128)(2,1)S(1)} %get-tuple-element.122), channel_id=1, source_target_pairs={{0,6},{1,97},{2,0},{3,99},{4,2},{5,101},{6,4},{7,103},{8,14},{9,10... | collective-permute-start | bytes 1376264 | tf_op jit(solution)/shard_map/ppermute | solution.py:100
  98.3 10.9 %collective-permute-start.22 = (bf16[64,3584]{1,0:T(8,128)(2,1)S(1)}, bf16[64,3584]{1,0:T(8,128)(2,1)S(1)}, u32[]{:S(2)}, u32[]{:S(2)}) collective-permute-start(bf16[64,3584]{1,0:T(8,128)(2,1)S(1)} %get-tuple-element.123), channel_id=1, source_target_pairs={{0,4},{1,65},{2,6},{3,67},{4,0},{5,69},{6,2},{7,71},{8,12},{9,73},... | collective-permute-start | bytes 1376264 | tf_op jit(solution)/shard_map/ppermute | solution.py:100
  99.1 14.1 %collective-permute-start.21 = (bf16[64,3584]{1,0:T(8,128)(2,1)S(1)}, bf16[64,3584]{1,0:T(8,128)(2,1)S(1)}, u32[]{:S(2)}, u32[]{:S(2)}) collective-permute-start(bf16[64,3584]{1,0:T(8,128)(2,1)S(1)} %get-tuple-element.121), channel_id=1, source_target_pairs={{0,2},{1,33},{2,4},{3,35},{4,6},{5,37},{6,0},{7,39},{8,10},{9,41},... | collective-permute-start | bytes 1376264 | tf_op jit(solution)/shard_map/ppermute | solution.py:100
  113.6 6.8 %collective-permute-start.26 = (bf16[16,3584]{1,0:T(8,128)(2,1)S(1)}, bf16[16,3584]{1,0:T(8,128)(2,1)S(1)}, u32[]{:S(2)}, u32[]{:S(2)}) collective-permute-start(bf16[16,3584]{1,0:T(8,128)(2,1)S(1)} %get-tuple-element.125), channel_id=1, source_target_pairs={{0,24},{1,25},{2,26},{3,27},{4,28},{5,29},{6,30},{7,31},{8,0},{9,1... | collective-permute-start | bytes 344072 | tf_op jit(solution)/shard_map/ppermute | solution.py:100
  116.9 6.4 %collective-permute-start.25 = (bf16[16,3584]{1,0:T(8,128)(2,1)S(1)}, bf16[16,3584]{1,0:T(8,128)(2,1)S(1)}, u32[]{:S(2)}, u32[]{:S(2)}) collective-permute-start(bf16[16,3584]{1,0:T(8,128)(2,1)S(1)} %get-tuple-element.126), channel_id=1, source_target_pairs={{0,16},{1,17},{2,18},{3,19},{4,20},{5,21},{6,22},{7,23},{8,24},{9,... | collective-permute-start | bytes 344072 | tf_op jit(solution)/shard_map/ppermute | solution.py:100
  117.4 7.0 %collective-permute-start.24 = (bf16[16,3584]{1,0:T(8,128)(2,1)S(1)}, bf16[16,3584]{1,0:T(8,128)(2,1)S(1)}, u32[]{:S(2)}, u32[]{:S(2)}) collective-permute-start(bf16[16,3584]{1,0:T(8,128)(2,1)S(1)} %get-tuple-element.124), channel_id=1, source_target_pairs={{0,8},{1,9},{2,10},{3,11},{4,12},{5,13},{6,14},{7,15},{8,16},{9,17... | collective-permute-start | bytes 344072 | tf_op jit(solution)/shard_map/ppermute | solution.py:100
  124.5 3.9 %collective-permute-start.29 = (bf16[4,3584]{1,0:T(4,128)(2,1)S(1)}, bf16[4,3584]{1,0:T(4,128)(2,1)S(1)}, u32[]{:S(2)}, u32[]{:S(2)}) collective-permute-start(bf16[4,3584]{1,0:T(4,128)(2,1)S(1)} %get-tuple-element.128), channel_id=1, source_target_pairs={{0,96},{1,7},{2,98},{3,1},{4,100},{5,3},{6,102},{7,5},{8,104},{9,1... | collective-permute-start | bytes 86024 | tf_op jit(solution)/shard_map/ppermute | solution.py:100
  126.2 5.4 %collective-permute-start.28 = (bf16[4,3584]{1,0:T(4,128)(2,1)S(1)}, bf16[4,3584]{1,0:T(4,128)(2,1)S(1)}, u32[]{:S(2)}, u32[]{:S(2)}) collective-permute-start(bf16[4,3584]{1,0:T(4,128)(2,1)S(1)} %get-tuple-element.129), channel_id=1, source_target_pairs={{0,64},{1,5},{2,66},{3,7},{4,68},{5,1},{6,70},{7,3},{8,72},{9,13},... | collective-permute-start | bytes 86024 | tf_op jit(solution)/shard_map/ppermute | solution.py:100
  127.2 5.1 %collective-permute-start.27 = (bf16[4,3584]{1,0:T(4,128)(2,1)S(1)}, bf16[4,3584]{1,0:T(4,128)(2,1)S(1)}, u32[]{:S(2)}, u32[]{:S(2)}) collective-permute-start(bf16[4,3584]{1,0:T(4,128)(2,1)S(1)} %get-tuple-element.127), channel_id=1, source_target_pairs={{0,32},{1,3},{2,34},{3,5},{4,36},{5,7},{6,38},{7,1},{8,40},{9,11},... | collective-permute-start | bytes 86024 | tf_op jit(solution)/shard_map/ppermute | solution.py:100

commit v4 on v3

--- a/solution.py
+++ b/solution.py
@@ -129,6 +129,12 @@
     return (((s_c * RING + s_r3) * RING + s_y) * RING + s_r1) * 4 + i
 
 
+def half_logits(rows_block, head_weight):
+    return lax.dot_general(
+        rows_block, head_weight, (((1,), (1,)), ((), ())), preferred_element_type=jnp.float32
+    )
+
+
 def per_device(hidden_rows, head_weight, teacher_index, teacher_logprob, n_dev, voc_n):
     voc_dev = head_weight.shape[0]
     tok_dev = hidden_rows.shape[0]
@@ -144,21 +150,27 @@
     probs_arr = jnp.exp(logprob_arr)
     target = teacher_target(local, probs_arr, voc_dev)
 
-    every = hidden_rows
-    for stage in ("r1", "r2", "r3", "c"):
-        got = exchange(lambda s: every, stage, n_dev, voc_n)
-        every = got.reshape(-1, width)
+    own = hidden_rows
+    for stage in ("r1", "r2", "r3"):
+        own = exchange(lambda s: own, stage, n_dev, voc_n).reshape(-1, width)
         if stage == "r3":
-            every, target = lax.optimization_barrier((every, target))
-
-    logits = lax.dot_general(
-        every, head_weight, (((1,), (1,)), ((), ())), preferred_element_type=jnp.float32
-    )
-    part_dot = jnp.sum(logits * target, axis=1)
-    local_peak = jnp.max(logits, axis=1)
-    local_sum = jnp.sum(jnp.exp(logits - local_peak[:, None]), axis=1)
-
-    stats = jnp.take(jnp.stack([local_peak, local_sum, part_dot]), natural_rows(at), axis=1)
+            own, target = lax.optimization_barrier((own, target))
+    other = lax.ppermute(own, AXES, stage_pairs("c", 1, n_dev, voc_n))
+    logits_own = half_logits(own, head_weight)
+    logits_other = half_logits(other, head_weight)
+    every = jnp.concatenate([own, other], axis=0)
+    half = own.shape[0]
+    target_own, target_other = target[:half], target[half:]
+
+    def local_stats(logits, tgt):
+        peak = jnp.max(logits, axis=1)
+        return peak, jnp.sum(jnp.exp(logits - peak[:, None]), axis=1), jnp.sum(logits * tgt, axis=1)
+
+    own_stats = local_stats(logits_own, target_own)
+    other_stats = local_stats(logits_other, target_other)
+    stats = jnp.stack([jnp.concatenate([a, b]) for a, b in zip(own_stats, other_stats)])
+
+    stats = jnp.take(stats, natural_rows(at), axis=1)
     for stage in ("c", "z", "y", "x"):
         got = exchange(lambda s: stats, stage, n_dev, voc_n)
         peak = jnp.max(got[:, 0], axis=0)
@@ -173,20 +185,28 @@
     own_term = jnp.sum(probs * teacher_logprob, axis=1)
     loss_all = own_term - dotted + total_p * lse
     row_loss = lax.dynamic_slice_in_dim(loss_all, position * tok_dev, tok_dev, 0)
-    lse_arr = jnp.take(lse, rows, axis=0)
-    total_arr = jnp.sum(probs_arr, axis=1)
-    grad = (loss_scale * (total_arr[:, None] * jnp.exp(logits - lse_arr[:, None]) - target)).astype(
-        jnp.bfloat16
-    )
-    partial = jnp.dot(grad, head_weight, preferred_element_type=jnp.float32)
+    back = jnp.take(jnp.stack([lse, total_p], axis=1), rows, axis=0)
+    lse_arr, total_arr = back[:, 0], back[:, 1]
+
+    def half_grad(logits, tgt, lse_h, total_h):
+        return (loss_scale * (total_h[:, None] * jnp.exp(logits - lse_h[:, None]) - tgt)).astype(
+            jnp.bfloat16
+        )
+
+    grad_other = half_grad(logits_other, target_other, lse_arr[half:], total_arr[half:])
+    grad_own = half_grad(logits_own, target_own, lse_arr[:half], total_arr[:half])
+
+    sent = jnp.dot(grad_other, head_weight, preferred_element_type=jnp.float32).astype(jnp.bfloat16)
+    received = lax.ppermute(sent, AXES, stage_pairs("c", 1, n_dev, voc_n))
+    acc = jnp.dot(grad_own, head_weight, preferred_element_type=jnp.float32)
+    acc, received = lax.optimization_barrier((acc, received))
+    acc = (acc + received.astype(jnp.float32)).reshape(RING, -1, width)
+    grad = jnp.concatenate([grad_own, grad_other], axis=0)
     head_grad = lax.dot_general(
         grad, every, (((0,), (0,)), ((), ())), preferred_element_type=jnp.float32
     ).astype(jnp.bfloat16)
-
-    acc = partial.reshape(2, -1, width)
-    for stage in ("c", "r3", "r2", "r1"):
-        n = acc.shape[0]
-        got = exchange(lambda s: acc[(-s) % n].astype(jnp.bfloat16), stage, n_dev, voc_n)
+    for stage in ("r3", "r2", "r1"):
+        got = exchange(lambda s: acc[(-s) % RING].astype(jnp.bfloat16), stage, n_dev, voc_n)
         acc = acc[0] + jnp.sum(got[1:].astype(jnp.float32), axis=0)
         if stage == "r3":
             acc, head_grad = lax.optimization_barrier((acc, head_grad))

time: 133 us -> 125 us (0.940)
  waiting for transfers between devices: 47.6 us -> 34.8 us
  starting transfers between devices: 36.5 us -> 42.1 us
  local copies, waits for them, and re-layouts: 9.46 us -> 7.31 us
  matrix products: 22.9 us -> 24.8 us
    ppermute x30 -> x28, waiting for transfers between devices: 47.6 us -> 33.6 us  [exchange(): lax.ppermute(block_for(shift), AXES, stage_pairs(stage, shift, n_dev, voc...]
    ppermute x30 -> x28, starting transfers between devices: 36.5 us -> 41.5 us  [exchange(): lax.ppermute(block_for(shift), AXES, stage_pairs(stage, shift, n_dev, voc...]
    gather x2, local copies, waits for them, and re-layouts: 4.53 us -> 2.08 us  [the longest x1 1.04 us: per_device(): stats = jnp.take(stats, natural_rows(at), axis=1)]
    dot_general x2 -> x4, matrix products: 16.2 us -> 18.1 us  [the longest x2 9.55 us: half_logits(): lax.dot_general(rows_block, head_weight, (((1,), (1,)), ((), ())), prefer...]
    reduce_sum x2 -> x1, other arithmetic: 2.68 us -> 2.23 us  [local_stats(): jnp.sum(logits * tgt, axis=1)]
  transfers between devices with their start and end apart: 30 -> 30, of which waited for: 25 -> 22; matrix products, arithmetic and copies ran while one was open for 13% -> 21% of each run, Pallas kernels for 0% -> 0%
where the time goes in v4:
time: 125 us
  starting transfers between devices  42.1 us (34%)
  waiting for transfers between devices  34.8 us (28%)
  matrix products  24.8 us (20%)
  other arithmetic  13.7 us (11%)
  local copies, waits for them, and re-layouts  7.31 us (6%)
  between operations  1.78 us (1%)
    ppermute x28, starting transfers between devices, exchange(): lax.ppermute(block_for(shift), AXES, stage_pairs(stage, shift, n_dev, voc...  41.5 us
    ppermute x28, waiting for transfers between devices, exchange(): lax.ppermute(block_for(shift), AXES, stage_pairs(stage, shift, n_dev, voc...  33.6 us
    dot_general x2, matrix products, half_logits(): lax.dot_general(rows_block, head_weight, (((1,), (1,)), ((), ())), prefer...  9.55 us
    dot_general x1, matrix products, per_device(): lax.dot_general(grad, every, (((0,), (0,)), ((), ())), preferred_element_...  6.72 us
    dot_general x1, matrix products, per_device(): jnp.dot(grad_other, head_weight, preferred_element_type=jnp.float32)  6.02 us
    add x1, other arithmetic, compact_target(): target + jnp.where(slot_local[:, j:j + 1] == columns, slot_probs[:, j:j +...  3.57 us
    dot_general x1, matrix products, per_device(): acc = jnp.dot(grad_own, head_weight, preferred_element_type=jnp.float32)  2.53 us
  transfers between devices with their start and end apart: 30, of which 22 were waited for; matrix products, arithmetic and copies ran while one was open for 21% of the time, Pallas kernels for 0%

profile of v4, /device:TPU:0, one launch (start us, length us, event | category | flops | bytes accessed | tf_op | source)
XLA Modules:
  0.0 124.6 jit_solution(17395206992087767902)
XLA Ops:
  0.6 1.6 %collective-permute-start = (bf16[4,3584]{1,0:T(4,128)(2,1)}, bf16[4,3584]{1,0:T(4,128)(2,1)S(1)}, u32[]{:S(2)}, u32[]{:S(2)}) collective-permute-start(bf16[4,3584]{1,0:T(4,128)(2,1)} %param.8), channel_id=1, source_target_pairs={{0,32},{1,3},{2,34},{3,5},{4,36},{5,7},{6,38},{7,1},{8,40},{9,11},... | collective-permute-start | bytes 86024 | tf_op jit(solution)/shard_map/ppermute | solution.py:100
  2.3 1.7 %collective-permute-start.2 = (bf16[4,3584]{1,0:T(4,128)(2,1)}, bf16[4,3584]{1,0:T(4,128)(2,1)S(1)}, u32[]{:S(2)}, u32[]{:S(2)}) collective-permute-start(bf16[4,3584]{1,0:T(4,128)(2,1)} %param.8), channel_id=1, source_target_pairs={{0,96},{1,7},{2,98},{3,1},{4,100},{5,3},{6,102},{7,5},{8,104},{9,1... | collective-permute-start | bytes 86024 | tf_op jit(solution)/shard_map/ppermute | solution.py:100
  3.9 1.9 %collective-permute-start.1 = (bf16[4,3584]{1,0:T(4,128)(2,1)}, bf16[4,3584]{1,0:T(4,128)(2,1)S(1)}, u32[]{:S(2)}, u32[]{:S(2)}) collective-permute-start(bf16[4,3584]{1,0:T(4,128)(2,1)} %param.8), channel_id=1, source_target_pairs={{0,64},{1,5},{2,66},{3,7},{4,68},{5,1},{6,70},{7,3},{8,72},{9,13},... | collective-permute-start | bytes 86024 | tf_op jit(solution)/shard_map/ppermute | solution.py:100
  6.4 3.2 %collective-permute-done.1 = bf16[4,3584]{1,0:T(4,128)(2,1)S(1)} collective-permute-done((bf16[4,3584]{1,0:T(4,128)(2,1)}, bf16[4,3584]{1,0:T(4,128)(2,1)S(1)}, u32[]{:S(2)}, u32[]{:S(2)}) %collective-permute-start.1) | collective-permute-done | bytes 28704 | tf_op jit(solution)/shard_map/ppermute | solution.py:100
  10.4 3.2 %collective-permute-start.5 = (bf16[16,3584]{1,0:T(8,128)(2,1)S(1)}, bf16[16,3584]{1,0:T(8,128)(2,1)S(1)}, u32[]{:S(2)}, u32[]{:S(2)}) collective-permute-start(bf16[16,3584]{1,0:T(8,128)(2,1)S(1)} %reshape.862), channel_id=1, source_target_pairs={{0,24},{1,25},{2,26},{3,27},{4,28},{5,29},{6,30},{7,31},{8,0},{9,1... | collective-permute-start | bytes 344072 | tf_op jit(solution)/shard_map/ppermute | solution.py:100
  15.3 1.0 copy.81
  16.3 1.0 gather_fusion.2
  17.9 2.5 %collective-permute-done.4 = bf16[16,3584]{1,0:T(8,128)(2,1)S(1)} collective-permute-done((bf16[16,3584]{1,0:T(8,128)(2,1)S(1)}, bf16[16,3584]{1,0:T(8,128)(2,1)S(1)}, u32[]{:S(2)}, u32[]{:S(2)}) %collective-permute-start.4) | collective-permute-done | bytes 114720 | tf_op jit(solution)/shard_map/ppermute | solution.py:100
  20.4 1.2 collective-permute-done.3
  21.7 3.6 %collective-permute-start.8 = (bf16[64,3584]{1,0:T(8,128)(2,1)S(1)}, bf16[64,3584]{1,0:T(8,128)(2,1)S(1)}, u32[]{:S(2)}, u32[]{:S(2)}) collective-permute-start(bf16[64,3584]{1,0:T(8,128)(2,1)S(1)} %bitcast.143), channel_id=1, source_target_pairs={{0,6},{1,97},{2,0},{3,99},{4,2},{5,101},{6,4},{7,103},{8,14},{9,10... | collective-permute-start | bytes 1376264 | tf_op jit(solution)/shard_map/ppermute | solution.py:100
  25.3 1.3 %collective-permute-start.6 = (bf16[64,3584]{1,0:T(8,128)(2,1)S(1)}, bf16[64,3584]{1,0:T(8,128)(2,1)S(1)}, u32[]{:S(2)}, u32[]{:S(2)}) collective-permute-start(bf16[64,3584]{1,0:T(8,128)(2,1)S(1)} %bitcast.145), channel_id=1, source_target_pairs={{0,2},{1,33},{2,4},{3,35},{4,6},{5,37},{6,0},{7,39},{8,10},{9,41},... | collective-permute-start | bytes 1376264 | tf_op jit(solution)/shard_map/ppermute | solution.py:100
  28.1 5.8 %conditional.1 = (f32[512,1152]{1,0:T(8,128)}) conditional(s32[]{:T(128)} %convert_element_type.46, (s32[512,64]{1,0:T(8,128)S(1)}, pred[512]{0:T(512)(128)(4,1)S(1)}, f32[512,64]{0,1:T(8,128)S(1)}, s32[512,1]{0,1:T(1,128)S(1)}) %tuple.100, (s32[512,64]{1,0:T(8,128)S(1)}, pred[512]{0:T(512)(128)(4,1)S(1)}, f32[512,64]{0,1:T(8,128)S(1)}, ...), branch_computations={%region_3.7_spmd, %region_7.11_spmd} | conditional | flops 17916928 | bytes 5218828 | solution.py:44
  28.9 1.0 gather_fusion
  30.4 3.6 %select_add_fusion = f32[512,1152]{1,0:T(8,128)} fusion(f32[512]{0:T(512)S(1)} %bitcast.188, s32[512]{0:T(512)S(1)} %bitcast.180, f32[512]{0:T(512)S(1)} %bitcast.189, s32[512]{0:T(512)S(1)} %bitcast.181, f32[512]{0:T(512)S(1)} %bitcast.190, s32[512]{0:T(512)S(1)} %bitcast.182, f32[512]{0:T(512)S(1)} %bitcast.191, s32[512]{0:T(512)S(1)} %bitcast.183, ...), kind=kLoop, calls=%fused_computation.6 | loop fusion | flops 13565952 | bytes 2392064 | tf_op jit(solution)/shard_map/cond/branch_0_fun/add | solution.py:37
  33.9 2.3 %collective-permute-done.8 = bf16[64,3584]{1,0:T(8,128)(2,1)S(1)} collective-permute-done((bf16[64,3584]{1,0:T(8,128)(2,1)S(1)}, bf16[64,3584]{1,0:T(8,128)(2,1)S(1)}, u32[]{:S(2)}, u32[]{:S(2)}) %collective-permute-start.8) | collective-permute-done | bytes 458784 | tf_op jit(solution)/shard_map/ppermute | solution.py:100
  36.2 3.7 %collective-permute-done.6 = bf16[64,3584]{1,0:T(8,128)(2,1)S(1)} collective-permute-done((bf16[64,3584]{1,0:T(8,128)(2,1)S(1)}, bf16[64,3584]{1,0:T(8,128)(2,1)S(1)}, u32[]{:S(2)}, u32[]{:S(2)}) %collective-permute-start.6) | collective-permute-done | bytes 458784 | tf_op jit(solution)/shard_map/ppermute | solution.py:100
  40.4 6.9 %fusion.114 = (f32[256]{0:T(256)S(1)}, f32[256,1152]{1,0:T(8,128)S(1)}) fusion(bf16[256,3584]{1,0:T(8,128)(2,1)S(1)} %bitcast.148, bf16[1152,3584]{1,0:T(8,128)(2,1)} %param.9), kind=kOutput, calls=%fused_computation.334 | convolution fusion | flops 2114223872 | bytes 11273216 | tf_op jit(solution)/shard_map/dot_general | solution.py:133
  47.4 2.6 %fusion.113 = (f32[256]{0:T(256)S(1)}, f32[256,1152]{1,0:T(8,128)S(1)}) fusion(bf16[256,3584]{1,0:T(8,128)(2,1)S(1)} %collective-permute-done.9, bf16[1152,3584]{1,0:T(8,128)(2,1)S(1)} %bitcast.213), kind=kOutput, calls=%fused_computation.333 | convolution fusion | flops 2114223872 | bytes 11273216 | tf_op jit(solution)/shard_map/dot_general | solution.py:133
  50.1 2.2 %multiply_reduce_fusion.1 = (f32[256]{0:T(256)S(1)}, f32[256]{0:T(256)S(1)}, f32[256]{0:T(256)S(1)}, f32[256]{0:T(256)S(1)}) fusion(f32[256,1152]{1,0:T(8,128)S(1)} %get-tuple-element.212, f32[512,1152]{1,0:T(8,128)} %get-tuple-element.257, f32[256,1152]{1,0:T(8,128)S(1)} %get-tuple-element.210, f32[256]{0:T(256)S(1)} %get-tuple-element.209, ...), kind=kLoop, calls=%fused_computation.44 | loop fusion | flops 2358272 | bytes 4724736 | tf_op jit(solution)/shard_map/reduce_sum | solution.py:167
  52.5 1.0 gather_fusion.3
  54.0 1.3 %collective-permute-done.10 = f32[3,512]{0,1:T(8,128)S(1)} collective-permute-done((f32[3,512]{0,1:T(8,128)S(1)}, f32[3,512]{0,1:T(8,128)S(1)}, u32[]{:S(2)}, u32[]{:S(2)}) %collective-permute-start.10) | collective-permute-done | bytes 6176 | tf_op jit(solution)/shard_map/ppermute | solution.py:100
  55.9 1.5 %collective-permute-start.11 = (f32[3,512]{1,0:T(4,128)S(1)}, f32[3,512]{1,0:T(4,128)S(1)}, u32[]{:S(2)}, u32[]{:S(2)}) collective-permute-start(f32[3,512]{1,0:T(4,128)S(1)} %get-tuple-element.208), channel_id=1, source_target_pairs={{0,2},{1,3},{2,4},{3,5},{4,6},{5,7},{6,0},{7,1},{8,10},{9,11},{10,... | collective-permute-start | bytes 18440 | tf_op jit(solution)/shard_map/ppermute | solution.py:100
  57.3 1.8 %collective-permute-start.13 = (f32[3,512]{1,0:T(4,128)S(1)}, f32[3,512]{1,0:T(4,128)S(1)}, u32[]{:S(2)}, u32[]{:S(2)}) collective-permute-start(f32[3,512]{1,0:T(4,128)S(1)} %get-tuple-element.208), channel_id=1, source_target_pairs={{0,6},{1,7},{2,0},{3,1},{4,2},{5,3},{6,4},{7,5},{8,14},{9,15},{10,... | collective-permute-start | bytes 18440 | tf_op jit(solution)/shard_map/ppermute | solution.py:100
  59.1 1.6 %collective-permute-done.12 = f32[3,512]{1,0:T(4,128)S(1)} collective-permute-done((f32[3,512]{1,0:T(4,128)S(1)}, f32[3,512]{1,0:T(4,128)S(1)}, u32[]{:S(2)}, u32[]{:S(2)}) %collective-permute-start.12) | collective-permute-done | bytes 6176 | tf_op jit(solution)/shard_map/ppermute | solution.py:100
  62.6 2.6 %collective-permute-start.16 = (f32[3,512]{1,0:T(4,128)S(1)}, f32[3,512]{1,0:T(4,128)S(1)}, u32[]{:S(2)}, u32[]{:S(2)}) collective-permute-start(f32[3,512]{1,0:T(4,128)S(1)} %get-tuple-element.206), channel_id=1, source_target_pairs={{0,24},{1,25},{2,26},{3,27},{4,28},{5,29},{6,30},{7,31},{8,0},{9,1... | collective-permute-start | bytes 18440 | tf_op jit(solution)/shard_map/ppermute | solution.py:100
  65.2 1.1 collective-permute-done.15
  67.0 1.9 %collective-permute-start.18 = (f32[3,512]{1,0:T(4,128)S(1)}, f32[3,512]{1,0:T(4,128)S(1)}, u32[]{:S(2)}, u32[]{:S(2)}) collective-permute-start(f32[3,512]{1,0:T(4,128)S(1)} %get-tuple-element.204), channel_id=1, source_target_pairs={{0,64},{1,65},{2,66},{3,67},{4,68},{5,69},{6,70},{7,71},{8,72},{9,... | collective-permute-start | bytes 18440 | tf_op jit(solution)/shard_map/ppermute | solution.py:100
  69.5 2.6 %collective-permute-start.19 = (f32[3,512]{1,0:T(4,128)S(1)}, f32[3,512]{1,0:T(4,128)S(1)}, u32[]{:S(2)}, u32[]{:S(2)}) collective-permute-start(f32[3,512]{1,0:T(4,128)S(1)} %get-tuple-element.204), channel_id=1, source_target_pairs={{0,96},{1,97},{2,98},{3,99},{4,100},{5,101},{6,102},{7,103},{8,104... | collective-permute-start | bytes 18440 | tf_op jit(solution)/shard_map/ppermute | solution.py:100
  72.2 1.5 %collective-permute-done.17 = f32[3,512]{1,0:T(4,128)S(1)} collective-permute-done((f32[3,512]{1,0:T(4,128)S(1)}, f32[3,512]{1,0:T(4,128)S(1)}, u32[]{:S(2)}, u32[]{:S(2)}) %collective-permute-start.17) | collective-permute-done | bytes 6176 | tf_op jit(solution)/shard_map/ppermute | solution.py:100
  74.0 1.0 gather_fusion.4
  75.5 2.4 %multiply_convert_fusion = (bf16[256,1152]{1,0:T(8,128)(2,1)S(1)}, bf16[256,1152]{1,0:T(8,128)(2,1)S(1)}) fusion(f32[256,1152]{1,0:T(8,128)S(1)} %get-tuple-element.210, f32[512,1152]{1,0:T(8,128)} %get-tuple-element.257, f32[256]{0:T(256)S(1)} %get-tuple-element.144, f32[256]{0:T(256)S(1)} %get-tuple-element.143, f32[256,1152]{1,0:T(8,128)S(1)} %get-tuple-element.212, ...), kind=kLoop, calls=%fused_computation.41 | loop fusion | flops 2949120 | bytes 5902336 | tf_op jit(solution)/shard_map/convert_element_type | solution.py:192
  78.0 6.0 %convolution_convert_fusion.1 = bf16[256,3584]{1,0:T(8,128)(2,1)S(1)} fusion(bf16[256,1152]{1,0:T(8,128)(2,1)S(1)} %get-tuple-element.191, bf16[1152,3584]{1,0:T(8,128)(2,1)} %param.9), kind=kOutput, calls=%fused_computation.31 | convolution fusion | flops 2114846720 | bytes 10682368 | tf_op jit(solution)/shard_map/dot_general | solution.py:199
  84.3 2.5 %fusion.115 = f32[256,3584]{1,0:T(8,128)S(1)} fusion(bf16[256,1152]{1,0:T(8,128)(2,1)S(1)} %get-tuple-element.192, bf16[1152,3584]{1,0:T(8,128)(2,1)S(1)} %bitcast.215), kind=kOutput, calls=%fused_computation.335 | convolution fusion | flops 2113929216 | bytes 12517376 | tf_op jit(solution)/shard_map/dot_general | solution.py:201
  86.9 1.2 collective-permute-done.20
  88.8 1.8 %collective-permute-start.21 = (bf16[64,3584]{1,0:T(8,128)(2,1)S(1)}, bf16[64,3584]{1,0:T(8,128)(2,1)S(1)}, u32[]{:S(2)}, u32[]{:S(2)}) collective-permute-start(bf16[64,3584]{1,0:T(8,128)(2,1)S(1)} %get-tuple-element.193), channel_id=1, source_target_pairs={{0,2},{1,33},{2,4},{3,35},{4,6},{5,37},{6,0},{7,39},{8,10},{9,41},... | collective-permute-start | bytes 1376264 | tf_op jit(solution)/shard_map/ppermute | solution.py:100
  90.6 1.5 %collective-permute-start.23 = (bf16[64,3584]{1,0:T(8,128)(2,1)S(1)}, bf16[64,3584]{1,0:T(8,128)(2,1)S(1)}, u32[]{:S(2)}, u32[]{:S(2)}) collective-permute-start(bf16[64,3584]{1,0:T(8,128)(2,1)S(1)} %get-tuple-element.194), channel_id=1, source_target_pairs={{0,6},{1,97},{2,0},{3,99},{4,2},{5,101},{6,4},{7,103},{8,14},{9,10... | collective-permute-start | bytes 1376264 | tf_op jit(solution)/shard_map/ppermute | solution.py:100
  92.1 1.2 collective-permute-start.22
  93.3 6.7 %convolution_convert_fusion = bf16[1152,3584]{1,0:T(8,128)(2,1)} fusion(bf16[256,3584]{1,0:T(8,128)(2,1)S(1)} %copy-done.4, bf16[256,3584]{1,0:T(8,128)(2,1)S(1)} %bitcast.149, bf16[256,1152]{1,0:T(8,128)(2,1)S(1)} %get-tuple-element.191, bf16[256,1152]{1,0:T(8,128)(2,1)S(1)} %get-tuple-element.192), kind=kOutput, calls=%fused_computation.30 | convolution fusion | flops 4241686528 | bytes 13107200 | tf_op jit(solution)/shard_map/dot_general | solution.py:205
  100.0 4.6 %collective-permute-done.22 = bf16[64,3584]{1,0:T(8,128)(2,1)S(1)} collective-permute-done((bf16[64,3584]{1,0:T(8,128)(2,1)S(1)}, bf16[64,3584]{1,0:T(8,128)(2,1)S(1)}, u32[]{:S(2)}, u32[]{:S(2)}) %collective-permute-start.22) | collective-permute-done | bytes 458784 | tf_op jit(solution)/shard_map/ppermute | solution.py:100
  105.1 1.5 %collective-permute-start.24 = (bf16[16,3584]{1,0:T(8,128)(2,1)S(1)}, bf16[16,3584]{1,0:T(8,128)(2,1)S(1)}, u32[]{:S(2)}, u32[]{:S(2)}) collective-permute-start(bf16[16,3584]{1,0:T(8,128)(2,1)S(1)} %get-tuple-element.196), channel_id=1, source_target_pairs={{0,8},{1,9},{2,10},{3,11},{4,12},{5,13},{6,14},{7,15},{8,16},{9,17... | collective-permute-start | bytes 344072 | tf_op jit(solution)/shard_map/ppermute | solution.py:100
  106.6 1.8 %collective-permute-start.26 = (bf16[16,3584]{1,0:T(8,128)(2,1)S(1)}, bf16[16,3584]{1,0:T(8,128)(2,1)S(1)}, u32[]{:S(2)}, u32[]{:S(2)}) collective-permute-start(bf16[16,3584]{1,0:T(8,128)(2,1)S(1)} %get-tuple-element.197), channel_id=1, source_target_pairs={{0,24},{1,25},{2,26},{3,27},{4,28},{5,29},{6,30},{7,31},{8,0},{9,1... | collective-permute-start | bytes 344072 | tf_op jit(solution)/shard_map/ppermute | solution.py:100
  108.5 1.4 %collective-permute-start.25 = (bf16[16,3584]{1,0:T(8,128)(2,1)S(1)}, bf16[16,3584]{1,0:T(8,128)(2,1)S(1)}, u32[]{:S(2)}, u32[]{:S(2)}) collective-permute-start(bf16[16,3584]{1,0:T(8,128)(2,1)S(1)} %get-tuple-element.198), channel_id=1, source_target_pairs={{0,16},{1,17},{2,18},{3,19},{4,20},{5,21},{6,22},{7,23},{8,24},{9,... | collective-permute-start | bytes 344072 | tf_op jit(solution)/shard_map/ppermute | solution.py:100
  109.9 1.4 %collective-permute-done.24 = bf16[16,3584]{1,0:T(8,128)(2,1)S(1)} collective-permute-done((bf16[16,3584]{1,0:T(8,128)(2,1)S(1)}, bf16[16,3584]{1,0:T(8,128)(2,1)S(1)}, u32[]{:S(2)}, u32[]{:S(2)}) %collective-permute-start.24) | collective-permute-done | bytes 114720 | tf_op jit(solution)/shard_map/ppermute | solution.py:100
  111.2 1.2 collective-permute-done.26
  112.5 2.6 %collective-permute-done.25 = bf16[16,3584]{1,0:T(8,128)(2,1)S(1)} collective-permute-done((bf16[16,3584]{1,0:T(8,128)(2,1)S(1)}, bf16[16,3584]{1,0:T(8,128)(2,1)S(1)}, u32[]{:S(2)}, u32[]{:S(2)}) %collective-permute-start.25) | collective-permute-done | bytes 114720 | tf_op jit(solution)/shard_map/ppermute | solution.py:100
  116.1 2.4 %collective-permute-start.29 = (bf16[4,3584]{1,0:T(4,128)(2,1)S(1)}, bf16[4,3584]{1,0:T(4,128)(2,1)S(1)}, u32[]{:S(2)}, u32[]{:S(2)}) collective-permute-start(bf16[4,3584]{1,0:T(4,128)(2,1)S(1)} %get-tuple-element.200), channel_id=1, source_target_pairs={{0,96},{1,7},{2,98},{3,1},{4,100},{5,3},{6,102},{7,5},{8,104},{9,1... | collective-permute-start | bytes 86024 | tf_op jit(solution)/shard_map/ppermute | solution.py:100
  118.5 1.1 collective-permute-start.28
  120.4 3.5 %collective-permute-done.28 = bf16[4,3584]{1,0:T(4,128)(2,1)S(1)} collective-permute-done((bf16[4,3584]{1,0:T(4,128)(2,1)S(1)}, bf16[4,3584]{1,0:T(4,128)(2,1)S(1)}, u32[]{:S(2)}, u32[]{:S(2)}) %collective-permute-start.28) | collective-permute-done | bytes 28704 | tf_op jit(solution)/shard_map/ppermute | solution.py:100
  (122 shorter events, 15.2 us)
Async XLA Ops:
  0.6 5.4 %collective-permute-start = (bf16[4,3584]{1,0:T(4,128)(2,1)}, bf16[4,3584]{1,0:T(4,128)(2,1)S(1)}, u32[]{:S(2)}, u32[]{:S(2)}) collective-permute-start(bf16[4,3584]{1,0:T(4,128)(2,1)} %param.8), channel_id=1, source_target_pairs={{0,32},{1,3},{2,34},{3,5},{4,36},{5,7},{6,38},{7,1},{8,40},{9,11},... | collective-permute-start | bytes 86024 | tf_op jit(solution)/shard_map/ppermute | solution.py:100
  2.3 4.1 %collective-permute-start.2 = (bf16[4,3584]{1,0:T(4,128)(2,1)}, bf16[4,3584]{1,0:T(4,128)(2,1)S(1)}, u32[]{:S(2)}, u32[]{:S(2)}) collective-permute-start(bf16[4,3584]{1,0:T(4,128)(2,1)} %param.8), channel_id=1, source_target_pairs={{0,96},{1,7},{2,98},{3,1},{4,100},{5,3},{6,102},{7,5},{8,104},{9,1... | collective-permute-start | bytes 86024 | tf_op jit(solution)/shard_map/ppermute | solution.py:100
  3.9 5.6 %collective-permute-start.1 = (bf16[4,3584]{1,0:T(4,128)(2,1)}, bf16[4,3584]{1,0:T(4,128)(2,1)S(1)}, u32[]{:S(2)}, u32[]{:S(2)}) collective-permute-start(bf16[4,3584]{1,0:T(4,128)(2,1)} %param.8), channel_id=1, source_target_pairs={{0,64},{1,5},{2,66},{3,7},{4,68},{5,1},{6,70},{7,3},{8,72},{9,13},... | collective-permute-start | bytes 86024 | tf_op jit(solution)/shard_map/ppermute | solution.py:100
  10.4 17.7 %copy-start.2 = (f32[512,64]{0,1:T(8,128)S(1)}, f32[512,64]{0,1:T(8,128)}, u32[]{:S(2)}) copy-start(f32[512,64]{0,1:T(8,128)} %param.11) | copy-start | bytes 393220
  10.4 7.5 %collective-permute-start.5 = (bf16[16,3584]{1,0:T(8,128)(2,1)S(1)}, bf16[16,3584]{1,0:T(8,128)(2,1)S(1)}, u32[]{:S(2)}, u32[]{:S(2)}) collective-permute-start(bf16[16,3584]{1,0:T(8,128)(2,1)S(1)} %reshape.862), channel_id=1, source_target_pairs={{0,24},{1,25},{2,26},{3,27},{4,28},{5,29},{6,30},{7,31},{8,0},{9,1... | collective-permute-start | bytes 344072 | tf_op jit(solution)/shard_map/ppermute | solution.py:100
  13.6 6.9 %collective-permute-start.4 = (bf16[16,3584]{1,0:T(8,128)(2,1)S(1)}, bf16[16,3584]{1,0:T(8,128)(2,1)S(1)}, u32[]{:S(2)}, u32[]{:S(2)}) collective-permute-start(bf16[16,3584]{1,0:T(8,128)(2,1)S(1)} %reshape.862), channel_id=1, source_target_pairs={{0,16},{1,17},{2,18},{3,19},{4,20},{5,21},{6,22},{7,23},{8,24},{9,... | collective-permute-start | bytes 344072 | tf_op jit(solution)/shard_map/ppermute | solution.py:100
  14.2 7.4 %collective-permute-start.3 = (bf16[16,3584]{1,0:T(8,128)(2,1)S(1)}, bf16[16,3584]{1,0:T(8,128)(2,1)S(1)}, u32[]{:S(2)}, u32[]{:S(2)}) collective-permute-start(bf16[16,3584]{1,0:T(8,128)(2,1)S(1)} %reshape.862), channel_id=1, source_target_pairs={{0,8},{1,9},{2,10},{3,11},{4,12},{5,13},{6,14},{7,15},{8,16},{9,17... | collective-permute-start | bytes 344072 | tf_op jit(solution)/shard_map/ppermute | solution.py:100
  21.7 14.5 %collective-permute-start.8 = (bf16[64,3584]{1,0:T(8,128)(2,1)S(1)}, bf16[64,3584]{1,0:T(8,128)(2,1)S(1)}, u32[]{:S(2)}, u32[]{:S(2)}) collective-permute-start(bf16[64,3584]{1,0:T(8,128)(2,1)S(1)} %bitcast.143), channel_id=1, source_target_pairs={{0,6},{1,97},{2,0},{3,99},{4,2},{5,101},{6,4},{7,103},{8,14},{9,10... | collective-permute-start | bytes 1376264 | tf_op jit(solution)/shard_map/ppermute | solution.py:100
  25.3 10.9 %collective-permute-start.7 = (bf16[64,3584]{1,0:T(8,128)(2,1)S(1)}, bf16[64,3584]{1,0:T(8,128)(2,1)S(1)}, u32[]{:S(2)}, u32[]{:S(2)}) collective-permute-start(bf16[64,3584]{1,0:T(8,128)(2,1)S(1)} %bitcast.144), channel_id=1, source_target_pairs={{0,4},{1,65},{2,6},{3,67},{4,0},{5,69},{6,2},{7,71},{8,12},{9,73},... | collective-permute-start | bytes 1376264 | tf_op jit(solution)/shard_map/ppermute | solution.py:100
  25.3 14.6 %collective-permute-start.6 = (bf16[64,3584]{1,0:T(8,128)(2,1)S(1)}, bf16[64,3584]{1,0:T(8,128)(2,1)S(1)}, u32[]{:S(2)}, u32[]{:S(2)}) collective-permute-start(bf16[64,3584]{1,0:T(8,128)(2,1)S(1)} %bitcast.145), channel_id=1, source_target_pairs={{0,2},{1,33},{2,4},{3,35},{4,6},{5,37},{6,0},{7,39},{8,10},{9,41},... | collective-permute-start | bytes 1376264 | tf_op jit(solution)/shard_map/ppermute | solution.py:100
  39.9 7.5 %slice-start = ((s8[8257536]{0:T(1024)(128)(4,1)}), s8[4194304]{0:T(1024)(128)(4,1)S(1)}, s32[]{:S(2)}) async-start(s8[8257536]{0:T(1024)(128)(4,1)} %bitcast.212), calls=%async_computation | async-start | bytes 8388608
  40.1 7.2 %copy-start = (bf16[4,64,3584]{2,1,0:T(8,128)(2,1)}, bf16[4,64,3584]{2,1,0:T(8,128)(2,1)S(1)}, u32[]{:S(2)}) copy-start(bf16[4,64,3584]{2,1,0:T(8,128)(2,1)S(1)} %pad_maximum_fusion) | copy-start | bytes 5505028
  40.1 7.2 %collective-permute-start.9 = (bf16[256,3584]{1,0:T(8,128)(2,1)S(1)}, bf16[256,3584]{1,0:T(8,128)(2,1)S(1)}, u32[]{:S(2)}, u32[]{:S(2)}) collective-permute-start(bf16[256,3584]{1,0:T(8,128)(2,1)S(1)} %bitcast.147), channel_id=1, source_target_pairs={{0,1},{1,0},{2,3},{3,2},{4,5},{5,4},{6,7},{7,6},{8,9},{9,8},{10,11... | collective-permute-start | bytes 5505032 | tf_op jit(solution)/shard_map/ppermute | solution.py:158
  40.4 7.0 %slice-start.1 = ((s8[8257536]{0:T(1024)(128)(4,1)}), s8[4063232]{0:T(1024)(128)(4,1)S(1)}, s32[]{:S(2)}) async-start(s8[8257536]{0:T(1024)(128)(4,1)} %bitcast.212), calls=%async_computation.1 | async-start | bytes 8126464
  47.4 2.6 %copy-start.3 = (bf16[256,3584]{1,0:T(8,128)(2,1)}, bf16[256,3584]{1,0:T(8,128)(2,1)S(1)}, u32[]{:S(2)}) copy-start(bf16[256,3584]{1,0:T(8,128)(2,1)S(1)} %collective-permute-done.9) | copy-start | bytes 5505028
  53.7 1.6 %collective-permute-start.10 = (f32[3,512]{0,1:T(8,128)S(1)}, f32[3,512]{0,1:T(8,128)S(1)}, u32[]{:S(2)}, u32[]{:S(2)}) collective-permute-start(f32[3,512]{0,1:T(8,128)S(1)} %bitcast_select_fusion.1), channel_id=1, source_target_pairs={{0,1},{1,0},{2,3},{3,2},{4,5},{5,4},{6,7},{7,6},{8,9},{9,8},{10,11... | collective-permute-start | bytes 18440 | tf_op jit(solution)/shard_map/ppermute | solution.py:100
  55.5 5.2 %collective-permute-start.12 = (f32[3,512]{1,0:T(4,128)S(1)}, f32[3,512]{1,0:T(4,128)S(1)}, u32[]{:S(2)}, u32[]{:S(2)}) collective-permute-start(f32[3,512]{1,0:T(4,128)S(1)} %get-tuple-element.208), channel_id=1, source_target_pairs={{0,4},{1,5},{2,6},{3,7},{4,0},{5,1},{6,2},{7,3},{8,12},{9,13},{10,... | collective-permute-start | bytes 18440 | tf_op jit(solution)/shard_map/ppermute | solution.py:100
  55.9 4.9 %collective-permute-start.11 = (f32[3,512]{1,0:T(4,128)S(1)}, f32[3,512]{1,0:T(4,128)S(1)}, u32[]{:S(2)}, u32[]{:S(2)}) collective-permute-start(f32[3,512]{1,0:T(4,128)S(1)} %get-tuple-element.208), channel_id=1, source_target_pairs={{0,2},{1,3},{2,4},{3,5},{4,6},{5,7},{6,0},{7,1},{8,10},{9,11},{10,... | collective-permute-start | bytes 18440 | tf_op jit(solution)/shard_map/ppermute | solution.py:100
  57.3 3.7 %collective-permute-start.13 = (f32[3,512]{1,0:T(4,128)S(1)}, f32[3,512]{1,0:T(4,128)S(1)}, u32[]{:S(2)}, u32[]{:S(2)}) collective-permute-start(f32[3,512]{1,0:T(4,128)S(1)} %get-tuple-element.208), channel_id=1, source_target_pairs={{0,6},{1,7},{2,0},{3,1},{4,2},{5,3},{6,4},{7,5},{8,14},{9,15},{10,... | collective-permute-start | bytes 18440 | tf_op jit(solution)/shard_map/ppermute | solution.py:100
  61.1 5.2 %collective-permute-start.15 = (f32[3,512]{1,0:T(4,128)S(1)}, f32[3,512]{1,0:T(4,128)S(1)}, u32[]{:S(2)}, u32[]{:S(2)}) collective-permute-start(f32[3,512]{1,0:T(4,128)S(1)} %get-tuple-element.206), channel_id=1, source_target_pairs={{0,16},{1,17},{2,18},{3,19},{4,20},{5,21},{6,22},{7,23},{8,24},{9,... | collective-permute-start | bytes 18440 | tf_op jit(solution)/shard_map/ppermute | solution.py:100
  62.0 4.9 %collective-permute-start.14 = (f32[3,512]{1,0:T(4,128)S(1)}, f32[3,512]{1,0:T(4,128)S(1)}, u32[]{:S(2)}, u32[]{:S(2)}) collective-permute-start(f32[3,512]{1,0:T(4,128)S(1)} %get-tuple-element.206), channel_id=1, source_target_pairs={{0,8},{1,9},{2,10},{3,11},{4,12},{5,13},{6,14},{7,15},{8,16},{9,17... | collective-permute-start | bytes 18440 | tf_op jit(solution)/shard_map/ppermute | solution.py:100
  62.6 4.2 %collective-permute-start.16 = (f32[3,512]{1,0:T(4,128)S(1)}, f32[3,512]{1,0:T(4,128)S(1)}, u32[]{:S(2)}, u32[]{:S(2)}) collective-permute-start(f32[3,512]{1,0:T(4,128)S(1)} %get-tuple-element.206), channel_id=1, source_target_pairs={{0,24},{1,25},{2,26},{3,27},{4,28},{5,29},{6,30},{7,31},{8,0},{9,1... | collective-permute-start | bytes 18440 | tf_op jit(solution)/shard_map/ppermute | solution.py:100
  67.0 5.2 %collective-permute-start.18 = (f32[3,512]{1,0:T(4,128)S(1)}, f32[3,512]{1,0:T(4,128)S(1)}, u32[]{:S(2)}, u32[]{:S(2)}) collective-permute-start(f32[3,512]{1,0:T(4,128)S(1)} %get-tuple-element.204), channel_id=1, source_target_pairs={{0,64},{1,65},{2,66},{3,67},{4,68},{5,69},{6,70},{7,71},{8,72},{9,... | collective-permute-start | bytes 18440 | tf_op jit(solution)/shard_map/ppermute | solution.py:100
  68.9 4.9 %collective-permute-start.17 = (f32[3,512]{1,0:T(4,128)S(1)}, f32[3,512]{1,0:T(4,128)S(1)}, u32[]{:S(2)}, u32[]{:S(2)}) collective-permute-start(f32[3,512]{1,0:T(4,128)S(1)} %get-tuple-element.204), channel_id=1, source_target_pairs={{0,32},{1,33},{2,34},{3,35},{4,36},{5,37},{6,38},{7,39},{8,40},{9,... | collective-permute-start | bytes 18440 | tf_op jit(solution)/shard_map/ppermute | solution.py:100
  69.5 4.3 %collective-permute-start.19 = (f32[3,512]{1,0:T(4,128)S(1)}, f32[3,512]{1,0:T(4,128)S(1)}, u32[]{:S(2)}, u32[]{:S(2)}) collective-permute-start(f32[3,512]{1,0:T(4,128)S(1)} %get-tuple-element.204), channel_id=1, source_target_pairs={{0,96},{1,97},{2,98},{3,99},{4,100},{5,101},{6,102},{7,103},{8,104... | collective-permute-start | bytes 18440 | tf_op jit(solution)/shard_map/ppermute | solution.py:100
  75.5 8.8 %slice-start.2 = ((s8[8257536]{0:T(1024)(128)(4,1)}), s8[4063232]{0:T(1024)(128)(4,1)S(1)}, s32[]{:S(2)}) async-start(s8[8257536]{0:T(1024)(128)(4,1)} %bitcast.214), calls=%async_computation.2 | async-start | bytes 8126464
  77.9 6.4 %slice-start.3 = ((s8[8257536]{0:T(1024)(128)(4,1)}), s8[4194304]{0:T(1024)(128)(4,1)S(1)}, s32[]{:S(2)}) async-start(s8[8257536]{0:T(1024)(128)(4,1)} %bitcast.214), calls=%async_computation.3 | async-start | bytes 8388608
  84.0 4.1 %collective-permute-start.20 = (bf16[256,3584]{1,0:T(8,128)(2,1)S(1)}, bf16[256,3584]{1,0:T(8,128)(2,1)S(1)}, u32[]{:S(2)}, u32[]{:S(2)}) collective-permute-start(bf16[256,3584]{1,0:T(8,128)(2,1)S(1)} %convolution_convert_fusion.1), channel_id=1, source_target_pairs={{0,1},{1,0},{2,3},{3,2},{4,5},{5,4},{6,7},{7,6},{8,9},{9,8},{10,11... | collective-permute-start | bytes 5505032 | tf_op jit(solution)/shard_map/ppermute | solution.py:200
  88.1 5.2 %copy-start.4 = (bf16[256,3584]{1,0:T(8,128)(2,1)S(1)}, bf16[256,3584]{1,0:T(8,128)(2,1)}, u32[]{:S(2)}) copy-start(bf16[256,3584]{1,0:T(8,128)(2,1)} %copy-done.3) | copy-start | bytes 5505028
  88.7 4.6 %copy-start.1 = (bf16[4,64,3584]{2,1,0:T(8,128)(2,1)S(1)}, bf16[4,64,3584]{2,1,0:T(8,128)(2,1)}, u32[]{:S(2)}) copy-start(bf16[4,64,3584]{2,1,0:T(8,128)(2,1)} %copy-done) | copy-start | bytes 5505028
  88.8 11.3 %collective-permute-start.21 = (bf16[64,3584]{1,0:T(8,128)(2,1)S(1)}, bf16[64,3584]{1,0:T(8,128)(2,1)S(1)}, u32[]{:S(2)}, u32[]{:S(2)}) collective-permute-start(bf16[64,3584]{1,0:T(8,128)(2,1)S(1)} %get-tuple-element.193), channel_id=1, source_target_pairs={{0,2},{1,33},{2,4},{3,35},{4,6},{5,37},{6,0},{7,39},{8,10},{9,41},... | collective-permute-start | bytes 1376264 | tf_op jit(solution)/shard_map/ppermute | solution.py:100
  90.6 9.4 %collective-permute-start.23 = (bf16[64,3584]{1,0:T(8,128)(2,1)S(1)}, bf16[64,3584]{1,0:T(8,128)(2,1)S(1)}, u32[]{:S(2)}, u32[]{:S(2)}) collective-permute-start(bf16[64,3584]{1,0:T(8,128)(2,1)S(1)} %get-tuple-element.194), channel_id=1, source_target_pairs={{0,6},{1,97},{2,0},{3,99},{4,2},{5,101},{6,4},{7,103},{8,14},{9,10... | collective-permute-start | bytes 1376264 | tf_op jit(solution)/shard_map/ppermute | solution.py:100
  92.1 12.6 %collective-permute-start.22 = (bf16[64,3584]{1,0:T(8,128)(2,1)S(1)}, bf16[64,3584]{1,0:T(8,128)(2,1)S(1)}, u32[]{:S(2)}, u32[]{:S(2)}) collective-permute-start(bf16[64,3584]{1,0:T(8,128)(2,1)S(1)} %get-tuple-element.195), channel_id=1, source_target_pairs={{0,4},{1,65},{2,6},{3,67},{4,0},{5,69},{6,2},{7,71},{8,12},{9,73},... | collective-permute-start | bytes 1376264 | tf_op jit(solution)/shard_map/ppermute | solution.py:100
  105.1 6.1 %collective-permute-start.24 = (bf16[16,3584]{1,0:T(8,128)(2,1)S(1)}, bf16[16,3584]{1,0:T(8,128)(2,1)S(1)}, u32[]{:S(2)}, u32[]{:S(2)}) collective-permute-start(bf16[16,3584]{1,0:T(8,128)(2,1)S(1)} %get-tuple-element.196), channel_id=1, source_target_pairs={{0,8},{1,9},{2,10},{3,11},{4,12},{5,13},{6,14},{7,15},{8,16},{9,17... | collective-permute-start | bytes 344072 | tf_op jit(solution)/shard_map/ppermute | solution.py:100
  106.6 5.8 %collective-permute-start.26 = (bf16[16,3584]{1,0:T(8,128)(2,1)S(1)}, bf16[16,3584]{1,0:T(8,128)(2,1)S(1)}, u32[]{:S(2)}, u32[]{:S(2)}) collective-permute-start(bf16[16,3584]{1,0:T(8,128)(2,1)S(1)} %get-tuple-element.197), channel_id=1, source_target_pairs={{0,24},{1,25},{2,26},{3,27},{4,28},{5,29},{6,30},{7,31},{8,0},{9,1... | collective-permute-start | bytes 344072 | tf_op jit(solution)/shard_map/ppermute | solution.py:100
  108.5 6.6 %collective-permute-start.25 = (bf16[16,3584]{1,0:T(8,128)(2,1)S(1)}, bf16[16,3584]{1,0:T(8,128)(2,1)S(1)}, u32[]{:S(2)}, u32[]{:S(2)}) collective-permute-start(bf16[16,3584]{1,0:T(8,128)(2,1)S(1)} %get-tuple-element.198), channel_id=1, source_target_pairs={{0,16},{1,17},{2,18},{3,19},{4,20},{5,21},{6,22},{7,23},{8,24},{9,... | collective-permute-start | bytes 344072 | tf_op jit(solution)/shard_map/ppermute | solution.py:100
  115.2 5.2 %collective-permute-start.27 = (bf16[4,3584]{1,0:T(4,128)(2,1)S(1)}, bf16[4,3584]{1,0:T(4,128)(2,1)S(1)}, u32[]{:S(2)}, u32[]{:S(2)}) collective-permute-start(bf16[4,3584]{1,0:T(4,128)(2,1)S(1)} %get-tuple-element.199), channel_id=1, source_target_pairs={{0,32},{1,3},{2,34},{3,5},{4,36},{5,7},{6,38},{7,1},{8,40},{9,11},... | collective-permute-start | bytes 86024 | tf_op jit(solution)/shard_map/ppermute | solution.py:100
  116.1 4.3 %collective-permute-start.29 = (bf16[4,3584]{1,0:T(4,128)(2,1)S(1)}, bf16[4,3584]{1,0:T(4,128)(2,1)S(1)}, u32[]{:S(2)}, u32[]{:S(2)}) collective-permute-start(bf16[4,3584]{1,0:T(4,128)(2,1)S(1)} %get-tuple-element.200), channel_id=1, source_target_pairs={{0,96},{1,7},{2,98},{3,1},{4,100},{5,3},{6,102},{7,5},{8,104},{9,1... | collective-permute-start | bytes 86024 | tf_op jit(solution)/shard_map/ppermute | solution.py:100
  118.5 5.4 %collective-permute-start.28 = (bf16[4,3584]{1,0:T(4,128)(2,1)S(1)}, bf16[4,3584]{1,0:T(4,128)(2,1)S(1)}, u32[]{:S(2)}, u32[]{:S(2)}) collective-permute-start(bf16[4,3584]{1,0:T(4,128)(2,1)S(1)} %get-tuple-element.201), channel_id=1, source_target_pairs={{0,64},{1,5},{2,66},{3,7},{4,68},{5,1},{6,70},{7,3},{8,72},{9,13},... | collective-permute-start | bytes 86024 | tf_op jit(solution)/shard_map/ppermute | solution.py:100

commit v5 on v4

--- a/solution.py
+++ b/solution.py
@@ -2,6 +2,8 @@
 import jax.numpy as jnp
 from jax import lax
 from jax.sharding import PartitionSpec as P
+from jax.experimental import pallas as pl
+from jax.experimental.pallas import tpu as pltpu
 
 loss_scale = 256.0
 RING = 4
@@ -129,10 +131,46 @@
     return (((s_c * RING + s_r3) * RING + s_y) * RING + s_r1) * 4 + i
 
 
-def half_logits(rows_block, head_weight):
-    return lax.dot_general(
-        rows_block, head_weight, (((1,), (1,)), ((), ())), preferred_element_type=jnp.float32
+def _rows_by_weight(g_ref, w_ref, o_ref):
+    o_ref[...] = jnp.dot(g_ref[...], w_ref[...], preferred_element_type=jnp.float32).astype(o_ref.dtype)
+
+
+def rows_by_weight(g, w, out_dtype, tile=512):
+    m, k = g.shape
+    n = w.shape[1]
+    return pl.pallas_call(
+        _rows_by_weight,
+        grid=(n // tile,),
+        in_specs=[pl.BlockSpec((m, k), lambda j: (0, 0)), pl.BlockSpec((k, tile), lambda j: (0, j))],
+        out_specs=pl.BlockSpec((m, tile), lambda j: (0, j)),
+        out_shape=jax.ShapeDtypeStruct((m, n), out_dtype),
+        cost_estimate=pl.CostEstimate(
+            flops=2 * m * k * n,
+            transcendentals=0,
+            bytes_accessed=(m * k + k * n) * 2 + m * n * jnp.dtype(out_dtype).itemsize,
+        ),
+    )(g, w)
+
+
+def _rows_by_weight_t(x_ref, w_ref, o_ref):
+    o_ref[...] = lax.dot_general(
+        x_ref[...], w_ref[...], (((1,), (1,)), ((), ())), preferred_element_type=jnp.float32
     )
+
+
+def half_logits(x, w, tile=384):
+    m, d = x.shape
+    v = w.shape[0]
+    return pl.pallas_call(
+        _rows_by_weight_t,
+        grid=(v // tile,),
+        in_specs=[pl.BlockSpec((m, d), lambda j: (0, 0)), pl.BlockSpec((tile, d), lambda j: (j, 0))],
+        out_specs=pl.BlockSpec((m, tile), lambda j: (0, j)),
+        out_shape=jax.ShapeDtypeStruct((m, v), jnp.float32),
+        cost_estimate=pl.CostEstimate(
+            flops=2 * m * d * v, transcendentals=0, bytes_accessed=(m * d + v * d) * 2 + m * v * 4
+        ),
+    )(x, w)
 
 
 def per_device(hidden_rows, head_weight, teacher_index, teacher_logprob, n_dev, voc_n):
@@ -196,9 +234,9 @@
     grad_other = half_grad(logits_other, target_other, lse_arr[half:], total_arr[half:])
     grad_own = half_grad(logits_own, target_own, lse_arr[:half], total_arr[:half])
 
-    sent = jnp.dot(grad_other, head_weight, preferred_element_type=jnp.float32).astype(jnp.bfloat16)
+    sent = rows_by_weight(grad_other, head_weight, jnp.bfloat16)
     received = lax.ppermute(sent, AXES, stage_pairs("c", 1, n_dev, voc_n))
-    acc = jnp.dot(grad_own, head_weight, preferred_element_type=jnp.float32)
+    acc = rows_by_weight(grad_own, head_weight, jnp.float32)
     acc, received = lax.optimization_barrier((acc, received))
     acc = (acc + received.astype(jnp.float32)).reshape(RING, -1, width)
     grad = jnp.concatenate([grad_own, grad_other], axis=0)

time: 125 us -> 147 us (1.18)
  Pallas kernels: 0 us -> 31.9 us
  matrix products: 24.8 us -> 7.96 us
  other arithmetic: 13.7 us -> 21.1 us
  waiting for transfers between devices: 34.8 us -> 32.6 us
  local copies, waits for them, and re-layouts: 7.31 us -> 9.19 us
    pallas_call x0 -> x4, Pallas kernels: none -> 31.9 us  [the longest x2 17.2 us: rows_by_weight(): pl.pallas_call(_rows_by_weight, grid=(n // tile,), in_specs=[pl.BlockSpec...]
    dot_general x4 -> x0, matrix products: 18.1 us -> none  [the longest x2 9.55 us: half_logits(): lax.dot_general(rows_block, head_weight, (((1,), (1,)), ((), ())), prefer...]
    reduce_max x0 -> x2, other arithmetic: none -> 2.82 us  [local_stats(): peak = jnp.max(logits, axis=1)]
    another operation x3, other arithmetic: 0.69 us -> 2.78 us
    unnamed x19 -> x21, local copies, waits for them, and re-layouts: 1.07 us -> 2.95 us
  transfers between devices with their start and end apart: 30 -> 30, of which waited for: 22 -> 20; matrix products, arithmetic and copies ran while one was open for 21% -> 13% of each run, Pallas kernels for 0% -> 11%
where the time goes in v5:
time: 147 us; the launch traced here: 146 us
  starting transfers between devices  41.4 us (28%)
  waiting for transfers between devices  32.6 us (22%)
  Pallas kernels  31.9 us (22%)
  other arithmetic  21.1 us (14%)
  local copies, waits for them, and re-layouts  9.19 us (6%)
  matrix products  7.96 us (5%)
  between operations  1.7 us (1%)
    ppermute x28, starting transfers between devices, exchange(): lax.ppermute(block_for(shift), AXES, stage_pairs(stage, shift, n_dev, voc...  41.3 us
    ppermute x28, waiting for transfers between devices, exchange(): lax.ppermute(block_for(shift), AXES, stage_pairs(stage, shift, n_dev, voc...  32.6 us
    pallas_call x2, Pallas kernels, rows_by_weight(): pl.pallas_call(_rows_by_weight, grid=(n // tile,), in_specs=[pl.BlockSpec...  17.2 us
    pallas_call x2, Pallas kernels, half_logits(): pl.pallas_call(_rows_by_weight_t, grid=(v // tile,), in_specs=[pl.BlockSp...  14.7 us
    dot_general x1, matrix products, per_device(): lax.dot_general(grad, every, (((0,), (0,)), ((), ())), preferred_element_...  7.96 us
    add x1, other arithmetic, compact_target(): target + jnp.where(slot_local[:, j:j + 1] == columns, slot_probs[:, j:j +...  3.57 us
    convert_element_type x1, other arithmetic, half_grad(): (loss_scale * (total_h[:, None] * jnp.exp(logits - lse_h[:, None]) - tgt)...  3.27 us
    unnamed x21, local copies, waits for them, and re-layouts  2.95 us
  transfers between devices with their start and end apart: 30, of which 20 were waited for; matrix products, arithmetic and copies ran while one was open for 13% of the time, Pallas kernels for 11%

profile of v5, /device:TPU:0, one launch (start us, length us, event | category | flops | bytes accessed | tf_op | source)
XLA Modules:
  0.0 146.0 jit_solution(10955674729816675526)
XLA Ops:
  0.6 1.6 %collective-permute-start = (bf16[4,3584]{1,0:T(4,128)(2,1)}, bf16[4,3584]{1,0:T(4,128)(2,1)S(1)}, u32[]{:S(2)}, u32[]{:S(2)}) collective-permute-start(bf16[4,3584]{1,0:T(4,128)(2,1)} %param.8), channel_id=1, source_target_pairs={{0,32},{1,3},{2,34},{3,5},{4,36},{5,7},{6,38},{7,1},{8,40},{9,11},... | collective-permute-start | bytes 86024 | tf_op jit(solution)/shard_map/ppermute | solution.py:102
  2.3 1.7 %collective-permute-start.2 = (bf16[4,3584]{1,0:T(4,128)(2,1)}, bf16[4,3584]{1,0:T(4,128)(2,1)S(1)}, u32[]{:S(2)}, u32[]{:S(2)}) collective-permute-start(bf16[4,3584]{1,0:T(4,128)(2,1)} %param.8), channel_id=1, source_target_pairs={{0,96},{1,7},{2,98},{3,1},{4,100},{5,3},{6,102},{7,5},{8,104},{9,1... | collective-permute-start | bytes 86024 | tf_op jit(solution)/shard_map/ppermute | solution.py:102
  3.9 1.9 %collective-permute-start.1 = (bf16[4,3584]{1,0:T(4,128)(2,1)}, bf16[4,3584]{1,0:T(4,128)(2,1)S(1)}, u32[]{:S(2)}, u32[]{:S(2)}) collective-permute-start(bf16[4,3584]{1,0:T(4,128)(2,1)} %param.8), channel_id=1, source_target_pairs={{0,64},{1,5},{2,66},{3,7},{4,68},{5,1},{6,70},{7,3},{8,72},{9,13},... | collective-permute-start | bytes 86024 | tf_op jit(solution)/shard_map/ppermute | solution.py:102
  6.4 3.2 %collective-permute-done.1 = bf16[4,3584]{1,0:T(4,128)(2,1)S(1)} collective-permute-done((bf16[4,3584]{1,0:T(4,128)(2,1)}, bf16[4,3584]{1,0:T(4,128)(2,1)S(1)}, u32[]{:S(2)}, u32[]{:S(2)}) %collective-permute-start.1) | collective-permute-done | bytes 28704 | tf_op jit(solution)/shard_map/ppermute | solution.py:102
  10.4 3.2 %collective-permute-start.5 = (bf16[16,3584]{1,0:T(8,128)(2,1)S(1)}, bf16[16,3584]{1,0:T(8,128)(2,1)S(1)}, u32[]{:S(2)}, u32[]{:S(2)}) collective-permute-start(bf16[16,3584]{1,0:T(8,128)(2,1)S(1)} %reshape.862), channel_id=1, source_target_pairs={{0,24},{1,25},{2,26},{3,27},{4,28},{5,29},{6,30},{7,31},{8,0},{9,1... | collective-permute-start | bytes 344072 | tf_op jit(solution)/shard_map/ppermute | solution.py:102
  16.3 1.0 gather_fusion.2
  17.9 2.5 %collective-permute-done.4 = bf16[16,3584]{1,0:T(8,128)(2,1)S(1)} collective-permute-done((bf16[16,3584]{1,0:T(8,128)(2,1)S(1)}, bf16[16,3584]{1,0:T(8,128)(2,1)S(1)}, u32[]{:S(2)}, u32[]{:S(2)}) %collective-permute-start.4) | collective-permute-done | bytes 114720 | tf_op jit(solution)/shard_map/ppermute | solution.py:102
  20.4 1.2 collective-permute-done.3
  21.7 3.6 %collective-permute-start.8 = (bf16[64,3584]{1,0:T(8,128)(2,1)S(1)}, bf16[64,3584]{1,0:T(8,128)(2,1)S(1)}, u32[]{:S(2)}, u32[]{:S(2)}) collective-permute-start(bf16[64,3584]{1,0:T(8,128)(2,1)S(1)} %bitcast.138), channel_id=1, source_target_pairs={{0,6},{1,97},{2,0},{3,99},{4,2},{5,101},{6,4},{7,103},{8,14},{9,10... | collective-permute-start | bytes 1376264 | tf_op jit(solution)/shard_map/ppermute | solution.py:102
  25.3 1.3 collective-permute-start.6
  28.1 5.8 %conditional.1 = (f32[512,1152]{1,0:T(8,128)}) conditional(s32[]{:T(128)} %convert_element_type.43, (s32[512,64]{1,0:T(8,128)S(1)}, pred[512]{0:T(512)(128)(4,1)S(1)}, f32[512,64]{0,1:T(8,128)S(1)}, s32[512,1]{0,1:T(1,128)S(1)}) %tuple.98, (s32[512,64]{1,0:T(8,128)S(1)}, pred[512]{0:T(512)(128)(4,1)S(1)}, f32[512,64]{0,1:T(8,128)S(1)}, ...), branch_computations={%region_3.7_spmd, %region_7.11_spmd} | conditional | flops 17916928 | bytes 5218828 | solution.py:46
  30.4 3.6 %select_add_fusion = f32[512,1152]{1,0:T(8,128)} fusion(f32[512]{0:T(512)S(1)} %bitcast.180, s32[512]{0:T(512)S(1)} %bitcast.172, f32[512]{0:T(512)S(1)} %bitcast.181, s32[512]{0:T(512)S(1)} %bitcast.173, f32[512]{0:T(512)S(1)} %bitcast.182, s32[512]{0:T(512)S(1)} %bitcast.174, f32[512]{0:T(512)S(1)} %bitcast.183, s32[512]{0:T(512)S(1)} %bitcast.175, ...), kind=kLoop, calls=%fused_computation.6 | loop fusion | flops 13565952 | bytes 2392064 | tf_op jit(solution)/shard_map/cond/branch_0_fun/add | solution.py:39
  33.9 2.3 %collective-permute-done.8 = bf16[64,3584]{1,0:T(8,128)(2,1)S(1)} collective-permute-done((bf16[64,3584]{1,0:T(8,128)(2,1)S(1)}, bf16[64,3584]{1,0:T(8,128)(2,1)S(1)}, u32[]{:S(2)}, u32[]{:S(2)}) %collective-permute-start.8) | collective-permute-done | bytes 458784 | tf_op jit(solution)/shard_map/ppermute | solution.py:102
  36.2 3.7 %collective-permute-done.6 = bf16[64,3584]{1,0:T(8,128)(2,1)S(1)} collective-permute-done((bf16[64,3584]{1,0:T(8,128)(2,1)S(1)}, bf16[64,3584]{1,0:T(8,128)(2,1)S(1)}, u32[]{:S(2)}, u32[]{:S(2)}) %collective-permute-start.6) | collective-permute-done | bytes 458784 | tf_op jit(solution)/shard_map/ppermute | solution.py:102
  40.7 1.5 %pad_maximum_fusion = bf16[4,64,3584]{2,1,0:T(8,128)(2,1)S(1)} fusion(bf16[1,64,3584]{2,1,0:T(8,128)(2,1)} %bitcast.144, bf16[1,64,3584]{2,1,0:T(8,128)(2,1)} %bitcast.145, bf16[1,64,3584]{2,1,0:T(8,128)(2,1)} %bitcast.146, bf16[1,64,3584]{2,1,0:T(8,128)(2,1)S(1)} %bitcast.141), kind=kLoop, calls=%fused_computation.36 | loop fusion | flops 2752512 | bytes 3670016 | tf_op jit(solution)/shard_map/stack | solution.py:103
  42.3 1.1 copy-done.2
  43.4 7.3 %shard_map.67 = f32[256,1152]{1,0:T(8,128)} custom-call(bf16[256,3584]{1,0:T(8,128)(2,1)} %bitcast.136, bf16[1152,3584]{1,0:T(8,128)(2,1)} %w_ref.7), custom_call_target="tpu_custom_call" | custom-call | flops 2113929216 | bytes 11272192 | tf_op jit(solution)/shard_map/pallas_call | solution.py:164
  50.7 1.4 reduce_max.54
  52.1 7.4 %shard_map.68 = f32[256,1152]{1,0:T(8,128)} custom-call(bf16[256,3584]{1,0:T(8,128)(2,1)} %collective-permute-done.9.x_ref, bf16[1152,3584]{1,0:T(8,128)(2,1)} %w_ref.7), custom_call_target="tpu_custom_call" | custom-call | flops 2113929216 | bytes 11272192 | tf_op jit(solution)/shard_map/pallas_call | solution.py:164
  59.5 1.4 reduce_max.55
  61.0 2.6 %multiply_reduce_fusion.1 = (f32[256]{0:T(256)S(1)}, f32[256]{0:T(256)S(1)}, f32[256]{0:T(256)S(1)}, f32[256]{0:T(256)S(1)}) fusion(f32[256,1152]{1,0:T(8,128)S(1)} %copy-done, f32[512,1152]{1,0:T(8,128)} %get-tuple-element.253, f32[256,1152]{1,0:T(8,128)} %shard_map.68, f32[256]{0:T(256)S(1)} %reduce_max.55, f32[256]{0:T(256)S(1)} %reduce_max.54), kind=kLoop, calls=%fused_computation.43 | loop fusion | flops 2358272 | bytes 4724736 | tf_op jit(solution)/shard_map/reduce_sum | solution.py:205
  63.7 1.0 gather_fusion.3
  65.3 1.3 collective-permute-done.10
  67.1 1.5 %collective-permute-start.11 = (f32[3,512]{1,0:T(4,128)S(1)}, f32[3,512]{1,0:T(4,128)S(1)}, u32[]{:S(2)}, u32[]{:S(2)}) collective-permute-start(f32[3,512]{1,0:T(4,128)S(1)} %get-tuple-element.208), channel_id=1, source_target_pairs={{0,2},{1,3},{2,4},{3,5},{4,6},{5,7},{6,0},{7,1},{8,10},{9,11},{10,... | collective-permute-start | bytes 18440 | tf_op jit(solution)/shard_map/ppermute | solution.py:102
  68.6 1.8 %collective-permute-start.13 = (f32[3,512]{1,0:T(4,128)S(1)}, f32[3,512]{1,0:T(4,128)S(1)}, u32[]{:S(2)}, u32[]{:S(2)}) collective-permute-start(f32[3,512]{1,0:T(4,128)S(1)} %get-tuple-element.208), channel_id=1, source_target_pairs={{0,6},{1,7},{2,0},{3,1},{4,2},{5,3},{6,4},{7,5},{8,14},{9,15},{10,... | collective-permute-start | bytes 18440 | tf_op jit(solution)/shard_map/ppermute | solution.py:102
  70.4 1.7 %collective-permute-done.12 = f32[3,512]{1,0:T(4,128)S(1)} collective-permute-done((f32[3,512]{1,0:T(4,128)S(1)}, f32[3,512]{1,0:T(4,128)S(1)}, u32[]{:S(2)}, u32[]{:S(2)}) %collective-permute-start.12) | collective-permute-done | bytes 6176 | tf_op jit(solution)/shard_map/ppermute | solution.py:102
  73.9 2.6 %collective-permute-start.16 = (f32[3,512]{1,0:T(4,128)S(1)}, f32[3,512]{1,0:T(4,128)S(1)}, u32[]{:S(2)}, u32[]{:S(2)}) collective-permute-start(f32[3,512]{1,0:T(4,128)S(1)} %get-tuple-element.206), channel_id=1, source_target_pairs={{0,24},{1,25},{2,26},{3,27},{4,28},{5,29},{6,30},{7,31},{8,0},{9,1... | collective-permute-start | bytes 18440 | tf_op jit(solution)/shard_map/ppermute | solution.py:102
  76.5 1.1 collective-permute-done.15
  78.2 1.9 %collective-permute-start.18 = (f32[3,512]{1,0:T(4,128)S(1)}, f32[3,512]{1,0:T(4,128)S(1)}, u32[]{:S(2)}, u32[]{:S(2)}) collective-permute-start(f32[3,512]{1,0:T(4,128)S(1)} %get-tuple-element.204), channel_id=1, source_target_pairs={{0,64},{1,65},{2,66},{3,67},{4,68},{5,69},{6,70},{7,71},{8,72},{9,... | collective-permute-start | bytes 18440 | tf_op jit(solution)/shard_map/ppermute | solution.py:102
  80.7 2.6 %collective-permute-start.19 = (f32[3,512]{1,0:T(4,128)S(1)}, f32[3,512]{1,0:T(4,128)S(1)}, u32[]{:S(2)}, u32[]{:S(2)}) collective-permute-start(f32[3,512]{1,0:T(4,128)S(1)} %get-tuple-element.204), channel_id=1, source_target_pairs={{0,96},{1,97},{2,98},{3,99},{4,100},{5,101},{6,102},{7,103},{8,104... | collective-permute-start | bytes 18440 | tf_op jit(solution)/shard_map/ppermute | solution.py:102
  83.5 1.5 %collective-permute-done.17 = f32[3,512]{1,0:T(4,128)S(1)} collective-permute-done((f32[3,512]{1,0:T(4,128)S(1)}, f32[3,512]{1,0:T(4,128)S(1)}, u32[]{:S(2)}, u32[]{:S(2)}) %collective-permute-start.17) | collective-permute-done | bytes 6176 | tf_op jit(solution)/shard_map/ppermute | solution.py:102
  86.8 3.3 %multiply_convert_fusion = (bf16[256,1152]{1,0:T(8,128)(2,1)}, bf16[256,1152]{1,0:T(8,128)(2,1)}) fusion(f32[256,1152]{1,0:T(8,128)S(1)} %copy-done.1, f32[512,1152]{1,0:T(8,128)} %get-tuple-element.253, f32[256]{0:T(256)S(1)} %get-tuple-element.144, f32[256]{0:T(256)S(1)} %get-tuple-element.143, f32[256,1152]{1,0:T(8,128)S(1)} %copy-done, ...), kind=kLoop, calls=%fused_computation.40 | loop fusion | flops 2949120 | bytes 5902336 | tf_op jit(solution)/shard_map/convert_element_type | solution.py:230
  90.1 8.4 %shard_map.70 = bf16[256,3584]{1,0:T(8,128)(2,1)} custom-call(bf16[256,1152]{1,0:T(8,128)(2,1)} %get-tuple-element.191.g_ref, bf16[1152,3584]{1,0:T(8,128)(2,1)} %w_ref.7), custom_call_target="tpu_custom_call" | custom-call | flops 2113929216 | bytes 10682368 | tf_op jit(solution)/shard_map/pallas_call | solution.py:141
  98.5 8.8 %shard_map.69 = f32[256,3584]{1,0:T(8,128)} custom-call(bf16[256,1152]{1,0:T(8,128)(2,1)} %get-tuple-element.192.g_ref, bf16[1152,3584]{1,0:T(8,128)(2,1)} %w_ref.7), custom_call_target="tpu_custom_call" | custom-call | flops 2113929216 | bytes 12517376 | tf_op jit(solution)/shard_map/pallas_call | solution.py:141
  107.3 2.7 %fusion.105 = (bf16[256,3584]{1,0:T(8,128)(2,1)S(1)}, f32[256,3584]{1,0:T(8,128)S(1)}) fusion(f32[256,3584]{1,0:T(8,128)} %shard_map.69, bf16[256,3584]{1,0:T(8,128)(2,1)S(1)} %collective-permute-done.20), kind=kLoop, calls=%fused_computation.325 | loop fusion | flops 2752512 | bytes 11010048 | tf_op jit(solution)/shard_map/convert.8
  110.1 1.8 %collective-permute-start.21 = (bf16[64,3584]{1,0:T(8,128)(2,1)S(1)}, bf16[64,3584]{1,0:T(8,128)(2,1)S(1)}, u32[]{:S(2)}, u32[]{:S(2)}) collective-permute-start(bf16[64,3584]{1,0:T(8,128)(2,1)S(1)} %get-tuple-element.193), channel_id=1, source_target_pairs={{0,2},{1,33},{2,4},{3,35},{4,6},{5,37},{6,0},{7,39},{8,10},{9,41},... | collective-permute-start | bytes 1376264 | tf_op jit(solution)/shard_map/ppermute | solution.py:102
  111.9 1.5 %collective-permute-start.23 = (bf16[64,3584]{1,0:T(8,128)(2,1)S(1)}, bf16[64,3584]{1,0:T(8,128)(2,1)S(1)}, u32[]{:S(2)}, u32[]{:S(2)}) collective-permute-start(bf16[64,3584]{1,0:T(8,128)(2,1)S(1)} %get-tuple-element.194), channel_id=1, source_target_pairs={{0,6},{1,97},{2,0},{3,99},{4,2},{5,101},{6,4},{7,103},{8,14},{9,10... | collective-permute-start | bytes 1376264 | tf_op jit(solution)/shard_map/ppermute | solution.py:102
  113.4 1.2 collective-permute-start.22
  114.6 8.0 %convolution_convert_fusion = bf16[1152,3584]{1,0:T(8,128)(2,1)} fusion(bf16[256,3584]{1,0:T(8,128)(2,1)} %collective-permute-done.9.x_ref, bf16[256,3584]{1,0:T(8,128)(2,1)S(1)} %bitcast.137, bf16[256,1152]{1,0:T(8,128)(2,1)S(1)} %copy-done.5, bf16[256,1152]{1,0:T(8,128)(2,1)S(1)} %copy-done.4), kind=kOutput, calls=%fused_computation.30 | convolution fusion | flops 4241686528 | bytes 13107200 | tf_op jit(solution)/shard_map/dot_general | solution.py:243
  122.6 3.4 %collective-permute-done.22 = bf16[64,3584]{1,0:T(8,128)(2,1)S(1)} collective-permute-done((bf16[64,3584]{1,0:T(8,128)(2,1)S(1)}, bf16[64,3584]{1,0:T(8,128)(2,1)S(1)}, u32[]{:S(2)}, u32[]{:S(2)}) %collective-permute-start.22) | collective-permute-done | bytes 458784 | tf_op jit(solution)/shard_map/ppermute | solution.py:102
  126.4 1.5 %collective-permute-start.24 = (bf16[16,3584]{1,0:T(8,128)(2,1)S(1)}, bf16[16,3584]{1,0:T(8,128)(2,1)S(1)}, u32[]{:S(2)}, u32[]{:S(2)}) collective-permute-start(bf16[16,3584]{1,0:T(8,128)(2,1)S(1)} %get-tuple-element.196), channel_id=1, source_target_pairs={{0,8},{1,9},{2,10},{3,11},{4,12},{5,13},{6,14},{7,15},{8,16},{9,17... | collective-permute-start | bytes 344072 | tf_op jit(solution)/shard_map/ppermute | solution.py:102
  127.9 1.8 %collective-permute-start.26 = (bf16[16,3584]{1,0:T(8,128)(2,1)S(1)}, bf16[16,3584]{1,0:T(8,128)(2,1)S(1)}, u32[]{:S(2)}, u32[]{:S(2)}) collective-permute-start(bf16[16,3584]{1,0:T(8,128)(2,1)S(1)} %get-tuple-element.197), channel_id=1, source_target_pairs={{0,24},{1,25},{2,26},{3,27},{4,28},{5,29},{6,30},{7,31},{8,0},{9,1... | collective-permute-start | bytes 344072 | tf_op jit(solution)/shard_map/ppermute | solution.py:102
  129.8 1.4 collective-permute-start.25
  131.2 1.7 %collective-permute-done.24 = bf16[16,3584]{1,0:T(8,128)(2,1)S(1)} collective-permute-done((bf16[16,3584]{1,0:T(8,128)(2,1)S(1)}, bf16[16,3584]{1,0:T(8,128)(2,1)S(1)}, u32[]{:S(2)}, u32[]{:S(2)}) %collective-permute-start.24) | collective-permute-done | bytes 114720 | tf_op jit(solution)/shard_map/ppermute | solution.py:102
  132.9 1.8 %collective-permute-done.26 = bf16[16,3584]{1,0:T(8,128)(2,1)S(1)} collective-permute-done((bf16[16,3584]{1,0:T(8,128)(2,1)S(1)}, bf16[16,3584]{1,0:T(8,128)(2,1)S(1)}, u32[]{:S(2)}, u32[]{:S(2)}) %collective-permute-start.26) | collective-permute-done | bytes 114720 | tf_op jit(solution)/shard_map/ppermute | solution.py:102
  134.7 1.8 %collective-permute-done.25 = bf16[16,3584]{1,0:T(8,128)(2,1)S(1)} collective-permute-done((bf16[16,3584]{1,0:T(8,128)(2,1)S(1)}, bf16[16,3584]{1,0:T(8,128)(2,1)S(1)}, u32[]{:S(2)}, u32[]{:S(2)}) %collective-permute-start.25) | collective-permute-done | bytes 114720 | tf_op jit(solution)/shard_map/ppermute | solution.py:102
  137.6 2.4 %collective-permute-start.29 = (bf16[4,3584]{1,0:T(4,128)(2,1)S(1)}, bf16[4,3584]{1,0:T(4,128)(2,1)S(1)}, u32[]{:S(2)}, u32[]{:S(2)}) collective-permute-start(bf16[4,3584]{1,0:T(4,128)(2,1)S(1)} %get-tuple-element.200), channel_id=1, source_target_pairs={{0,96},{1,7},{2,98},{3,1},{4,100},{5,3},{6,102},{7,5},{8,104},{9,1... | collective-permute-start | bytes 86024 | tf_op jit(solution)/shard_map/ppermute | solution.py:102
  141.8 3.5 %collective-permute-done.28 = bf16[4,3584]{1,0:T(4,128)(2,1)S(1)} collective-permute-done((bf16[4,3584]{1,0:T(4,128)(2,1)S(1)}, bf16[4,3584]{1,0:T(4,128)(2,1)S(1)}, u32[]{:S(2)}, u32[]{:S(2)}) %collective-permute-start.28) | collective-permute-done | bytes 28704 | tf_op jit(solution)/shard_map/ppermute | solution.py:102
  (124 shorter events, 18.8 us)
Async XLA Ops:
  0.6 5.4 %collective-permute-start = (bf16[4,3584]{1,0:T(4,128)(2,1)}, bf16[4,3584]{1,0:T(4,128)(2,1)S(1)}, u32[]{:S(2)}, u32[]{:S(2)}) collective-permute-start(bf16[4,3584]{1,0:T(4,128)(2,1)} %param.8), channel_id=1, source_target_pairs={{0,32},{1,3},{2,34},{3,5},{4,36},{5,7},{6,38},{7,1},{8,40},{9,11},... | collective-permute-start | bytes 86024 | tf_op jit(solution)/shard_map/ppermute | solution.py:102
  2.3 4.1 %collective-permute-start.2 = (bf16[4,3584]{1,0:T(4,128)(2,1)}, bf16[4,3584]{1,0:T(4,128)(2,1)S(1)}, u32[]{:S(2)}, u32[]{:S(2)}) collective-permute-start(bf16[4,3584]{1,0:T(4,128)(2,1)} %param.8), channel_id=1, source_target_pairs={{0,96},{1,7},{2,98},{3,1},{4,100},{5,3},{6,102},{7,5},{8,104},{9,1... | collective-permute-start | bytes 86024 | tf_op jit(solution)/shard_map/ppermute | solution.py:102
  3.9 5.6 %collective-permute-start.1 = (bf16[4,3584]{1,0:T(4,128)(2,1)}, bf16[4,3584]{1,0:T(4,128)(2,1)S(1)}, u32[]{:S(2)}, u32[]{:S(2)}) collective-permute-start(bf16[4,3584]{1,0:T(4,128)(2,1)} %param.8), channel_id=1, source_target_pairs={{0,64},{1,5},{2,66},{3,7},{4,68},{5,1},{6,70},{7,3},{8,72},{9,13},... | collective-permute-start | bytes 86024 | tf_op jit(solution)/shard_map/ppermute | solution.py:102
  10.4 17.7 %copy-start.6 = (f32[512,64]{0,1:T(8,128)S(1)}, f32[512,64]{0,1:T(8,128)}, u32[]{:S(2)}) copy-start(f32[512,64]{0,1:T(8,128)} %param.11) | copy-start | bytes 393220
  10.4 7.5 %collective-permute-start.5 = (bf16[16,3584]{1,0:T(8,128)(2,1)S(1)}, bf16[16,3584]{1,0:T(8,128)(2,1)S(1)}, u32[]{:S(2)}, u32[]{:S(2)}) collective-permute-start(bf16[16,3584]{1,0:T(8,128)(2,1)S(1)} %reshape.862), channel_id=1, source_target_pairs={{0,24},{1,25},{2,26},{3,27},{4,28},{5,29},{6,30},{7,31},{8,0},{9,1... | collective-permute-start | bytes 344072 | tf_op jit(solution)/shard_map/ppermute | solution.py:102
  13.6 6.9 %collective-permute-start.4 = (bf16[16,3584]{1,0:T(8,128)(2,1)S(1)}, bf16[16,3584]{1,0:T(8,128)(2,1)S(1)}, u32[]{:S(2)}, u32[]{:S(2)}) collective-permute-start(bf16[16,3584]{1,0:T(8,128)(2,1)S(1)} %reshape.862), channel_id=1, source_target_pairs={{0,16},{1,17},{2,18},{3,19},{4,20},{5,21},{6,22},{7,23},{8,24},{9,... | collective-permute-start | bytes 344072 | tf_op jit(solution)/shard_map/ppermute | solution.py:102
  14.2 7.4 %collective-permute-start.3 = (bf16[16,3584]{1,0:T(8,128)(2,1)S(1)}, bf16[16,3584]{1,0:T(8,128)(2,1)S(1)}, u32[]{:S(2)}, u32[]{:S(2)}) collective-permute-start(bf16[16,3584]{1,0:T(8,128)(2,1)S(1)} %reshape.862), channel_id=1, source_target_pairs={{0,8},{1,9},{2,10},{3,11},{4,12},{5,13},{6,14},{7,15},{8,16},{9,17... | collective-permute-start | bytes 344072 | tf_op jit(solution)/shard_map/ppermute | solution.py:102
  21.7 14.5 %collective-permute-start.8 = (bf16[64,3584]{1,0:T(8,128)(2,1)S(1)}, bf16[64,3584]{1,0:T(8,128)(2,1)S(1)}, u32[]{:S(2)}, u32[]{:S(2)}) collective-permute-start(bf16[64,3584]{1,0:T(8,128)(2,1)S(1)} %bitcast.138), channel_id=1, source_target_pairs={{0,6},{1,97},{2,0},{3,99},{4,2},{5,101},{6,4},{7,103},{8,14},{9,10... | collective-permute-start | bytes 1376264 | tf_op jit(solution)/shard_map/ppermute | solution.py:102
  25.3 10.9 %collective-permute-start.7 = (bf16[64,3584]{1,0:T(8,128)(2,1)S(1)}, bf16[64,3584]{1,0:T(8,128)(2,1)S(1)}, u32[]{:S(2)}, u32[]{:S(2)}) collective-permute-start(bf16[64,3584]{1,0:T(8,128)(2,1)S(1)} %bitcast.139), channel_id=1, source_target_pairs={{0,4},{1,65},{2,6},{3,67},{4,0},{5,69},{6,2},{7,71},{8,12},{9,73},... | collective-permute-start | bytes 1376264 | tf_op jit(solution)/shard_map/ppermute | solution.py:102
  25.3 14.6 %collective-permute-start.6 = (bf16[64,3584]{1,0:T(8,128)(2,1)S(1)}, bf16[64,3584]{1,0:T(8,128)(2,1)S(1)}, u32[]{:S(2)}, u32[]{:S(2)}) collective-permute-start(bf16[64,3584]{1,0:T(8,128)(2,1)S(1)} %bitcast.140), channel_id=1, source_target_pairs={{0,2},{1,33},{2,4},{3,35},{4,6},{5,37},{6,0},{7,39},{8,10},{9,41},... | collective-permute-start | bytes 1376264 | tf_op jit(solution)/shard_map/ppermute | solution.py:102
  36.2 3.7 %copy-start.7 = (bf16[64,3584]{1,0:T(8,128)(2,1)}, bf16[64,3584]{1,0:T(8,128)(2,1)S(1)}, u32[]{:S(2)}) copy-start(bf16[64,3584]{1,0:T(8,128)(2,1)S(1)} %collective-permute-done.8) | copy-start | bytes 1376260
  36.2 3.7 %copy-start.8 = (bf16[64,3584]{1,0:T(8,128)(2,1)}, bf16[64,3584]{1,0:T(8,128)(2,1)S(1)}, u32[]{:S(2)}) copy-start(bf16[64,3584]{1,0:T(8,128)(2,1)S(1)} %collective-permute-done.7) | copy-start | bytes 1376260
  39.9 0.8 copy-start.9
  42.2 1.2 copy-start.2
  42.2 9.9 %collective-permute-start.9 = (bf16[256,3584]{1,0:T(8,128)(2,1)S(1)}, bf16[256,3584]{1,0:T(8,128)(2,1)}, u32[]{:S(2)}, u32[]{:S(2)}) collective-permute-start(bf16[256,3584]{1,0:T(8,128)(2,1)S(1)} %bitcast.135), channel_id=1, source_target_pairs={{0,1},{1,0},{2,3},{3,2},{4,5},{5,4},{6,7},{7,6},{8,9},{9,8},{10,11... | collective-permute-start | bytes 5505032 | tf_op jit(solution)/shard_map/ppermute | solution.py:196
  52.1 8.8 %copy-start = (f32[256,1152]{1,0:T(8,128)S(1)}, f32[256,1152]{1,0:T(8,128)}, u32[]{:S(2)}) copy-start(f32[256,1152]{1,0:T(8,128)} %shard_map.67) | copy-start | bytes 3538948
  64.9 1.6 %collective-permute-start.10 = (f32[3,512]{0,1:T(8,128)S(1)}, f32[3,512]{0,1:T(8,128)S(1)}, u32[]{:S(2)}, u32[]{:S(2)}) collective-permute-start(f32[3,512]{0,1:T(8,128)S(1)} %bitcast_select_fusion.1), channel_id=1, source_target_pairs={{0,1},{1,0},{2,3},{3,2},{4,5},{5,4},{6,7},{7,6},{8,9},{9,8},{10,11... | collective-permute-start | bytes 18440 | tf_op jit(solution)/shard_map/ppermute | solution.py:102
  66.6 20.2 %copy-start.1 = (f32[256,1152]{1,0:T(8,128)S(1)}, f32[256,1152]{1,0:T(8,128)}, u32[]{:S(2)}) copy-start(f32[256,1152]{1,0:T(8,128)} %shard_map.68) | copy-start | bytes 3538948
  66.8 5.3 %collective-permute-start.12 = (f32[3,512]{1,0:T(4,128)S(1)}, f32[3,512]{1,0:T(4,128)S(1)}, u32[]{:S(2)}, u32[]{:S(2)}) collective-permute-start(f32[3,512]{1,0:T(4,128)S(1)} %get-tuple-element.208), channel_id=1, source_target_pairs={{0,4},{1,5},{2,6},{3,7},{4,0},{5,1},{6,2},{7,3},{8,12},{9,13},{10,... | collective-permute-start | bytes 18440 | tf_op jit(solution)/shard_map/ppermute | solution.py:102
  67.1 5.0 %collective-permute-start.11 = (f32[3,512]{1,0:T(4,128)S(1)}, f32[3,512]{1,0:T(4,128)S(1)}, u32[]{:S(2)}, u32[]{:S(2)}) collective-permute-start(f32[3,512]{1,0:T(4,128)S(1)} %get-tuple-element.208), channel_id=1, source_target_pairs={{0,2},{1,3},{2,4},{3,5},{4,6},{5,7},{6,0},{7,1},{8,10},{9,11},{10,... | collective-permute-start | bytes 18440 | tf_op jit(solution)/shard_map/ppermute | solution.py:102
  68.6 3.7 %collective-permute-start.13 = (f32[3,512]{1,0:T(4,128)S(1)}, f32[3,512]{1,0:T(4,128)S(1)}, u32[]{:S(2)}, u32[]{:S(2)}) collective-permute-start(f32[3,512]{1,0:T(4,128)S(1)} %get-tuple-element.208), channel_id=1, source_target_pairs={{0,6},{1,7},{2,0},{3,1},{4,2},{5,3},{6,4},{7,5},{8,14},{9,15},{10,... | collective-permute-start | bytes 18440 | tf_op jit(solution)/shard_map/ppermute | solution.py:102
  72.3 5.2 %collective-permute-start.15 = (f32[3,512]{1,0:T(4,128)S(1)}, f32[3,512]{1,0:T(4,128)S(1)}, u32[]{:S(2)}, u32[]{:S(2)}) collective-permute-start(f32[3,512]{1,0:T(4,128)S(1)} %get-tuple-element.206), channel_id=1, source_target_pairs={{0,16},{1,17},{2,18},{3,19},{4,20},{5,21},{6,22},{7,23},{8,24},{9,... | collective-permute-start | bytes 18440 | tf_op jit(solution)/shard_map/ppermute | solution.py:102
  73.2 4.9 %collective-permute-start.14 = (f32[3,512]{1,0:T(4,128)S(1)}, f32[3,512]{1,0:T(4,128)S(1)}, u32[]{:S(2)}, u32[]{:S(2)}) collective-permute-start(f32[3,512]{1,0:T(4,128)S(1)} %get-tuple-element.206), channel_id=1, source_target_pairs={{0,8},{1,9},{2,10},{3,11},{4,12},{5,13},{6,14},{7,15},{8,16},{9,17... | collective-permute-start | bytes 18440 | tf_op jit(solution)/shard_map/ppermute | solution.py:102
  73.9 4.2 %collective-permute-start.16 = (f32[3,512]{1,0:T(4,128)S(1)}, f32[3,512]{1,0:T(4,128)S(1)}, u32[]{:S(2)}, u32[]{:S(2)}) collective-permute-start(f32[3,512]{1,0:T(4,128)S(1)} %get-tuple-element.206), channel_id=1, source_target_pairs={{0,24},{1,25},{2,26},{3,27},{4,28},{5,29},{6,30},{7,31},{8,0},{9,1... | collective-permute-start | bytes 18440 | tf_op jit(solution)/shard_map/ppermute | solution.py:102
  78.2 5.2 %collective-permute-start.18 = (f32[3,512]{1,0:T(4,128)S(1)}, f32[3,512]{1,0:T(4,128)S(1)}, u32[]{:S(2)}, u32[]{:S(2)}) collective-permute-start(f32[3,512]{1,0:T(4,128)S(1)} %get-tuple-element.204), channel_id=1, source_target_pairs={{0,64},{1,65},{2,66},{3,67},{4,68},{5,69},{6,70},{7,71},{8,72},{9,... | collective-permute-start | bytes 18440 | tf_op jit(solution)/shard_map/ppermute | solution.py:102
  80.1 4.9 %collective-permute-start.17 = (f32[3,512]{1,0:T(4,128)S(1)}, f32[3,512]{1,0:T(4,128)S(1)}, u32[]{:S(2)}, u32[]{:S(2)}) collective-permute-start(f32[3,512]{1,0:T(4,128)S(1)} %get-tuple-element.204), channel_id=1, source_target_pairs={{0,32},{1,33},{2,34},{3,35},{4,36},{5,37},{6,38},{7,39},{8,40},{9,... | collective-permute-start | bytes 18440 | tf_op jit(solution)/shard_map/ppermute | solution.py:102
  80.7 4.3 %collective-permute-start.19 = (f32[3,512]{1,0:T(4,128)S(1)}, f32[3,512]{1,0:T(4,128)S(1)}, u32[]{:S(2)}, u32[]{:S(2)}) collective-permute-start(f32[3,512]{1,0:T(4,128)S(1)} %get-tuple-element.204), channel_id=1, source_target_pairs={{0,96},{1,97},{2,98},{3,99},{4,100},{5,101},{6,102},{7,103},{8,104... | collective-permute-start | bytes 18440 | tf_op jit(solution)/shard_map/ppermute | solution.py:102
  98.5 8.8 %collective-permute-start.20 = (bf16[256,3584]{1,0:T(8,128)(2,1)}, bf16[256,3584]{1,0:T(8,128)(2,1)S(1)}, u32[]{:S(2)}, u32[]{:S(2)}) collective-permute-start(bf16[256,3584]{1,0:T(8,128)(2,1)} %shard_map.70), channel_id=1, source_target_pairs={{0,1},{1,0},{2,3},{3,2},{4,5},{5,4},{6,7},{7,6},{8,9},{9,8},{10,11... | collective-permute-start | bytes 5505032 | tf_op jit(solution)/shard_map/ppermute | solution.py:238
  107.3 7.4 %copy-start.5 = (bf16[256,1152]{1,0:T(8,128)(2,1)S(1)}, bf16[256,1152]{1,0:T(8,128)(2,1)}, u32[]{:S(2)}) copy-start(bf16[256,1152]{1,0:T(8,128)(2,1)} %get-tuple-element.191.g_ref) | copy-start | bytes 1769476
  110.0 4.7 %copy-start.3 = (bf16[4,64,3584]{2,1,0:T(8,128)(2,1)S(1)}, bf16[4,64,3584]{2,1,0:T(8,128)(2,1)}, u32[]{:S(2)}) copy-start(bf16[4,64,3584]{2,1,0:T(8,128)(2,1)} %copy-done.2) | copy-start | bytes 5505028
  110.0 4.6 %copy-start.4 = (bf16[256,1152]{1,0:T(8,128)(2,1)S(1)}, bf16[256,1152]{1,0:T(8,128)(2,1)}, u32[]{:S(2)}) copy-start(bf16[256,1152]{1,0:T(8,128)(2,1)} %get-tuple-element.192.g_ref) | copy-start | bytes 1769476
  110.1 12.5 %collective-permute-start.21 = (bf16[64,3584]{1,0:T(8,128)(2,1)S(1)}, bf16[64,3584]{1,0:T(8,128)(2,1)S(1)}, u32[]{:S(2)}, u32[]{:S(2)}) collective-permute-start(bf16[64,3584]{1,0:T(8,128)(2,1)S(1)} %get-tuple-element.193), channel_id=1, source_target_pairs={{0,2},{1,33},{2,4},{3,35},{4,6},{5,37},{6,0},{7,39},{8,10},{9,41},... | collective-permute-start | bytes 1376264 | tf_op jit(solution)/shard_map/ppermute | solution.py:102
  111.9 10.7 %collective-permute-start.23 = (bf16[64,3584]{1,0:T(8,128)(2,1)S(1)}, bf16[64,3584]{1,0:T(8,128)(2,1)S(1)}, u32[]{:S(2)}, u32[]{:S(2)}) collective-permute-start(bf16[64,3584]{1,0:T(8,128)(2,1)S(1)} %get-tuple-element.194), channel_id=1, source_target_pairs={{0,6},{1,97},{2,0},{3,99},{4,2},{5,101},{6,4},{7,103},{8,14},{9,10... | collective-permute-start | bytes 1376264 | tf_op jit(solution)/shard_map/ppermute | solution.py:102
  113.4 12.6 %collective-permute-start.22 = (bf16[64,3584]{1,0:T(8,128)(2,1)S(1)}, bf16[64,3584]{1,0:T(8,128)(2,1)S(1)}, u32[]{:S(2)}, u32[]{:S(2)}) collective-permute-start(bf16[64,3584]{1,0:T(8,128)(2,1)S(1)} %get-tuple-element.195), channel_id=1, source_target_pairs={{0,4},{1,65},{2,6},{3,67},{4,0},{5,69},{6,2},{7,71},{8,12},{9,73},... | collective-permute-start | bytes 1376264 | tf_op jit(solution)/shard_map/ppermute | solution.py:102
  126.4 6.5 %collective-permute-start.24 = (bf16[16,3584]{1,0:T(8,128)(2,1)S(1)}, bf16[16,3584]{1,0:T(8,128)(2,1)S(1)}, u32[]{:S(2)}, u32[]{:S(2)}) collective-permute-start(bf16[16,3584]{1,0:T(8,128)(2,1)S(1)} %get-tuple-element.196), channel_id=1, source_target_pairs={{0,8},{1,9},{2,10},{3,11},{4,12},{5,13},{6,14},{7,15},{8,16},{9,17... | collective-permute-start | bytes 344072 | tf_op jit(solution)/shard_map/ppermute | solution.py:102
  127.9 6.8 %collective-permute-start.26 = (bf16[16,3584]{1,0:T(8,128)(2,1)S(1)}, bf16[16,3584]{1,0:T(8,128)(2,1)S(1)}, u32[]{:S(2)}, u32[]{:S(2)}) collective-permute-start(bf16[16,3584]{1,0:T(8,128)(2,1)S(1)} %get-tuple-element.197), channel_id=1, source_target_pairs={{0,24},{1,25},{2,26},{3,27},{4,28},{5,29},{6,30},{7,31},{8,0},{9,1... | collective-permute-start | bytes 344072 | tf_op jit(solution)/shard_map/ppermute | solution.py:102
  129.8 6.7 %collective-permute-start.25 = (bf16[16,3584]{1,0:T(8,128)(2,1)S(1)}, bf16[16,3584]{1,0:T(8,128)(2,1)S(1)}, u32[]{:S(2)}, u32[]{:S(2)}) collective-permute-start(bf16[16,3584]{1,0:T(8,128)(2,1)S(1)} %get-tuple-element.198), channel_id=1, source_target_pairs={{0,16},{1,17},{2,18},{3,19},{4,20},{5,21},{6,22},{7,23},{8,24},{9,... | collective-permute-start | bytes 344072 | tf_op jit(solution)/shard_map/ppermute | solution.py:102
  136.6 5.2 %collective-permute-start.27 = (bf16[4,3584]{1,0:T(4,128)(2,1)S(1)}, bf16[4,3584]{1,0:T(4,128)(2,1)S(1)}, u32[]{:S(2)}, u32[]{:S(2)}) collective-permute-start(bf16[4,3584]{1,0:T(4,128)(2,1)S(1)} %get-tuple-element.199), channel_id=1, source_target_pairs={{0,32},{1,3},{2,34},{3,5},{4,36},{5,7},{6,38},{7,1},{8,40},{9,11},... | collective-permute-start | bytes 86024 | tf_op jit(solution)/shard_map/ppermute | solution.py:102
  137.6 4.2 %collective-permute-start.29 = (bf16[4,3584]{1,0:T(4,128)(2,1)S(1)}, bf16[4,3584]{1,0:T(4,128)(2,1)S(1)}, u32[]{:S(2)}, u32[]{:S(2)}) collective-permute-start(bf16[4,3584]{1,0:T(4,128)(2,1)S(1)} %get-tuple-element.200), channel_id=1, source_target_pairs={{0,96},{1,7},{2,98},{3,1},{4,100},{5,3},{6,102},{7,5},{8,104},{9,1... | collective-permute-start | bytes 86024 | tf_op jit(solution)/shard_map/ppermute | solution.py:102
  139.9 5.4 %collective-permute-start.28 = (bf16[4,3584]{1,0:T(4,128)(2,1)S(1)}, bf16[4,3584]{1,0:T(4,128)(2,1)S(1)}, u32[]{:S(2)}, u32[]{:S(2)}) collective-permute-start(bf16[4,3584]{1,0:T(4,128)(2,1)S(1)} %get-tuple-element.201), channel_id=1, source_target_pairs={{0,64},{1,5},{2,66},{3,7},{4,68},{5,1},{6,70},{7,3},{8,72},{9,13},... | collective-permute-start | bytes 86024 | tf_op jit(solution)/shard_map/ppermute | solution.py:102

commit v6 on v4

--- a/solution.py
+++ b/solution.py
@@ -194,10 +194,11 @@
         )
 
     grad_other = half_grad(logits_other, target_other, lse_arr[half:], total_arr[half:])
-    grad_own = half_grad(logits_own, target_own, lse_arr[:half], total_arr[:half])
 
     sent = jnp.dot(grad_other, head_weight, preferred_element_type=jnp.float32).astype(jnp.bfloat16)
     received = lax.ppermute(sent, AXES, stage_pairs("c", 1, n_dev, voc_n))
+    sent, logits_own = lax.optimization_barrier((sent, logits_own))
+    grad_own = half_grad(logits_own, target_own, lse_arr[:half], total_arr[:half])
     acc = jnp.dot(grad_own, head_weight, preferred_element_type=jnp.float32)
     acc, received = lax.optimization_barrier((acc, received))
     acc = (acc + received.astype(jnp.float32)).reshape(RING, -1, width)

time: 125 us -> 125 us (level)
    convert_element_type x1 -> x2, other arithmetic: 2.38 us -> 3.38 us  [half_grad(): (loss_scale * (total_h[:, None] * jnp.exp(logits - lse_h[:, None]) - tgt)...]
  transfers between devices with their start and end apart: 30 -> 30, of which waited for: 22 -> 21; matrix products, arithmetic and copies ran while one was open for 21% -> 22% of each run, Pallas kernels for 0% -> 0%
where the time goes in v6:
time: 125 us
  starting transfers between devices  41.9 us (34%)
  waiting for transfers between devices  33.9 us (27%)
  matrix products  24.8 us (20%)
  other arithmetic  14.7 us (12%)
  local copies, waits for them, and re-layouts  7.31 us (6%)
  between operations  1.81 us (1%)
    ppermute x28, starting transfers between devices, exchange(): lax.ppermute(block_for(shift), AXES, stage_pairs(stage, shift, n_dev, voc...  41.4 us
    ppermute x28, waiting for transfers between devices, exchange(): lax.ppermute(block_for(shift), AXES, stage_pairs(stage, shift, n_dev, voc...  33.9 us
    dot_general x2, matrix products, half_logits(): lax.dot_general(rows_block, head_weight, (((1,), (1,)), ((), ())), prefer...  9.55 us
    dot_general x1, matrix products, per_device(): lax.dot_general(grad, every, (((0,), (0,)), ((), ())), preferred_element_...  6.72 us
    dot_general x1, matrix products, per_device(): jnp.dot(grad_other, head_weight, preferred_element_type=jnp.float32)  6.02 us
    add x1, other arithmetic, compact_target(): target + jnp.where(slot_local[:, j:j + 1] == columns, slot_probs[:, j:j +...  3.57 us
    convert_element_type x2, other arithmetic, half_grad(): (loss_scale * (total_h[:, None] * jnp.exp(logits - lse_h[:, None]) - tgt)...  3.38 us
    dot_general x1, matrix products, per_device(): acc = jnp.dot(grad_own, head_weight, preferred_element_type=jnp.float32)  2.53 us
  transfers between devices with their start and end apart: 30, of which 21 were waited for; matrix products, arithmetic and copies ran while one was open for 22% of the time, Pallas kernels for 0%

profile of v6, /device:TPU:0, one launch (start us, length us, event | category | flops | bytes accessed | tf_op | source)
XLA Modules:
  0.0 124.5 jit_solution(12954016908052824035)
XLA Ops:
  0.6 1.6 %collective-permute-start = (bf16[4,3584]{1,0:T(4,128)(2,1)}, bf16[4,3584]{1,0:T(4,128)(2,1)S(1)}, u32[]{:S(2)}, u32[]{:S(2)}) collective-permute-start(bf16[4,3584]{1,0:T(4,128)(2,1)} %param.8), channel_id=1, source_target_pairs={{0,32},{1,3},{2,34},{3,5},{4,36},{5,7},{6,38},{7,1},{8,40},{9,11},... | collective-permute-start | bytes 86024 | tf_op jit(solution)/shard_map/ppermute | solution.py:100
  2.3 1.7 %collective-permute-start.2 = (bf16[4,3584]{1,0:T(4,128)(2,1)}, bf16[4,3584]{1,0:T(4,128)(2,1)S(1)}, u32[]{:S(2)}, u32[]{:S(2)}) collective-permute-start(bf16[4,3584]{1,0:T(4,128)(2,1)} %param.8), channel_id=1, source_target_pairs={{0,96},{1,7},{2,98},{3,1},{4,100},{5,3},{6,102},{7,5},{8,104},{9,1... | collective-permute-start | bytes 86024 | tf_op jit(solution)/shard_map/ppermute | solution.py:100
  3.9 1.9 %collective-permute-start.1 = (bf16[4,3584]{1,0:T(4,128)(2,1)}, bf16[4,3584]{1,0:T(4,128)(2,1)S(1)}, u32[]{:S(2)}, u32[]{:S(2)}) collective-permute-start(bf16[4,3584]{1,0:T(4,128)(2,1)} %param.8), channel_id=1, source_target_pairs={{0,64},{1,5},{2,66},{3,7},{4,68},{5,1},{6,70},{7,3},{8,72},{9,13},... | collective-permute-start | bytes 86024 | tf_op jit(solution)/shard_map/ppermute | solution.py:100
  6.4 3.2 %collective-permute-done.1 = bf16[4,3584]{1,0:T(4,128)(2,1)S(1)} collective-permute-done((bf16[4,3584]{1,0:T(4,128)(2,1)}, bf16[4,3584]{1,0:T(4,128)(2,1)S(1)}, u32[]{:S(2)}, u32[]{:S(2)}) %collective-permute-start.1) | collective-permute-done | bytes 28704 | tf_op jit(solution)/shard_map/ppermute | solution.py:100
  10.4 3.2 %collective-permute-start.5 = (bf16[16,3584]{1,0:T(8,128)(2,1)S(1)}, bf16[16,3584]{1,0:T(8,128)(2,1)S(1)}, u32[]{:S(2)}, u32[]{:S(2)}) collective-permute-start(bf16[16,3584]{1,0:T(8,128)(2,1)S(1)} %reshape.862), channel_id=1, source_target_pairs={{0,24},{1,25},{2,26},{3,27},{4,28},{5,29},{6,30},{7,31},{8,0},{9,1... | collective-permute-start | bytes 344072 | tf_op jit(solution)/shard_map/ppermute | solution.py:100
  15.3 1.0 copy.81
  16.3 1.0 gather_fusion.2
  17.9 2.5 %collective-permute-done.4 = bf16[16,3584]{1,0:T(8,128)(2,1)S(1)} collective-permute-done((bf16[16,3584]{1,0:T(8,128)(2,1)S(1)}, bf16[16,3584]{1,0:T(8,128)(2,1)S(1)}, u32[]{:S(2)}, u32[]{:S(2)}) %collective-permute-start.4) | collective-permute-done | bytes 114720 | tf_op jit(solution)/shard_map/ppermute | solution.py:100
  20.4 1.2 collective-permute-done.3
  21.7 3.6 %collective-permute-start.8 = (bf16[64,3584]{1,0:T(8,128)(2,1)S(1)}, bf16[64,3584]{1,0:T(8,128)(2,1)S(1)}, u32[]{:S(2)}, u32[]{:S(2)}) collective-permute-start(bf16[64,3584]{1,0:T(8,128)(2,1)S(1)} %bitcast.143), channel_id=1, source_target_pairs={{0,6},{1,97},{2,0},{3,99},{4,2},{5,101},{6,4},{7,103},{8,14},{9,10... | collective-permute-start | bytes 1376264 | tf_op jit(solution)/shard_map/ppermute | solution.py:100
  25.3 1.3 %collective-permute-start.6 = (bf16[64,3584]{1,0:T(8,128)(2,1)S(1)}, bf16[64,3584]{1,0:T(8,128)(2,1)S(1)}, u32[]{:S(2)}, u32[]{:S(2)}) collective-permute-start(bf16[64,3584]{1,0:T(8,128)(2,1)S(1)} %bitcast.145), channel_id=1, source_target_pairs={{0,2},{1,33},{2,4},{3,35},{4,6},{5,37},{6,0},{7,39},{8,10},{9,41},... | collective-permute-start | bytes 1376264 | tf_op jit(solution)/shard_map/ppermute | solution.py:100
  28.1 5.8 %conditional.1 = (f32[512,1152]{1,0:T(8,128)}) conditional(s32[]{:T(128)} %convert_element_type.46, (s32[512,64]{1,0:T(8,128)S(1)}, pred[512]{0:T(512)(128)(4,1)S(1)}, f32[512,64]{0,1:T(8,128)S(1)}, s32[512,1]{0,1:T(1,128)S(1)}) %tuple.101, (s32[512,64]{1,0:T(8,128)S(1)}, pred[512]{0:T(512)(128)(4,1)S(1)}, f32[512,64]{0,1:T(8,128)S(1)}, ...), branch_computations={%region_3.7_spmd, %region_7.11_spmd} | conditional | flops 17916928 | bytes 5218828 | solution.py:44
  28.9 1.0 gather_fusion
  30.4 3.6 %select_add_fusion = f32[512,1152]{1,0:T(8,128)} fusion(f32[512]{0:T(512)S(1)} %bitcast.188, s32[512]{0:T(512)S(1)} %bitcast.180, f32[512]{0:T(512)S(1)} %bitcast.189, s32[512]{0:T(512)S(1)} %bitcast.181, f32[512]{0:T(512)S(1)} %bitcast.190, s32[512]{0:T(512)S(1)} %bitcast.182, f32[512]{0:T(512)S(1)} %bitcast.191, s32[512]{0:T(512)S(1)} %bitcast.183, ...), kind=kLoop, calls=%fused_computation.6 | loop fusion | flops 13565952 | bytes 2392064 | tf_op jit(solution)/shard_map/cond/branch_0_fun/add | solution.py:37
  33.9 2.3 %collective-permute-done.8 = bf16[64,3584]{1,0:T(8,128)(2,1)S(1)} collective-permute-done((bf16[64,3584]{1,0:T(8,128)(2,1)S(1)}, bf16[64,3584]{1,0:T(8,128)(2,1)S(1)}, u32[]{:S(2)}, u32[]{:S(2)}) %collective-permute-start.8) | collective-permute-done | bytes 458784 | tf_op jit(solution)/shard_map/ppermute | solution.py:100
  36.2 3.7 %collective-permute-done.6 = bf16[64,3584]{1,0:T(8,128)(2,1)S(1)} collective-permute-done((bf16[64,3584]{1,0:T(8,128)(2,1)S(1)}, bf16[64,3584]{1,0:T(8,128)(2,1)S(1)}, u32[]{:S(2)}, u32[]{:S(2)}) %collective-permute-start.6) | collective-permute-done | bytes 458784 | tf_op jit(solution)/shard_map/ppermute | solution.py:100
  40.4 6.9 %fusion.114 = (f32[256]{0:T(256)S(1)}, f32[256,1152]{1,0:T(8,128)S(1)}) fusion(bf16[256,3584]{1,0:T(8,128)(2,1)S(1)} %bitcast.148, bf16[1152,3584]{1,0:T(8,128)(2,1)} %param.9), kind=kOutput, calls=%fused_computation.334 | convolution fusion | flops 2114223872 | bytes 11273216 | tf_op jit(solution)/shard_map/dot_general | solution.py:133
  47.4 2.6 %fusion.113 = (f32[256]{0:T(256)S(1)}, f32[256,1152]{1,0:T(8,128)S(1)}) fusion(bf16[256,3584]{1,0:T(8,128)(2,1)S(1)} %collective-permute-done.9, bf16[1152,3584]{1,0:T(8,128)(2,1)S(1)} %bitcast.213), kind=kOutput, calls=%fused_computation.333 | convolution fusion | flops 2114223872 | bytes 11273216 | tf_op jit(solution)/shard_map/dot_general | solution.py:133
  50.1 2.2 %multiply_reduce_fusion.1 = (f32[256]{0:T(256)S(1)}, f32[256]{0:T(256)S(1)}, f32[256]{0:T(256)S(1)}, f32[256]{0:T(256)S(1)}) fusion(f32[256,1152]{1,0:T(8,128)S(1)} %get-tuple-element.78, f32[512,1152]{1,0:T(8,128)} %get-tuple-element.257, f32[256,1152]{1,0:T(8,128)S(1)} %get-tuple-element.210, f32[256]{0:T(256)S(1)} %get-tuple-element.209, ...), kind=kLoop, calls=%fused_computation.44 | loop fusion | flops 2358272 | bytes 4724736 | tf_op jit(solution)/shard_map/reduce_sum | solution.py:167
  52.5 1.0 gather_fusion.3
  54.0 1.3 %collective-permute-done.10 = f32[3,512]{0,1:T(8,128)S(1)} collective-permute-done((f32[3,512]{0,1:T(8,128)S(1)}, f32[3,512]{0,1:T(8,128)S(1)}, u32[]{:S(2)}, u32[]{:S(2)}) %collective-permute-start.10) | collective-permute-done | bytes 6176 | tf_op jit(solution)/shard_map/ppermute | solution.py:100
  55.9 1.5 %collective-permute-start.11 = (f32[3,512]{1,0:T(4,128)S(1)}, f32[3,512]{1,0:T(4,128)S(1)}, u32[]{:S(2)}, u32[]{:S(2)}) collective-permute-start(f32[3,512]{1,0:T(4,128)S(1)} %get-tuple-element.208), channel_id=1, source_target_pairs={{0,2},{1,3},{2,4},{3,5},{4,6},{5,7},{6,0},{7,1},{8,10},{9,11},{10,... | collective-permute-start | bytes 18440 | tf_op jit(solution)/shard_map/ppermute | solution.py:100
  57.3 1.8 %collective-permute-start.13 = (f32[3,512]{1,0:T(4,128)S(1)}, f32[3,512]{1,0:T(4,128)S(1)}, u32[]{:S(2)}, u32[]{:S(2)}) collective-permute-start(f32[3,512]{1,0:T(4,128)S(1)} %get-tuple-element.208), channel_id=1, source_target_pairs={{0,6},{1,7},{2,0},{3,1},{4,2},{5,3},{6,4},{7,5},{8,14},{9,15},{10,... | collective-permute-start | bytes 18440 | tf_op jit(solution)/shard_map/ppermute | solution.py:100
  59.1 1.6 %collective-permute-done.12 = f32[3,512]{1,0:T(4,128)S(1)} collective-permute-done((f32[3,512]{1,0:T(4,128)S(1)}, f32[3,512]{1,0:T(4,128)S(1)}, u32[]{:S(2)}, u32[]{:S(2)}) %collective-permute-start.12) | collective-permute-done | bytes 6176 | tf_op jit(solution)/shard_map/ppermute | solution.py:100
  62.6 2.6 %collective-permute-start.16 = (f32[3,512]{1,0:T(4,128)S(1)}, f32[3,512]{1,0:T(4,128)S(1)}, u32[]{:S(2)}, u32[]{:S(2)}) collective-permute-start(f32[3,512]{1,0:T(4,128)S(1)} %get-tuple-element.206), channel_id=1, source_target_pairs={{0,24},{1,25},{2,26},{3,27},{4,28},{5,29},{6,30},{7,31},{8,0},{9,1... | collective-permute-start | bytes 18440 | tf_op jit(solution)/shard_map/ppermute | solution.py:100
  65.2 1.1 collective-permute-done.15
  67.0 1.9 %collective-permute-start.18 = (f32[3,512]{1,0:T(4,128)S(1)}, f32[3,512]{1,0:T(4,128)S(1)}, u32[]{:S(2)}, u32[]{:S(2)}) collective-permute-start(f32[3,512]{1,0:T(4,128)S(1)} %get-tuple-element.204), channel_id=1, source_target_pairs={{0,64},{1,65},{2,66},{3,67},{4,68},{5,69},{6,70},{7,71},{8,72},{9,... | collective-permute-start | bytes 18440 | tf_op jit(solution)/shard_map/ppermute | solution.py:100
  69.5 2.6 %collective-permute-start.19 = (f32[3,512]{1,0:T(4,128)S(1)}, f32[3,512]{1,0:T(4,128)S(1)}, u32[]{:S(2)}, u32[]{:S(2)}) collective-permute-start(f32[3,512]{1,0:T(4,128)S(1)} %get-tuple-element.204), channel_id=1, source_target_pairs={{0,96},{1,97},{2,98},{3,99},{4,100},{5,101},{6,102},{7,103},{8,104... | collective-permute-start | bytes 18440 | tf_op jit(solution)/shard_map/ppermute | solution.py:100
  72.2 1.5 %collective-permute-done.17 = f32[3,512]{1,0:T(4,128)S(1)} collective-permute-done((f32[3,512]{1,0:T(4,128)S(1)}, f32[3,512]{1,0:T(4,128)S(1)}, u32[]{:S(2)}, u32[]{:S(2)}) %collective-permute-start.17) | collective-permute-done | bytes 6176 | tf_op jit(solution)/shard_map/ppermute | solution.py:100
  74.0 1.0 gather_fusion.4
  75.5 1.8 %multiply_convert_fusion.1 = bf16[256,1152]{1,0:T(8,128)(2,1)S(1)} fusion(f32[256,1152]{1,0:T(8,128)S(1)} %get-tuple-element.210, f32[512,1152]{1,0:T(8,128)} %get-tuple-element.257, f32[256]{0:T(256)S(1)} %get-tuple-element.147, f32[256]{0:T(256)S(1)} %get-tuple-element.148), kind=kLoop, calls=%fused_computation.42 | loop fusion | flops 1474560 | bytes 2951168 | tf_op jit(solution)/shard_map/convert_element_type | solution.py:192
  77.3 6.0 %convolution_convert_fusion.1 = bf16[256,3584]{1,0:T(8,128)(2,1)S(1)} fusion(bf16[256,1152]{1,0:T(8,128)(2,1)S(1)} %multiply_convert_fusion.1, bf16[1152,3584]{1,0:T(8,128)(2,1)} %param.9), kind=kOutput, calls=%fused_computation.31 | convolution fusion | flops 2114846720 | bytes 10682368 | tf_op jit(solution)/shard_map/dot_general | solution.py:198
  83.7 1.6 %multiply_convert_fusion = bf16[256,1152]{1,0:T(8,128)(2,1)S(1)} fusion(f32[256,1152]{1,0:T(8,128)S(1)} %get-tuple-element.78, f32[512,1152]{1,0:T(8,128)} %get-tuple-element.257, f32[256]{0:T(256)S(1)} %get-tuple-element.146, f32[256]{0:T(256)S(1)} %get-tuple-element.145), kind=kLoop, calls=%fused_computation.41 | loop fusion | flops 1474560 | bytes 2951168 | tf_op jit(solution)/shard_map/convert_element_type | solution.py:192
  85.3 2.5 %fusion.115 = f32[256,3584]{1,0:T(8,128)S(1)} fusion(bf16[256,1152]{1,0:T(8,128)(2,1)S(1)} %multiply_convert_fusion, bf16[1152,3584]{1,0:T(8,128)(2,1)S(1)} %bitcast.215), kind=kOutput, calls=%fused_computation.335 | convolution fusion | flops 2113929216 | bytes 12517376 | tf_op jit(solution)/shard_map/dot_general | solution.py:202
  88.6 1.8 %collective-permute-start.21 = (bf16[64,3584]{1,0:T(8,128)(2,1)S(1)}, bf16[64,3584]{1,0:T(8,128)(2,1)S(1)}, u32[]{:S(2)}, u32[]{:S(2)}) collective-permute-start(bf16[64,3584]{1,0:T(8,128)(2,1)S(1)} %get-tuple-element.193), channel_id=1, source_target_pairs={{0,2},{1,33},{2,4},{3,35},{4,6},{5,37},{6,0},{7,39},{8,10},{9,41},... | collective-permute-start | bytes 1376264 | tf_op jit(solution)/shard_map/ppermute | solution.py:100
  90.4 1.5 %collective-permute-start.23 = (bf16[64,3584]{1,0:T(8,128)(2,1)S(1)}, bf16[64,3584]{1,0:T(8,128)(2,1)S(1)}, u32[]{:S(2)}, u32[]{:S(2)}) collective-permute-start(bf16[64,3584]{1,0:T(8,128)(2,1)S(1)} %get-tuple-element.194), channel_id=1, source_target_pairs={{0,6},{1,97},{2,0},{3,99},{4,2},{5,101},{6,4},{7,103},{8,14},{9,10... | collective-permute-start | bytes 1376264 | tf_op jit(solution)/shard_map/ppermute | solution.py:100
  91.9 1.2 collective-permute-start.22
  93.1 6.7 %convolution_convert_fusion = bf16[1152,3584]{1,0:T(8,128)(2,1)} fusion(bf16[256,3584]{1,0:T(8,128)(2,1)S(1)} %copy-done.4, bf16[256,3584]{1,0:T(8,128)(2,1)S(1)} %bitcast.149, bf16[256,1152]{1,0:T(8,128)(2,1)S(1)} %multiply_convert_fusion.1, bf16[256,1152]{1,0:T(8,128)(2,1)S(1)} %multiply_convert_fusion), kind=kOutput, calls=%fused_computation.30 | convolution fusion | flops 4241686528 | bytes 13107200 | tf_op jit(solution)/shard_map/dot_general | solution.py:206
  99.9 4.6 %collective-permute-done.22 = bf16[64,3584]{1,0:T(8,128)(2,1)S(1)} collective-permute-done((bf16[64,3584]{1,0:T(8,128)(2,1)S(1)}, bf16[64,3584]{1,0:T(8,128)(2,1)S(1)}, u32[]{:S(2)}, u32[]{:S(2)}) %collective-permute-start.22) | collective-permute-done | bytes 458784 | tf_op jit(solution)/shard_map/ppermute | solution.py:100
  104.9 1.5 %collective-permute-start.24 = (bf16[16,3584]{1,0:T(8,128)(2,1)S(1)}, bf16[16,3584]{1,0:T(8,128)(2,1)S(1)}, u32[]{:S(2)}, u32[]{:S(2)}) collective-permute-start(bf16[16,3584]{1,0:T(8,128)(2,1)S(1)} %get-tuple-element.196), channel_id=1, source_target_pairs={{0,8},{1,9},{2,10},{3,11},{4,12},{5,13},{6,14},{7,15},{8,16},{9,17... | collective-permute-start | bytes 344072 | tf_op jit(solution)/shard_map/ppermute | solution.py:100
  106.5 1.8 %collective-permute-start.26 = (bf16[16,3584]{1,0:T(8,128)(2,1)S(1)}, bf16[16,3584]{1,0:T(8,128)(2,1)S(1)}, u32[]{:S(2)}, u32[]{:S(2)}) collective-permute-start(bf16[16,3584]{1,0:T(8,128)(2,1)S(1)} %get-tuple-element.197), channel_id=1, source_target_pairs={{0,24},{1,25},{2,26},{3,27},{4,28},{5,29},{6,30},{7,31},{8,0},{9,1... | collective-permute-start | bytes 344072 | tf_op jit(solution)/shard_map/ppermute | solution.py:100
  108.3 1.4 %collective-permute-start.25 = (bf16[16,3584]{1,0:T(8,128)(2,1)S(1)}, bf16[16,3584]{1,0:T(8,128)(2,1)S(1)}, u32[]{:S(2)}, u32[]{:S(2)}) collective-permute-start(bf16[16,3584]{1,0:T(8,128)(2,1)S(1)} %get-tuple-element.198), channel_id=1, source_target_pairs={{0,16},{1,17},{2,18},{3,19},{4,20},{5,21},{6,22},{7,23},{8,24},{9,... | collective-permute-start | bytes 344072 | tf_op jit(solution)/shard_map/ppermute | solution.py:100
  109.7 1.7 %collective-permute-done.24 = bf16[16,3584]{1,0:T(8,128)(2,1)S(1)} collective-permute-done((bf16[16,3584]{1,0:T(8,128)(2,1)S(1)}, bf16[16,3584]{1,0:T(8,128)(2,1)S(1)}, u32[]{:S(2)}, u32[]{:S(2)}) %collective-permute-start.24) | collective-permute-done | bytes 114720 | tf_op jit(solution)/shard_map/ppermute | solution.py:100
  111.4 1.8 %collective-permute-done.26 = bf16[16,3584]{1,0:T(8,128)(2,1)S(1)} collective-permute-done((bf16[16,3584]{1,0:T(8,128)(2,1)S(1)}, bf16[16,3584]{1,0:T(8,128)(2,1)S(1)}, u32[]{:S(2)}, u32[]{:S(2)}) %collective-permute-start.26) | collective-permute-done | bytes 114720 | tf_op jit(solution)/shard_map/ppermute | solution.py:100
  113.2 1.8 %collective-permute-done.25 = bf16[16,3584]{1,0:T(8,128)(2,1)S(1)} collective-permute-done((bf16[16,3584]{1,0:T(8,128)(2,1)S(1)}, bf16[16,3584]{1,0:T(8,128)(2,1)S(1)}, u32[]{:S(2)}, u32[]{:S(2)}) %collective-permute-start.25) | collective-permute-done | bytes 114720 | tf_op jit(solution)/shard_map/ppermute | solution.py:100
  116.1 2.4 %collective-permute-start.29 = (bf16[4,3584]{1,0:T(4,128)(2,1)S(1)}, bf16[4,3584]{1,0:T(4,128)(2,1)S(1)}, u32[]{:S(2)}, u32[]{:S(2)}) collective-permute-start(bf16[4,3584]{1,0:T(4,128)(2,1)S(1)} %get-tuple-element.200), channel_id=1, source_target_pairs={{0,96},{1,7},{2,98},{3,1},{4,100},{5,3},{6,102},{7,5},{8,104},{9,1... | collective-permute-start | bytes 86024 | tf_op jit(solution)/shard_map/ppermute | solution.py:100
  118.5 1.0 collective-permute-start.28
  120.3 3.5 %collective-permute-done.28 = bf16[4,3584]{1,0:T(4,128)(2,1)S(1)} collective-permute-done((bf16[4,3584]{1,0:T(4,128)(2,1)S(1)}, bf16[4,3584]{1,0:T(4,128)(2,1)S(1)}, u32[]{:S(2)}, u32[]{:S(2)}) %collective-permute-start.28) | collective-permute-done | bytes 28704 | tf_op jit(solution)/shard_map/ppermute | solution.py:100
  (123 shorter events, 15.4 us)
Async XLA Ops:
  0.6 5.4 %collective-permute-start = (bf16[4,3584]{1,0:T(4,128)(2,1)}, bf16[4,3584]{1,0:T(4,128)(2,1)S(1)}, u32[]{:S(2)}, u32[]{:S(2)}) collective-permute-start(bf16[4,3584]{1,0:T(4,128)(2,1)} %param.8), channel_id=1, source_target_pairs={{0,32},{1,3},{2,34},{3,5},{4,36},{5,7},{6,38},{7,1},{8,40},{9,11},... | collective-permute-start | bytes 86024 | tf_op jit(solution)/shard_map/ppermute | solution.py:100
  2.3 4.1 %collective-permute-start.2 = (bf16[4,3584]{1,0:T(4,128)(2,1)}, bf16[4,3584]{1,0:T(4,128)(2,1)S(1)}, u32[]{:S(2)}, u32[]{:S(2)}) collective-permute-start(bf16[4,3584]{1,0:T(4,128)(2,1)} %param.8), channel_id=1, source_target_pairs={{0,96},{1,7},{2,98},{3,1},{4,100},{5,3},{6,102},{7,5},{8,104},{9,1... | collective-permute-start | bytes 86024 | tf_op jit(solution)/shard_map/ppermute | solution.py:100
  3.9 5.6 %collective-permute-start.1 = (bf16[4,3584]{1,0:T(4,128)(2,1)}, bf16[4,3584]{1,0:T(4,128)(2,1)S(1)}, u32[]{:S(2)}, u32[]{:S(2)}) collective-permute-start(bf16[4,3584]{1,0:T(4,128)(2,1)} %param.8), channel_id=1, source_target_pairs={{0,64},{1,5},{2,66},{3,7},{4,68},{5,1},{6,70},{7,3},{8,72},{9,13},... | collective-permute-start | bytes 86024 | tf_op jit(solution)/shard_map/ppermute | solution.py:100
  10.4 17.7 %copy-start.2 = (f32[512,64]{0,1:T(8,128)S(1)}, f32[512,64]{0,1:T(8,128)}, u32[]{:S(2)}) copy-start(f32[512,64]{0,1:T(8,128)} %param.11) | copy-start | bytes 393220
  10.4 7.5 %collective-permute-start.5 = (bf16[16,3584]{1,0:T(8,128)(2,1)S(1)}, bf16[16,3584]{1,0:T(8,128)(2,1)S(1)}, u32[]{:S(2)}, u32[]{:S(2)}) collective-permute-start(bf16[16,3584]{1,0:T(8,128)(2,1)S(1)} %reshape.862), channel_id=1, source_target_pairs={{0,24},{1,25},{2,26},{3,27},{4,28},{5,29},{6,30},{7,31},{8,0},{9,1... | collective-permute-start | bytes 344072 | tf_op jit(solution)/shard_map/ppermute | solution.py:100
  13.6 6.9 %collective-permute-start.4 = (bf16[16,3584]{1,0:T(8,128)(2,1)S(1)}, bf16[16,3584]{1,0:T(8,128)(2,1)S(1)}, u32[]{:S(2)}, u32[]{:S(2)}) collective-permute-start(bf16[16,3584]{1,0:T(8,128)(2,1)S(1)} %reshape.862), channel_id=1, source_target_pairs={{0,16},{1,17},{2,18},{3,19},{4,20},{5,21},{6,22},{7,23},{8,24},{9,... | collective-permute-start | bytes 344072 | tf_op jit(solution)/shard_map/ppermute | solution.py:100
  14.2 7.4 %collective-permute-start.3 = (bf16[16,3584]{1,0:T(8,128)(2,1)S(1)}, bf16[16,3584]{1,0:T(8,128)(2,1)S(1)}, u32[]{:S(2)}, u32[]{:S(2)}) collective-permute-start(bf16[16,3584]{1,0:T(8,128)(2,1)S(1)} %reshape.862), channel_id=1, source_target_pairs={{0,8},{1,9},{2,10},{3,11},{4,12},{5,13},{6,14},{7,15},{8,16},{9,17... | collective-permute-start | bytes 344072 | tf_op jit(solution)/shard_map/ppermute | solution.py:100
  21.7 14.5 %collective-permute-start.8 = (bf16[64,3584]{1,0:T(8,128)(2,1)S(1)}, bf16[64,3584]{1,0:T(8,128)(2,1)S(1)}, u32[]{:S(2)}, u32[]{:S(2)}) collective-permute-start(bf16[64,3584]{1,0:T(8,128)(2,1)S(1)} %bitcast.143), channel_id=1, source_target_pairs={{0,6},{1,97},{2,0},{3,99},{4,2},{5,101},{6,4},{7,103},{8,14},{9,10... | collective-permute-start | bytes 1376264 | tf_op jit(solution)/shard_map/ppermute | solution.py:100
  25.3 10.9 %collective-permute-start.7 = (bf16[64,3584]{1,0:T(8,128)(2,1)S(1)}, bf16[64,3584]{1,0:T(8,128)(2,1)S(1)}, u32[]{:S(2)}, u32[]{:S(2)}) collective-permute-start(bf16[64,3584]{1,0:T(8,128)(2,1)S(1)} %bitcast.144), channel_id=1, source_target_pairs={{0,4},{1,65},{2,6},{3,67},{4,0},{5,69},{6,2},{7,71},{8,12},{9,73},... | collective-permute-start | bytes 1376264 | tf_op jit(solution)/shard_map/ppermute | solution.py:100
  25.3 14.6 %collective-permute-start.6 = (bf16[64,3584]{1,0:T(8,128)(2,1)S(1)}, bf16[64,3584]{1,0:T(8,128)(2,1)S(1)}, u32[]{:S(2)}, u32[]{:S(2)}) collective-permute-start(bf16[64,3584]{1,0:T(8,128)(2,1)S(1)} %bitcast.145), channel_id=1, source_target_pairs={{0,2},{1,33},{2,4},{3,35},{4,6},{5,37},{6,0},{7,39},{8,10},{9,41},... | collective-permute-start | bytes 1376264 | tf_op jit(solution)/shard_map/ppermute | solution.py:100
  39.9 7.5 %slice-start = ((s8[8257536]{0:T(1024)(128)(4,1)}), s8[4194304]{0:T(1024)(128)(4,1)S(1)}, s32[]{:S(2)}) async-start(s8[8257536]{0:T(1024)(128)(4,1)} %bitcast.212), calls=%async_computation | async-start | bytes 8388608
  40.1 7.2 %copy-start = (bf16[4,64,3584]{2,1,0:T(8,128)(2,1)}, bf16[4,64,3584]{2,1,0:T(8,128)(2,1)S(1)}, u32[]{:S(2)}) copy-start(bf16[4,64,3584]{2,1,0:T(8,128)(2,1)S(1)} %pad_maximum_fusion) | copy-start | bytes 5505028
  40.1 7.2 %collective-permute-start.9 = (bf16[256,3584]{1,0:T(8,128)(2,1)S(1)}, bf16[256,3584]{1,0:T(8,128)(2,1)S(1)}, u32[]{:S(2)}, u32[]{:S(2)}) collective-permute-start(bf16[256,3584]{1,0:T(8,128)(2,1)S(1)} %bitcast.147), channel_id=1, source_target_pairs={{0,1},{1,0},{2,3},{3,2},{4,5},{5,4},{6,7},{7,6},{8,9},{9,8},{10,11... | collective-permute-start | bytes 5505032 | tf_op jit(solution)/shard_map/ppermute | solution.py:158
  40.4 7.0 %slice-start.1 = ((s8[8257536]{0:T(1024)(128)(4,1)}), s8[4063232]{0:T(1024)(128)(4,1)S(1)}, s32[]{:S(2)}) async-start(s8[8257536]{0:T(1024)(128)(4,1)} %bitcast.212), calls=%async_computation.1 | async-start | bytes 8126464
  47.4 2.6 %copy-start.3 = (bf16[256,3584]{1,0:T(8,128)(2,1)}, bf16[256,3584]{1,0:T(8,128)(2,1)S(1)}, u32[]{:S(2)}) copy-start(bf16[256,3584]{1,0:T(8,128)(2,1)S(1)} %collective-permute-done.9) | copy-start | bytes 5505028
  53.7 1.6 %collective-permute-start.10 = (f32[3,512]{0,1:T(8,128)S(1)}, f32[3,512]{0,1:T(8,128)S(1)}, u32[]{:S(2)}, u32[]{:S(2)}) collective-permute-start(f32[3,512]{0,1:T(8,128)S(1)} %bitcast_select_fusion.1), channel_id=1, source_target_pairs={{0,1},{1,0},{2,3},{3,2},{4,5},{5,4},{6,7},{7,6},{8,9},{9,8},{10,11... | collective-permute-start | bytes 18440 | tf_op jit(solution)/shard_map/ppermute | solution.py:100
  55.5 5.2 %collective-permute-start.12 = (f32[3,512]{1,0:T(4,128)S(1)}, f32[3,512]{1,0:T(4,128)S(1)}, u32[]{:S(2)}, u32[]{:S(2)}) collective-permute-start(f32[3,512]{1,0:T(4,128)S(1)} %get-tuple-element.208), channel_id=1, source_target_pairs={{0,4},{1,5},{2,6},{3,7},{4,0},{5,1},{6,2},{7,3},{8,12},{9,13},{10,... | collective-permute-start | bytes 18440 | tf_op jit(solution)/shard_map/ppermute | solution.py:100
  55.9 4.9 %collective-permute-start.11 = (f32[3,512]{1,0:T(4,128)S(1)}, f32[3,512]{1,0:T(4,128)S(1)}, u32[]{:S(2)}, u32[]{:S(2)}) collective-permute-start(f32[3,512]{1,0:T(4,128)S(1)} %get-tuple-element.208), channel_id=1, source_target_pairs={{0,2},{1,3},{2,4},{3,5},{4,6},{5,7},{6,0},{7,1},{8,10},{9,11},{10,... | collective-permute-start | bytes 18440 | tf_op jit(solution)/shard_map/ppermute | solution.py:100
  57.3 3.7 %collective-permute-start.13 = (f32[3,512]{1,0:T(4,128)S(1)}, f32[3,512]{1,0:T(4,128)S(1)}, u32[]{:S(2)}, u32[]{:S(2)}) collective-permute-start(f32[3,512]{1,0:T(4,128)S(1)} %get-tuple-element.208), channel_id=1, source_target_pairs={{0,6},{1,7},{2,0},{3,1},{4,2},{5,3},{6,4},{7,5},{8,14},{9,15},{10,... | collective-permute-start | bytes 18440 | tf_op jit(solution)/shard_map/ppermute | solution.py:100
  61.1 5.2 %collective-permute-start.15 = (f32[3,512]{1,0:T(4,128)S(1)}, f32[3,512]{1,0:T(4,128)S(1)}, u32[]{:S(2)}, u32[]{:S(2)}) collective-permute-start(f32[3,512]{1,0:T(4,128)S(1)} %get-tuple-element.206), channel_id=1, source_target_pairs={{0,16},{1,17},{2,18},{3,19},{4,20},{5,21},{6,22},{7,23},{8,24},{9,... | collective-permute-start | bytes 18440 | tf_op jit(solution)/shard_map/ppermute | solution.py:100
  62.0 4.9 %collective-permute-start.14 = (f32[3,512]{1,0:T(4,128)S(1)}, f32[3,512]{1,0:T(4,128)S(1)}, u32[]{:S(2)}, u32[]{:S(2)}) collective-permute-start(f32[3,512]{1,0:T(4,128)S(1)} %get-tuple-element.206), channel_id=1, source_target_pairs={{0,8},{1,9},{2,10},{3,11},{4,12},{5,13},{6,14},{7,15},{8,16},{9,17... | collective-permute-start | bytes 18440 | tf_op jit(solution)/shard_map/ppermute | solution.py:100
  62.6 4.2 %collective-permute-start.16 = (f32[3,512]{1,0:T(4,128)S(1)}, f32[3,512]{1,0:T(4,128)S(1)}, u32[]{:S(2)}, u32[]{:S(2)}) collective-permute-start(f32[3,512]{1,0:T(4,128)S(1)} %get-tuple-element.206), channel_id=1, source_target_pairs={{0,24},{1,25},{2,26},{3,27},{4,28},{5,29},{6,30},{7,31},{8,0},{9,1... | collective-permute-start | bytes 18440 | tf_op jit(solution)/shard_map/ppermute | solution.py:100
  67.0 5.2 %collective-permute-start.18 = (f32[3,512]{1,0:T(4,128)S(1)}, f32[3,512]{1,0:T(4,128)S(1)}, u32[]{:S(2)}, u32[]{:S(2)}) collective-permute-start(f32[3,512]{1,0:T(4,128)S(1)} %get-tuple-element.204), channel_id=1, source_target_pairs={{0,64},{1,65},{2,66},{3,67},{4,68},{5,69},{6,70},{7,71},{8,72},{9,... | collective-permute-start | bytes 18440 | tf_op jit(solution)/shard_map/ppermute | solution.py:100
  68.9 4.9 %collective-permute-start.17 = (f32[3,512]{1,0:T(4,128)S(1)}, f32[3,512]{1,0:T(4,128)S(1)}, u32[]{:S(2)}, u32[]{:S(2)}) collective-permute-start(f32[3,512]{1,0:T(4,128)S(1)} %get-tuple-element.204), channel_id=1, source_target_pairs={{0,32},{1,33},{2,34},{3,35},{4,36},{5,37},{6,38},{7,39},{8,40},{9,... | collective-permute-start | bytes 18440 | tf_op jit(solution)/shard_map/ppermute | solution.py:100
  69.5 4.3 %collective-permute-start.19 = (f32[3,512]{1,0:T(4,128)S(1)}, f32[3,512]{1,0:T(4,128)S(1)}, u32[]{:S(2)}, u32[]{:S(2)}) collective-permute-start(f32[3,512]{1,0:T(4,128)S(1)} %get-tuple-element.204), channel_id=1, source_target_pairs={{0,96},{1,97},{2,98},{3,99},{4,100},{5,101},{6,102},{7,103},{8,104... | collective-permute-start | bytes 18440 | tf_op jit(solution)/shard_map/ppermute | solution.py:100
  75.5 9.8 %slice-start.2 = ((s8[8257536]{0:T(1024)(128)(4,1)}), s8[4194304]{0:T(1024)(128)(4,1)S(1)}, s32[]{:S(2)}) async-start(s8[8257536]{0:T(1024)(128)(4,1)} %bitcast.214), calls=%async_computation.2 | async-start | bytes 8388608
  77.3 8.0 %slice-start.3 = ((s8[8257536]{0:T(1024)(128)(4,1)}), s8[4063232]{0:T(1024)(128)(4,1)S(1)}, s32[]{:S(2)}) async-start(s8[8257536]{0:T(1024)(128)(4,1)} %bitcast.214), calls=%async_computation.3 | async-start | bytes 8126464
  83.4 4.5 %collective-permute-start.20 = (bf16[256,3584]{1,0:T(8,128)(2,1)S(1)}, bf16[256,3584]{1,0:T(8,128)(2,1)S(1)}, u32[]{:S(2)}, u32[]{:S(2)}) collective-permute-start(bf16[256,3584]{1,0:T(8,128)(2,1)S(1)} %convolution_convert_fusion.1), channel_id=1, source_target_pairs={{0,1},{1,0},{2,3},{3,2},{4,5},{5,4},{6,7},{7,6},{8,9},{9,8},{10,11... | collective-permute-start | bytes 5505032 | tf_op jit(solution)/shard_map/ppermute | solution.py:199
  87.9 5.3 %copy-start.4 = (bf16[256,3584]{1,0:T(8,128)(2,1)S(1)}, bf16[256,3584]{1,0:T(8,128)(2,1)}, u32[]{:S(2)}) copy-start(bf16[256,3584]{1,0:T(8,128)(2,1)} %copy-done.3) | copy-start | bytes 5505028
  88.5 4.6 %copy-start.1 = (bf16[4,64,3584]{2,1,0:T(8,128)(2,1)S(1)}, bf16[4,64,3584]{2,1,0:T(8,128)(2,1)}, u32[]{:S(2)}) copy-start(bf16[4,64,3584]{2,1,0:T(8,128)(2,1)} %copy-done) | copy-start | bytes 5505028
  88.6 11.2 %collective-permute-start.21 = (bf16[64,3584]{1,0:T(8,128)(2,1)S(1)}, bf16[64,3584]{1,0:T(8,128)(2,1)S(1)}, u32[]{:S(2)}, u32[]{:S(2)}) collective-permute-start(bf16[64,3584]{1,0:T(8,128)(2,1)S(1)} %get-tuple-element.193), channel_id=1, source_target_pairs={{0,2},{1,33},{2,4},{3,35},{4,6},{5,37},{6,0},{7,39},{8,10},{9,41},... | collective-permute-start | bytes 1376264 | tf_op jit(solution)/shard_map/ppermute | solution.py:100
  90.4 9.4 %collective-permute-start.23 = (bf16[64,3584]{1,0:T(8,128)(2,1)S(1)}, bf16[64,3584]{1,0:T(8,128)(2,1)S(1)}, u32[]{:S(2)}, u32[]{:S(2)}) collective-permute-start(bf16[64,3584]{1,0:T(8,128)(2,1)S(1)} %get-tuple-element.194), channel_id=1, source_target_pairs={{0,6},{1,97},{2,0},{3,99},{4,2},{5,101},{6,4},{7,103},{8,14},{9,10... | collective-permute-start | bytes 1376264 | tf_op jit(solution)/shard_map/ppermute | solution.py:100
  91.9 12.6 %collective-permute-start.22 = (bf16[64,3584]{1,0:T(8,128)(2,1)S(1)}, bf16[64,3584]{1,0:T(8,128)(2,1)S(1)}, u32[]{:S(2)}, u32[]{:S(2)}) collective-permute-start(bf16[64,3584]{1,0:T(8,128)(2,1)S(1)} %get-tuple-element.195), channel_id=1, source_target_pairs={{0,4},{1,65},{2,6},{3,67},{4,0},{5,69},{6,2},{7,71},{8,12},{9,73},... | collective-permute-start | bytes 1376264 | tf_op jit(solution)/shard_map/ppermute | solution.py:100
  104.9 6.5 %collective-permute-start.24 = (bf16[16,3584]{1,0:T(8,128)(2,1)S(1)}, bf16[16,3584]{1,0:T(8,128)(2,1)S(1)}, u32[]{:S(2)}, u32[]{:S(2)}) collective-permute-start(bf16[16,3584]{1,0:T(8,128)(2,1)S(1)} %get-tuple-element.196), channel_id=1, source_target_pairs={{0,8},{1,9},{2,10},{3,11},{4,12},{5,13},{6,14},{7,15},{8,16},{9,17... | collective-permute-start | bytes 344072 | tf_op jit(solution)/shard_map/ppermute | solution.py:100
  106.5 6.8 %collective-permute-start.26 = (bf16[16,3584]{1,0:T(8,128)(2,1)S(1)}, bf16[16,3584]{1,0:T(8,128)(2,1)S(1)}, u32[]{:S(2)}, u32[]{:S(2)}) collective-permute-start(bf16[16,3584]{1,0:T(8,128)(2,1)S(1)} %get-tuple-element.197), channel_id=1, source_target_pairs={{0,24},{1,25},{2,26},{3,27},{4,28},{5,29},{6,30},{7,31},{8,0},{9,1... | collective-permute-start | bytes 344072 | tf_op jit(solution)/shard_map/ppermute | solution.py:100
  108.3 6.7 %collective-permute-start.25 = (bf16[16,3584]{1,0:T(8,128)(2,1)S(1)}, bf16[16,3584]{1,0:T(8,128)(2,1)S(1)}, u32[]{:S(2)}, u32[]{:S(2)}) collective-permute-start(bf16[16,3584]{1,0:T(8,128)(2,1)S(1)} %get-tuple-element.198), channel_id=1, source_target_pairs={{0,16},{1,17},{2,18},{3,19},{4,20},{5,21},{6,22},{7,23},{8,24},{9,... | collective-permute-start | bytes 344072 | tf_op jit(solution)/shard_map/ppermute | solution.py:100
  115.2 5.2 %collective-permute-start.27 = (bf16[4,3584]{1,0:T(4,128)(2,1)S(1)}, bf16[4,3584]{1,0:T(4,128)(2,1)S(1)}, u32[]{:S(2)}, u32[]{:S(2)}) collective-permute-start(bf16[4,3584]{1,0:T(4,128)(2,1)S(1)} %get-tuple-element.199), channel_id=1, source_target_pairs={{0,32},{1,3},{2,34},{3,5},{4,36},{5,7},{6,38},{7,1},{8,40},{9,11},... | collective-permute-start | bytes 86024 | tf_op jit(solution)/shard_map/ppermute | solution.py:100
  116.1 4.2 %collective-permute-start.29 = (bf16[4,3584]{1,0:T(4,128)(2,1)S(1)}, bf16[4,3584]{1,0:T(4,128)(2,1)S(1)}, u32[]{:S(2)}, u32[]{:S(2)}) collective-permute-start(bf16[4,3584]{1,0:T(4,128)(2,1)S(1)} %get-tuple-element.200), channel_id=1, source_target_pairs={{0,96},{1,7},{2,98},{3,1},{4,100},{5,3},{6,102},{7,5},{8,104},{9,1... | collective-permute-start | bytes 86024 | tf_op jit(solution)/shard_map/ppermute | solution.py:100
  118.5 5.4 %collective-permute-start.28 = (bf16[4,3584]{1,0:T(4,128)(2,1)S(1)}, bf16[4,3584]{1,0:T(4,128)(2,1)S(1)}, u32[]{:S(2)}, u32[]{:S(2)}) collective-permute-start(bf16[4,3584]{1,0:T(4,128)(2,1)S(1)} %get-tuple-element.201), channel_id=1, source_target_pairs={{0,64},{1,5},{2,66},{3,7},{4,68},{5,1},{6,70},{7,3},{8,72},{9,13},... | collective-permute-start | bytes 86024 | tf_op jit(solution)/shard_map/ppermute | solution.py:100

commit v7 on v6

--- a/solution.py
+++ b/solution.py
@@ -151,12 +151,16 @@
     target = teacher_target(local, probs_arr, voc_dev)
 
     own = hidden_rows
-    for stage in ("r1", "r2", "r3"):
+    for stage in ("r1", "r2"):
         own = exchange(lambda s: own, stage, n_dev, voc_n).reshape(-1, width)
-        if stage == "r3":
-            own, target = lax.optimization_barrier((own, target))
+    got = exchange(lambda s: own, "r3", n_dev, voc_n)
+    first_logits = half_logits(own, head_weight)
+    got, target, first_logits = lax.optimization_barrier((got, target, first_logits))
+    own = got.reshape(-1, width)
     other = lax.ppermute(own, AXES, stage_pairs("c", 1, n_dev, voc_n))
-    logits_own = half_logits(own, head_weight)
+    logits_own = jnp.concatenate(
+        [first_logits, half_logits(got[1:].reshape(-1, width), head_weight)], axis=0
+    )
     logits_other = half_logits(other, head_weight)
     every = jnp.concatenate([own, other], axis=0)
     half = own.shape[0]

time: 125 us -> 130 us (1.040)
  waiting for transfers between devices: 33.9 us -> 27.4 us
  local copies, waits for them, and re-layouts: 7.31 us -> 11.6 us
  other arithmetic: 14.7 us -> 17.4 us
  starting transfers between devices: 41.9 us -> 44.2 us
  matrix products: 24.8 us -> 26.7 us
    ppermute x28, waiting for transfers between devices: 33.9 us -> 27.4 us  [exchange(): lax.ppermute(block_for(shift), AXES, stage_pairs(stage, shift, n_dev, voc...]
    ppermute x28, starting transfers between devices: 41.4 us -> 43.6 us  [exchange(): lax.ppermute(block_for(shift), AXES, stage_pairs(stage, shift, n_dev, voc...]
    dot_general x2 -> x3, matrix products: 9.55 us -> 11.4 us  [half_logits(): lax.dot_general(rows_block, head_weight, (((1,), (1,)), ((), ())), prefer...]
    select_n x3, other arithmetic: 0.36 us -> 1.76 us  [per_device(): stats = jnp.take(stats, natural_rows(at), axis=1)]
  transfers between devices with their start and end apart: 30 -> 30, of which waited for: 21 -> 13; matrix products, arithmetic and copies ran while one was open for 22% -> 25% of each run, Pallas kernels for 0% -> 0%
where the time goes in v7:
time: 130 us; the launch traced here: 129 us
  starting transfers between devices  44.2 us (34%)
  waiting for transfers between devices  27.4 us (21%)
  matrix products  26.7 us (21%)
  other arithmetic  17.4 us (13%)
  local copies, waits for them, and re-layouts  11.6 us (9%)
  between operations  1.86 us (1%)
    ppermute x28, starting transfers between devices, exchange(): lax.ppermute(block_for(shift), AXES, stage_pairs(stage, shift, n_dev, voc...  43.6 us
    ppermute x28, waiting for transfers between devices, exchange(): lax.ppermute(block_for(shift), AXES, stage_pairs(stage, shift, n_dev, voc...  27.4 us
    dot_general x3, matrix products, half_logits(): lax.dot_general(rows_block, head_weight, (((1,), (1,)), ((), ())), prefer...  11.4 us
    dot_general x1, matrix products, per_device(): lax.dot_general(grad, every, (((0,), (0,)), ((), ())), preferred_element_...  6.72 us
    dot_general x1, matrix products, per_device(): jnp.dot(grad_other, head_weight, preferred_element_type=jnp.float32)  6.02 us
    add x1, other arithmetic, compact_target(): target + jnp.where(slot_local[:, j:j + 1] == columns, slot_probs[:, j:j +...  3.57 us
    convert_element_type x2, other arithmetic, half_grad(): (loss_scale * (total_h[:, None] * jnp.exp(logits - lse_h[:, None]) - tgt)...  3.38 us
  transfers between devices with their start and end apart: 30, of which 13 were waited for; matrix products, arithmetic and copies ran while one was open for 25% of the time, Pallas kernels for 0%

profile of v7, /device:TPU:0, one launch (start us, length us, event | category | flops | bytes accessed | tf_op | source)
XLA Modules:
  0.0 129.2 jit_solution(4396896512960528683)
XLA Ops:
  0.6 1.6 %collective-permute-start = (bf16[4,3584]{1,0:T(4,128)(2,1)}, bf16[4,3584]{1,0:T(4,128)(2,1)S(1)}, u32[]{:S(2)}, u32[]{:S(2)}) collective-permute-start(bf16[4,3584]{1,0:T(4,128)(2,1)} %param.8), channel_id=1, source_target_pairs={{0,32},{1,3},{2,34},{3,5},{4,36},{5,7},{6,38},{7,1},{8,40},{9,11},... | collective-permute-start | bytes 86024 | tf_op jit(solution)/shard_map/ppermute | solution.py:100
  2.3 1.7 %collective-permute-start.2 = (bf16[4,3584]{1,0:T(4,128)(2,1)}, bf16[4,3584]{1,0:T(4,128)(2,1)S(1)}, u32[]{:S(2)}, u32[]{:S(2)}) collective-permute-start(bf16[4,3584]{1,0:T(4,128)(2,1)} %param.8), channel_id=1, source_target_pairs={{0,96},{1,7},{2,98},{3,1},{4,100},{5,3},{6,102},{7,5},{8,104},{9,1... | collective-permute-start | bytes 86024 | tf_op jit(solution)/shard_map/ppermute | solution.py:100
  4.0 1.9 %collective-permute-start.1 = (bf16[4,3584]{1,0:T(4,128)(2,1)}, bf16[4,3584]{1,0:T(4,128)(2,1)S(1)}, u32[]{:S(2)}, u32[]{:S(2)}) collective-permute-start(bf16[4,3584]{1,0:T(4,128)(2,1)} %param.8), channel_id=1, source_target_pairs={{0,64},{1,5},{2,66},{3,7},{4,68},{5,1},{6,70},{7,3},{8,72},{9,13},... | collective-permute-start | bytes 86024 | tf_op jit(solution)/shard_map/ppermute | solution.py:100
  7.0 1.0 gather_fusion.2
  8.1 1.4 %collective-permute-done.1 = bf16[4,3584]{1,0:T(4,128)(2,1)S(1)} collective-permute-done((bf16[4,3584]{1,0:T(4,128)(2,1)}, bf16[4,3584]{1,0:T(4,128)(2,1)S(1)}, u32[]{:S(2)}, u32[]{:S(2)}) %collective-permute-start.1) | collective-permute-done | bytes 28704 | tf_op jit(solution)/shard_map/ppermute | solution.py:100
  9.7 3.2 %collective-permute-start.5 = (bf16[16,3584]{1,0:T(8,128)(2,1)S(1)}, bf16[16,3584]{1,0:T(8,128)(2,1)S(1)}, u32[]{:S(2)}, u32[]{:S(2)}) collective-permute-start(bf16[16,3584]{1,0:T(8,128)(2,1)S(1)} %reshape.865), channel_id=1, source_target_pairs={{0,24},{1,25},{2,26},{3,27},{4,28},{5,29},{6,30},{7,31},{8,0},{9,1... | collective-permute-start | bytes 344072 | tf_op jit(solution)/shard_map/ppermute | solution.py:100
  16.0 5.8 %conditional.1 = (f32[512,1152]{1,0:T(8,128)}) conditional(s32[]{:T(128)} %convert_element_type.46, (s32[512,64]{1,0:T(8,128)S(1)}, pred[512]{0:T(512)(128)(4,1)S(1)}, f32[512,64]{0,1:T(8,128)S(1)}, s32[512,1]{0,1:T(1,128)S(1)}) %tuple.101, (s32[512,64]{1,0:T(8,128)S(1)}, pred[512]{0:T(512)(128)(4,1)S(1)}, f32[512,64]{0,1:T(8,128)S(1)}, ...), branch_computations={%region_3.7_spmd, %region_7.11_spmd} | conditional | flops 17916928 | bytes 5218828 | solution.py:44
  18.2 3.6 %select_add_fusion = f32[512,1152]{1,0:T(8,128)} fusion(f32[512]{0:T(512)S(1)} %bitcast.195, s32[512]{0:T(512)S(1)} %bitcast.187, f32[512]{0:T(512)S(1)} %bitcast.196, s32[512]{0:T(512)S(1)} %bitcast.188, f32[512]{0:T(512)S(1)} %bitcast.197, s32[512]{0:T(512)S(1)} %bitcast.189, f32[512]{0:T(512)S(1)} %bitcast.198, s32[512]{0:T(512)S(1)} %bitcast.190, ...), kind=kLoop, calls=%fused_computation.6 | loop fusion | flops 13565952 | bytes 2392064 | tf_op jit(solution)/shard_map/cond/branch_0_fun/add | solution.py:37
  22.0 4.1 %collective-permute-start.8 = (bf16[64,3584]{1,0:T(8,128)(2,1)S(1)}, bf16[64,3584]{1,0:T(8,128)(2,1)S(1)}, u32[]{:S(2)}, u32[]{:S(2)}) collective-permute-start(bf16[64,3584]{1,0:T(8,128)(2,1)S(1)} %bitcast.152), channel_id=1, source_target_pairs={{0,6},{1,97},{2,0},{3,99},{4,2},{5,101},{6,4},{7,103},{8,14},{9,10... | collective-permute-start | bytes 1376264 | tf_op jit(solution)/shard_map/ppermute | solution.py:100
  26.1 1.3 collective-permute-start.6
  27.3 5.9 %fusion.115 = f32[64,1152]{1,0:T(8,128)S(1)} fusion(bf16[64,3584]{1,0:T(8,128)(2,1)S(1)} %bitcast.155, bf16[1152,3584]{1,0:T(8,128)(2,1)} %param.9), kind=kOutput, calls=%fused_computation.336 | convolution fusion | flops 528482304 | bytes 9011200 | tf_op jit(solution)/shard_map/dot_general | solution.py:133
  33.3 3.7 %collective-permute-done.8 = bf16[64,3584]{1,0:T(8,128)(2,1)S(1)} collective-permute-done((bf16[64,3584]{1,0:T(8,128)(2,1)S(1)}, bf16[64,3584]{1,0:T(8,128)(2,1)S(1)}, u32[]{:S(2)}, u32[]{:S(2)}) %collective-permute-start.8) | collective-permute-done | bytes 458784 | tf_op jit(solution)/shard_map/ppermute | solution.py:100
  37.0 3.7 %collective-permute-done.6 = bf16[64,3584]{1,0:T(8,128)(2,1)S(1)} collective-permute-done((bf16[64,3584]{1,0:T(8,128)(2,1)S(1)}, bf16[64,3584]{1,0:T(8,128)(2,1)S(1)}, u32[]{:S(2)}, u32[]{:S(2)}) %collective-permute-start.6) | collective-permute-done | bytes 458784 | tf_op jit(solution)/shard_map/ppermute | solution.py:100
  41.3 2.8 %fusion.116 = f32[192,1152]{1,0:T(8,128)S(1)} fusion(bf16[192,3584]{1,0:T(8,128)(2,1)S(1)} %bitcast.158, bf16[1152,3584]{1,0:T(8,128)(2,1)S(1)} %bitcast.147), kind=kOutput, calls=%fused_computation.337 | convolution fusion | flops 1585446912 | bytes 10518528 | tf_op jit(solution)/shard_map/dot_general | solution.py:133
  44.2 1.1 pad_maximum_fusion.1
  45.2 2.6 %fusion.114 = (f32[256]{0:T(256)S(1)}, f32[256,1152]{1,0:T(8,128)S(1)}) fusion(bf16[256,3584]{1,0:T(8,128)(2,1)S(1)} %collective-permute-done.9, bf16[1152,3584]{1,0:T(8,128)(2,1)S(1)} %bitcast.147), kind=kOutput, calls=%fused_computation.335 | convolution fusion | flops 2114223872 | bytes 11273216 | tf_op jit(solution)/shard_map/dot_general | solution.py:133
  47.9 2.3 %multiply_reduce_fusion.1 = (f32[256]{0:T(256)S(1)}, f32[256]{0:T(256)S(1)}, f32[256]{0:T(256)S(1)}, f32[256]{0:T(256)S(1)}) fusion(f32[512,1152]{1,0:T(8,128)} %get-tuple-element.259, f32[192,1152]{1,0:T(8,128)S(1)} %fusion.116, f32[64,1152]{1,0:T(8,128)S(1)} %fusion.115, f32[256,1152]{1,0:T(8,128)S(1)} %get-tuple-element.214, ...), kind=kLoop, calls=%fused_computation.45 | loop fusion | flops 2653184 | bytes 4724736 | tf_op jit(solution)/shard_map/reduce_sum | solution.py:171
  51.1 2.0 %gather_fusion.3 = f32[512,3]{1,0:T(8,128)S(1)} fusion(f32[3,512]{0,1:T(8,128)} %copy.85, s32[1024]{0:T(1024)S(1)} %pad_clamp_fusion.2), kind=kCustom, calls=%fused_computation.3 | custom fusion | bytes 14336 | tf_op jit(solution)/shard_map/jit(_take)/gather | solution.py:177
  55.3 1.1 copy.86
  56.3 1.1 copy.87
  57.9 1.5 %collective-permute-start.11 = (f32[3,512]{1,0:T(4,128)S(1)}, f32[3,512]{1,0:T(4,128)S(1)}, u32[]{:S(2)}, u32[]{:S(2)}) collective-permute-start(f32[3,512]{1,0:T(4,128)S(1)} %get-tuple-element.212), channel_id=1, source_target_pairs={{0,2},{1,3},{2,4},{3,5},{4,6},{5,7},{6,0},{7,1},{8,10},{9,11},{10,... | collective-permute-start | bytes 18440 | tf_op jit(solution)/shard_map/ppermute | solution.py:100
  59.3 1.8 %collective-permute-start.13 = (f32[3,512]{1,0:T(4,128)S(1)}, f32[3,512]{1,0:T(4,128)S(1)}, u32[]{:S(2)}, u32[]{:S(2)}) collective-permute-start(f32[3,512]{1,0:T(4,128)S(1)} %get-tuple-element.212), channel_id=1, source_target_pairs={{0,6},{1,7},{2,0},{3,1},{4,2},{5,3},{6,4},{7,5},{8,14},{9,15},{10,... | collective-permute-start | bytes 18440 | tf_op jit(solution)/shard_map/ppermute | solution.py:100
  61.1 1.7 %collective-permute-done.12 = f32[3,512]{1,0:T(4,128)S(1)} collective-permute-done((f32[3,512]{1,0:T(4,128)S(1)}, f32[3,512]{1,0:T(4,128)S(1)}, u32[]{:S(2)}, u32[]{:S(2)}) %collective-permute-start.12) | collective-permute-done | bytes 6176 | tf_op jit(solution)/shard_map/ppermute | solution.py:100
  63.1 2.0 %collective-permute-start.15 = (f32[3,512]{1,0:T(4,128)S(1)}, f32[3,512]{1,0:T(4,128)S(1)}, u32[]{:S(2)}, u32[]{:S(2)}) collective-permute-start(f32[3,512]{1,0:T(4,128)S(1)} %get-tuple-element.210), channel_id=1, source_target_pairs={{0,16},{1,17},{2,18},{3,19},{4,20},{5,21},{6,22},{7,23},{8,24},{9,... | collective-permute-start | bytes 18440 | tf_op jit(solution)/shard_map/ppermute | solution.py:100
  65.1 1.2 collective-permute-start.14
  66.3 2.0 %collective-permute-start.16 = (f32[3,512]{1,0:T(4,128)S(1)}, f32[3,512]{1,0:T(4,128)S(1)}, u32[]{:S(2)}, u32[]{:S(2)}) collective-permute-start(f32[3,512]{1,0:T(4,128)S(1)} %get-tuple-element.210), channel_id=1, source_target_pairs={{0,24},{1,25},{2,26},{3,27},{4,28},{5,29},{6,30},{7,31},{8,0},{9,1... | collective-permute-start | bytes 18440 | tf_op jit(solution)/shard_map/ppermute | solution.py:100
  68.4 1.6 %collective-permute-done.14 = f32[3,512]{1,0:T(4,128)S(1)} collective-permute-done((f32[3,512]{1,0:T(4,128)S(1)}, f32[3,512]{1,0:T(4,128)S(1)}, u32[]{:S(2)}, u32[]{:S(2)}) %collective-permute-start.14) | collective-permute-done | bytes 6176 | tf_op jit(solution)/shard_map/ppermute | solution.py:100
  70.1 1.9 %collective-permute-start.18 = (f32[3,512]{1,0:T(4,128)S(1)}, f32[3,512]{1,0:T(4,128)S(1)}, u32[]{:S(2)}, u32[]{:S(2)}) collective-permute-start(f32[3,512]{1,0:T(4,128)S(1)} %get-tuple-element.208), channel_id=1, source_target_pairs={{0,64},{1,65},{2,66},{3,67},{4,68},{5,69},{6,70},{7,71},{8,72},{9,... | collective-permute-start | bytes 18440 | tf_op jit(solution)/shard_map/ppermute | solution.py:100
  72.6 2.6 %collective-permute-start.19 = (f32[3,512]{1,0:T(4,128)S(1)}, f32[3,512]{1,0:T(4,128)S(1)}, u32[]{:S(2)}, u32[]{:S(2)}) collective-permute-start(f32[3,512]{1,0:T(4,128)S(1)} %get-tuple-element.208), channel_id=1, source_target_pairs={{0,96},{1,97},{2,98},{3,99},{4,100},{5,101},{6,102},{7,103},{8,104... | collective-permute-start | bytes 18440 | tf_op jit(solution)/shard_map/ppermute | solution.py:100
  75.3 1.5 %collective-permute-done.17 = f32[3,512]{1,0:T(4,128)S(1)} collective-permute-done((f32[3,512]{1,0:T(4,128)S(1)}, f32[3,512]{1,0:T(4,128)S(1)}, u32[]{:S(2)}, u32[]{:S(2)}) %collective-permute-start.17) | collective-permute-done | bytes 6176 | tf_op jit(solution)/shard_map/ppermute | solution.py:100
  77.2 1.6 %gather_fusion.4 = f32[512,2]{1,0:T(8,128)} fusion(f32[512,2]{1,0:T(8,128)S(1)} %copy.97, s32[1024]{0:T(1024)S(1)} %pad_clamp_fusion.3), kind=kCustom, calls=%fused_computation.4 | custom fusion | bytes 10240 | tf_op jit(solution)/shard_map/jit(_take)/gather | solution.py:192
  78.8 1.1 broadcast_select_fusion
  80.2 1.8 %multiply_convert_fusion.1 = bf16[256,1152]{1,0:T(8,128)(2,1)S(1)} fusion(f32[256,1152]{1,0:T(8,128)S(1)} %get-tuple-element.214, f32[512,1152]{1,0:T(8,128)} %get-tuple-element.259, f32[256]{0:T(256)S(1)} %get-tuple-element.149, f32[256]{0:T(256)S(1)} %get-tuple-element.150), kind=kLoop, calls=%fused_computation.43 | loop fusion | flops 1474560 | bytes 2951168 | tf_op jit(solution)/shard_map/convert_element_type | solution.py:196
  82.0 6.0 %convolution_convert_fusion.1 = bf16[256,3584]{1,0:T(8,128)(2,1)S(1)} fusion(bf16[256,1152]{1,0:T(8,128)(2,1)S(1)} %multiply_convert_fusion.1, bf16[1152,3584]{1,0:T(8,128)(2,1)} %param.9), kind=kOutput, calls=%fused_computation.31 | convolution fusion | flops 2114846720 | bytes 10682368 | tf_op jit(solution)/shard_map/dot_general | solution.py:202
  88.4 1.6 %multiply_convert_fusion = bf16[256,1152]{1,0:T(8,128)(2,1)S(1)} fusion(f32[256,1152]{1,0:T(8,128)S(1)} %copy-done, f32[512,1152]{1,0:T(8,128)} %get-tuple-element.259, f32[256]{0:T(256)S(1)} %get-tuple-element.148, f32[256]{0:T(256)S(1)} %get-tuple-element.147), kind=kLoop, calls=%fused_computation.42 | loop fusion | flops 1474560 | bytes 2951168 | tf_op jit(solution)/shard_map/convert_element_type | solution.py:196
  90.0 2.5 %fusion.117 = f32[256,3584]{1,0:T(8,128)S(1)} fusion(bf16[256,1152]{1,0:T(8,128)(2,1)S(1)} %multiply_convert_fusion, bf16[1152,3584]{1,0:T(8,128)(2,1)S(1)} %bitcast.149), kind=kOutput, calls=%fused_computation.338 | convolution fusion | flops 2113929216 | bytes 12517376 | tf_op jit(solution)/shard_map/dot_general | solution.py:206
  93.3 1.8 %collective-permute-start.21 = (bf16[64,3584]{1,0:T(8,128)(2,1)S(1)}, bf16[64,3584]{1,0:T(8,128)(2,1)S(1)}, u32[]{:S(2)}, u32[]{:S(2)}) collective-permute-start(bf16[64,3584]{1,0:T(8,128)(2,1)S(1)} %get-tuple-element.195), channel_id=1, source_target_pairs={{0,2},{1,33},{2,4},{3,35},{4,6},{5,37},{6,0},{7,39},{8,10},{9,41},... | collective-permute-start | bytes 1376264 | tf_op jit(solution)/shard_map/ppermute | solution.py:100
  95.1 1.5 %collective-permute-start.23 = (bf16[64,3584]{1,0:T(8,128)(2,1)S(1)}, bf16[64,3584]{1,0:T(8,128)(2,1)S(1)}, u32[]{:S(2)}, u32[]{:S(2)}) collective-permute-start(bf16[64,3584]{1,0:T(8,128)(2,1)S(1)} %get-tuple-element.196), channel_id=1, source_target_pairs={{0,6},{1,97},{2,0},{3,99},{4,2},{5,101},{6,4},{7,103},{8,14},{9,10... | collective-permute-start | bytes 1376264 | tf_op jit(solution)/shard_map/ppermute | solution.py:100
  96.6 1.2 collective-permute-start.22
  97.8 6.7 %convolution_convert_fusion = bf16[1152,3584]{1,0:T(8,128)(2,1)} fusion(bf16[256,3584]{1,0:T(8,128)(2,1)S(1)} %copy-done.4, bf16[256,3584]{1,0:T(8,128)(2,1)S(1)} %bitcast.151, bf16[256,1152]{1,0:T(8,128)(2,1)S(1)} %multiply_convert_fusion.1, bf16[256,1152]{1,0:T(8,128)(2,1)S(1)} %multiply_convert_fusion), kind=kOutput, calls=%fused_computation.30 | convolution fusion | flops 4241686528 | bytes 13107200 | tf_op jit(solution)/shard_map/dot_general | solution.py:210
  104.6 4.6 %collective-permute-done.22 = bf16[64,3584]{1,0:T(8,128)(2,1)S(1)} collective-permute-done((bf16[64,3584]{1,0:T(8,128)(2,1)S(1)}, bf16[64,3584]{1,0:T(8,128)(2,1)S(1)}, u32[]{:S(2)}, u32[]{:S(2)}) %collective-permute-start.22) | collective-permute-done | bytes 458784 | tf_op jit(solution)/shard_map/ppermute | solution.py:100
  110.5 2.5 %collective-permute-start.26 = (bf16[16,3584]{1,0:T(8,128)(2,1)S(1)}, bf16[16,3584]{1,0:T(8,128)(2,1)S(1)}, u32[]{:S(2)}, u32[]{:S(2)}) collective-permute-start(bf16[16,3584]{1,0:T(8,128)(2,1)S(1)} %get-tuple-element.201), channel_id=1, source_target_pairs={{0,24},{1,25},{2,26},{3,27},{4,28},{5,29},{6,30},{7,31},{8,0},{9,1... | collective-permute-start | bytes 344072 | tf_op jit(solution)/shard_map/ppermute | solution.py:100
  113.0 1.6 %collective-permute-start.25 = (bf16[16,3584]{1,0:T(8,128)(2,1)S(1)}, bf16[16,3584]{1,0:T(8,128)(2,1)S(1)}, u32[]{:S(2)}, u32[]{:S(2)}) collective-permute-start(bf16[16,3584]{1,0:T(8,128)(2,1)S(1)} %get-tuple-element.202), channel_id=1, source_target_pairs={{0,16},{1,17},{2,18},{3,19},{4,20},{5,21},{6,22},{7,23},{8,24},{9,... | collective-permute-start | bytes 344072 | tf_op jit(solution)/shard_map/ppermute | solution.py:100
  114.6 1.5 %collective-permute-done.24 = bf16[16,3584]{1,0:T(8,128)(2,1)S(1)} collective-permute-done((bf16[16,3584]{1,0:T(8,128)(2,1)S(1)}, bf16[16,3584]{1,0:T(8,128)(2,1)S(1)}, u32[]{:S(2)}, u32[]{:S(2)}) %collective-permute-start.24) | collective-permute-done | bytes 114720 | tf_op jit(solution)/shard_map/ppermute | solution.py:100
  116.1 1.8 %collective-permute-done.26 = bf16[16,3584]{1,0:T(8,128)(2,1)S(1)} collective-permute-done((bf16[16,3584]{1,0:T(8,128)(2,1)S(1)}, bf16[16,3584]{1,0:T(8,128)(2,1)S(1)}, u32[]{:S(2)}, u32[]{:S(2)}) %collective-permute-start.26) | collective-permute-done | bytes 114720 | tf_op jit(solution)/shard_map/ppermute | solution.py:100
  117.9 1.8 %collective-permute-done.25 = bf16[16,3584]{1,0:T(8,128)(2,1)S(1)} collective-permute-done((bf16[16,3584]{1,0:T(8,128)(2,1)S(1)}, bf16[16,3584]{1,0:T(8,128)(2,1)S(1)}, u32[]{:S(2)}, u32[]{:S(2)}) %collective-permute-start.25) | collective-permute-done | bytes 114720 | tf_op jit(solution)/shard_map/ppermute | solution.py:100
  120.7 2.4 %collective-permute-start.29 = (bf16[4,3584]{1,0:T(4,128)(2,1)S(1)}, bf16[4,3584]{1,0:T(4,128)(2,1)S(1)}, u32[]{:S(2)}, u32[]{:S(2)}) collective-permute-start(bf16[4,3584]{1,0:T(4,128)(2,1)S(1)} %get-tuple-element.204), channel_id=1, source_target_pairs={{0,96},{1,7},{2,98},{3,1},{4,100},{5,3},{6,102},{7,5},{8,104},{9,1... | collective-permute-start | bytes 86024 | tf_op jit(solution)/shard_map/ppermute | solution.py:100
  125.0 3.5 %collective-permute-done.28 = bf16[4,3584]{1,0:T(4,128)(2,1)S(1)} collective-permute-done((bf16[4,3584]{1,0:T(4,128)(2,1)S(1)}, bf16[4,3584]{1,0:T(4,128)(2,1)S(1)}, u32[]{:S(2)}, u32[]{:S(2)}) %collective-permute-start.28) | collective-permute-done | bytes 28704 | tf_op jit(solution)/shard_map/ppermute | solution.py:100
  (126 shorter events, 17.7 us)
Async XLA Ops:
  0.6 8.9 %copy-start.2 = (bf16[4,3584]{1,0:T(4,128)(2,1)S(1)}, bf16[4,3584]{1,0:T(4,128)(2,1)}, u32[]{:S(2)}) copy-start(bf16[4,3584]{1,0:T(4,128)(2,1)} %param.8) | copy-start | bytes 86020
  0.6 15.3 %copy-start.1 = (f32[512,64]{0,1:T(8,128)S(1)}, f32[512,64]{0,1:T(8,128)}, u32[]{:S(2)}) copy-start(f32[512,64]{0,1:T(8,128)} %param.11) | copy-start | bytes 393220
  0.6 7.4 %collective-permute-start = (bf16[4,3584]{1,0:T(4,128)(2,1)}, bf16[4,3584]{1,0:T(4,128)(2,1)S(1)}, u32[]{:S(2)}, u32[]{:S(2)}) collective-permute-start(bf16[4,3584]{1,0:T(4,128)(2,1)} %param.8), channel_id=1, source_target_pairs={{0,32},{1,3},{2,34},{3,5},{4,36},{5,7},{6,38},{7,1},{8,40},{9,11},... | collective-permute-start | bytes 86024 | tf_op jit(solution)/shard_map/ppermute | solution.py:100
  2.3 5.8 %collective-permute-start.2 = (bf16[4,3584]{1,0:T(4,128)(2,1)}, bf16[4,3584]{1,0:T(4,128)(2,1)S(1)}, u32[]{:S(2)}, u32[]{:S(2)}) collective-permute-start(bf16[4,3584]{1,0:T(4,128)(2,1)} %param.8), channel_id=1, source_target_pairs={{0,96},{1,7},{2,98},{3,1},{4,100},{5,3},{6,102},{7,5},{8,104},{9,1... | collective-permute-start | bytes 86024 | tf_op jit(solution)/shard_map/ppermute | solution.py:100
  4.0 5.6 %collective-permute-start.1 = (bf16[4,3584]{1,0:T(4,128)(2,1)}, bf16[4,3584]{1,0:T(4,128)(2,1)S(1)}, u32[]{:S(2)}, u32[]{:S(2)}) collective-permute-start(bf16[4,3584]{1,0:T(4,128)(2,1)} %param.8), channel_id=1, source_target_pairs={{0,64},{1,5},{2,66},{3,7},{4,68},{5,1},{6,70},{7,3},{8,72},{9,13},... | collective-permute-start | bytes 86024 | tf_op jit(solution)/shard_map/ppermute | solution.py:100
  9.7 12.2 %collective-permute-start.5 = (bf16[16,3584]{1,0:T(8,128)(2,1)S(1)}, bf16[16,3584]{1,0:T(8,128)(2,1)S(1)}, u32[]{:S(2)}, u32[]{:S(2)}) collective-permute-start(bf16[16,3584]{1,0:T(8,128)(2,1)S(1)} %reshape.865), channel_id=1, source_target_pairs={{0,24},{1,25},{2,26},{3,27},{4,28},{5,29},{6,30},{7,31},{8,0},{9,1... | collective-permute-start | bytes 344072 | tf_op jit(solution)/shard_map/ppermute | solution.py:100
  12.9 9.0 %collective-permute-start.4 = (bf16[16,3584]{1,0:T(8,128)(2,1)S(1)}, bf16[16,3584]{1,0:T(8,128)(2,1)S(1)}, u32[]{:S(2)}, u32[]{:S(2)}) collective-permute-start(bf16[16,3584]{1,0:T(8,128)(2,1)S(1)} %reshape.865), channel_id=1, source_target_pairs={{0,16},{1,17},{2,18},{3,19},{4,20},{5,21},{6,22},{7,23},{8,24},{9,... | collective-permute-start | bytes 344072 | tf_op jit(solution)/shard_map/ppermute | solution.py:100
  13.5 8.4 %collective-permute-start.3 = (bf16[16,3584]{1,0:T(8,128)(2,1)S(1)}, bf16[16,3584]{1,0:T(8,128)(2,1)S(1)}, u32[]{:S(2)}, u32[]{:S(2)}) collective-permute-start(bf16[16,3584]{1,0:T(8,128)(2,1)S(1)} %reshape.865), channel_id=1, source_target_pairs={{0,8},{1,9},{2,10},{3,11},{4,12},{5,13},{6,14},{7,15},{8,16},{9,17... | collective-permute-start | bytes 344072 | tf_op jit(solution)/shard_map/ppermute | solution.py:100
  21.9 19.4 %slice-start = ((s8[8257536]{0:T(1024)(128)(4,1)}), s8[4194304]{0:T(1024)(128)(4,1)S(1)}, s32[]{:S(2)}) async-start(s8[8257536]{0:T(1024)(128)(4,1)} %bitcast.146), calls=%async_computation | async-start | bytes 8388608
  22.0 19.4 %slice-start.1 = ((s8[8257536]{0:T(1024)(128)(4,1)}), s8[4063232]{0:T(1024)(128)(4,1)S(1)}, s32[]{:S(2)}) async-start(s8[8257536]{0:T(1024)(128)(4,1)} %bitcast.146), calls=%async_computation.1 | async-start | bytes 8126464
  22.0 15.0 %collective-permute-start.8 = (bf16[64,3584]{1,0:T(8,128)(2,1)S(1)}, bf16[64,3584]{1,0:T(8,128)(2,1)S(1)}, u32[]{:S(2)}, u32[]{:S(2)}) collective-permute-start(bf16[64,3584]{1,0:T(8,128)(2,1)S(1)} %bitcast.152), channel_id=1, source_target_pairs={{0,6},{1,97},{2,0},{3,99},{4,2},{5,101},{6,4},{7,103},{8,14},{9,10... | collective-permute-start | bytes 1376264 | tf_op jit(solution)/shard_map/ppermute | solution.py:100
  26.1 10.9 %collective-permute-start.7 = (bf16[64,3584]{1,0:T(8,128)(2,1)S(1)}, bf16[64,3584]{1,0:T(8,128)(2,1)S(1)}, u32[]{:S(2)}, u32[]{:S(2)}) collective-permute-start(bf16[64,3584]{1,0:T(8,128)(2,1)S(1)} %bitcast.153), channel_id=1, source_target_pairs={{0,4},{1,65},{2,6},{3,67},{4,0},{5,69},{6,2},{7,71},{8,12},{9,73},... | collective-permute-start | bytes 1376264 | tf_op jit(solution)/shard_map/ppermute | solution.py:100
  26.1 14.6 %collective-permute-start.6 = (bf16[64,3584]{1,0:T(8,128)(2,1)S(1)}, bf16[64,3584]{1,0:T(8,128)(2,1)S(1)}, u32[]{:S(2)}, u32[]{:S(2)}) collective-permute-start(bf16[64,3584]{1,0:T(8,128)(2,1)S(1)} %bitcast.154), channel_id=1, source_target_pairs={{0,2},{1,33},{2,4},{3,35},{4,6},{5,37},{6,0},{7,39},{8,10},{9,41},... | collective-permute-start | bytes 1376264 | tf_op jit(solution)/shard_map/ppermute | solution.py:100
  40.9 4.3 %collective-permute-start.9 = (bf16[256,3584]{1,0:T(8,128)(2,1)S(1)}, bf16[256,3584]{1,0:T(8,128)(2,1)S(1)}, u32[]{:S(2)}, u32[]{:S(2)}) collective-permute-start(bf16[256,3584]{1,0:T(8,128)(2,1)S(1)} %bitcast.150), channel_id=1, source_target_pairs={{0,1},{1,0},{2,3},{3,2},{4,5},{5,4},{6,7},{7,6},{8,9},{9,8},{10,11... | collective-permute-start | bytes 5505032 | tf_op jit(solution)/shard_map/ppermute | solution.py:160
  45.2 2.6 %copy-start.3 = (bf16[256,3584]{1,0:T(8,128)(2,1)}, bf16[256,3584]{1,0:T(8,128)(2,1)S(1)}, u32[]{:S(2)}) copy-start(bf16[256,3584]{1,0:T(8,128)(2,1)S(1)} %collective-permute-done.9) | copy-start | bytes 5505028
  54.0 2.4 %collective-permute-start.10 = (f32[3,512]{0,1:T(8,128)}, f32[3,512]{0,1:T(8,128)}, u32[]{:S(2)}, u32[]{:S(2)}) collective-permute-start(f32[3,512]{0,1:T(8,128)} %bitcast_select_fusion.1), channel_id=1, source_target_pairs={{0,1},{1,0},{2,3},{3,2},{4,5},{5,4},{6,7},{7,6},{8,9},{9,8},{10,11... | collective-permute-start | bytes 18440 | tf_op jit(solution)/shard_map/ppermute | solution.py:100
  57.5 5.3 %collective-permute-start.12 = (f32[3,512]{1,0:T(4,128)S(1)}, f32[3,512]{1,0:T(4,128)S(1)}, u32[]{:S(2)}, u32[]{:S(2)}) collective-permute-start(f32[3,512]{1,0:T(4,128)S(1)} %get-tuple-element.212), channel_id=1, source_target_pairs={{0,4},{1,5},{2,6},{3,7},{4,0},{5,1},{6,2},{7,3},{8,12},{9,13},{10,... | collective-permute-start | bytes 18440 | tf_op jit(solution)/shard_map/ppermute | solution.py:100
  57.9 5.0 %collective-permute-start.11 = (f32[3,512]{1,0:T(4,128)S(1)}, f32[3,512]{1,0:T(4,128)S(1)}, u32[]{:S(2)}, u32[]{:S(2)}) collective-permute-start(f32[3,512]{1,0:T(4,128)S(1)} %get-tuple-element.212), channel_id=1, source_target_pairs={{0,2},{1,3},{2,4},{3,5},{4,6},{5,7},{6,0},{7,1},{8,10},{9,11},{10,... | collective-permute-start | bytes 18440 | tf_op jit(solution)/shard_map/ppermute | solution.py:100
  59.3 3.7 %collective-permute-start.13 = (f32[3,512]{1,0:T(4,128)S(1)}, f32[3,512]{1,0:T(4,128)S(1)}, u32[]{:S(2)}, u32[]{:S(2)}) collective-permute-start(f32[3,512]{1,0:T(4,128)S(1)} %get-tuple-element.212), channel_id=1, source_target_pairs={{0,6},{1,7},{2,0},{3,1},{4,2},{5,3},{6,4},{7,5},{8,14},{9,15},{10,... | collective-permute-start | bytes 18440 | tf_op jit(solution)/shard_map/ppermute | solution.py:100
  63.1 5.3 %collective-permute-start.15 = (f32[3,512]{1,0:T(4,128)S(1)}, f32[3,512]{1,0:T(4,128)S(1)}, u32[]{:S(2)}, u32[]{:S(2)}) collective-permute-start(f32[3,512]{1,0:T(4,128)S(1)} %get-tuple-element.210), channel_id=1, source_target_pairs={{0,16},{1,17},{2,18},{3,19},{4,20},{5,21},{6,22},{7,23},{8,24},{9,... | collective-permute-start | bytes 18440 | tf_op jit(solution)/shard_map/ppermute | solution.py:100
  65.1 4.9 %collective-permute-start.14 = (f32[3,512]{1,0:T(4,128)S(1)}, f32[3,512]{1,0:T(4,128)S(1)}, u32[]{:S(2)}, u32[]{:S(2)}) collective-permute-start(f32[3,512]{1,0:T(4,128)S(1)} %get-tuple-element.210), channel_id=1, source_target_pairs={{0,8},{1,9},{2,10},{3,11},{4,12},{5,13},{6,14},{7,15},{8,16},{9,17... | collective-permute-start | bytes 18440 | tf_op jit(solution)/shard_map/ppermute | solution.py:100
  66.3 3.7 %collective-permute-start.16 = (f32[3,512]{1,0:T(4,128)S(1)}, f32[3,512]{1,0:T(4,128)S(1)}, u32[]{:S(2)}, u32[]{:S(2)}) collective-permute-start(f32[3,512]{1,0:T(4,128)S(1)} %get-tuple-element.210), channel_id=1, source_target_pairs={{0,24},{1,25},{2,26},{3,27},{4,28},{5,29},{6,30},{7,31},{8,0},{9,1... | collective-permute-start | bytes 18440 | tf_op jit(solution)/shard_map/ppermute | solution.py:100
  70.1 5.2 %collective-permute-start.18 = (f32[3,512]{1,0:T(4,128)S(1)}, f32[3,512]{1,0:T(4,128)S(1)}, u32[]{:S(2)}, u32[]{:S(2)}) collective-permute-start(f32[3,512]{1,0:T(4,128)S(1)} %get-tuple-element.208), channel_id=1, source_target_pairs={{0,64},{1,65},{2,66},{3,67},{4,68},{5,69},{6,70},{7,71},{8,72},{9,... | collective-permute-start | bytes 18440 | tf_op jit(solution)/shard_map/ppermute | solution.py:100
  72.0 4.9 %collective-permute-start.17 = (f32[3,512]{1,0:T(4,128)S(1)}, f32[3,512]{1,0:T(4,128)S(1)}, u32[]{:S(2)}, u32[]{:S(2)}) collective-permute-start(f32[3,512]{1,0:T(4,128)S(1)} %get-tuple-element.208), channel_id=1, source_target_pairs={{0,32},{1,33},{2,34},{3,35},{4,36},{5,37},{6,38},{7,39},{8,40},{9,... | collective-permute-start | bytes 18440 | tf_op jit(solution)/shard_map/ppermute | solution.py:100
  72.6 4.3 %collective-permute-start.19 = (f32[3,512]{1,0:T(4,128)S(1)}, f32[3,512]{1,0:T(4,128)S(1)}, u32[]{:S(2)}, u32[]{:S(2)}) collective-permute-start(f32[3,512]{1,0:T(4,128)S(1)} %get-tuple-element.208), channel_id=1, source_target_pairs={{0,96},{1,97},{2,98},{3,99},{4,100},{5,101},{6,102},{7,103},{8,104... | collective-permute-start | bytes 18440 | tf_op jit(solution)/shard_map/ppermute | solution.py:100
  80.2 9.8 %slice-start.2 = ((s8[8257536]{0:T(1024)(128)(4,1)}), s8[4194304]{0:T(1024)(128)(4,1)S(1)}, s32[]{:S(2)}) async-start(s8[8257536]{0:T(1024)(128)(4,1)} %bitcast.148), calls=%async_computation.2 | async-start | bytes 8388608
  82.0 6.4 %copy-start = (f32[256,1152]{1,0:T(8,128)S(1)}, f32[256,1152]{1,0:T(8,128)}, u32[]{:S(2)}) copy-start(f32[256,1152]{1,0:T(8,128)} %get-tuple-element.80) | copy-start | bytes 3538948
  82.0 8.0 %slice-start.3 = ((s8[8257536]{0:T(1024)(128)(4,1)}), s8[4063232]{0:T(1024)(128)(4,1)S(1)}, s32[]{:S(2)}) async-start(s8[8257536]{0:T(1024)(128)(4,1)} %bitcast.148), calls=%async_computation.3 | async-start | bytes 8126464
  88.1 4.5 %collective-permute-start.20 = (bf16[256,3584]{1,0:T(8,128)(2,1)S(1)}, bf16[256,3584]{1,0:T(8,128)(2,1)S(1)}, u32[]{:S(2)}, u32[]{:S(2)}) collective-permute-start(bf16[256,3584]{1,0:T(8,128)(2,1)S(1)} %convolution_convert_fusion.1), channel_id=1, source_target_pairs={{0,1},{1,0},{2,3},{3,2},{4,5},{5,4},{6,7},{7,6},{8,9},{9,8},{10,11... | collective-permute-start | bytes 5505032 | tf_op jit(solution)/shard_map/ppermute | solution.py:203
  93.2 4.6 %copy-start.4 = (bf16[256,3584]{1,0:T(8,128)(2,1)S(1)}, bf16[256,3584]{1,0:T(8,128)(2,1)}, u32[]{:S(2)}) copy-start(bf16[256,3584]{1,0:T(8,128)(2,1)} %copy-done.3) | copy-start | bytes 5505028
  93.3 11.2 %collective-permute-start.21 = (bf16[64,3584]{1,0:T(8,128)(2,1)S(1)}, bf16[64,3584]{1,0:T(8,128)(2,1)S(1)}, u32[]{:S(2)}, u32[]{:S(2)}) collective-permute-start(bf16[64,3584]{1,0:T(8,128)(2,1)S(1)} %get-tuple-element.195), channel_id=1, source_target_pairs={{0,2},{1,33},{2,4},{3,35},{4,6},{5,37},{6,0},{7,39},{8,10},{9,41},... | collective-permute-start | bytes 1376264 | tf_op jit(solution)/shard_map/ppermute | solution.py:100
  95.1 9.4 %collective-permute-start.23 = (bf16[64,3584]{1,0:T(8,128)(2,1)S(1)}, bf16[64,3584]{1,0:T(8,128)(2,1)S(1)}, u32[]{:S(2)}, u32[]{:S(2)}) collective-permute-start(bf16[64,3584]{1,0:T(8,128)(2,1)S(1)} %get-tuple-element.196), channel_id=1, source_target_pairs={{0,6},{1,97},{2,0},{3,99},{4,2},{5,101},{6,4},{7,103},{8,14},{9,10... | collective-permute-start | bytes 1376264 | tf_op jit(solution)/shard_map/ppermute | solution.py:100
  96.6 12.6 %collective-permute-start.22 = (bf16[64,3584]{1,0:T(8,128)(2,1)S(1)}, bf16[64,3584]{1,0:T(8,128)(2,1)S(1)}, u32[]{:S(2)}, u32[]{:S(2)}) collective-permute-start(bf16[64,3584]{1,0:T(8,128)(2,1)S(1)} %get-tuple-element.197), channel_id=1, source_target_pairs={{0,4},{1,65},{2,6},{3,67},{4,0},{5,69},{6,2},{7,71},{8,12},{9,73},... | collective-permute-start | bytes 1376264 | tf_op jit(solution)/shard_map/ppermute | solution.py:100
  109.6 6.5 %collective-permute-start.24 = (bf16[16,3584]{1,0:T(8,128)(2,1)S(1)}, bf16[16,3584]{1,0:T(8,128)(2,1)S(1)}, u32[]{:S(2)}, u32[]{:S(2)}) collective-permute-start(bf16[16,3584]{1,0:T(8,128)(2,1)S(1)} %get-tuple-element.200), channel_id=1, source_target_pairs={{0,8},{1,9},{2,10},{3,11},{4,12},{5,13},{6,14},{7,15},{8,16},{9,17... | collective-permute-start | bytes 344072 | tf_op jit(solution)/shard_map/ppermute | solution.py:100
  110.5 7.4 %collective-permute-start.26 = (bf16[16,3584]{1,0:T(8,128)(2,1)S(1)}, bf16[16,3584]{1,0:T(8,128)(2,1)S(1)}, u32[]{:S(2)}, u32[]{:S(2)}) collective-permute-start(bf16[16,3584]{1,0:T(8,128)(2,1)S(1)} %get-tuple-element.201), channel_id=1, source_target_pairs={{0,24},{1,25},{2,26},{3,27},{4,28},{5,29},{6,30},{7,31},{8,0},{9,1... | collective-permute-start | bytes 344072 | tf_op jit(solution)/shard_map/ppermute | solution.py:100
  113.0 6.7 %collective-permute-start.25 = (bf16[16,3584]{1,0:T(8,128)(2,1)S(1)}, bf16[16,3584]{1,0:T(8,128)(2,1)S(1)}, u32[]{:S(2)}, u32[]{:S(2)}) collective-permute-start(bf16[16,3584]{1,0:T(8,128)(2,1)S(1)} %get-tuple-element.202), channel_id=1, source_target_pairs={{0,16},{1,17},{2,18},{3,19},{4,20},{5,21},{6,22},{7,23},{8,24},{9,... | collective-permute-start | bytes 344072 | tf_op jit(solution)/shard_map/ppermute | solution.py:100
  119.8 5.2 %collective-permute-start.27 = (bf16[4,3584]{1,0:T(4,128)(2,1)S(1)}, bf16[4,3584]{1,0:T(4,128)(2,1)S(1)}, u32[]{:S(2)}, u32[]{:S(2)}) collective-permute-start(bf16[4,3584]{1,0:T(4,128)(2,1)S(1)} %get-tuple-element.203), channel_id=1, source_target_pairs={{0,32},{1,3},{2,34},{3,5},{4,36},{5,7},{6,38},{7,1},{8,40},{9,11},... | collective-permute-start | bytes 86024 | tf_op jit(solution)/shard_map/ppermute | solution.py:100
  120.7 4.2 %collective-permute-start.29 = (bf16[4,3584]{1,0:T(4,128)(2,1)S(1)}, bf16[4,3584]{1,0:T(4,128)(2,1)S(1)}, u32[]{:S(2)}, u32[]{:S(2)}) collective-permute-start(bf16[4,3584]{1,0:T(4,128)(2,1)S(1)} %get-tuple-element.204), channel_id=1, source_target_pairs={{0,96},{1,7},{2,98},{3,1},{4,100},{5,3},{6,102},{7,5},{8,104},{9,1... | collective-permute-start | bytes 86024 | tf_op jit(solution)/shard_map/ppermute | solution.py:100
  123.1 5.4 %collective-permute-start.28 = (bf16[4,3584]{1,0:T(4,128)(2,1)S(1)}, bf16[4,3584]{1,0:T(4,128)(2,1)S(1)}, u32[]{:S(2)}, u32[]{:S(2)}) collective-permute-start(bf16[4,3584]{1,0:T(4,128)(2,1)S(1)} %get-tuple-element.205), channel_id=1, source_target_pairs={{0,64},{1,5},{2,66},{3,7},{4,68},{5,1},{6,70},{7,3},{8,72},{9,13},... | collective-permute-start | bytes 86024 | tf_op jit(solution)/shard_map/ppermute | solution.py:100

commit v8 on v6

--- a/solution.py
+++ b/solution.py
@@ -170,7 +170,8 @@
     other_stats = local_stats(logits_other, target_other)
     stats = jnp.stack([jnp.concatenate([a, b]) for a, b in zip(own_stats, other_stats)])
 
-    stats = jnp.take(stats, natural_rows(at), axis=1)
+    place = (rows[:, None] == jnp.arange(rows.shape[0], dtype=jnp.int32)[None, :]).astype(jnp.float32)
+    stats = jnp.dot(stats, place, precision=lax.Precision.HIGHEST)
     for stage in ("c", "z", "y", "x"):
         got = exchange(lambda s: stats, stage, n_dev, voc_n)
         peak = jnp.max(got[:, 0], axis=0)
@@ -185,7 +186,7 @@
     own_term = jnp.sum(probs * teacher_logprob, axis=1)
     loss_all = own_term - dotted + total_p * lse
     row_loss = lax.dynamic_slice_in_dim(loss_all, position * tok_dev, tok_dev, 0)
-    back = jnp.take(jnp.stack([lse, total_p], axis=1), rows, axis=0)
+    back = jnp.dot(place, jnp.stack([lse, total_p], axis=1), precision=lax.Precision.HIGHEST)
     lse_arr, total_arr = back[:, 0], back[:, 1]
 
     def half_grad(logits, tgt, lse_h, total_h):

time: 125 us -> 118 us (0.944)
  matrix products: 24.8 us -> 21.8 us
  local copies, waits for them, and re-layouts: 7.31 us -> 4.43 us
    dot_general x1, matrix products: 6.02 us -> 2.53 us  [per_device(): jnp.dot(grad_other, head_weight, preferred_element_type=jnp.float32)]
    gather x2 -> x0, local copies, waits for them, and re-layouts: 2.08 us -> none  [the longest x1 1.04 us: per_device(): stats = jnp.take(stats, natural_rows(at), axis=1)]
  transfers between devices with their start and end apart: 30 -> 30, of which waited for: 21 -> 20; matrix products, arithmetic and copies ran while one was open for 22% -> 23% of each run, Pallas kernels for 0% -> 0%
where the time goes in v8:
time: 118 us
  starting transfers between devices  42.1 us (36%)
  waiting for transfers between devices  33.5 us (28%)
  matrix products  21.8 us (18%)
  other arithmetic  14.3 us (12%)
  local copies, waits for them, and re-layouts  4.43 us (4%)
  between operations  1.69 us (1%)
    ppermute x28, starting transfers between devices, exchange(): lax.ppermute(block_for(shift), AXES, stage_pairs(stage, shift, n_dev, voc...  41.9 us
    ppermute x28, waiting for transfers between devices, exchange(): lax.ppermute(block_for(shift), AXES, stage_pairs(stage, shift, n_dev, voc...  33.5 us
    dot_general x2, matrix products, half_logits(): lax.dot_general(rows_block, head_weight, (((1,), (1,)), ((), ())), prefer...  8.8 us
    dot_general x1, matrix products, per_device(): lax.dot_general(grad, every, (((0,), (0,)), ((), ())), preferred_element_...  6.72 us
    add x1, other arithmetic, compact_target(): target + jnp.where(slot_local[:, j:j + 1] == columns, slot_probs[:, j:j +...  3.57 us
    convert_element_type x2, other arithmetic, half_grad(): (loss_scale * (total_h[:, None] * jnp.exp(logits - lse_h[:, None]) - tgt)...  3.4 us
    dot_general x1, matrix products, per_device(): acc = jnp.dot(grad_own, head_weight, preferred_element_type=jnp.float32)  2.59 us
    dot_general x1, matrix products, per_device(): jnp.dot(grad_other, head_weight, preferred_element_type=jnp.float32)  2.53 us
  transfers between devices with their start and end apart: 30, of which 20 were waited for; matrix products, arithmetic and copies ran while one was open for 23% of the time, Pallas kernels for 0%

profile of v8, /device:TPU:0, one launch (start us, length us, event | category | flops | bytes accessed | tf_op | source)
XLA Modules:
  0.0 117.9 jit_solution(8231977230983391158)
XLA Ops:
  0.6 1.6 %collective-permute-start = (bf16[4,3584]{1,0:T(4,128)(2,1)}, bf16[4,3584]{1,0:T(4,128)(2,1)S(1)}, u32[]{:S(2)}, u32[]{:S(2)}) collective-permute-start(bf16[4,3584]{1,0:T(4,128)(2,1)} %param.8), channel_id=1, source_target_pairs={{0,32},{1,3},{2,34},{3,5},{4,36},{5,7},{6,38},{7,1},{8,40},{9,11},... | collective-permute-start | bytes 86024 | tf_op jit(solution)/shard_map/ppermute | solution.py:100
  2.3 1.7 %collective-permute-start.2 = (bf16[4,3584]{1,0:T(4,128)(2,1)}, bf16[4,3584]{1,0:T(4,128)(2,1)S(1)}, u32[]{:S(2)}, u32[]{:S(2)}) collective-permute-start(bf16[4,3584]{1,0:T(4,128)(2,1)} %param.8), channel_id=1, source_target_pairs={{0,96},{1,7},{2,98},{3,1},{4,100},{5,3},{6,102},{7,5},{8,104},{9,1... | collective-permute-start | bytes 86024 | tf_op jit(solution)/shard_map/ppermute | solution.py:100
  3.9 1.9 %collective-permute-start.1 = (bf16[4,3584]{1,0:T(4,128)(2,1)}, bf16[4,3584]{1,0:T(4,128)(2,1)S(1)}, u32[]{:S(2)}, u32[]{:S(2)}) collective-permute-start(bf16[4,3584]{1,0:T(4,128)(2,1)} %param.8), channel_id=1, source_target_pairs={{0,64},{1,5},{2,66},{3,7},{4,68},{5,1},{6,70},{7,3},{8,72},{9,13},... | collective-permute-start | bytes 86024 | tf_op jit(solution)/shard_map/ppermute | solution.py:100
  6.4 3.2 %collective-permute-done.1 = bf16[4,3584]{1,0:T(4,128)(2,1)S(1)} collective-permute-done((bf16[4,3584]{1,0:T(4,128)(2,1)}, bf16[4,3584]{1,0:T(4,128)(2,1)S(1)}, u32[]{:S(2)}, u32[]{:S(2)}) %collective-permute-start.1) | collective-permute-done | bytes 28704 | tf_op jit(solution)/shard_map/ppermute | solution.py:100
  10.4 3.2 %collective-permute-start.5 = (bf16[16,3584]{1,0:T(8,128)(2,1)S(1)}, bf16[16,3584]{1,0:T(8,128)(2,1)S(1)}, u32[]{:S(2)}, u32[]{:S(2)}) collective-permute-start(bf16[16,3584]{1,0:T(8,128)(2,1)S(1)} %reshape.482), channel_id=1, source_target_pairs={{0,24},{1,25},{2,26},{3,27},{4,28},{5,29},{6,30},{7,31},{8,0},{9,1... | collective-permute-start | bytes 344072 | tf_op jit(solution)/shard_map/ppermute | solution.py:100
  14.2 1.0 collective-permute-start.3
  15.2 1.0 copy.45
  16.3 1.0 gather_fusion.2
  17.9 2.5 %collective-permute-done.4 = bf16[16,3584]{1,0:T(8,128)(2,1)S(1)} collective-permute-done((bf16[16,3584]{1,0:T(8,128)(2,1)S(1)}, bf16[16,3584]{1,0:T(8,128)(2,1)S(1)}, u32[]{:S(2)}, u32[]{:S(2)}) %collective-permute-start.4) | collective-permute-done | bytes 114720 | tf_op jit(solution)/shard_map/ppermute | solution.py:100
  20.4 1.2 collective-permute-done.3
  21.7 3.6 %collective-permute-start.8 = (bf16[64,3584]{1,0:T(8,128)(2,1)S(1)}, bf16[64,3584]{1,0:T(8,128)(2,1)S(1)}, u32[]{:S(2)}, u32[]{:S(2)}) collective-permute-start(bf16[64,3584]{1,0:T(8,128)(2,1)S(1)} %bitcast.146), channel_id=1, source_target_pairs={{0,6},{1,97},{2,0},{3,99},{4,2},{5,101},{6,4},{7,103},{8,14},{9,10... | collective-permute-start | bytes 1376264 | tf_op jit(solution)/shard_map/ppermute | solution.py:100
  25.3 1.3 %collective-permute-start.6 = (bf16[64,3584]{1,0:T(8,128)(2,1)S(1)}, bf16[64,3584]{1,0:T(8,128)(2,1)S(1)}, u32[]{:S(2)}, u32[]{:S(2)}) collective-permute-start(bf16[64,3584]{1,0:T(8,128)(2,1)S(1)} %bitcast.148), channel_id=1, source_target_pairs={{0,2},{1,33},{2,4},{3,35},{4,6},{5,37},{6,0},{7,39},{8,10},{9,41},... | collective-permute-start | bytes 1376264 | tf_op jit(solution)/shard_map/ppermute | solution.py:100
  28.1 5.8 %conditional.1 = (f32[512,1152]{1,0:T(8,128)}) conditional(s32[]{:T(128)} %convert_element_type.48, (s32[512,64]{1,0:T(8,128)S(1)}, pred[512]{0:T(512)(128)(4,1)S(1)}, f32[512,64]{0,1:T(8,128)S(1)}, s32[512,1]{0,1:T(1,128)S(1)}) %tuple.102, (s32[512,64]{1,0:T(8,128)S(1)}, pred[512]{0:T(512)(128)(4,1)S(1)}, f32[512,64]{0,1:T(8,128)S(1)}, ...), branch_computations={%region_3.7_spmd, %region_7.11_spmd} | conditional | flops 17916928 | bytes 5218828 | solution.py:44
  28.9 1.0 gather_fusion
  30.4 3.6 %select_add_fusion = f32[512,1152]{1,0:T(8,128)} fusion(f32[512]{0:T(512)S(1)} %bitcast.190, s32[512]{0:T(512)S(1)} %bitcast.182, f32[512]{0:T(512)S(1)} %bitcast.191, s32[512]{0:T(512)S(1)} %bitcast.183, f32[512]{0:T(512)S(1)} %bitcast.192, s32[512]{0:T(512)S(1)} %bitcast.184, f32[512]{0:T(512)S(1)} %bitcast.193, s32[512]{0:T(512)S(1)} %bitcast.185, ...), kind=kLoop, calls=%fused_computation.4 | loop fusion | flops 13565952 | bytes 2392064 | tf_op jit(solution)/shard_map/cond/branch_0_fun/add | solution.py:37
  33.9 2.3 %collective-permute-done.8 = bf16[64,3584]{1,0:T(8,128)(2,1)S(1)} collective-permute-done((bf16[64,3584]{1,0:T(8,128)(2,1)S(1)}, bf16[64,3584]{1,0:T(8,128)(2,1)S(1)}, u32[]{:S(2)}, u32[]{:S(2)}) %collective-permute-start.8) | collective-permute-done | bytes 458784 | tf_op jit(solution)/shard_map/ppermute | solution.py:100
  36.2 3.7 %collective-permute-done.6 = bf16[64,3584]{1,0:T(8,128)(2,1)S(1)} collective-permute-done((bf16[64,3584]{1,0:T(8,128)(2,1)S(1)}, bf16[64,3584]{1,0:T(8,128)(2,1)S(1)}, u32[]{:S(2)}, u32[]{:S(2)}) %collective-permute-start.6) | collective-permute-done | bytes 458784 | tf_op jit(solution)/shard_map/ppermute | solution.py:100
  40.3 6.2 %fusion.95 = (f32[256]{0:T(256)S(1)}, f32[256,1152]{1,0:T(8,128)S(1)}) fusion(bf16[256,3584]{1,0:T(8,128)(2,1)S(1)} %bitcast.151, bf16[1152,3584]{1,0:T(8,128)(2,1)} %param.9), kind=kOutput, calls=%fused_computation.241 | convolution fusion | flops 2114223872 | bytes 11273216 | tf_op jit(solution)/shard_map/dot_general | solution.py:133
  46.5 2.6 %fusion.94 = (f32[256]{0:T(256)S(1)}, f32[256,1152]{1,0:T(8,128)S(1)}) fusion(bf16[256,3584]{1,0:T(8,128)(2,1)S(1)} %collective-permute-done.9, bf16[1152,3584]{1,0:T(8,128)(2,1)S(1)} %bitcast.220), kind=kOutput, calls=%fused_computation.240 | convolution fusion | flops 2114223872 | bytes 11273216 | tf_op jit(solution)/shard_map/dot_general | solution.py:133
  49.1 2.3 %multiply_reduce_fusion.1 = (f32[256]{0:T(256)S(1)}, f32[256]{0:T(256)S(1)}, f32[256]{0:T(256)S(1)}, f32[256]{0:T(256)S(1)}) fusion(f32[256,1152]{1,0:T(8,128)S(1)} %get-tuple-element.94, f32[512,1152]{1,0:T(8,128)} %get-tuple-element.256, f32[256,1152]{1,0:T(8,128)S(1)} %get-tuple-element.211, f32[256]{0:T(256)S(1)} %get-tuple-element.210, ...), kind=kLoop, calls=%fused_computation.42 | loop fusion | flops 2358272 | bytes 4724736 | tf_op jit(solution)/shard_map/reduce_sum | solution.py:167
  53.8 1.5 %collective-permute-start.11 = (f32[3,512]{1,0:T(4,128)S(1)}, f32[3,512]{1,0:T(4,128)S(1)}, u32[]{:S(2)}, u32[]{:S(2)}) collective-permute-start(f32[3,512]{1,0:T(4,128)S(1)} %get-tuple-element.205), channel_id=1, source_target_pairs={{0,2},{1,3},{2,4},{3,5},{4,6},{5,7},{6,0},{7,1},{8,10},{9,11},{10,... | collective-permute-start | bytes 18440 | tf_op jit(solution)/shard_map/ppermute | solution.py:100
  55.3 1.8 %collective-permute-start.13 = (f32[3,512]{1,0:T(4,128)S(1)}, f32[3,512]{1,0:T(4,128)S(1)}, u32[]{:S(2)}, u32[]{:S(2)}) collective-permute-start(f32[3,512]{1,0:T(4,128)S(1)} %get-tuple-element.205), channel_id=1, source_target_pairs={{0,6},{1,7},{2,0},{3,1},{4,2},{5,3},{6,4},{7,5},{8,14},{9,15},{10,... | collective-permute-start | bytes 18440 | tf_op jit(solution)/shard_map/ppermute | solution.py:100
  57.1 1.7 %collective-permute-done.12 = f32[3,512]{1,0:T(4,128)S(1)} collective-permute-done((f32[3,512]{1,0:T(4,128)S(1)}, f32[3,512]{1,0:T(4,128)S(1)}, u32[]{:S(2)}, u32[]{:S(2)}) %collective-permute-start.12) | collective-permute-done | bytes 6176 | tf_op jit(solution)/shard_map/ppermute | solution.py:100
  59.1 0.9 collective-permute-start.15
  60.6 2.6 %collective-permute-start.16 = (f32[3,512]{1,0:T(4,128)S(1)}, f32[3,512]{1,0:T(4,128)S(1)}, u32[]{:S(2)}, u32[]{:S(2)}) collective-permute-start(f32[3,512]{1,0:T(4,128)S(1)} %get-tuple-element.203), channel_id=1, source_target_pairs={{0,24},{1,25},{2,26},{3,27},{4,28},{5,29},{6,30},{7,31},{8,0},{9,1... | collective-permute-start | bytes 18440 | tf_op jit(solution)/shard_map/ppermute | solution.py:100
  63.2 1.1 collective-permute-done.15
  64.9 1.9 %collective-permute-start.18 = (f32[3,512]{1,0:T(4,128)S(1)}, f32[3,512]{1,0:T(4,128)S(1)}, u32[]{:S(2)}, u32[]{:S(2)}) collective-permute-start(f32[3,512]{1,0:T(4,128)S(1)} %get-tuple-element.201), channel_id=1, source_target_pairs={{0,64},{1,65},{2,66},{3,67},{4,68},{5,69},{6,70},{7,71},{8,72},{9,... | collective-permute-start | bytes 18440 | tf_op jit(solution)/shard_map/ppermute | solution.py:100
  67.4 2.6 %collective-permute-start.19 = (f32[3,512]{1,0:T(4,128)S(1)}, f32[3,512]{1,0:T(4,128)S(1)}, u32[]{:S(2)}, u32[]{:S(2)}) collective-permute-start(f32[3,512]{1,0:T(4,128)S(1)} %get-tuple-element.201), channel_id=1, source_target_pairs={{0,96},{1,97},{2,98},{3,99},{4,100},{5,101},{6,102},{7,103},{8,104... | collective-permute-start | bytes 18440 | tf_op jit(solution)/shard_map/ppermute | solution.py:100
  70.2 1.5 %collective-permute-done.17 = f32[3,512]{1,0:T(4,128)S(1)} collective-permute-done((f32[3,512]{1,0:T(4,128)S(1)}, f32[3,512]{1,0:T(4,128)S(1)}, u32[]{:S(2)}, u32[]{:S(2)}) %collective-permute-start.17) | collective-permute-done | bytes 6176 | tf_op jit(solution)/shard_map/ppermute | solution.py:100
  72.5 1.8 %multiply_convert_fusion.1 = bf16[256,1152]{1,0:T(8,128)(2,1)S(1)} fusion(f32[256,1152]{1,0:T(8,128)S(1)} %get-tuple-element.211, f32[512,1152]{1,0:T(8,128)} %get-tuple-element.256, f32[256]{0:T(256)S(1)} %bitcast.213, f32[256]{0:T(256)S(1)} %bitcast.214), kind=kLoop, calls=%fused_computation.40 | loop fusion | flops 1474560 | bytes 2951168 | tf_op jit(solution)/shard_map/convert_element_type | solution.py:193
  74.3 2.5 %convolution_convert_fusion.1 = bf16[256,3584]{1,0:T(8,128)(2,1)S(1)} fusion(bf16[256,1152]{1,0:T(8,128)(2,1)S(1)} %multiply_convert_fusion.1, bf16[1152,3584]{1,0:T(8,128)(2,1)S(1)} %bitcast.220), kind=kOutput, calls=%fused_computation.29 | convolution fusion | flops 2114846720 | bytes 10682368 | tf_op jit(solution)/shard_map/dot_general | solution.py:199
  76.9 1.6 %multiply_convert_fusion = bf16[256,1152]{1,0:T(8,128)(2,1)S(1)} fusion(f32[256,1152]{1,0:T(8,128)S(1)} %get-tuple-element.94, f32[512,1152]{1,0:T(8,128)} %get-tuple-element.256, f32[256]{0:T(256)S(1)} %bitcast.212, f32[256]{0:T(256)S(1)} %bitcast.211), kind=kLoop, calls=%fused_computation.39 | loop fusion | flops 1474560 | bytes 2951168 | tf_op jit(solution)/shard_map/convert_element_type | solution.py:193
  78.6 2.6 %fusion.96 = f32[256,3584]{1,0:T(8,128)S(1)} fusion(bf16[256,1152]{1,0:T(8,128)(2,1)S(1)} %multiply_convert_fusion, bf16[1152,3584]{1,0:T(8,128)(2,1)S(1)} %bitcast.222), kind=kOutput, calls=%fused_computation.242 | convolution fusion | flops 2113929216 | bytes 12517376 | tf_op jit(solution)/shard_map/dot_general | solution.py:203
  82.0 1.8 %collective-permute-start.21 = (bf16[64,3584]{1,0:T(8,128)(2,1)S(1)}, bf16[64,3584]{1,0:T(8,128)(2,1)S(1)}, u32[]{:S(2)}, u32[]{:S(2)}) collective-permute-start(bf16[64,3584]{1,0:T(8,128)(2,1)S(1)} %get-tuple-element.189), channel_id=1, source_target_pairs={{0,2},{1,33},{2,4},{3,35},{4,6},{5,37},{6,0},{7,39},{8,10},{9,41},... | collective-permute-start | bytes 1376264 | tf_op jit(solution)/shard_map/ppermute | solution.py:100
  83.8 1.5 %collective-permute-start.23 = (bf16[64,3584]{1,0:T(8,128)(2,1)S(1)}, bf16[64,3584]{1,0:T(8,128)(2,1)S(1)}, u32[]{:S(2)}, u32[]{:S(2)}) collective-permute-start(bf16[64,3584]{1,0:T(8,128)(2,1)S(1)} %get-tuple-element.190), channel_id=1, source_target_pairs={{0,6},{1,97},{2,0},{3,99},{4,2},{5,101},{6,4},{7,103},{8,14},{9,10... | collective-permute-start | bytes 1376264 | tf_op jit(solution)/shard_map/ppermute | solution.py:100
  85.3 1.2 %collective-permute-start.22 = (bf16[64,3584]{1,0:T(8,128)(2,1)S(1)}, bf16[64,3584]{1,0:T(8,128)(2,1)S(1)}, u32[]{:S(2)}, u32[]{:S(2)}) collective-permute-start(bf16[64,3584]{1,0:T(8,128)(2,1)S(1)} %get-tuple-element.191), channel_id=1, source_target_pairs={{0,4},{1,65},{2,6},{3,67},{4,0},{5,69},{6,2},{7,71},{8,12},{9,73},... | collective-permute-start | bytes 1376264 | tf_op jit(solution)/shard_map/ppermute | solution.py:100
  86.5 6.7 %convolution_convert_fusion = bf16[1152,3584]{1,0:T(8,128)(2,1)} fusion(bf16[256,3584]{1,0:T(8,128)(2,1)S(1)} %collective-permute-done.9, bf16[256,3584]{1,0:T(8,128)(2,1)S(1)} %bitcast.152, bf16[256,1152]{1,0:T(8,128)(2,1)S(1)} %multiply_convert_fusion.1, bf16[256,1152]{1,0:T(8,128)(2,1)S(1)} %multiply_convert_fusion), kind=kOutput, calls=%fused_computation.28 | convolution fusion | flops 4241686528 | bytes 13107200 | tf_op jit(solution)/shard_map/dot_general | solution.py:207
  93.2 4.6 %collective-permute-done.22 = bf16[64,3584]{1,0:T(8,128)(2,1)S(1)} collective-permute-done((bf16[64,3584]{1,0:T(8,128)(2,1)S(1)}, bf16[64,3584]{1,0:T(8,128)(2,1)S(1)}, u32[]{:S(2)}, u32[]{:S(2)}) %collective-permute-start.22) | collective-permute-done | bytes 458784 | tf_op jit(solution)/shard_map/ppermute | solution.py:100
  98.3 1.5 %collective-permute-start.24 = (bf16[16,3584]{1,0:T(8,128)(2,1)S(1)}, bf16[16,3584]{1,0:T(8,128)(2,1)S(1)}, u32[]{:S(2)}, u32[]{:S(2)}) collective-permute-start(bf16[16,3584]{1,0:T(8,128)(2,1)S(1)} %get-tuple-element.192), channel_id=1, source_target_pairs={{0,8},{1,9},{2,10},{3,11},{4,12},{5,13},{6,14},{7,15},{8,16},{9,17... | collective-permute-start | bytes 344072 | tf_op jit(solution)/shard_map/ppermute | solution.py:100
  99.8 1.8 %collective-permute-start.26 = (bf16[16,3584]{1,0:T(8,128)(2,1)S(1)}, bf16[16,3584]{1,0:T(8,128)(2,1)S(1)}, u32[]{:S(2)}, u32[]{:S(2)}) collective-permute-start(bf16[16,3584]{1,0:T(8,128)(2,1)S(1)} %get-tuple-element.193), channel_id=1, source_target_pairs={{0,24},{1,25},{2,26},{3,27},{4,28},{5,29},{6,30},{7,31},{8,0},{9,1... | collective-permute-start | bytes 344072 | tf_op jit(solution)/shard_map/ppermute | solution.py:100
  101.6 1.4 %collective-permute-start.25 = (bf16[16,3584]{1,0:T(8,128)(2,1)S(1)}, bf16[16,3584]{1,0:T(8,128)(2,1)S(1)}, u32[]{:S(2)}, u32[]{:S(2)}) collective-permute-start(bf16[16,3584]{1,0:T(8,128)(2,1)S(1)} %get-tuple-element.194), channel_id=1, source_target_pairs={{0,16},{1,17},{2,18},{3,19},{4,20},{5,21},{6,22},{7,23},{8,24},{9,... | collective-permute-start | bytes 344072 | tf_op jit(solution)/shard_map/ppermute | solution.py:100
  103.0 1.7 %collective-permute-done.24 = bf16[16,3584]{1,0:T(8,128)(2,1)S(1)} collective-permute-done((bf16[16,3584]{1,0:T(8,128)(2,1)S(1)}, bf16[16,3584]{1,0:T(8,128)(2,1)S(1)}, u32[]{:S(2)}, u32[]{:S(2)}) %collective-permute-start.24) | collective-permute-done | bytes 114720 | tf_op jit(solution)/shard_map/ppermute | solution.py:100
  104.7 1.8 %collective-permute-done.26 = bf16[16,3584]{1,0:T(8,128)(2,1)S(1)} collective-permute-done((bf16[16,3584]{1,0:T(8,128)(2,1)S(1)}, bf16[16,3584]{1,0:T(8,128)(2,1)S(1)}, u32[]{:S(2)}, u32[]{:S(2)}) %collective-permute-start.26) | collective-permute-done | bytes 114720 | tf_op jit(solution)/shard_map/ppermute | solution.py:100
  106.6 1.8 %collective-permute-done.25 = bf16[16,3584]{1,0:T(8,128)(2,1)S(1)} collective-permute-done((bf16[16,3584]{1,0:T(8,128)(2,1)S(1)}, bf16[16,3584]{1,0:T(8,128)(2,1)S(1)}, u32[]{:S(2)}, u32[]{:S(2)}) %collective-permute-start.25) | collective-permute-done | bytes 114720 | tf_op jit(solution)/shard_map/ppermute | solution.py:100
  108.5 0.9 collective-permute-start.27
  109.4 2.4 %collective-permute-start.29 = (bf16[4,3584]{1,0:T(4,128)(2,1)S(1)}, bf16[4,3584]{1,0:T(4,128)(2,1)S(1)}, u32[]{:S(2)}, u32[]{:S(2)}) collective-permute-start(bf16[4,3584]{1,0:T(4,128)(2,1)S(1)} %get-tuple-element.196), channel_id=1, source_target_pairs={{0,96},{1,7},{2,98},{3,1},{4,100},{5,3},{6,102},{7,5},{8,104},{9,1... | collective-permute-start | bytes 86024 | tf_op jit(solution)/shard_map/ppermute | solution.py:100
  111.8 1.0 collective-permute-start.28
  113.6 3.5 %collective-permute-done.28 = bf16[4,3584]{1,0:T(4,128)(2,1)S(1)} collective-permute-done((bf16[4,3584]{1,0:T(4,128)(2,1)S(1)}, bf16[4,3584]{1,0:T(4,128)(2,1)S(1)}, u32[]{:S(2)}, u32[]{:S(2)}) %collective-permute-start.28) | collective-permute-done | bytes 28704 | tf_op jit(solution)/shard_map/ppermute | solution.py:100
  (105 shorter events, 13.4 us)
Async XLA Ops:
  0.6 5.4 %collective-permute-start = (bf16[4,3584]{1,0:T(4,128)(2,1)}, bf16[4,3584]{1,0:T(4,128)(2,1)S(1)}, u32[]{:S(2)}, u32[]{:S(2)}) collective-permute-start(bf16[4,3584]{1,0:T(4,128)(2,1)} %param.8), channel_id=1, source_target_pairs={{0,32},{1,3},{2,34},{3,5},{4,36},{5,7},{6,38},{7,1},{8,40},{9,11},... | collective-permute-start | bytes 86024 | tf_op jit(solution)/shard_map/ppermute | solution.py:100
  2.3 4.1 %collective-permute-start.2 = (bf16[4,3584]{1,0:T(4,128)(2,1)}, bf16[4,3584]{1,0:T(4,128)(2,1)S(1)}, u32[]{:S(2)}, u32[]{:S(2)}) collective-permute-start(bf16[4,3584]{1,0:T(4,128)(2,1)} %param.8), channel_id=1, source_target_pairs={{0,96},{1,7},{2,98},{3,1},{4,100},{5,3},{6,102},{7,5},{8,104},{9,1... | collective-permute-start | bytes 86024 | tf_op jit(solution)/shard_map/ppermute | solution.py:100
  3.9 5.6 %collective-permute-start.1 = (bf16[4,3584]{1,0:T(4,128)(2,1)}, bf16[4,3584]{1,0:T(4,128)(2,1)S(1)}, u32[]{:S(2)}, u32[]{:S(2)}) collective-permute-start(bf16[4,3584]{1,0:T(4,128)(2,1)} %param.8), channel_id=1, source_target_pairs={{0,64},{1,5},{2,66},{3,7},{4,68},{5,1},{6,70},{7,3},{8,72},{9,13},... | collective-permute-start | bytes 86024 | tf_op jit(solution)/shard_map/ppermute | solution.py:100
  10.4 17.7 %copy-start = (f32[512,64]{0,1:T(8,128)S(1)}, f32[512,64]{0,1:T(8,128)}, u32[]{:S(2)}) copy-start(f32[512,64]{0,1:T(8,128)} %param.11) | copy-start | bytes 393220
  10.4 7.5 %collective-permute-start.5 = (bf16[16,3584]{1,0:T(8,128)(2,1)S(1)}, bf16[16,3584]{1,0:T(8,128)(2,1)S(1)}, u32[]{:S(2)}, u32[]{:S(2)}) collective-permute-start(bf16[16,3584]{1,0:T(8,128)(2,1)S(1)} %reshape.482), channel_id=1, source_target_pairs={{0,24},{1,25},{2,26},{3,27},{4,28},{5,29},{6,30},{7,31},{8,0},{9,1... | collective-permute-start | bytes 344072 | tf_op jit(solution)/shard_map/ppermute | solution.py:100
  13.6 6.9 %collective-permute-start.4 = (bf16[16,3584]{1,0:T(8,128)(2,1)S(1)}, bf16[16,3584]{1,0:T(8,128)(2,1)S(1)}, u32[]{:S(2)}, u32[]{:S(2)}) collective-permute-start(bf16[16,3584]{1,0:T(8,128)(2,1)S(1)} %reshape.482), channel_id=1, source_target_pairs={{0,16},{1,17},{2,18},{3,19},{4,20},{5,21},{6,22},{7,23},{8,24},{9,... | collective-permute-start | bytes 344072 | tf_op jit(solution)/shard_map/ppermute | solution.py:100
  14.2 7.4 %collective-permute-start.3 = (bf16[16,3584]{1,0:T(8,128)(2,1)S(1)}, bf16[16,3584]{1,0:T(8,128)(2,1)S(1)}, u32[]{:S(2)}, u32[]{:S(2)}) collective-permute-start(bf16[16,3584]{1,0:T(8,128)(2,1)S(1)} %reshape.482), channel_id=1, source_target_pairs={{0,8},{1,9},{2,10},{3,11},{4,12},{5,13},{6,14},{7,15},{8,16},{9,17... | collective-permute-start | bytes 344072 | tf_op jit(solution)/shard_map/ppermute | solution.py:100
  21.7 14.5 %collective-permute-start.8 = (bf16[64,3584]{1,0:T(8,128)(2,1)S(1)}, bf16[64,3584]{1,0:T(8,128)(2,1)S(1)}, u32[]{:S(2)}, u32[]{:S(2)}) collective-permute-start(bf16[64,3584]{1,0:T(8,128)(2,1)S(1)} %bitcast.146), channel_id=1, source_target_pairs={{0,6},{1,97},{2,0},{3,99},{4,2},{5,101},{6,4},{7,103},{8,14},{9,10... | collective-permute-start | bytes 1376264 | tf_op jit(solution)/shard_map/ppermute | solution.py:100
  25.3 10.9 %collective-permute-start.7 = (bf16[64,3584]{1,0:T(8,128)(2,1)S(1)}, bf16[64,3584]{1,0:T(8,128)(2,1)S(1)}, u32[]{:S(2)}, u32[]{:S(2)}) collective-permute-start(bf16[64,3584]{1,0:T(8,128)(2,1)S(1)} %bitcast.147), channel_id=1, source_target_pairs={{0,4},{1,65},{2,6},{3,67},{4,0},{5,69},{6,2},{7,71},{8,12},{9,73},... | collective-permute-start | bytes 1376264 | tf_op jit(solution)/shard_map/ppermute | solution.py:100
  25.3 14.6 %collective-permute-start.6 = (bf16[64,3584]{1,0:T(8,128)(2,1)S(1)}, bf16[64,3584]{1,0:T(8,128)(2,1)S(1)}, u32[]{:S(2)}, u32[]{:S(2)}) collective-permute-start(bf16[64,3584]{1,0:T(8,128)(2,1)S(1)} %bitcast.148), channel_id=1, source_target_pairs={{0,2},{1,33},{2,4},{3,35},{4,6},{5,37},{6,0},{7,39},{8,10},{9,41},... | collective-permute-start | bytes 1376264 | tf_op jit(solution)/shard_map/ppermute | solution.py:100
  39.9 6.5 %slice-start = ((s8[8257536]{0:T(1024)(128)(4,1)}), s8[4194304]{0:T(1024)(128)(4,1)S(1)}, s32[]{:S(2)}) async-start(s8[8257536]{0:T(1024)(128)(4,1)} %bitcast.219), calls=%async_computation | async-start | bytes 8388608
  40.1 6.3 %collective-permute-start.9 = (bf16[256,3584]{1,0:T(8,128)(2,1)S(1)}, bf16[256,3584]{1,0:T(8,128)(2,1)S(1)}, u32[]{:S(2)}, u32[]{:S(2)}) collective-permute-start(bf16[256,3584]{1,0:T(8,128)(2,1)S(1)} %bitcast.150), channel_id=1, source_target_pairs={{0,1},{1,0},{2,3},{3,2},{4,5},{5,4},{6,7},{7,6},{8,9},{9,8},{10,11... | collective-permute-start | bytes 5505032 | tf_op jit(solution)/shard_map/ppermute | solution.py:158
  40.2 6.2 %slice-start.1 = ((s8[8257536]{0:T(1024)(128)(4,1)}), s8[4063232]{0:T(1024)(128)(4,1)S(1)}, s32[]{:S(2)}) async-start(s8[8257536]{0:T(1024)(128)(4,1)} %bitcast.219), calls=%async_computation.1 | async-start | bytes 8126464
  51.9 1.5 %collective-permute-start.10 = (f32[3,512]{1,0:T(4,128)S(1)}, f32[3,512]{1,0:T(4,128)S(1)}, u32[]{:S(2)}, u32[]{:S(2)}) collective-permute-start(f32[3,512]{1,0:T(4,128)S(1)} %fusion.10), channel_id=1, source_target_pairs={{0,1},{1,0},{2,3},{3,2},{4,5},{5,4},{6,7},{7,6},{8,9},{9,8},{10,11... | collective-permute-start | bytes 18440 | tf_op jit(solution)/shard_map/ppermute | solution.py:100
  53.5 5.3 %collective-permute-start.12 = (f32[3,512]{1,0:T(4,128)S(1)}, f32[3,512]{1,0:T(4,128)S(1)}, u32[]{:S(2)}, u32[]{:S(2)}) collective-permute-start(f32[3,512]{1,0:T(4,128)S(1)} %get-tuple-element.205), channel_id=1, source_target_pairs={{0,4},{1,5},{2,6},{3,7},{4,0},{5,1},{6,2},{7,3},{8,12},{9,13},{10,... | collective-permute-start | bytes 18440 | tf_op jit(solution)/shard_map/ppermute | solution.py:100
  53.8 5.0 %collective-permute-start.11 = (f32[3,512]{1,0:T(4,128)S(1)}, f32[3,512]{1,0:T(4,128)S(1)}, u32[]{:S(2)}, u32[]{:S(2)}) collective-permute-start(f32[3,512]{1,0:T(4,128)S(1)} %get-tuple-element.205), channel_id=1, source_target_pairs={{0,2},{1,3},{2,4},{3,5},{4,6},{5,7},{6,0},{7,1},{8,10},{9,11},{10,... | collective-permute-start | bytes 18440 | tf_op jit(solution)/shard_map/ppermute | solution.py:100
  55.3 3.7 %collective-permute-start.13 = (f32[3,512]{1,0:T(4,128)S(1)}, f32[3,512]{1,0:T(4,128)S(1)}, u32[]{:S(2)}, u32[]{:S(2)}) collective-permute-start(f32[3,512]{1,0:T(4,128)S(1)} %get-tuple-element.205), channel_id=1, source_target_pairs={{0,6},{1,7},{2,0},{3,1},{4,2},{5,3},{6,4},{7,5},{8,14},{9,15},{10,... | collective-permute-start | bytes 18440 | tf_op jit(solution)/shard_map/ppermute | solution.py:100
  59.1 5.2 %collective-permute-start.15 = (f32[3,512]{1,0:T(4,128)S(1)}, f32[3,512]{1,0:T(4,128)S(1)}, u32[]{:S(2)}, u32[]{:S(2)}) collective-permute-start(f32[3,512]{1,0:T(4,128)S(1)} %get-tuple-element.203), channel_id=1, source_target_pairs={{0,16},{1,17},{2,18},{3,19},{4,20},{5,21},{6,22},{7,23},{8,24},{9,... | collective-permute-start | bytes 18440 | tf_op jit(solution)/shard_map/ppermute | solution.py:100
  59.9 4.9 %collective-permute-start.14 = (f32[3,512]{1,0:T(4,128)S(1)}, f32[3,512]{1,0:T(4,128)S(1)}, u32[]{:S(2)}, u32[]{:S(2)}) collective-permute-start(f32[3,512]{1,0:T(4,128)S(1)} %get-tuple-element.203), channel_id=1, source_target_pairs={{0,8},{1,9},{2,10},{3,11},{4,12},{5,13},{6,14},{7,15},{8,16},{9,17... | collective-permute-start | bytes 18440 | tf_op jit(solution)/shard_map/ppermute | solution.py:100
  60.6 4.2 %collective-permute-start.16 = (f32[3,512]{1,0:T(4,128)S(1)}, f32[3,512]{1,0:T(4,128)S(1)}, u32[]{:S(2)}, u32[]{:S(2)}) collective-permute-start(f32[3,512]{1,0:T(4,128)S(1)} %get-tuple-element.203), channel_id=1, source_target_pairs={{0,24},{1,25},{2,26},{3,27},{4,28},{5,29},{6,30},{7,31},{8,0},{9,1... | collective-permute-start | bytes 18440 | tf_op jit(solution)/shard_map/ppermute | solution.py:100
  64.9 5.2 %collective-permute-start.18 = (f32[3,512]{1,0:T(4,128)S(1)}, f32[3,512]{1,0:T(4,128)S(1)}, u32[]{:S(2)}, u32[]{:S(2)}) collective-permute-start(f32[3,512]{1,0:T(4,128)S(1)} %get-tuple-element.201), channel_id=1, source_target_pairs={{0,64},{1,65},{2,66},{3,67},{4,68},{5,69},{6,70},{7,71},{8,72},{9,... | collective-permute-start | bytes 18440 | tf_op jit(solution)/shard_map/ppermute | solution.py:100
  66.8 4.9 %collective-permute-start.17 = (f32[3,512]{1,0:T(4,128)S(1)}, f32[3,512]{1,0:T(4,128)S(1)}, u32[]{:S(2)}, u32[]{:S(2)}) collective-permute-start(f32[3,512]{1,0:T(4,128)S(1)} %get-tuple-element.201), channel_id=1, source_target_pairs={{0,32},{1,33},{2,34},{3,35},{4,36},{5,37},{6,38},{7,39},{8,40},{9,... | collective-permute-start | bytes 18440 | tf_op jit(solution)/shard_map/ppermute | solution.py:100
  67.4 4.3 %collective-permute-start.19 = (f32[3,512]{1,0:T(4,128)S(1)}, f32[3,512]{1,0:T(4,128)S(1)}, u32[]{:S(2)}, u32[]{:S(2)}) collective-permute-start(f32[3,512]{1,0:T(4,128)S(1)} %get-tuple-element.201), channel_id=1, source_target_pairs={{0,96},{1,97},{2,98},{3,99},{4,100},{5,101},{6,102},{7,103},{8,104... | collective-permute-start | bytes 18440 | tf_op jit(solution)/shard_map/ppermute | solution.py:100
  72.5 6.1 %slice-start.2 = ((s8[8257536]{0:T(1024)(128)(4,1)}), s8[4063232]{0:T(1024)(128)(4,1)S(1)}, s32[]{:S(2)}) async-start(s8[8257536]{0:T(1024)(128)(4,1)} %bitcast.221), calls=%async_computation.2 | async-start | bytes 8126464
  74.3 4.3 %slice-start.3 = ((s8[8257536]{0:T(1024)(128)(4,1)}), s8[4194304]{0:T(1024)(128)(4,1)S(1)}, s32[]{:S(2)}) async-start(s8[8257536]{0:T(1024)(128)(4,1)} %bitcast.221), calls=%async_computation.3 | async-start | bytes 8388608
  76.8 4.4 %collective-permute-start.20 = (bf16[256,3584]{1,0:T(8,128)(2,1)S(1)}, bf16[256,3584]{1,0:T(8,128)(2,1)S(1)}, u32[]{:S(2)}, u32[]{:S(2)}) collective-permute-start(bf16[256,3584]{1,0:T(8,128)(2,1)S(1)} %convolution_convert_fusion.1), channel_id=1, source_target_pairs={{0,1},{1,0},{2,3},{3,2},{4,5},{5,4},{6,7},{7,6},{8,9},{9,8},{10,11... | collective-permute-start | bytes 5505032 | tf_op jit(solution)/shard_map/ppermute | solution.py:200
  82.0 11.2 %collective-permute-start.21 = (bf16[64,3584]{1,0:T(8,128)(2,1)S(1)}, bf16[64,3584]{1,0:T(8,128)(2,1)S(1)}, u32[]{:S(2)}, u32[]{:S(2)}) collective-permute-start(bf16[64,3584]{1,0:T(8,128)(2,1)S(1)} %get-tuple-element.189), channel_id=1, source_target_pairs={{0,2},{1,33},{2,4},{3,35},{4,6},{5,37},{6,0},{7,39},{8,10},{9,41},... | collective-permute-start | bytes 1376264 | tf_op jit(solution)/shard_map/ppermute | solution.py:100
  83.8 9.4 %collective-permute-start.23 = (bf16[64,3584]{1,0:T(8,128)(2,1)S(1)}, bf16[64,3584]{1,0:T(8,128)(2,1)S(1)}, u32[]{:S(2)}, u32[]{:S(2)}) collective-permute-start(bf16[64,3584]{1,0:T(8,128)(2,1)S(1)} %get-tuple-element.190), channel_id=1, source_target_pairs={{0,6},{1,97},{2,0},{3,99},{4,2},{5,101},{6,4},{7,103},{8,14},{9,10... | collective-permute-start | bytes 1376264 | tf_op jit(solution)/shard_map/ppermute | solution.py:100
  85.3 12.6 %collective-permute-start.22 = (bf16[64,3584]{1,0:T(8,128)(2,1)S(1)}, bf16[64,3584]{1,0:T(8,128)(2,1)S(1)}, u32[]{:S(2)}, u32[]{:S(2)}) collective-permute-start(bf16[64,3584]{1,0:T(8,128)(2,1)S(1)} %get-tuple-element.191), channel_id=1, source_target_pairs={{0,4},{1,65},{2,6},{3,67},{4,0},{5,69},{6,2},{7,71},{8,12},{9,73},... | collective-permute-start | bytes 1376264 | tf_op jit(solution)/shard_map/ppermute | solution.py:100
  98.3 6.5 %collective-permute-start.24 = (bf16[16,3584]{1,0:T(8,128)(2,1)S(1)}, bf16[16,3584]{1,0:T(8,128)(2,1)S(1)}, u32[]{:S(2)}, u32[]{:S(2)}) collective-permute-start(bf16[16,3584]{1,0:T(8,128)(2,1)S(1)} %get-tuple-element.192), channel_id=1, source_target_pairs={{0,8},{1,9},{2,10},{3,11},{4,12},{5,13},{6,14},{7,15},{8,16},{9,17... | collective-permute-start | bytes 344072 | tf_op jit(solution)/shard_map/ppermute | solution.py:100
  99.8 6.8 %collective-permute-start.26 = (bf16[16,3584]{1,0:T(8,128)(2,1)S(1)}, bf16[16,3584]{1,0:T(8,128)(2,1)S(1)}, u32[]{:S(2)}, u32[]{:S(2)}) collective-permute-start(bf16[16,3584]{1,0:T(8,128)(2,1)S(1)} %get-tuple-element.193), channel_id=1, source_target_pairs={{0,24},{1,25},{2,26},{3,27},{4,28},{5,29},{6,30},{7,31},{8,0},{9,1... | collective-permute-start | bytes 344072 | tf_op jit(solution)/shard_map/ppermute | solution.py:100
  101.6 6.7 %collective-permute-start.25 = (bf16[16,3584]{1,0:T(8,128)(2,1)S(1)}, bf16[16,3584]{1,0:T(8,128)(2,1)S(1)}, u32[]{:S(2)}, u32[]{:S(2)}) collective-permute-start(bf16[16,3584]{1,0:T(8,128)(2,1)S(1)} %get-tuple-element.194), channel_id=1, source_target_pairs={{0,16},{1,17},{2,18},{3,19},{4,20},{5,21},{6,22},{7,23},{8,24},{9,... | collective-permute-start | bytes 344072 | tf_op jit(solution)/shard_map/ppermute | solution.py:100
  108.5 5.2 %collective-permute-start.27 = (bf16[4,3584]{1,0:T(4,128)(2,1)S(1)}, bf16[4,3584]{1,0:T(4,128)(2,1)S(1)}, u32[]{:S(2)}, u32[]{:S(2)}) collective-permute-start(bf16[4,3584]{1,0:T(4,128)(2,1)S(1)} %get-tuple-element.195), channel_id=1, source_target_pairs={{0,32},{1,3},{2,34},{3,5},{4,36},{5,7},{6,38},{7,1},{8,40},{9,11},... | collective-permute-start | bytes 86024 | tf_op jit(solution)/shard_map/ppermute | solution.py:100
  109.4 4.2 %collective-permute-start.29 = (bf16[4,3584]{1,0:T(4,128)(2,1)S(1)}, bf16[4,3584]{1,0:T(4,128)(2,1)S(1)}, u32[]{:S(2)}, u32[]{:S(2)}) collective-permute-start(bf16[4,3584]{1,0:T(4,128)(2,1)S(1)} %get-tuple-element.196), channel_id=1, source_target_pairs={{0,96},{1,7},{2,98},{3,1},{4,100},{5,3},{6,102},{7,5},{8,104},{9,1... | collective-permute-start | bytes 86024 | tf_op jit(solution)/shard_map/ppermute | solution.py:100
  111.8 5.4 %collective-permute-start.28 = (bf16[4,3584]{1,0:T(4,128)(2,1)S(1)}, bf16[4,3584]{1,0:T(4,128)(2,1)S(1)}, u32[]{:S(2)}, u32[]{:S(2)}) collective-permute-start(bf16[4,3584]{1,0:T(4,128)(2,1)S(1)} %get-tuple-element.197), channel_id=1, source_target_pairs={{0,64},{1,5},{2,66},{3,7},{4,68},{5,1},{6,70},{7,3},{8,72},{9,13},... | collective-permute-start | bytes 86024 | tf_op jit(solution)/shard_map/ppermute | solution.py:100

commit v9 on v8

--- a/solution.py
+++ b/solution.py
@@ -68,11 +68,11 @@
 
 def ring_axis(stage, core):
     if stage == "r1":
+        return "y"
+    if stage == "r2":
         return "x" if core == 0 else "z"
     if stage == "r3":
         return "z" if core == 0 else "x"
-    if stage == "r2":
-        return "y"
     return stage
 
 
@@ -108,10 +108,10 @@
     s_r2 = (r // 16) % RING
     s_r3 = (r // 64) % RING
     c = at["c"] ^ (r // 256)
-    s_x = jnp.where(c == 0, s_r1, s_r3)
-    s_z = jnp.where(c == 0, s_r3, s_r1)
+    s_x = jnp.where(c == 0, s_r2, s_r3)
+    s_z = jnp.where(c == 0, s_r3, s_r2)
     x = (at["x"] - s_x) % RING
-    y = (at["y"] - s_r2) % RING
+    y = (at["y"] - s_r1) % RING
     z = (at["z"] - s_z) % RING
     return (((x * RING + y) * RING + z) * 2 + c) * 4 + i
 
@@ -124,9 +124,9 @@
     s_z = (at["z"] - (t // 8) % RING) % RING
     s_y = (at["y"] - (t // 32) % RING) % RING
     s_x = (at["x"] - (t // 128) % RING) % RING
-    s_r1 = jnp.where(c == 0, s_x, s_z)
+    s_r2 = jnp.where(c == 0, s_x, s_z)
     s_r3 = jnp.where(c == 0, s_z, s_x)
-    return (((s_c * RING + s_r3) * RING + s_y) * RING + s_r1) * 4 + i
+    return (((s_c * RING + s_r3) * RING + s_r2) * RING + s_y) * 4 + i
 
 
 def half_logits(rows_block, head_weight):

time: 118 us -> 118 us (level)
  waiting for transfers between devices: 33.5 us -> 31.9 us
    ppermute x28, waiting for transfers between devices: 33.5 us -> 31.9 us  [exchange(): lax.ppermute(block_for(shift), AXES, stage_pairs(stage, shift, n_dev, voc...]
  transfers between devices with their start and end apart: 30 -> 30, of which waited for: 20 -> 18; matrix products, arithmetic and copies ran while one was open for 23% -> 23% of each run, Pallas kernels for 0% -> 0%
where the time goes in v9:
time: 118 us; the launch traced here: 117 us
  starting transfers between devices  43.2 us (37%)
  waiting for transfers between devices  31.9 us (27%)
  matrix products  21.8 us (18%)
  other arithmetic  14.3 us (12%)
  local copies, waits for them, and re-layouts  4.43 us (4%)
  between operations  1.69 us (1%)
    ppermute x28, starting transfers between devices, exchange(): lax.ppermute(block_for(shift), AXES, stage_pairs(stage, shift, n_dev, voc...  43 us
    ppermute x28, waiting for transfers between devices, exchange(): lax.ppermute(block_for(shift), AXES, stage_pairs(stage, shift, n_dev, voc...  31.9 us
    dot_general x2, matrix products, half_logits(): lax.dot_general(rows_block, head_weight, (((1,), (1,)), ((), ())), prefer...  8.8 us
    dot_general x1, matrix products, per_device(): lax.dot_general(grad, every, (((0,), (0,)), ((), ())), preferred_element_...  6.72 us
    add x1, other arithmetic, compact_target(): target + jnp.where(slot_local[:, j:j + 1] == columns, slot_probs[:, j:j +...  3.57 us
    convert_element_type x2, other arithmetic, half_grad(): (loss_scale * (total_h[:, None] * jnp.exp(logits - lse_h[:, None]) - tgt)...  3.4 us
    dot_general x1, matrix products, per_device(): acc = jnp.dot(grad_own, head_weight, preferred_element_type=jnp.float32)  2.59 us
    dot_general x1, matrix products, per_device(): jnp.dot(grad_other, head_weight, preferred_element_type=jnp.float32)  2.53 us
  transfers between devices with their start and end apart: 30, of which 18 were waited for; matrix products, arithmetic and copies ran while one was open for 23% of the time, Pallas kernels for 0%

profile of v9, /device:TPU:0, one launch (start us, length us, event | category | flops | bytes accessed | tf_op | source)
XLA Modules:
  0.0 117.4 jit_solution(6054991903893877325)
XLA Ops:
  0.6 1.7 %collective-permute-start = (bf16[4,3584]{1,0:T(4,128)(2,1)}, bf16[4,3584]{1,0:T(4,128)(2,1)S(1)}, u32[]{:S(2)}, u32[]{:S(2)}) collective-permute-start(bf16[4,3584]{1,0:T(4,128)(2,1)} %param.8), channel_id=1, source_target_pairs={{0,8},{1,9},{2,10},{3,11},{4,12},{5,13},{6,14},{7,15},{8,16},{9,17... | collective-permute-start | bytes 86024 | tf_op jit(solution)/shard_map/ppermute | solution.py:100
  2.4 1.6 %collective-permute-start.2 = (bf16[4,3584]{1,0:T(4,128)(2,1)}, bf16[4,3584]{1,0:T(4,128)(2,1)S(1)}, u32[]{:S(2)}, u32[]{:S(2)}) collective-permute-start(bf16[4,3584]{1,0:T(4,128)(2,1)} %param.8), channel_id=1, source_target_pairs={{0,24},{1,25},{2,26},{3,27},{4,28},{5,29},{6,30},{7,31},{8,0},{9,1... | collective-permute-start | bytes 86024 | tf_op jit(solution)/shard_map/ppermute | solution.py:100
  3.9 2.1 %collective-permute-start.1 = (bf16[4,3584]{1,0:T(4,128)(2,1)}, bf16[4,3584]{1,0:T(4,128)(2,1)S(1)}, u32[]{:S(2)}, u32[]{:S(2)}) collective-permute-start(bf16[4,3584]{1,0:T(4,128)(2,1)} %param.8), channel_id=1, source_target_pairs={{0,16},{1,17},{2,18},{3,19},{4,20},{5,21},{6,22},{7,23},{8,24},{9,... | collective-permute-start | bytes 86024 | tf_op jit(solution)/shard_map/ppermute | solution.py:100
  6.4 3.1 %collective-permute-done.1 = bf16[4,3584]{1,0:T(4,128)(2,1)S(1)} collective-permute-done((bf16[4,3584]{1,0:T(4,128)(2,1)}, bf16[4,3584]{1,0:T(4,128)(2,1)S(1)}, u32[]{:S(2)}, u32[]{:S(2)}) %collective-permute-start.1) | collective-permute-done | bytes 28704 | tf_op jit(solution)/shard_map/ppermute | solution.py:100
  9.5 0.8 pad_maximum_fusion.2
  10.4 2.9 %collective-permute-start.5 = (bf16[16,3584]{1,0:T(8,128)(2,1)S(1)}, bf16[16,3584]{1,0:T(8,128)(2,1)S(1)}, u32[]{:S(2)}, u32[]{:S(2)}) collective-permute-start(bf16[16,3584]{1,0:T(8,128)(2,1)S(1)} %reshape.482), channel_id=1, source_target_pairs={{0,96},{1,7},{2,98},{3,1},{4,100},{5,3},{6,102},{7,5},{8,104},{9,1... | collective-permute-start | bytes 344072 | tf_op jit(solution)/shard_map/ppermute | solution.py:100
  14.1 0.9 collective-permute-start.3
  15.1 1.0 copy.45
  16.1 1.0 gather_fusion.2
  17.2 2.5 %collective-permute-done.4 = bf16[16,3584]{1,0:T(8,128)(2,1)S(1)} collective-permute-done((bf16[16,3584]{1,0:T(8,128)(2,1)S(1)}, bf16[16,3584]{1,0:T(8,128)(2,1)S(1)}, u32[]{:S(2)}, u32[]{:S(2)}) %collective-permute-start.4) | collective-permute-done | bytes 114720 | tf_op jit(solution)/shard_map/ppermute | solution.py:100
  19.7 1.2 collective-permute-done.3
  20.9 4.1 %collective-permute-start.8 = (bf16[64,3584]{1,0:T(8,128)(2,1)S(1)}, bf16[64,3584]{1,0:T(8,128)(2,1)S(1)}, u32[]{:S(2)}, u32[]{:S(2)}) collective-permute-start(bf16[64,3584]{1,0:T(8,128)(2,1)S(1)} %bitcast.146), channel_id=1, source_target_pairs={{0,6},{1,97},{2,0},{3,99},{4,2},{5,101},{6,4},{7,103},{8,14},{9,10... | collective-permute-start | bytes 1376264 | tf_op jit(solution)/shard_map/ppermute | solution.py:100
  25.0 1.3 %collective-permute-start.6 = (bf16[64,3584]{1,0:T(8,128)(2,1)S(1)}, bf16[64,3584]{1,0:T(8,128)(2,1)S(1)}, u32[]{:S(2)}, u32[]{:S(2)}) collective-permute-start(bf16[64,3584]{1,0:T(8,128)(2,1)S(1)} %bitcast.148), channel_id=1, source_target_pairs={{0,2},{1,33},{2,4},{3,35},{4,6},{5,37},{6,0},{7,39},{8,10},{9,41},... | collective-permute-start | bytes 1376264 | tf_op jit(solution)/shard_map/ppermute | solution.py:100
  27.9 5.8 %conditional.1 = (f32[512,1152]{1,0:T(8,128)}) conditional(s32[]{:T(128)} %convert_element_type.48, (s32[512,64]{1,0:T(8,128)S(1)}, pred[512]{0:T(512)(128)(4,1)S(1)}, f32[512,64]{0,1:T(8,128)S(1)}, s32[512,1]{0,1:T(1,128)S(1)}) %tuple.102, (s32[512,64]{1,0:T(8,128)S(1)}, pred[512]{0:T(512)(128)(4,1)S(1)}, f32[512,64]{0,1:T(8,128)S(1)}, ...), branch_computations={%region_3.7_spmd, %region_7.11_spmd} | conditional | flops 17916928 | bytes 5218828 | solution.py:44
  28.6 1.0 gather_fusion
  30.1 3.6 %select_add_fusion = f32[512,1152]{1,0:T(8,128)} fusion(f32[512]{0:T(512)S(1)} %bitcast.190, s32[512]{0:T(512)S(1)} %bitcast.182, f32[512]{0:T(512)S(1)} %bitcast.191, s32[512]{0:T(512)S(1)} %bitcast.183, f32[512]{0:T(512)S(1)} %bitcast.192, s32[512]{0:T(512)S(1)} %bitcast.184, f32[512]{0:T(512)S(1)} %bitcast.193, s32[512]{0:T(512)S(1)} %bitcast.185, ...), kind=kLoop, calls=%fused_computation.4 | loop fusion | flops 13565952 | bytes 2392064 | tf_op jit(solution)/shard_map/cond/branch_0_fun/add | solution.py:37
  33.7 2.3 %collective-permute-done.8 = bf16[64,3584]{1,0:T(8,128)(2,1)S(1)} collective-permute-done((bf16[64,3584]{1,0:T(8,128)(2,1)S(1)}, bf16[64,3584]{1,0:T(8,128)(2,1)S(1)}, u32[]{:S(2)}, u32[]{:S(2)}) %collective-permute-start.8) | collective-permute-done | bytes 458784 | tf_op jit(solution)/shard_map/ppermute | solution.py:100
  35.9 3.7 %collective-permute-done.6 = bf16[64,3584]{1,0:T(8,128)(2,1)S(1)} collective-permute-done((bf16[64,3584]{1,0:T(8,128)(2,1)S(1)}, bf16[64,3584]{1,0:T(8,128)(2,1)S(1)}, u32[]{:S(2)}, u32[]{:S(2)}) %collective-permute-start.6) | collective-permute-done | bytes 458784 | tf_op jit(solution)/shard_map/ppermute | solution.py:100
  40.0 6.2 %fusion.95 = (f32[256]{0:T(256)S(1)}, f32[256,1152]{1,0:T(8,128)S(1)}) fusion(bf16[256,3584]{1,0:T(8,128)(2,1)S(1)} %bitcast.151, bf16[1152,3584]{1,0:T(8,128)(2,1)} %param.9), kind=kOutput, calls=%fused_computation.241 | convolution fusion | flops 2114223872 | bytes 11273216 | tf_op jit(solution)/shard_map/dot_general | solution.py:133
  46.2 2.6 %fusion.94 = (f32[256]{0:T(256)S(1)}, f32[256,1152]{1,0:T(8,128)S(1)}) fusion(bf16[256,3584]{1,0:T(8,128)(2,1)S(1)} %collective-permute-done.9, bf16[1152,3584]{1,0:T(8,128)(2,1)S(1)} %bitcast.220), kind=kOutput, calls=%fused_computation.240 | convolution fusion | flops 2114223872 | bytes 11273216 | tf_op jit(solution)/shard_map/dot_general | solution.py:133
  48.9 2.3 %multiply_reduce_fusion.1 = (f32[256]{0:T(256)S(1)}, f32[256]{0:T(256)S(1)}, f32[256]{0:T(256)S(1)}, f32[256]{0:T(256)S(1)}) fusion(f32[256,1152]{1,0:T(8,128)S(1)} %get-tuple-element.94, f32[512,1152]{1,0:T(8,128)} %get-tuple-element.256, f32[256,1152]{1,0:T(8,128)S(1)} %get-tuple-element.211, f32[256]{0:T(256)S(1)} %get-tuple-element.210, ...), kind=kLoop, calls=%fused_computation.42 | loop fusion | flops 2358272 | bytes 4724736 | tf_op jit(solution)/shard_map/reduce_sum | solution.py:167
  52.3 0.8 collective-permute-done.10
  53.6 1.5 %collective-permute-start.11 = (f32[3,512]{1,0:T(4,128)S(1)}, f32[3,512]{1,0:T(4,128)S(1)}, u32[]{:S(2)}, u32[]{:S(2)}) collective-permute-start(f32[3,512]{1,0:T(4,128)S(1)} %get-tuple-element.205), channel_id=1, source_target_pairs={{0,2},{1,3},{2,4},{3,5},{4,6},{5,7},{6,0},{7,1},{8,10},{9,11},{10,... | collective-permute-start | bytes 18440 | tf_op jit(solution)/shard_map/ppermute | solution.py:100
  55.1 1.8 %collective-permute-start.13 = (f32[3,512]{1,0:T(4,128)S(1)}, f32[3,512]{1,0:T(4,128)S(1)}, u32[]{:S(2)}, u32[]{:S(2)}) collective-permute-start(f32[3,512]{1,0:T(4,128)S(1)} %get-tuple-element.205), channel_id=1, source_target_pairs={{0,6},{1,7},{2,0},{3,1},{4,2},{5,3},{6,4},{7,5},{8,14},{9,15},{10,... | collective-permute-start | bytes 18440 | tf_op jit(solution)/shard_map/ppermute | solution.py:100
  56.8 1.6 %collective-permute-done.12 = f32[3,512]{1,0:T(4,128)S(1)} collective-permute-done((f32[3,512]{1,0:T(4,128)S(1)}, f32[3,512]{1,0:T(4,128)S(1)}, u32[]{:S(2)}, u32[]{:S(2)}) %collective-permute-start.12) | collective-permute-done | bytes 6176 | tf_op jit(solution)/shard_map/ppermute | solution.py:100
  58.8 2.1 %collective-permute-start.15 = (f32[3,512]{1,0:T(4,128)S(1)}, f32[3,512]{1,0:T(4,128)S(1)}, u32[]{:S(2)}, u32[]{:S(2)}) collective-permute-start(f32[3,512]{1,0:T(4,128)S(1)} %get-tuple-element.203), channel_id=1, source_target_pairs={{0,16},{1,17},{2,18},{3,19},{4,20},{5,21},{6,22},{7,23},{8,24},{9,... | collective-permute-start | bytes 18440 | tf_op jit(solution)/shard_map/ppermute | solution.py:100
  61.6 2.6 %collective-permute-start.16 = (f32[3,512]{1,0:T(4,128)S(1)}, f32[3,512]{1,0:T(4,128)S(1)}, u32[]{:S(2)}, u32[]{:S(2)}) collective-permute-start(f32[3,512]{1,0:T(4,128)S(1)} %get-tuple-element.203), channel_id=1, source_target_pairs={{0,24},{1,25},{2,26},{3,27},{4,28},{5,29},{6,30},{7,31},{8,0},{9,1... | collective-permute-start | bytes 18440 | tf_op jit(solution)/shard_map/ppermute | solution.py:100
  64.1 1.6 %collective-permute-done.14 = f32[3,512]{1,0:T(4,128)S(1)} collective-permute-done((f32[3,512]{1,0:T(4,128)S(1)}, f32[3,512]{1,0:T(4,128)S(1)}, u32[]{:S(2)}, u32[]{:S(2)}) %collective-permute-start.14) | collective-permute-done | bytes 6176 | tf_op jit(solution)/shard_map/ppermute | solution.py:100
  65.9 0.9 collective-permute-start.18
  67.4 2.6 %collective-permute-start.19 = (f32[3,512]{1,0:T(4,128)S(1)}, f32[3,512]{1,0:T(4,128)S(1)}, u32[]{:S(2)}, u32[]{:S(2)}) collective-permute-start(f32[3,512]{1,0:T(4,128)S(1)} %get-tuple-element.201), channel_id=1, source_target_pairs={{0,96},{1,97},{2,98},{3,99},{4,100},{5,101},{6,102},{7,103},{8,104... | collective-permute-start | bytes 18440 | tf_op jit(solution)/shard_map/ppermute | solution.py:100
  70.0 1.1 collective-permute-done.18
  72.4 1.8 %multiply_convert_fusion.1 = bf16[256,1152]{1,0:T(8,128)(2,1)S(1)} fusion(f32[256,1152]{1,0:T(8,128)S(1)} %get-tuple-element.211, f32[512,1152]{1,0:T(8,128)} %get-tuple-element.256, f32[256]{0:T(256)S(1)} %bitcast.213, f32[256]{0:T(256)S(1)} %bitcast.214), kind=kLoop, calls=%fused_computation.40 | loop fusion | flops 1474560 | bytes 2951168 | tf_op jit(solution)/shard_map/convert_element_type | solution.py:193
  74.2 2.5 %convolution_convert_fusion.1 = bf16[256,3584]{1,0:T(8,128)(2,1)S(1)} fusion(bf16[256,1152]{1,0:T(8,128)(2,1)S(1)} %multiply_convert_fusion.1, bf16[1152,3584]{1,0:T(8,128)(2,1)S(1)} %bitcast.220), kind=kOutput, calls=%fused_computation.29 | convolution fusion | flops 2114846720 | bytes 10682368 | tf_op jit(solution)/shard_map/dot_general | solution.py:199
  76.8 1.6 %multiply_convert_fusion = bf16[256,1152]{1,0:T(8,128)(2,1)S(1)} fusion(f32[256,1152]{1,0:T(8,128)S(1)} %get-tuple-element.94, f32[512,1152]{1,0:T(8,128)} %get-tuple-element.256, f32[256]{0:T(256)S(1)} %bitcast.212, f32[256]{0:T(256)S(1)} %bitcast.211), kind=kLoop, calls=%fused_computation.39 | loop fusion | flops 1474560 | bytes 2951168 | tf_op jit(solution)/shard_map/convert_element_type | solution.py:193
  78.5 2.6 %fusion.96 = f32[256,3584]{1,0:T(8,128)S(1)} fusion(bf16[256,1152]{1,0:T(8,128)(2,1)S(1)} %multiply_convert_fusion, bf16[1152,3584]{1,0:T(8,128)(2,1)S(1)} %bitcast.222), kind=kOutput, calls=%fused_computation.242 | convolution fusion | flops 2113929216 | bytes 12517376 | tf_op jit(solution)/shard_map/dot_general | solution.py:203
  81.9 1.8 %collective-permute-start.21 = (bf16[64,3584]{1,0:T(8,128)(2,1)S(1)}, bf16[64,3584]{1,0:T(8,128)(2,1)S(1)}, u32[]{:S(2)}, u32[]{:S(2)}) collective-permute-start(bf16[64,3584]{1,0:T(8,128)(2,1)S(1)} %get-tuple-element.189), channel_id=1, source_target_pairs={{0,2},{1,33},{2,4},{3,35},{4,6},{5,37},{6,0},{7,39},{8,10},{9,41},... | collective-permute-start | bytes 1376264 | tf_op jit(solution)/shard_map/ppermute | solution.py:100
  83.7 1.5 %collective-permute-start.23 = (bf16[64,3584]{1,0:T(8,128)(2,1)S(1)}, bf16[64,3584]{1,0:T(8,128)(2,1)S(1)}, u32[]{:S(2)}, u32[]{:S(2)}) collective-permute-start(bf16[64,3584]{1,0:T(8,128)(2,1)S(1)} %get-tuple-element.190), channel_id=1, source_target_pairs={{0,6},{1,97},{2,0},{3,99},{4,2},{5,101},{6,4},{7,103},{8,14},{9,10... | collective-permute-start | bytes 1376264 | tf_op jit(solution)/shard_map/ppermute | solution.py:100
  85.2 1.2 %collective-permute-start.22 = (bf16[64,3584]{1,0:T(8,128)(2,1)S(1)}, bf16[64,3584]{1,0:T(8,128)(2,1)S(1)}, u32[]{:S(2)}, u32[]{:S(2)}) collective-permute-start(bf16[64,3584]{1,0:T(8,128)(2,1)S(1)} %get-tuple-element.191), channel_id=1, source_target_pairs={{0,4},{1,65},{2,6},{3,67},{4,0},{5,69},{6,2},{7,71},{8,12},{9,73},... | collective-permute-start | bytes 1376264 | tf_op jit(solution)/shard_map/ppermute | solution.py:100
  86.4 6.7 %convolution_convert_fusion = bf16[1152,3584]{1,0:T(8,128)(2,1)} fusion(bf16[256,3584]{1,0:T(8,128)(2,1)S(1)} %collective-permute-done.9, bf16[256,3584]{1,0:T(8,128)(2,1)S(1)} %bitcast.152, bf16[256,1152]{1,0:T(8,128)(2,1)S(1)} %multiply_convert_fusion.1, bf16[256,1152]{1,0:T(8,128)(2,1)S(1)} %multiply_convert_fusion), kind=kOutput, calls=%fused_computation.28 | convolution fusion | flops 4241686528 | bytes 13107200 | tf_op jit(solution)/shard_map/dot_general | solution.py:207
  93.1 4.6 %collective-permute-done.22 = bf16[64,3584]{1,0:T(8,128)(2,1)S(1)} collective-permute-done((bf16[64,3584]{1,0:T(8,128)(2,1)S(1)}, bf16[64,3584]{1,0:T(8,128)(2,1)S(1)}, u32[]{:S(2)}, u32[]{:S(2)}) %collective-permute-start.22) | collective-permute-done | bytes 458784 | tf_op jit(solution)/shard_map/ppermute | solution.py:100
  98.2 1.5 %collective-permute-start.24 = (bf16[16,3584]{1,0:T(8,128)(2,1)S(1)}, bf16[16,3584]{1,0:T(8,128)(2,1)S(1)}, u32[]{:S(2)}, u32[]{:S(2)}) collective-permute-start(bf16[16,3584]{1,0:T(8,128)(2,1)S(1)} %get-tuple-element.192), channel_id=1, source_target_pairs={{0,32},{1,3},{2,34},{3,5},{4,36},{5,7},{6,38},{7,1},{8,40},{9,11},... | collective-permute-start | bytes 344072 | tf_op jit(solution)/shard_map/ppermute | solution.py:100
  99.7 1.8 %collective-permute-start.26 = (bf16[16,3584]{1,0:T(8,128)(2,1)S(1)}, bf16[16,3584]{1,0:T(8,128)(2,1)S(1)}, u32[]{:S(2)}, u32[]{:S(2)}) collective-permute-start(bf16[16,3584]{1,0:T(8,128)(2,1)S(1)} %get-tuple-element.193), channel_id=1, source_target_pairs={{0,96},{1,7},{2,98},{3,1},{4,100},{5,3},{6,102},{7,5},{8,104},{9,1... | collective-permute-start | bytes 344072 | tf_op jit(solution)/shard_map/ppermute | solution.py:100
  101.6 1.4 %collective-permute-start.25 = (bf16[16,3584]{1,0:T(8,128)(2,1)S(1)}, bf16[16,3584]{1,0:T(8,128)(2,1)S(1)}, u32[]{:S(2)}, u32[]{:S(2)}) collective-permute-start(bf16[16,3584]{1,0:T(8,128)(2,1)S(1)} %get-tuple-element.194), channel_id=1, source_target_pairs={{0,64},{1,5},{2,66},{3,7},{4,68},{5,1},{6,70},{7,3},{8,72},{9,13},... | collective-permute-start | bytes 344072 | tf_op jit(solution)/shard_map/ppermute | solution.py:100
  102.9 1.3 %collective-permute-done.24 = bf16[16,3584]{1,0:T(8,128)(2,1)S(1)} collective-permute-done((bf16[16,3584]{1,0:T(8,128)(2,1)S(1)}, bf16[16,3584]{1,0:T(8,128)(2,1)S(1)}, u32[]{:S(2)}, u32[]{:S(2)}) %collective-permute-start.24) | collective-permute-done | bytes 114720 | tf_op jit(solution)/shard_map/ppermute | solution.py:100
  104.5 3.3 %collective-permute-done.25 = bf16[16,3584]{1,0:T(8,128)(2,1)S(1)} collective-permute-done((bf16[16,3584]{1,0:T(8,128)(2,1)S(1)}, bf16[16,3584]{1,0:T(8,128)(2,1)S(1)}, u32[]{:S(2)}, u32[]{:S(2)}) %collective-permute-start.25) | collective-permute-done | bytes 114720 | tf_op jit(solution)/shard_map/ppermute | solution.py:100
  108.3 3.0 %collective-permute-start.29 = (bf16[4,3584]{1,0:T(4,128)(2,1)S(1)}, bf16[4,3584]{1,0:T(4,128)(2,1)S(1)}, u32[]{:S(2)}, u32[]{:S(2)}) collective-permute-start(bf16[4,3584]{1,0:T(4,128)(2,1)S(1)} %get-tuple-element.196), channel_id=1, source_target_pairs={{0,24},{1,25},{2,26},{3,27},{4,28},{5,29},{6,30},{7,31},{8,0},{9,1... | collective-permute-start | bytes 86024 | tf_op jit(solution)/shard_map/ppermute | solution.py:100
  111.3 1.4 %collective-permute-start.28 = (bf16[4,3584]{1,0:T(4,128)(2,1)S(1)}, bf16[4,3584]{1,0:T(4,128)(2,1)S(1)}, u32[]{:S(2)}, u32[]{:S(2)}) collective-permute-start(bf16[4,3584]{1,0:T(4,128)(2,1)S(1)} %get-tuple-element.197), channel_id=1, source_target_pairs={{0,16},{1,17},{2,18},{3,19},{4,20},{5,21},{6,22},{7,23},{8,24},{9,... | collective-permute-start | bytes 86024 | tf_op jit(solution)/shard_map/ppermute | solution.py:100
  113.3 3.4 %collective-permute-done.28 = bf16[4,3584]{1,0:T(4,128)(2,1)S(1)} collective-permute-done((bf16[4,3584]{1,0:T(4,128)(2,1)S(1)}, bf16[4,3584]{1,0:T(4,128)(2,1)S(1)}, u32[]{:S(2)}, u32[]{:S(2)}) %collective-permute-start.28) | collective-permute-done | bytes 28704 | tf_op jit(solution)/shard_map/ppermute | solution.py:100
  (105 shorter events, 11.7 us)
Async XLA Ops:
  0.6 5.4 %collective-permute-start = (bf16[4,3584]{1,0:T(4,128)(2,1)}, bf16[4,3584]{1,0:T(4,128)(2,1)S(1)}, u32[]{:S(2)}, u32[]{:S(2)}) collective-permute-start(bf16[4,3584]{1,0:T(4,128)(2,1)} %param.8), channel_id=1, source_target_pairs={{0,8},{1,9},{2,10},{3,11},{4,12},{5,13},{6,14},{7,15},{8,16},{9,17... | collective-permute-start | bytes 86024 | tf_op jit(solution)/shard_map/ppermute | solution.py:100
  2.4 4.1 %collective-permute-start.2 = (bf16[4,3584]{1,0:T(4,128)(2,1)}, bf16[4,3584]{1,0:T(4,128)(2,1)S(1)}, u32[]{:S(2)}, u32[]{:S(2)}) collective-permute-start(bf16[4,3584]{1,0:T(4,128)(2,1)} %param.8), channel_id=1, source_target_pairs={{0,24},{1,25},{2,26},{3,27},{4,28},{5,29},{6,30},{7,31},{8,0},{9,1... | collective-permute-start | bytes 86024 | tf_op jit(solution)/shard_map/ppermute | solution.py:100
  3.9 5.6 %collective-permute-start.1 = (bf16[4,3584]{1,0:T(4,128)(2,1)}, bf16[4,3584]{1,0:T(4,128)(2,1)S(1)}, u32[]{:S(2)}, u32[]{:S(2)}) collective-permute-start(bf16[4,3584]{1,0:T(4,128)(2,1)} %param.8), channel_id=1, source_target_pairs={{0,16},{1,17},{2,18},{3,19},{4,20},{5,21},{6,22},{7,23},{8,24},{9,... | collective-permute-start | bytes 86024 | tf_op jit(solution)/shard_map/ppermute | solution.py:100
  10.4 17.5 %copy-start = (f32[512,64]{0,1:T(8,128)S(1)}, f32[512,64]{0,1:T(8,128)}, u32[]{:S(2)}) copy-start(f32[512,64]{0,1:T(8,128)} %param.11) | copy-start | bytes 393220
  10.4 6.8 %collective-permute-start.5 = (bf16[16,3584]{1,0:T(8,128)(2,1)S(1)}, bf16[16,3584]{1,0:T(8,128)(2,1)S(1)}, u32[]{:S(2)}, u32[]{:S(2)}) collective-permute-start(bf16[16,3584]{1,0:T(8,128)(2,1)S(1)} %reshape.482), channel_id=1, source_target_pairs={{0,96},{1,7},{2,98},{3,1},{4,100},{5,3},{6,102},{7,5},{8,104},{9,1... | collective-permute-start | bytes 344072 | tf_op jit(solution)/shard_map/ppermute | solution.py:100
  13.3 6.4 %collective-permute-start.4 = (bf16[16,3584]{1,0:T(8,128)(2,1)S(1)}, bf16[16,3584]{1,0:T(8,128)(2,1)S(1)}, u32[]{:S(2)}, u32[]{:S(2)}) collective-permute-start(bf16[16,3584]{1,0:T(8,128)(2,1)S(1)} %reshape.482), channel_id=1, source_target_pairs={{0,64},{1,5},{2,66},{3,7},{4,68},{5,1},{6,70},{7,3},{8,72},{9,13},... | collective-permute-start | bytes 344072 | tf_op jit(solution)/shard_map/ppermute | solution.py:100
  14.1 6.7 %collective-permute-start.3 = (bf16[16,3584]{1,0:T(8,128)(2,1)S(1)}, bf16[16,3584]{1,0:T(8,128)(2,1)S(1)}, u32[]{:S(2)}, u32[]{:S(2)}) collective-permute-start(bf16[16,3584]{1,0:T(8,128)(2,1)S(1)} %reshape.482), channel_id=1, source_target_pairs={{0,32},{1,3},{2,34},{3,5},{4,36},{5,7},{6,38},{7,1},{8,40},{9,11},... | collective-permute-start | bytes 344072 | tf_op jit(solution)/shard_map/ppermute | solution.py:100
  20.9 15.0 %collective-permute-start.8 = (bf16[64,3584]{1,0:T(8,128)(2,1)S(1)}, bf16[64,3584]{1,0:T(8,128)(2,1)S(1)}, u32[]{:S(2)}, u32[]{:S(2)}) collective-permute-start(bf16[64,3584]{1,0:T(8,128)(2,1)S(1)} %bitcast.146), channel_id=1, source_target_pairs={{0,6},{1,97},{2,0},{3,99},{4,2},{5,101},{6,4},{7,103},{8,14},{9,10... | collective-permute-start | bytes 1376264 | tf_op jit(solution)/shard_map/ppermute | solution.py:100
  25.0 10.9 %collective-permute-start.7 = (bf16[64,3584]{1,0:T(8,128)(2,1)S(1)}, bf16[64,3584]{1,0:T(8,128)(2,1)S(1)}, u32[]{:S(2)}, u32[]{:S(2)}) collective-permute-start(bf16[64,3584]{1,0:T(8,128)(2,1)S(1)} %bitcast.147), channel_id=1, source_target_pairs={{0,4},{1,65},{2,6},{3,67},{4,0},{5,69},{6,2},{7,71},{8,12},{9,73},... | collective-permute-start | bytes 1376264 | tf_op jit(solution)/shard_map/ppermute | solution.py:100
  25.0 14.6 %collective-permute-start.6 = (bf16[64,3584]{1,0:T(8,128)(2,1)S(1)}, bf16[64,3584]{1,0:T(8,128)(2,1)S(1)}, u32[]{:S(2)}, u32[]{:S(2)}) collective-permute-start(bf16[64,3584]{1,0:T(8,128)(2,1)S(1)} %bitcast.148), channel_id=1, source_target_pairs={{0,2},{1,33},{2,4},{3,35},{4,6},{5,37},{6,0},{7,39},{8,10},{9,41},... | collective-permute-start | bytes 1376264 | tf_op jit(solution)/shard_map/ppermute | solution.py:100
  39.6 6.5 %slice-start = ((s8[8257536]{0:T(1024)(128)(4,1)}), s8[4194304]{0:T(1024)(128)(4,1)S(1)}, s32[]{:S(2)}) async-start(s8[8257536]{0:T(1024)(128)(4,1)} %bitcast.219), calls=%async_computation | async-start | bytes 8388608
  39.9 6.3 %collective-permute-start.9 = (bf16[256,3584]{1,0:T(8,128)(2,1)S(1)}, bf16[256,3584]{1,0:T(8,128)(2,1)S(1)}, u32[]{:S(2)}, u32[]{:S(2)}) collective-permute-start(bf16[256,3584]{1,0:T(8,128)(2,1)S(1)} %bitcast.150), channel_id=1, source_target_pairs={{0,1},{1,0},{2,3},{3,2},{4,5},{5,4},{6,7},{7,6},{8,9},{9,8},{10,11... | collective-permute-start | bytes 5505032 | tf_op jit(solution)/shard_map/ppermute | solution.py:158
  40.0 6.2 %slice-start.1 = ((s8[8257536]{0:T(1024)(128)(4,1)}), s8[4063232]{0:T(1024)(128)(4,1)S(1)}, s32[]{:S(2)}) async-start(s8[8257536]{0:T(1024)(128)(4,1)} %bitcast.219), calls=%async_computation.1 | async-start | bytes 8126464
  51.7 1.5 %collective-permute-start.10 = (f32[3,512]{1,0:T(4,128)S(1)}, f32[3,512]{1,0:T(4,128)S(1)}, u32[]{:S(2)}, u32[]{:S(2)}) collective-permute-start(f32[3,512]{1,0:T(4,128)S(1)} %fusion.10), channel_id=1, source_target_pairs={{0,1},{1,0},{2,3},{3,2},{4,5},{5,4},{6,7},{7,6},{8,9},{9,8},{10,11... | collective-permute-start | bytes 18440 | tf_op jit(solution)/shard_map/ppermute | solution.py:100
  53.2 5.2 %collective-permute-start.12 = (f32[3,512]{1,0:T(4,128)S(1)}, f32[3,512]{1,0:T(4,128)S(1)}, u32[]{:S(2)}, u32[]{:S(2)}) collective-permute-start(f32[3,512]{1,0:T(4,128)S(1)} %get-tuple-element.205), channel_id=1, source_target_pairs={{0,4},{1,5},{2,6},{3,7},{4,0},{5,1},{6,2},{7,3},{8,12},{9,13},{10,... | collective-permute-start | bytes 18440 | tf_op jit(solution)/shard_map/ppermute | solution.py:100
  53.6 4.9 %collective-permute-start.11 = (f32[3,512]{1,0:T(4,128)S(1)}, f32[3,512]{1,0:T(4,128)S(1)}, u32[]{:S(2)}, u32[]{:S(2)}) collective-permute-start(f32[3,512]{1,0:T(4,128)S(1)} %get-tuple-element.205), channel_id=1, source_target_pairs={{0,2},{1,3},{2,4},{3,5},{4,6},{5,7},{6,0},{7,1},{8,10},{9,11},{10,... | collective-permute-start | bytes 18440 | tf_op jit(solution)/shard_map/ppermute | solution.py:100
  55.1 3.7 %collective-permute-start.13 = (f32[3,512]{1,0:T(4,128)S(1)}, f32[3,512]{1,0:T(4,128)S(1)}, u32[]{:S(2)}, u32[]{:S(2)}) collective-permute-start(f32[3,512]{1,0:T(4,128)S(1)} %get-tuple-element.205), channel_id=1, source_target_pairs={{0,6},{1,7},{2,0},{3,1},{4,2},{5,3},{6,4},{7,5},{8,14},{9,15},{10,... | collective-permute-start | bytes 18440 | tf_op jit(solution)/shard_map/ppermute | solution.py:100
  58.8 5.3 %collective-permute-start.15 = (f32[3,512]{1,0:T(4,128)S(1)}, f32[3,512]{1,0:T(4,128)S(1)}, u32[]{:S(2)}, u32[]{:S(2)}) collective-permute-start(f32[3,512]{1,0:T(4,128)S(1)} %get-tuple-element.203), channel_id=1, source_target_pairs={{0,16},{1,17},{2,18},{3,19},{4,20},{5,21},{6,22},{7,23},{8,24},{9,... | collective-permute-start | bytes 18440 | tf_op jit(solution)/shard_map/ppermute | solution.py:100
  60.9 4.9 %collective-permute-start.14 = (f32[3,512]{1,0:T(4,128)S(1)}, f32[3,512]{1,0:T(4,128)S(1)}, u32[]{:S(2)}, u32[]{:S(2)}) collective-permute-start(f32[3,512]{1,0:T(4,128)S(1)} %get-tuple-element.203), channel_id=1, source_target_pairs={{0,8},{1,9},{2,10},{3,11},{4,12},{5,13},{6,14},{7,15},{8,16},{9,17... | collective-permute-start | bytes 18440 | tf_op jit(solution)/shard_map/ppermute | solution.py:100
  61.6 4.2 %collective-permute-start.16 = (f32[3,512]{1,0:T(4,128)S(1)}, f32[3,512]{1,0:T(4,128)S(1)}, u32[]{:S(2)}, u32[]{:S(2)}) collective-permute-start(f32[3,512]{1,0:T(4,128)S(1)} %get-tuple-element.203), channel_id=1, source_target_pairs={{0,24},{1,25},{2,26},{3,27},{4,28},{5,29},{6,30},{7,31},{8,0},{9,1... | collective-permute-start | bytes 18440 | tf_op jit(solution)/shard_map/ppermute | solution.py:100
  65.9 5.2 %collective-permute-start.18 = (f32[3,512]{1,0:T(4,128)S(1)}, f32[3,512]{1,0:T(4,128)S(1)}, u32[]{:S(2)}, u32[]{:S(2)}) collective-permute-start(f32[3,512]{1,0:T(4,128)S(1)} %get-tuple-element.201), channel_id=1, source_target_pairs={{0,64},{1,65},{2,66},{3,67},{4,68},{5,69},{6,70},{7,71},{8,72},{9,... | collective-permute-start | bytes 18440 | tf_op jit(solution)/shard_map/ppermute | solution.py:100
  66.7 4.9 %collective-permute-start.17 = (f32[3,512]{1,0:T(4,128)S(1)}, f32[3,512]{1,0:T(4,128)S(1)}, u32[]{:S(2)}, u32[]{:S(2)}) collective-permute-start(f32[3,512]{1,0:T(4,128)S(1)} %get-tuple-element.201), channel_id=1, source_target_pairs={{0,32},{1,33},{2,34},{3,35},{4,36},{5,37},{6,38},{7,39},{8,40},{9,... | collective-permute-start | bytes 18440 | tf_op jit(solution)/shard_map/ppermute | solution.py:100
  67.4 4.2 %collective-permute-start.19 = (f32[3,512]{1,0:T(4,128)S(1)}, f32[3,512]{1,0:T(4,128)S(1)}, u32[]{:S(2)}, u32[]{:S(2)}) collective-permute-start(f32[3,512]{1,0:T(4,128)S(1)} %get-tuple-element.201), channel_id=1, source_target_pairs={{0,96},{1,97},{2,98},{3,99},{4,100},{5,101},{6,102},{7,103},{8,104... | collective-permute-start | bytes 18440 | tf_op jit(solution)/shard_map/ppermute | solution.py:100
  72.4 6.1 %slice-start.2 = ((s8[8257536]{0:T(1024)(128)(4,1)}), s8[4063232]{0:T(1024)(128)(4,1)S(1)}, s32[]{:S(2)}) async-start(s8[8257536]{0:T(1024)(128)(4,1)} %bitcast.221), calls=%async_computation.2 | async-start | bytes 8126464
  74.2 4.3 %slice-start.3 = ((s8[8257536]{0:T(1024)(128)(4,1)}), s8[4194304]{0:T(1024)(128)(4,1)S(1)}, s32[]{:S(2)}) async-start(s8[8257536]{0:T(1024)(128)(4,1)} %bitcast.221), calls=%async_computation.3 | async-start | bytes 8388608
  76.7 4.4 %collective-permute-start.20 = (bf16[256,3584]{1,0:T(8,128)(2,1)S(1)}, bf16[256,3584]{1,0:T(8,128)(2,1)S(1)}, u32[]{:S(2)}, u32[]{:S(2)}) collective-permute-start(bf16[256,3584]{1,0:T(8,128)(2,1)S(1)} %convolution_convert_fusion.1), channel_id=1, source_target_pairs={{0,1},{1,0},{2,3},{3,2},{4,5},{5,4},{6,7},{7,6},{8,9},{9,8},{10,11... | collective-permute-start | bytes 5505032 | tf_op jit(solution)/shard_map/ppermute | solution.py:200
  81.9 11.2 %collective-permute-start.21 = (bf16[64,3584]{1,0:T(8,128)(2,1)S(1)}, bf16[64,3584]{1,0:T(8,128)(2,1)S(1)}, u32[]{:S(2)}, u32[]{:S(2)}) collective-permute-start(bf16[64,3584]{1,0:T(8,128)(2,1)S(1)} %get-tuple-element.189), channel_id=1, source_target_pairs={{0,2},{1,33},{2,4},{3,35},{4,6},{5,37},{6,0},{7,39},{8,10},{9,41},... | collective-permute-start | bytes 1376264 | tf_op jit(solution)/shard_map/ppermute | solution.py:100
  83.7 9.4 %collective-permute-start.23 = (bf16[64,3584]{1,0:T(8,128)(2,1)S(1)}, bf16[64,3584]{1,0:T(8,128)(2,1)S(1)}, u32[]{:S(2)}, u32[]{:S(2)}) collective-permute-start(bf16[64,3584]{1,0:T(8,128)(2,1)S(1)} %get-tuple-element.190), channel_id=1, source_target_pairs={{0,6},{1,97},{2,0},{3,99},{4,2},{5,101},{6,4},{7,103},{8,14},{9,10... | collective-permute-start | bytes 1376264 | tf_op jit(solution)/shard_map/ppermute | solution.py:100
  85.2 12.6 %collective-permute-start.22 = (bf16[64,3584]{1,0:T(8,128)(2,1)S(1)}, bf16[64,3584]{1,0:T(8,128)(2,1)S(1)}, u32[]{:S(2)}, u32[]{:S(2)}) collective-permute-start(bf16[64,3584]{1,0:T(8,128)(2,1)S(1)} %get-tuple-element.191), channel_id=1, source_target_pairs={{0,4},{1,65},{2,6},{3,67},{4,0},{5,69},{6,2},{7,71},{8,12},{9,73},... | collective-permute-start | bytes 1376264 | tf_op jit(solution)/shard_map/ppermute | solution.py:100
  98.2 6.1 %collective-permute-start.24 = (bf16[16,3584]{1,0:T(8,128)(2,1)S(1)}, bf16[16,3584]{1,0:T(8,128)(2,1)S(1)}, u32[]{:S(2)}, u32[]{:S(2)}) collective-permute-start(bf16[16,3584]{1,0:T(8,128)(2,1)S(1)} %get-tuple-element.192), channel_id=1, source_target_pairs={{0,32},{1,3},{2,34},{3,5},{4,36},{5,7},{6,38},{7,1},{8,40},{9,11},... | collective-permute-start | bytes 344072 | tf_op jit(solution)/shard_map/ppermute | solution.py:100
  99.7 4.8 %collective-permute-start.26 = (bf16[16,3584]{1,0:T(8,128)(2,1)S(1)}, bf16[16,3584]{1,0:T(8,128)(2,1)S(1)}, u32[]{:S(2)}, u32[]{:S(2)}) collective-permute-start(bf16[16,3584]{1,0:T(8,128)(2,1)S(1)} %get-tuple-element.193), channel_id=1, source_target_pairs={{0,96},{1,7},{2,98},{3,1},{4,100},{5,3},{6,102},{7,5},{8,104},{9,1... | collective-permute-start | bytes 344072 | tf_op jit(solution)/shard_map/ppermute | solution.py:100
  101.6 6.3 %collective-permute-start.25 = (bf16[16,3584]{1,0:T(8,128)(2,1)S(1)}, bf16[16,3584]{1,0:T(8,128)(2,1)S(1)}, u32[]{:S(2)}, u32[]{:S(2)}) collective-permute-start(bf16[16,3584]{1,0:T(8,128)(2,1)S(1)} %get-tuple-element.194), channel_id=1, source_target_pairs={{0,64},{1,5},{2,66},{3,7},{4,68},{5,1},{6,70},{7,3},{8,72},{9,13},... | collective-permute-start | bytes 344072 | tf_op jit(solution)/shard_map/ppermute | solution.py:100
  108.0 5.3 %collective-permute-start.27 = (bf16[4,3584]{1,0:T(4,128)(2,1)S(1)}, bf16[4,3584]{1,0:T(4,128)(2,1)S(1)}, u32[]{:S(2)}, u32[]{:S(2)}) collective-permute-start(bf16[4,3584]{1,0:T(4,128)(2,1)S(1)} %get-tuple-element.195), channel_id=1, source_target_pairs={{0,8},{1,9},{2,10},{3,11},{4,12},{5,13},{6,14},{7,15},{8,16},{9,17... | collective-permute-start | bytes 86024 | tf_op jit(solution)/shard_map/ppermute | solution.py:100
  108.3 5.0 %collective-permute-start.29 = (bf16[4,3584]{1,0:T(4,128)(2,1)S(1)}, bf16[4,3584]{1,0:T(4,128)(2,1)S(1)}, u32[]{:S(2)}, u32[]{:S(2)}) collective-permute-start(bf16[4,3584]{1,0:T(4,128)(2,1)S(1)} %get-tuple-element.196), channel_id=1, source_target_pairs={{0,24},{1,25},{2,26},{3,27},{4,28},{5,29},{6,30},{7,31},{8,0},{9,1... | collective-permute-start | bytes 86024 | tf_op jit(solution)/shard_map/ppermute | solution.py:100
  111.3 5.4 %collective-permute-start.28 = (bf16[4,3584]{1,0:T(4,128)(2,1)S(1)}, bf16[4,3584]{1,0:T(4,128)(2,1)S(1)}, u32[]{:S(2)}, u32[]{:S(2)}) collective-permute-start(bf16[4,3584]{1,0:T(4,128)(2,1)S(1)} %get-tuple-element.197), channel_id=1, source_target_pairs={{0,16},{1,17},{2,18},{3,19},{4,20},{5,21},{6,22},{7,23},{8,24},{9,... | collective-permute-start | bytes 86024 | tf_op jit(solution)/shard_map/ppermute | solution.py:100

commit v10 on v9

--- a/solution.py
+++ b/solution.py
@@ -151,12 +151,18 @@
     target = teacher_target(local, probs_arr, voc_dev)
 
     own = hidden_rows
-    for stage in ("r1", "r2", "r3"):
+    for stage in ("r1", "r2"):
         own = exchange(lambda s: own, stage, n_dev, voc_n).reshape(-1, width)
-        if stage == "r3":
+        if stage == "r2":
             own, target = lax.optimization_barrier((own, target))
+    got = exchange(lambda s: own, "r3", n_dev, voc_n)
+    first_logits = half_logits(own, head_weight)
+    got, first_logits = lax.optimization_barrier((got, first_logits))
+    own = got.reshape(-1, width)
     other = lax.ppermute(own, AXES, stage_pairs("c", 1, n_dev, voc_n))
-    logits_own = half_logits(own, head_weight)
+    logits_own = jnp.concatenate(
+        [first_logits, half_logits(got[1:].reshape(-1, width), head_weight)], axis=0
+    )
     logits_other = half_logits(other, head_weight)
     every = jnp.concatenate([own, other], axis=0)
     half = own.shape[0]

time: 118 us -> 117 us (level)
  waiting for transfers between devices: 31.9 us -> 28.4 us
  matrix products: 21.8 us -> 24.4 us
    ppermute x28, waiting for transfers between devices: 31.9 us -> 27.7 us  [exchange(): lax.ppermute(block_for(shift), AXES, stage_pairs(stage, shift, n_dev, voc...]
    dot_general x2 -> x3, matrix products: 8.8 us -> 11.4 us  [half_logits(): lax.dot_general(rows_block, head_weight, (((1,), (1,)), ((), ())), prefer...]
  transfers between devices with their start and end apart: 30 -> 30, of which waited for: 18 -> 14; matrix products, arithmetic and copies ran while one was open for 23% -> 25% of each run, Pallas kernels for 0% -> 0%
where the time goes in v10:
time: 117 us
  starting transfers between devices  44.2 us (38%)
  waiting for transfers between devices  28.4 us (24%)
  matrix products  24.4 us (21%)
  other arithmetic  13.6 us (12%)
  local copies, waits for them, and re-layouts  4.5 us (4%)
  between operations  1.71 us (1%)
    ppermute x28, starting transfers between devices, exchange(): lax.ppermute(block_for(shift), AXES, stage_pairs(stage, shift, n_dev, voc...  43.6 us
    ppermute x28, waiting for transfers between devices, exchange(): lax.ppermute(block_for(shift), AXES, stage_pairs(stage, shift, n_dev, voc...  27.7 us
    dot_general x3, matrix products, half_logits(): lax.dot_general(rows_block, head_weight, (((1,), (1,)), ((), ())), prefer...  11.4 us
    dot_general x1, matrix products, per_device(): lax.dot_general(grad, every, (((0,), (0,)), ((), ())), preferred_element_...  6.72 us
    add x1, other arithmetic, compact_target(): target + jnp.where(slot_local[:, j:j + 1] == columns, slot_probs[:, j:j +...  3.57 us
    convert_element_type x2, other arithmetic, half_grad(): (loss_scale * (total_h[:, None] * jnp.exp(logits - lse_h[:, None]) - tgt)...  3.27 us
    dot_general x1, matrix products, per_device(): jnp.dot(grad_other, head_weight, preferred_element_type=jnp.float32)  2.6 us
    dot_general x1, matrix products, per_device(): acc = jnp.dot(grad_own, head_weight, preferred_element_type=jnp.float32)  2.59 us
  transfers between devices with their start and end apart: 30, of which 14 were waited for; matrix products, arithmetic and copies ran while one was open for 25% of the time, Pallas kernels for 0%

profile of v10, /device:TPU:0, one launch (start us, length us, event | category | flops | bytes accessed | tf_op | source)
XLA Modules:
  0.0 116.9 jit_solution(5772498437477052154)
XLA Ops:
  0.6 1.7 %collective-permute-start = (bf16[4,3584]{1,0:T(4,128)(2,1)}, bf16[4,3584]{1,0:T(4,128)(2,1)S(1)}, u32[]{:S(2)}, u32[]{:S(2)}) collective-permute-start(bf16[4,3584]{1,0:T(4,128)(2,1)} %param.8), channel_id=1, source_target_pairs={{0,8},{1,9},{2,10},{3,11},{4,12},{5,13},{6,14},{7,15},{8,16},{9,17... | collective-permute-start | bytes 86024 | tf_op jit(solution)/shard_map/ppermute | solution.py:100
  2.4 1.6 %collective-permute-start.2 = (bf16[4,3584]{1,0:T(4,128)(2,1)}, bf16[4,3584]{1,0:T(4,128)(2,1)S(1)}, u32[]{:S(2)}, u32[]{:S(2)}) collective-permute-start(bf16[4,3584]{1,0:T(4,128)(2,1)} %param.8), channel_id=1, source_target_pairs={{0,24},{1,25},{2,26},{3,27},{4,28},{5,29},{6,30},{7,31},{8,0},{9,1... | collective-permute-start | bytes 86024 | tf_op jit(solution)/shard_map/ppermute | solution.py:100
  4.0 2.1 %collective-permute-start.1 = (bf16[4,3584]{1,0:T(4,128)(2,1)}, bf16[4,3584]{1,0:T(4,128)(2,1)S(1)}, u32[]{:S(2)}, u32[]{:S(2)}) collective-permute-start(bf16[4,3584]{1,0:T(4,128)(2,1)} %param.8), channel_id=1, source_target_pairs={{0,16},{1,17},{2,18},{3,19},{4,20},{5,21},{6,22},{7,23},{8,24},{9,... | collective-permute-start | bytes 86024 | tf_op jit(solution)/shard_map/ppermute | solution.py:100
  6.1 1.0 copy.45
  7.2 1.0 gather_fusion.2
  8.2 1.3 %collective-permute-done.1 = bf16[4,3584]{1,0:T(4,128)(2,1)S(1)} collective-permute-done((bf16[4,3584]{1,0:T(4,128)(2,1)}, bf16[4,3584]{1,0:T(4,128)(2,1)S(1)}, u32[]{:S(2)}, u32[]{:S(2)}) %collective-permute-start.1) | collective-permute-done | bytes 28704 | tf_op jit(solution)/shard_map/ppermute | solution.py:100
  9.7 2.9 %collective-permute-start.5 = (bf16[16,3584]{1,0:T(8,128)(2,1)S(1)}, bf16[16,3584]{1,0:T(8,128)(2,1)S(1)}, u32[]{:S(2)}, u32[]{:S(2)}) collective-permute-start(bf16[16,3584]{1,0:T(8,128)(2,1)S(1)} %reshape.485), channel_id=1, source_target_pairs={{0,96},{1,7},{2,98},{3,1},{4,100},{5,3},{6,102},{7,5},{8,104},{9,1... | collective-permute-start | bytes 344072 | tf_op jit(solution)/shard_map/ppermute | solution.py:100
  12.6 0.8 collective-permute-start.4
  13.4 0.9 collective-permute-start.3
  15.8 5.8 %conditional.1 = (f32[512,1152]{1,0:T(8,128)}) conditional(s32[]{:T(128)} %convert_element_type.48, (s32[512,64]{1,0:T(8,128)S(1)}, pred[512]{0:T(512)(128)(4,1)S(1)}, f32[512,64]{0,1:T(8,128)S(1)}, s32[512,1]{0,1:T(1,128)S(1)}) %tuple.104, (s32[512,64]{1,0:T(8,128)S(1)}, pred[512]{0:T(512)(128)(4,1)S(1)}, f32[512,64]{0,1:T(8,128)S(1)}, ...), branch_computations={%region_3.7_spmd, %region_7.11_spmd} | conditional | flops 17916928 | bytes 5218828 | solution.py:44
  16.6 1.0 gather_fusion
  18.1 3.6 %select_add_fusion = f32[512,1152]{1,0:T(8,128)} fusion(f32[512]{0:T(512)S(1)} %bitcast.196, s32[512]{0:T(512)S(1)} %bitcast.188, f32[512]{0:T(512)S(1)} %bitcast.197, s32[512]{0:T(512)S(1)} %bitcast.189, f32[512]{0:T(512)S(1)} %bitcast.198, s32[512]{0:T(512)S(1)} %bitcast.190, f32[512]{0:T(512)S(1)} %bitcast.199, s32[512]{0:T(512)S(1)} %bitcast.191, ...), kind=kLoop, calls=%fused_computation.4 | loop fusion | flops 13565952 | bytes 2392064 | tf_op jit(solution)/shard_map/cond/branch_0_fun/add | solution.py:37
  21.8 4.1 %collective-permute-start.8 = (bf16[64,3584]{1,0:T(8,128)(2,1)S(1)}, bf16[64,3584]{1,0:T(8,128)(2,1)S(1)}, u32[]{:S(2)}, u32[]{:S(2)}) collective-permute-start(bf16[64,3584]{1,0:T(8,128)(2,1)S(1)} %bitcast.153), channel_id=1, source_target_pairs={{0,6},{1,97},{2,0},{3,99},{4,2},{5,101},{6,4},{7,103},{8,14},{9,10... | collective-permute-start | bytes 1376264 | tf_op jit(solution)/shard_map/ppermute | solution.py:100
  25.9 1.3 %collective-permute-start.6 = (bf16[64,3584]{1,0:T(8,128)(2,1)S(1)}, bf16[64,3584]{1,0:T(8,128)(2,1)S(1)}, u32[]{:S(2)}, u32[]{:S(2)}) collective-permute-start(bf16[64,3584]{1,0:T(8,128)(2,1)S(1)} %bitcast.155), channel_id=1, source_target_pairs={{0,2},{1,33},{2,4},{3,35},{4,6},{5,37},{6,0},{7,39},{8,10},{9,41},... | collective-permute-start | bytes 1376264 | tf_op jit(solution)/shard_map/ppermute | solution.py:100
  27.2 5.9 %fusion.96 = f32[64,1152]{1,0:T(8,128)S(1)} fusion(bf16[64,3584]{1,0:T(8,128)(2,1)S(1)} %bitcast.156, bf16[1152,3584]{1,0:T(8,128)(2,1)} %param.9), kind=kOutput, calls=%fused_computation.243 | convolution fusion | flops 528482304 | bytes 9011200 | tf_op jit(solution)/shard_map/dot_general | solution.py:133
  33.1 3.7 %collective-permute-done.8 = bf16[64,3584]{1,0:T(8,128)(2,1)S(1)} collective-permute-done((bf16[64,3584]{1,0:T(8,128)(2,1)S(1)}, bf16[64,3584]{1,0:T(8,128)(2,1)S(1)}, u32[]{:S(2)}, u32[]{:S(2)}) %collective-permute-start.8) | collective-permute-done | bytes 458784 | tf_op jit(solution)/shard_map/ppermute | solution.py:100
  36.8 3.7 %collective-permute-done.6 = bf16[64,3584]{1,0:T(8,128)(2,1)S(1)} collective-permute-done((bf16[64,3584]{1,0:T(8,128)(2,1)S(1)}, bf16[64,3584]{1,0:T(8,128)(2,1)S(1)}, u32[]{:S(2)}, u32[]{:S(2)}) %collective-permute-start.6) | collective-permute-done | bytes 458784 | tf_op jit(solution)/shard_map/ppermute | solution.py:100
  41.2 2.8 %fusion.97 = f32[192,1152]{1,0:T(8,128)S(1)} fusion(bf16[192,3584]{1,0:T(8,128)(2,1)S(1)} %bitcast.159, bf16[1152,3584]{1,0:T(8,128)(2,1)S(1)} %bitcast.150), kind=kOutput, calls=%fused_computation.244 | convolution fusion | flops 1585446912 | bytes 10518528 | tf_op jit(solution)/shard_map/dot_general | solution.py:133
  44.8 2.7 %fusion.95 = (f32[256]{0:T(256)S(1)}, f32[256,1152]{1,0:T(8,128)S(1)}) fusion(bf16[256,3584]{1,0:T(8,128)(2,1)S(1)} %collective-permute-done.9, bf16[1152,3584]{1,0:T(8,128)(2,1)S(1)} %bitcast.150), kind=kOutput, calls=%fused_computation.242 | convolution fusion | flops 2114223872 | bytes 11273216 | tf_op jit(solution)/shard_map/dot_general | solution.py:133
  47.5 2.3 %multiply_reduce_fusion.1 = (f32[256]{0:T(256)S(1)}, f32[256]{0:T(256)S(1)}, f32[256]{0:T(256)S(1)}, f32[256]{0:T(256)S(1)}) fusion(f32[512,1152]{1,0:T(8,128)} %get-tuple-element.260, f32[192,1152]{1,0:T(8,128)S(1)} %fusion.97, f32[64,1152]{1,0:T(8,128)S(1)} %fusion.96, f32[256,1152]{1,0:T(8,128)S(1)} %get-tuple-element.217, f32[256]{0:T(256)S(1)} %get-tuple-element.216, ...), kind=kLoop, calls=%fused_computation.43 | loop fusion | flops 2653184 | bytes 4724736 | tf_op jit(solution)/shard_map/reduce_sum | solution.py:173
  50.4 1.0 collective-permute-done.10
  51.9 1.5 %collective-permute-start.11 = (f32[3,512]{1,0:T(4,128)S(1)}, f32[3,512]{1,0:T(4,128)S(1)}, u32[]{:S(2)}, u32[]{:S(2)}) collective-permute-start(f32[3,512]{1,0:T(4,128)S(1)} %get-tuple-element.211), channel_id=1, source_target_pairs={{0,2},{1,3},{2,4},{3,5},{4,6},{5,7},{6,0},{7,1},{8,10},{9,11},{10,... | collective-permute-start | bytes 18440 | tf_op jit(solution)/shard_map/ppermute | solution.py:100
  53.4 1.8 %collective-permute-start.13 = (f32[3,512]{1,0:T(4,128)S(1)}, f32[3,512]{1,0:T(4,128)S(1)}, u32[]{:S(2)}, u32[]{:S(2)}) collective-permute-start(f32[3,512]{1,0:T(4,128)S(1)} %get-tuple-element.211), channel_id=1, source_target_pairs={{0,6},{1,7},{2,0},{3,1},{4,2},{5,3},{6,4},{7,5},{8,14},{9,15},{10,... | collective-permute-start | bytes 18440 | tf_op jit(solution)/shard_map/ppermute | solution.py:100
  55.2 1.7 %collective-permute-done.12 = f32[3,512]{1,0:T(4,128)S(1)} collective-permute-done((f32[3,512]{1,0:T(4,128)S(1)}, f32[3,512]{1,0:T(4,128)S(1)}, u32[]{:S(2)}, u32[]{:S(2)}) %collective-permute-start.12) | collective-permute-done | bytes 6176 | tf_op jit(solution)/shard_map/ppermute | solution.py:100
  57.1 2.1 %collective-permute-start.15 = (f32[3,512]{1,0:T(4,128)S(1)}, f32[3,512]{1,0:T(4,128)S(1)}, u32[]{:S(2)}, u32[]{:S(2)}) collective-permute-start(f32[3,512]{1,0:T(4,128)S(1)} %get-tuple-element.209), channel_id=1, source_target_pairs={{0,16},{1,17},{2,18},{3,19},{4,20},{5,21},{6,22},{7,23},{8,24},{9,... | collective-permute-start | bytes 18440 | tf_op jit(solution)/shard_map/ppermute | solution.py:100
  59.9 2.6 %collective-permute-start.16 = (f32[3,512]{1,0:T(4,128)S(1)}, f32[3,512]{1,0:T(4,128)S(1)}, u32[]{:S(2)}, u32[]{:S(2)}) collective-permute-start(f32[3,512]{1,0:T(4,128)S(1)} %get-tuple-element.209), channel_id=1, source_target_pairs={{0,24},{1,25},{2,26},{3,27},{4,28},{5,29},{6,30},{7,31},{8,0},{9,1... | collective-permute-start | bytes 18440 | tf_op jit(solution)/shard_map/ppermute | solution.py:100
  62.5 1.6 %collective-permute-done.14 = f32[3,512]{1,0:T(4,128)S(1)} collective-permute-done((f32[3,512]{1,0:T(4,128)S(1)}, f32[3,512]{1,0:T(4,128)S(1)}, u32[]{:S(2)}, u32[]{:S(2)}) %collective-permute-start.14) | collective-permute-done | bytes 6176 | tf_op jit(solution)/shard_map/ppermute | solution.py:100
  64.2 1.9 %collective-permute-start.18 = (f32[3,512]{1,0:T(4,128)S(1)}, f32[3,512]{1,0:T(4,128)S(1)}, u32[]{:S(2)}, u32[]{:S(2)}) collective-permute-start(f32[3,512]{1,0:T(4,128)S(1)} %get-tuple-element.207), channel_id=1, source_target_pairs={{0,64},{1,65},{2,66},{3,67},{4,68},{5,69},{6,70},{7,71},{8,72},{9,... | collective-permute-start | bytes 18440 | tf_op jit(solution)/shard_map/ppermute | solution.py:100
  66.1 1.4 %collective-permute-start.17 = (f32[3,512]{1,0:T(4,128)S(1)}, f32[3,512]{1,0:T(4,128)S(1)}, u32[]{:S(2)}, u32[]{:S(2)}) collective-permute-start(f32[3,512]{1,0:T(4,128)S(1)} %get-tuple-element.207), channel_id=1, source_target_pairs={{0,32},{1,33},{2,34},{3,35},{4,36},{5,37},{6,38},{7,39},{8,40},{9,... | collective-permute-start | bytes 18440 | tf_op jit(solution)/shard_map/ppermute | solution.py:100
  67.5 1.9 %collective-permute-start.19 = (f32[3,512]{1,0:T(4,128)S(1)}, f32[3,512]{1,0:T(4,128)S(1)}, u32[]{:S(2)}, u32[]{:S(2)}) collective-permute-start(f32[3,512]{1,0:T(4,128)S(1)} %get-tuple-element.207), channel_id=1, source_target_pairs={{0,96},{1,97},{2,98},{3,99},{4,100},{5,101},{6,102},{7,103},{8,104... | collective-permute-start | bytes 18440 | tf_op jit(solution)/shard_map/ppermute | solution.py:100
  69.5 1.5 %collective-permute-done.17 = f32[3,512]{1,0:T(4,128)S(1)} collective-permute-done((f32[3,512]{1,0:T(4,128)S(1)}, f32[3,512]{1,0:T(4,128)S(1)}, u32[]{:S(2)}, u32[]{:S(2)}) %collective-permute-start.17) | collective-permute-done | bytes 6176 | tf_op jit(solution)/shard_map/ppermute | solution.py:100
  71.9 1.6 %multiply_convert_fusion.1 = bf16[256,1152]{1,0:T(8,128)(2,1)S(1)} fusion(f32[256,1152]{1,0:T(8,128)S(1)} %get-tuple-element.217, f32[512,1152]{1,0:T(8,128)} %get-tuple-element.260, f32[256]{0:T(256)S(1)} %bitcast.219, f32[256]{0:T(256)S(1)} %bitcast.220), kind=kLoop, calls=%fused_computation.41 | loop fusion | flops 1474560 | bytes 2951168 | tf_op jit(solution)/shard_map/convert_element_type | solution.py:199
  73.5 2.6 %convolution_convert_fusion.1 = bf16[256,3584]{1,0:T(8,128)(2,1)S(1)} fusion(bf16[256,1152]{1,0:T(8,128)(2,1)S(1)} %multiply_convert_fusion.1, bf16[1152,3584]{1,0:T(8,128)(2,1)S(1)} %bitcast.150), kind=kOutput, calls=%fused_computation.29 | convolution fusion | flops 2114846720 | bytes 10682368 | tf_op jit(solution)/shard_map/dot_general | solution.py:205
  76.5 1.6 %multiply_convert_fusion = bf16[256,1152]{1,0:T(8,128)(2,1)S(1)} fusion(f32[256,1152]{1,0:T(8,128)S(1)} %get-tuple-element.98, f32[512,1152]{1,0:T(8,128)} %get-tuple-element.260, f32[256]{0:T(256)S(1)} %bitcast.218, f32[256]{0:T(256)S(1)} %bitcast.217), kind=kLoop, calls=%fused_computation.40 | loop fusion | flops 1474560 | bytes 2951168 | tf_op jit(solution)/shard_map/convert_element_type | solution.py:199
  78.1 2.6 %fusion.98 = f32[256,3584]{1,0:T(8,128)S(1)} fusion(bf16[256,1152]{1,0:T(8,128)(2,1)S(1)} %multiply_convert_fusion, bf16[1152,3584]{1,0:T(8,128)(2,1)S(1)} %bitcast.150), kind=kOutput, calls=%fused_computation.245 | convolution fusion | flops 2113929216 | bytes 12517376 | tf_op jit(solution)/shard_map/dot_general | solution.py:209
  81.4 1.8 %collective-permute-start.21 = (bf16[64,3584]{1,0:T(8,128)(2,1)S(1)}, bf16[64,3584]{1,0:T(8,128)(2,1)S(1)}, u32[]{:S(2)}, u32[]{:S(2)}) collective-permute-start(bf16[64,3584]{1,0:T(8,128)(2,1)S(1)} %get-tuple-element.193), channel_id=1, source_target_pairs={{0,2},{1,33},{2,4},{3,35},{4,6},{5,37},{6,0},{7,39},{8,10},{9,41},... | collective-permute-start | bytes 1376264 | tf_op jit(solution)/shard_map/ppermute | solution.py:100
  83.2 1.5 %collective-permute-start.23 = (bf16[64,3584]{1,0:T(8,128)(2,1)S(1)}, bf16[64,3584]{1,0:T(8,128)(2,1)S(1)}, u32[]{:S(2)}, u32[]{:S(2)}) collective-permute-start(bf16[64,3584]{1,0:T(8,128)(2,1)S(1)} %get-tuple-element.194), channel_id=1, source_target_pairs={{0,6},{1,97},{2,0},{3,99},{4,2},{5,101},{6,4},{7,103},{8,14},{9,10... | collective-permute-start | bytes 1376264 | tf_op jit(solution)/shard_map/ppermute | solution.py:100
  84.8 1.2 %collective-permute-start.22 = (bf16[64,3584]{1,0:T(8,128)(2,1)S(1)}, bf16[64,3584]{1,0:T(8,128)(2,1)S(1)}, u32[]{:S(2)}, u32[]{:S(2)}) collective-permute-start(bf16[64,3584]{1,0:T(8,128)(2,1)S(1)} %get-tuple-element.195), channel_id=1, source_target_pairs={{0,4},{1,65},{2,6},{3,67},{4,0},{5,69},{6,2},{7,71},{8,12},{9,73},... | collective-permute-start | bytes 1376264 | tf_op jit(solution)/shard_map/ppermute | solution.py:100
  86.0 6.7 %convolution_convert_fusion = bf16[1152,3584]{1,0:T(8,128)(2,1)} fusion(bf16[256,3584]{1,0:T(8,128)(2,1)S(1)} %collective-permute-done.9, bf16[256,3584]{1,0:T(8,128)(2,1)S(1)} %bitcast.152, bf16[256,1152]{1,0:T(8,128)(2,1)S(1)} %multiply_convert_fusion.1, bf16[256,1152]{1,0:T(8,128)(2,1)S(1)} %multiply_convert_fusion), kind=kOutput, calls=%fused_computation.28 | convolution fusion | flops 4241686528 | bytes 13107200 | tf_op jit(solution)/shard_map/dot_general | solution.py:213
  92.7 4.6 %collective-permute-done.22 = bf16[64,3584]{1,0:T(8,128)(2,1)S(1)} collective-permute-done((bf16[64,3584]{1,0:T(8,128)(2,1)S(1)}, bf16[64,3584]{1,0:T(8,128)(2,1)S(1)}, u32[]{:S(2)}, u32[]{:S(2)}) %collective-permute-start.22) | collective-permute-done | bytes 458784 | tf_op jit(solution)/shard_map/ppermute | solution.py:100
  97.8 0.7 collective-permute-start.24
  98.5 2.6 %collective-permute-start.26 = (bf16[16,3584]{1,0:T(8,128)(2,1)S(1)}, bf16[16,3584]{1,0:T(8,128)(2,1)S(1)}, u32[]{:S(2)}, u32[]{:S(2)}) collective-permute-start(bf16[16,3584]{1,0:T(8,128)(2,1)S(1)} %get-tuple-element.199), channel_id=1, source_target_pairs={{0,96},{1,7},{2,98},{3,1},{4,100},{5,3},{6,102},{7,5},{8,104},{9,1... | collective-permute-start | bytes 344072 | tf_op jit(solution)/shard_map/ppermute | solution.py:100
  101.1 1.5 %collective-permute-start.25 = (bf16[16,3584]{1,0:T(8,128)(2,1)S(1)}, bf16[16,3584]{1,0:T(8,128)(2,1)S(1)}, u32[]{:S(2)}, u32[]{:S(2)}) collective-permute-start(bf16[16,3584]{1,0:T(8,128)(2,1)S(1)} %get-tuple-element.200), channel_id=1, source_target_pairs={{0,64},{1,5},{2,66},{3,7},{4,68},{5,1},{6,70},{7,3},{8,72},{9,13},... | collective-permute-start | bytes 344072 | tf_op jit(solution)/shard_map/ppermute | solution.py:100
  102.6 1.3 %collective-permute-done.24 = bf16[16,3584]{1,0:T(8,128)(2,1)S(1)} collective-permute-done((bf16[16,3584]{1,0:T(8,128)(2,1)S(1)}, bf16[16,3584]{1,0:T(8,128)(2,1)S(1)}, u32[]{:S(2)}, u32[]{:S(2)}) %collective-permute-start.24) | collective-permute-done | bytes 114720 | tf_op jit(solution)/shard_map/ppermute | solution.py:100
  103.9 3.5 %collective-permute-done.25 = bf16[16,3584]{1,0:T(8,128)(2,1)S(1)} collective-permute-done((bf16[16,3584]{1,0:T(8,128)(2,1)S(1)}, bf16[16,3584]{1,0:T(8,128)(2,1)S(1)}, u32[]{:S(2)}, u32[]{:S(2)}) %collective-permute-start.25) | collective-permute-done | bytes 114720 | tf_op jit(solution)/shard_map/ppermute | solution.py:100
  107.8 3.0 %collective-permute-start.29 = (bf16[4,3584]{1,0:T(4,128)(2,1)S(1)}, bf16[4,3584]{1,0:T(4,128)(2,1)S(1)}, u32[]{:S(2)}, u32[]{:S(2)}) collective-permute-start(bf16[4,3584]{1,0:T(4,128)(2,1)S(1)} %get-tuple-element.202), channel_id=1, source_target_pairs={{0,24},{1,25},{2,26},{3,27},{4,28},{5,29},{6,30},{7,31},{8,0},{9,1... | collective-permute-start | bytes 86024 | tf_op jit(solution)/shard_map/ppermute | solution.py:100
  110.9 1.4 %collective-permute-start.28 = (bf16[4,3584]{1,0:T(4,128)(2,1)S(1)}, bf16[4,3584]{1,0:T(4,128)(2,1)S(1)}, u32[]{:S(2)}, u32[]{:S(2)}) collective-permute-start(bf16[4,3584]{1,0:T(4,128)(2,1)S(1)} %get-tuple-element.203), channel_id=1, source_target_pairs={{0,16},{1,17},{2,18},{3,19},{4,20},{5,21},{6,22},{7,23},{8,24},{9,... | collective-permute-start | bytes 86024 | tf_op jit(solution)/shard_map/ppermute | solution.py:100
  112.9 3.4 %collective-permute-done.28 = bf16[4,3584]{1,0:T(4,128)(2,1)S(1)} collective-permute-done((bf16[4,3584]{1,0:T(4,128)(2,1)S(1)}, bf16[4,3584]{1,0:T(4,128)(2,1)S(1)}, u32[]{:S(2)}, u32[]{:S(2)}) %collective-permute-start.28) | collective-permute-done | bytes 28704 | tf_op jit(solution)/shard_map/ppermute | solution.py:100
  (105 shorter events, 10.0 us)
Async XLA Ops:
  0.6 8.9 %copy-start.1 = (bf16[4,3584]{1,0:T(4,128)(2,1)S(1)}, bf16[4,3584]{1,0:T(4,128)(2,1)}, u32[]{:S(2)}) copy-start(bf16[4,3584]{1,0:T(4,128)(2,1)} %param.8) | copy-start | bytes 86020
  0.6 15.2 %copy-start = (f32[512,64]{0,1:T(8,128)S(1)}, f32[512,64]{0,1:T(8,128)}, u32[]{:S(2)}) copy-start(f32[512,64]{0,1:T(8,128)} %param.11) | copy-start | bytes 393220
  0.6 7.6 %collective-permute-start = (bf16[4,3584]{1,0:T(4,128)(2,1)}, bf16[4,3584]{1,0:T(4,128)(2,1)S(1)}, u32[]{:S(2)}, u32[]{:S(2)}) collective-permute-start(bf16[4,3584]{1,0:T(4,128)(2,1)} %param.8), channel_id=1, source_target_pairs={{0,8},{1,9},{2,10},{3,11},{4,12},{5,13},{6,14},{7,15},{8,16},{9,17... | collective-permute-start | bytes 86024 | tf_op jit(solution)/shard_map/ppermute | solution.py:100
  2.4 5.8 %collective-permute-start.2 = (bf16[4,3584]{1,0:T(4,128)(2,1)}, bf16[4,3584]{1,0:T(4,128)(2,1)S(1)}, u32[]{:S(2)}, u32[]{:S(2)}) collective-permute-start(bf16[4,3584]{1,0:T(4,128)(2,1)} %param.8), channel_id=1, source_target_pairs={{0,24},{1,25},{2,26},{3,27},{4,28},{5,29},{6,30},{7,31},{8,0},{9,1... | collective-permute-start | bytes 86024 | tf_op jit(solution)/shard_map/ppermute | solution.py:100
  4.0 5.6 %collective-permute-start.1 = (bf16[4,3584]{1,0:T(4,128)(2,1)}, bf16[4,3584]{1,0:T(4,128)(2,1)S(1)}, u32[]{:S(2)}, u32[]{:S(2)}) collective-permute-start(bf16[4,3584]{1,0:T(4,128)(2,1)} %param.8), channel_id=1, source_target_pairs={{0,16},{1,17},{2,18},{3,19},{4,20},{5,21},{6,22},{7,23},{8,24},{9,... | collective-permute-start | bytes 86024 | tf_op jit(solution)/shard_map/ppermute | solution.py:100
  9.7 12.0 %collective-permute-start.5 = (bf16[16,3584]{1,0:T(8,128)(2,1)S(1)}, bf16[16,3584]{1,0:T(8,128)(2,1)S(1)}, u32[]{:S(2)}, u32[]{:S(2)}) collective-permute-start(bf16[16,3584]{1,0:T(8,128)(2,1)S(1)} %reshape.485), channel_id=1, source_target_pairs={{0,96},{1,7},{2,98},{3,1},{4,100},{5,3},{6,102},{7,5},{8,104},{9,1... | collective-permute-start | bytes 344072 | tf_op jit(solution)/shard_map/ppermute | solution.py:100
  12.6 9.1 %collective-permute-start.4 = (bf16[16,3584]{1,0:T(8,128)(2,1)S(1)}, bf16[16,3584]{1,0:T(8,128)(2,1)S(1)}, u32[]{:S(2)}, u32[]{:S(2)}) collective-permute-start(bf16[16,3584]{1,0:T(8,128)(2,1)S(1)} %reshape.485), channel_id=1, source_target_pairs={{0,64},{1,5},{2,66},{3,7},{4,68},{5,1},{6,70},{7,3},{8,72},{9,13},... | collective-permute-start | bytes 344072 | tf_op jit(solution)/shard_map/ppermute | solution.py:100
  13.4 8.3 %collective-permute-start.3 = (bf16[16,3584]{1,0:T(8,128)(2,1)S(1)}, bf16[16,3584]{1,0:T(8,128)(2,1)S(1)}, u32[]{:S(2)}, u32[]{:S(2)}) collective-permute-start(bf16[16,3584]{1,0:T(8,128)(2,1)S(1)} %reshape.485), channel_id=1, source_target_pairs={{0,32},{1,3},{2,34},{3,5},{4,36},{5,7},{6,38},{7,1},{8,40},{9,11},... | collective-permute-start | bytes 344072 | tf_op jit(solution)/shard_map/ppermute | solution.py:100
  21.7 19.4 %slice-start = ((s8[8257536]{0:T(1024)(128)(4,1)}), s8[4194304]{0:T(1024)(128)(4,1)S(1)}, s32[]{:S(2)}) async-start(s8[8257536]{0:T(1024)(128)(4,1)} %bitcast.149), calls=%async_computation | async-start | bytes 8388608
  21.8 19.4 %slice-start.1 = ((s8[8257536]{0:T(1024)(128)(4,1)}), s8[4063232]{0:T(1024)(128)(4,1)S(1)}, s32[]{:S(2)}) async-start(s8[8257536]{0:T(1024)(128)(4,1)} %bitcast.149), calls=%async_computation.1 | async-start | bytes 8126464
  21.8 15.0 %collective-permute-start.8 = (bf16[64,3584]{1,0:T(8,128)(2,1)S(1)}, bf16[64,3584]{1,0:T(8,128)(2,1)S(1)}, u32[]{:S(2)}, u32[]{:S(2)}) collective-permute-start(bf16[64,3584]{1,0:T(8,128)(2,1)S(1)} %bitcast.153), channel_id=1, source_target_pairs={{0,6},{1,97},{2,0},{3,99},{4,2},{5,101},{6,4},{7,103},{8,14},{9,10... | collective-permute-start | bytes 1376264 | tf_op jit(solution)/shard_map/ppermute | solution.py:100
  25.9 10.9 %collective-permute-start.7 = (bf16[64,3584]{1,0:T(8,128)(2,1)S(1)}, bf16[64,3584]{1,0:T(8,128)(2,1)S(1)}, u32[]{:S(2)}, u32[]{:S(2)}) collective-permute-start(bf16[64,3584]{1,0:T(8,128)(2,1)S(1)} %bitcast.154), channel_id=1, source_target_pairs={{0,4},{1,65},{2,6},{3,67},{4,0},{5,69},{6,2},{7,71},{8,12},{9,73},... | collective-permute-start | bytes 1376264 | tf_op jit(solution)/shard_map/ppermute | solution.py:100
  25.9 14.6 %collective-permute-start.6 = (bf16[64,3584]{1,0:T(8,128)(2,1)S(1)}, bf16[64,3584]{1,0:T(8,128)(2,1)S(1)}, u32[]{:S(2)}, u32[]{:S(2)}) collective-permute-start(bf16[64,3584]{1,0:T(8,128)(2,1)S(1)} %bitcast.155), channel_id=1, source_target_pairs={{0,2},{1,33},{2,4},{3,35},{4,6},{5,37},{6,0},{7,39},{8,10},{9,41},... | collective-permute-start | bytes 1376264 | tf_op jit(solution)/shard_map/ppermute | solution.py:100
  40.7 4.0 %collective-permute-start.9 = (bf16[256,3584]{1,0:T(8,128)(2,1)S(1)}, bf16[256,3584]{1,0:T(8,128)(2,1)S(1)}, u32[]{:S(2)}, u32[]{:S(2)}) collective-permute-start(bf16[256,3584]{1,0:T(8,128)(2,1)S(1)} %bitcast.151), channel_id=1, source_target_pairs={{0,1},{1,0},{2,3},{3,2},{4,5},{5,4},{6,7},{7,6},{8,9},{9,8},{10,11... | collective-permute-start | bytes 5505032 | tf_op jit(solution)/shard_map/ppermute | solution.py:162
  50.3 1.2 %collective-permute-start.10 = (f32[3,512]{1,0:T(4,128)S(1)}, f32[3,512]{1,0:T(4,128)S(1)}, u32[]{:S(2)}, u32[]{:S(2)}) collective-permute-start(f32[3,512]{1,0:T(4,128)S(1)} %fusion.10), channel_id=1, source_target_pairs={{0,1},{1,0},{2,3},{3,2},{4,5},{5,4},{6,7},{7,6},{8,9},{9,8},{10,11... | collective-permute-start | bytes 18440 | tf_op jit(solution)/shard_map/ppermute | solution.py:100
  51.5 5.3 %collective-permute-start.12 = (f32[3,512]{1,0:T(4,128)S(1)}, f32[3,512]{1,0:T(4,128)S(1)}, u32[]{:S(2)}, u32[]{:S(2)}) collective-permute-start(f32[3,512]{1,0:T(4,128)S(1)} %get-tuple-element.211), channel_id=1, source_target_pairs={{0,4},{1,5},{2,6},{3,7},{4,0},{5,1},{6,2},{7,3},{8,12},{9,13},{10,... | collective-permute-start | bytes 18440 | tf_op jit(solution)/shard_map/ppermute | solution.py:100
  51.9 5.0 %collective-permute-start.11 = (f32[3,512]{1,0:T(4,128)S(1)}, f32[3,512]{1,0:T(4,128)S(1)}, u32[]{:S(2)}, u32[]{:S(2)}) collective-permute-start(f32[3,512]{1,0:T(4,128)S(1)} %get-tuple-element.211), channel_id=1, source_target_pairs={{0,2},{1,3},{2,4},{3,5},{4,6},{5,7},{6,0},{7,1},{8,10},{9,11},{10,... | collective-permute-start | bytes 18440 | tf_op jit(solution)/shard_map/ppermute | solution.py:100
  53.4 3.7 %collective-permute-start.13 = (f32[3,512]{1,0:T(4,128)S(1)}, f32[3,512]{1,0:T(4,128)S(1)}, u32[]{:S(2)}, u32[]{:S(2)}) collective-permute-start(f32[3,512]{1,0:T(4,128)S(1)} %get-tuple-element.211), channel_id=1, source_target_pairs={{0,6},{1,7},{2,0},{3,1},{4,2},{5,3},{6,4},{7,5},{8,14},{9,15},{10,... | collective-permute-start | bytes 18440 | tf_op jit(solution)/shard_map/ppermute | solution.py:100
  57.1 5.3 %collective-permute-start.15 = (f32[3,512]{1,0:T(4,128)S(1)}, f32[3,512]{1,0:T(4,128)S(1)}, u32[]{:S(2)}, u32[]{:S(2)}) collective-permute-start(f32[3,512]{1,0:T(4,128)S(1)} %get-tuple-element.209), channel_id=1, source_target_pairs={{0,16},{1,17},{2,18},{3,19},{4,20},{5,21},{6,22},{7,23},{8,24},{9,... | collective-permute-start | bytes 18440 | tf_op jit(solution)/shard_map/ppermute | solution.py:100
  59.2 4.9 %collective-permute-start.14 = (f32[3,512]{1,0:T(4,128)S(1)}, f32[3,512]{1,0:T(4,128)S(1)}, u32[]{:S(2)}, u32[]{:S(2)}) collective-permute-start(f32[3,512]{1,0:T(4,128)S(1)} %get-tuple-element.209), channel_id=1, source_target_pairs={{0,8},{1,9},{2,10},{3,11},{4,12},{5,13},{6,14},{7,15},{8,16},{9,17... | collective-permute-start | bytes 18440 | tf_op jit(solution)/shard_map/ppermute | solution.py:100
  59.9 4.2 %collective-permute-start.16 = (f32[3,512]{1,0:T(4,128)S(1)}, f32[3,512]{1,0:T(4,128)S(1)}, u32[]{:S(2)}, u32[]{:S(2)}) collective-permute-start(f32[3,512]{1,0:T(4,128)S(1)} %get-tuple-element.209), channel_id=1, source_target_pairs={{0,24},{1,25},{2,26},{3,27},{4,28},{5,29},{6,30},{7,31},{8,0},{9,1... | collective-permute-start | bytes 18440 | tf_op jit(solution)/shard_map/ppermute | solution.py:100
  64.2 5.2 %collective-permute-start.18 = (f32[3,512]{1,0:T(4,128)S(1)}, f32[3,512]{1,0:T(4,128)S(1)}, u32[]{:S(2)}, u32[]{:S(2)}) collective-permute-start(f32[3,512]{1,0:T(4,128)S(1)} %get-tuple-element.207), channel_id=1, source_target_pairs={{0,64},{1,65},{2,66},{3,67},{4,68},{5,69},{6,70},{7,71},{8,72},{9,... | collective-permute-start | bytes 18440 | tf_op jit(solution)/shard_map/ppermute | solution.py:100
  66.1 4.9 %collective-permute-start.17 = (f32[3,512]{1,0:T(4,128)S(1)}, f32[3,512]{1,0:T(4,128)S(1)}, u32[]{:S(2)}, u32[]{:S(2)}) collective-permute-start(f32[3,512]{1,0:T(4,128)S(1)} %get-tuple-element.207), channel_id=1, source_target_pairs={{0,32},{1,33},{2,34},{3,35},{4,36},{5,37},{6,38},{7,39},{8,40},{9,... | collective-permute-start | bytes 18440 | tf_op jit(solution)/shard_map/ppermute | solution.py:100
  67.5 3.7 %collective-permute-start.19 = (f32[3,512]{1,0:T(4,128)S(1)}, f32[3,512]{1,0:T(4,128)S(1)}, u32[]{:S(2)}, u32[]{:S(2)}) collective-permute-start(f32[3,512]{1,0:T(4,128)S(1)} %get-tuple-element.207), channel_id=1, source_target_pairs={{0,96},{1,97},{2,98},{3,99},{4,100},{5,101},{6,102},{7,103},{8,104... | collective-permute-start | bytes 18440 | tf_op jit(solution)/shard_map/ppermute | solution.py:100
  76.2 4.5 %collective-permute-start.20 = (bf16[256,3584]{1,0:T(8,128)(2,1)S(1)}, bf16[256,3584]{1,0:T(8,128)(2,1)S(1)}, u32[]{:S(2)}, u32[]{:S(2)}) collective-permute-start(bf16[256,3584]{1,0:T(8,128)(2,1)S(1)} %convolution_convert_fusion.1), channel_id=1, source_target_pairs={{0,1},{1,0},{2,3},{3,2},{4,5},{5,4},{6,7},{7,6},{8,9},{9,8},{10,11... | collective-permute-start | bytes 5505032 | tf_op jit(solution)/shard_map/ppermute | solution.py:206
  81.4 11.3 %collective-permute-start.21 = (bf16[64,3584]{1,0:T(8,128)(2,1)S(1)}, bf16[64,3584]{1,0:T(8,128)(2,1)S(1)}, u32[]{:S(2)}, u32[]{:S(2)}) collective-permute-start(bf16[64,3584]{1,0:T(8,128)(2,1)S(1)} %get-tuple-element.193), channel_id=1, source_target_pairs={{0,2},{1,33},{2,4},{3,35},{4,6},{5,37},{6,0},{7,39},{8,10},{9,41},... | collective-permute-start | bytes 1376264 | tf_op jit(solution)/shard_map/ppermute | solution.py:100
  83.2 9.5 %collective-permute-start.23 = (bf16[64,3584]{1,0:T(8,128)(2,1)S(1)}, bf16[64,3584]{1,0:T(8,128)(2,1)S(1)}, u32[]{:S(2)}, u32[]{:S(2)}) collective-permute-start(bf16[64,3584]{1,0:T(8,128)(2,1)S(1)} %get-tuple-element.194), channel_id=1, source_target_pairs={{0,6},{1,97},{2,0},{3,99},{4,2},{5,101},{6,4},{7,103},{8,14},{9,10... | collective-permute-start | bytes 1376264 | tf_op jit(solution)/shard_map/ppermute | solution.py:100
  84.8 12.6 %collective-permute-start.22 = (bf16[64,3584]{1,0:T(8,128)(2,1)S(1)}, bf16[64,3584]{1,0:T(8,128)(2,1)S(1)}, u32[]{:S(2)}, u32[]{:S(2)}) collective-permute-start(bf16[64,3584]{1,0:T(8,128)(2,1)S(1)} %get-tuple-element.195), channel_id=1, source_target_pairs={{0,4},{1,65},{2,6},{3,67},{4,0},{5,69},{6,2},{7,71},{8,12},{9,73},... | collective-permute-start | bytes 1376264 | tf_op jit(solution)/shard_map/ppermute | solution.py:100
  97.8 6.1 %collective-permute-start.24 = (bf16[16,3584]{1,0:T(8,128)(2,1)S(1)}, bf16[16,3584]{1,0:T(8,128)(2,1)S(1)}, u32[]{:S(2)}, u32[]{:S(2)}) collective-permute-start(bf16[16,3584]{1,0:T(8,128)(2,1)S(1)} %get-tuple-element.198), channel_id=1, source_target_pairs={{0,32},{1,3},{2,34},{3,5},{4,36},{5,7},{6,38},{7,1},{8,40},{9,11},... | collective-permute-start | bytes 344072 | tf_op jit(solution)/shard_map/ppermute | solution.py:100
  98.5 5.4 %collective-permute-start.26 = (bf16[16,3584]{1,0:T(8,128)(2,1)S(1)}, bf16[16,3584]{1,0:T(8,128)(2,1)S(1)}, u32[]{:S(2)}, u32[]{:S(2)}) collective-permute-start(bf16[16,3584]{1,0:T(8,128)(2,1)S(1)} %get-tuple-element.199), channel_id=1, source_target_pairs={{0,96},{1,7},{2,98},{3,1},{4,100},{5,3},{6,102},{7,5},{8,104},{9,1... | collective-permute-start | bytes 344072 | tf_op jit(solution)/shard_map/ppermute | solution.py:100
  101.1 6.3 %collective-permute-start.25 = (bf16[16,3584]{1,0:T(8,128)(2,1)S(1)}, bf16[16,3584]{1,0:T(8,128)(2,1)S(1)}, u32[]{:S(2)}, u32[]{:S(2)}) collective-permute-start(bf16[16,3584]{1,0:T(8,128)(2,1)S(1)} %get-tuple-element.200), channel_id=1, source_target_pairs={{0,64},{1,5},{2,66},{3,7},{4,68},{5,1},{6,70},{7,3},{8,72},{9,13},... | collective-permute-start | bytes 344072 | tf_op jit(solution)/shard_map/ppermute | solution.py:100
  107.5 5.3 %collective-permute-start.27 = (bf16[4,3584]{1,0:T(4,128)(2,1)S(1)}, bf16[4,3584]{1,0:T(4,128)(2,1)S(1)}, u32[]{:S(2)}, u32[]{:S(2)}) collective-permute-start(bf16[4,3584]{1,0:T(4,128)(2,1)S(1)} %get-tuple-element.201), channel_id=1, source_target_pairs={{0,8},{1,9},{2,10},{3,11},{4,12},{5,13},{6,14},{7,15},{8,16},{9,17... | collective-permute-start | bytes 86024 | tf_op jit(solution)/shard_map/ppermute | solution.py:100
  107.8 5.0 %collective-permute-start.29 = (bf16[4,3584]{1,0:T(4,128)(2,1)S(1)}, bf16[4,3584]{1,0:T(4,128)(2,1)S(1)}, u32[]{:S(2)}, u32[]{:S(2)}) collective-permute-start(bf16[4,3584]{1,0:T(4,128)(2,1)S(1)} %get-tuple-element.202), channel_id=1, source_target_pairs={{0,24},{1,25},{2,26},{3,27},{4,28},{5,29},{6,30},{7,31},{8,0},{9,1... | collective-permute-start | bytes 86024 | tf_op jit(solution)/shard_map/ppermute | solution.py:100
  110.9 5.4 %collective-permute-start.28 = (bf16[4,3584]{1,0:T(4,128)(2,1)S(1)}, bf16[4,3584]{1,0:T(4,128)(2,1)S(1)}, u32[]{:S(2)}, u32[]{:S(2)}) collective-permute-start(bf16[4,3584]{1,0:T(4,128)(2,1)S(1)} %get-tuple-element.203), channel_id=1, source_target_pairs={{0,16},{1,17},{2,18},{3,19},{4,20},{5,21},{6,22},{7,23},{8,24},{9,... | collective-permute-start | bytes 86024 | tf_op jit(solution)/shard_map/ppermute | solution.py:100

commit v11 on v10

--- a/solution.py
+++ b/solution.py
@@ -163,8 +163,6 @@
     logits_own = jnp.concatenate(
         [first_logits, half_logits(got[1:].reshape(-1, width), head_weight)], axis=0
     )
-    logits_other = half_logits(other, head_weight)
-    every = jnp.concatenate([own, other], axis=0)
     half = own.shape[0]
     target_own, target_other = target[:half], target[half:]
 
@@ -173,6 +171,8 @@
         return peak, jnp.sum(jnp.exp(logits - peak[:, None]), axis=1), jnp.sum(logits * tgt, axis=1)
 
     own_stats = local_stats(logits_own, target_own)
+    own_stats, other = lax.optimization_barrier((own_stats, other))
+    logits_other = half_logits(other, head_weight)
     other_stats = local_stats(logits_other, target_other)
     stats = jnp.stack([jnp.concatenate([a, b]) for a, b in zip(own_stats, other_stats)])
 
@@ -209,6 +209,7 @@
     acc = jnp.dot(grad_own, head_weight, preferred_element_type=jnp.float32)
     acc, received = lax.optimization_barrier((acc, received))
     acc = (acc + received.astype(jnp.float32)).reshape(RING, -1, width)
+    every = jnp.concatenate([own, other], axis=0)
     grad = jnp.concatenate([grad_own, grad_other], axis=0)
     head_grad = lax.dot_general(
         grad, every, (((0,), (0,)), ((), ())), preferred_element_type=jnp.float32

time: 117 us -> 118 us (level)
  other arithmetic: 13.6 us -> 14.8 us
    reduce_sum x0 -> x1, other arithmetic: none -> 1.73 us  [local_stats(): jnp.sum(jnp.exp(logits - peak[:, None]), axis=1)]
  transfers between devices with their start and end apart: 30 -> 30, of which waited for: 14 -> 13; matrix products, arithmetic and copies ran while one was open for 25% -> 27% of each run, Pallas kernels for 0% -> 0%
where the time goes in v11:
time: 118 us
  starting transfers between devices  44.6 us (38%)
  waiting for transfers between devices  27.5 us (23%)
  matrix products  24.4 us (21%)
  other arithmetic  14.8 us (13%)
  local copies, waits for them, and re-layouts  4.5 us (4%)
  between operations  1.71 us (1%)
    ppermute x28, starting transfers between devices, exchange(): lax.ppermute(block_for(shift), AXES, stage_pairs(stage, shift, n_dev, voc...  44 us
    ppermute x28, waiting for transfers between devices, exchange(): lax.ppermute(block_for(shift), AXES, stage_pairs(stage, shift, n_dev, voc...  27.5 us
    dot_general x3, matrix products, half_logits(): lax.dot_general(rows_block, head_weight, (((1,), (1,)), ((), ())), prefer...  11.4 us
    dot_general x1, matrix products, per_device(): lax.dot_general(grad, every, (((0,), (0,)), ((), ())), preferred_element_...  6.72 us
    add x1, other arithmetic, compact_target(): target + jnp.where(slot_local[:, j:j + 1] == columns, slot_probs[:, j:j +...  3.57 us
    convert_element_type x2, other arithmetic, half_grad(): (loss_scale * (total_h[:, None] * jnp.exp(logits - lse_h[:, None]) - tgt)...  3.27 us
    dot_general x1, matrix products, per_device(): jnp.dot(grad_other, head_weight, preferred_element_type=jnp.float32)  2.6 us
    dot_general x1, matrix products, per_device(): acc = jnp.dot(grad_own, head_weight, preferred_element_type=jnp.float32)  2.59 us
  transfers between devices with their start and end apart: 30, of which 13 were waited for; matrix products, arithmetic and copies ran while one was open for 27% of the time, Pallas kernels for 0%

profile of v11, /device:TPU:0, one launch (start us, length us, event | category | flops | bytes accessed | tf_op | source)
XLA Modules:
  0.0 117.6 jit_solution(12357418755404123960)
XLA Ops:
  0.6 1.7 %collective-permute-start = (bf16[4,3584]{1,0:T(4,128)(2,1)}, bf16[4,3584]{1,0:T(4,128)(2,1)S(1)}, u32[]{:S(2)}, u32[]{:S(2)}) collective-permute-start(bf16[4,3584]{1,0:T(4,128)(2,1)} %param.8), channel_id=1, source_target_pairs={{0,8},{1,9},{2,10},{3,11},{4,12},{5,13},{6,14},{7,15},{8,16},{9,17... | collective-permute-start | bytes 86024 | tf_op jit(solution)/shard_map/ppermute | solution.py:100
  2.4 1.6 %collective-permute-start.2 = (bf16[4,3584]{1,0:T(4,128)(2,1)}, bf16[4,3584]{1,0:T(4,128)(2,1)S(1)}, u32[]{:S(2)}, u32[]{:S(2)}) collective-permute-start(bf16[4,3584]{1,0:T(4,128)(2,1)} %param.8), channel_id=1, source_target_pairs={{0,24},{1,25},{2,26},{3,27},{4,28},{5,29},{6,30},{7,31},{8,0},{9,1... | collective-permute-start | bytes 86024 | tf_op jit(solution)/shard_map/ppermute | solution.py:100
  4.0 2.1 %collective-permute-start.1 = (bf16[4,3584]{1,0:T(4,128)(2,1)}, bf16[4,3584]{1,0:T(4,128)(2,1)S(1)}, u32[]{:S(2)}, u32[]{:S(2)}) collective-permute-start(bf16[4,3584]{1,0:T(4,128)(2,1)} %param.8), channel_id=1, source_target_pairs={{0,16},{1,17},{2,18},{3,19},{4,20},{5,21},{6,22},{7,23},{8,24},{9,... | collective-permute-start | bytes 86024 | tf_op jit(solution)/shard_map/ppermute | solution.py:100
  6.1 1.0 copy.45
  7.2 1.0 gather_fusion.2
  8.2 1.3 %collective-permute-done.1 = bf16[4,3584]{1,0:T(4,128)(2,1)S(1)} collective-permute-done((bf16[4,3584]{1,0:T(4,128)(2,1)}, bf16[4,3584]{1,0:T(4,128)(2,1)S(1)}, u32[]{:S(2)}, u32[]{:S(2)}) %collective-permute-start.1) | collective-permute-done | bytes 28704 | tf_op jit(solution)/shard_map/ppermute | solution.py:100
  9.7 2.9 %collective-permute-start.5 = (bf16[16,3584]{1,0:T(8,128)(2,1)S(1)}, bf16[16,3584]{1,0:T(8,128)(2,1)S(1)}, u32[]{:S(2)}, u32[]{:S(2)}) collective-permute-start(bf16[16,3584]{1,0:T(8,128)(2,1)S(1)} %reshape.485), channel_id=1, source_target_pairs={{0,96},{1,7},{2,98},{3,1},{4,100},{5,3},{6,102},{7,5},{8,104},{9,1... | collective-permute-start | bytes 344072 | tf_op jit(solution)/shard_map/ppermute | solution.py:100
  12.6 0.8 collective-permute-start.4
  13.4 0.9 collective-permute-start.3
  15.8 5.8 %conditional.1 = (f32[512,1152]{1,0:T(8,128)}) conditional(s32[]{:T(128)} %convert_element_type.48, (s32[512,64]{1,0:T(8,128)S(1)}, pred[512]{0:T(512)(128)(4,1)S(1)}, f32[512,64]{0,1:T(8,128)S(1)}, s32[512,1]{0,1:T(1,128)S(1)}) %tuple.105, (s32[512,64]{1,0:T(8,128)S(1)}, pred[512]{0:T(512)(128)(4,1)S(1)}, f32[512,64]{0,1:T(8,128)S(1)}, ...), branch_computations={%region_3.7_spmd, %region_7.11_spmd} | conditional | flops 17916928 | bytes 5218828 | solution.py:44
  16.6 1.0 gather_fusion
  18.1 3.6 %select_add_fusion = f32[512,1152]{1,0:T(8,128)} fusion(f32[512]{0:T(512)S(1)} %bitcast.196, s32[512]{0:T(512)S(1)} %bitcast.188, f32[512]{0:T(512)S(1)} %bitcast.197, s32[512]{0:T(512)S(1)} %bitcast.189, f32[512]{0:T(512)S(1)} %bitcast.198, s32[512]{0:T(512)S(1)} %bitcast.190, f32[512]{0:T(512)S(1)} %bitcast.199, s32[512]{0:T(512)S(1)} %bitcast.191, ...), kind=kLoop, calls=%fused_computation.4 | loop fusion | flops 13565952 | bytes 2392064 | tf_op jit(solution)/shard_map/cond/branch_0_fun/add | solution.py:37
  21.8 4.1 %collective-permute-start.8 = (bf16[64,3584]{1,0:T(8,128)(2,1)S(1)}, bf16[64,3584]{1,0:T(8,128)(2,1)S(1)}, u32[]{:S(2)}, u32[]{:S(2)}) collective-permute-start(bf16[64,3584]{1,0:T(8,128)(2,1)S(1)} %bitcast.153), channel_id=1, source_target_pairs={{0,6},{1,97},{2,0},{3,99},{4,2},{5,101},{6,4},{7,103},{8,14},{9,10... | collective-permute-start | bytes 1376264 | tf_op jit(solution)/shard_map/ppermute | solution.py:100
  25.9 1.3 %collective-permute-start.6 = (bf16[64,3584]{1,0:T(8,128)(2,1)S(1)}, bf16[64,3584]{1,0:T(8,128)(2,1)S(1)}, u32[]{:S(2)}, u32[]{:S(2)}) collective-permute-start(bf16[64,3584]{1,0:T(8,128)(2,1)S(1)} %bitcast.155), channel_id=1, source_target_pairs={{0,2},{1,33},{2,4},{3,35},{4,6},{5,37},{6,0},{7,39},{8,10},{9,41},... | collective-permute-start | bytes 1376264 | tf_op jit(solution)/shard_map/ppermute | solution.py:100
  27.2 5.9 %fusion.96 = f32[64,1152]{1,0:T(8,128)S(1)} fusion(bf16[64,3584]{1,0:T(8,128)(2,1)S(1)} %bitcast.156, bf16[1152,3584]{1,0:T(8,128)(2,1)} %param.9), kind=kOutput, calls=%fused_computation.243 | convolution fusion | flops 528482304 | bytes 9011200 | tf_op jit(solution)/shard_map/dot_general | solution.py:133
  33.1 3.7 %collective-permute-done.8 = bf16[64,3584]{1,0:T(8,128)(2,1)S(1)} collective-permute-done((bf16[64,3584]{1,0:T(8,128)(2,1)S(1)}, bf16[64,3584]{1,0:T(8,128)(2,1)S(1)}, u32[]{:S(2)}, u32[]{:S(2)}) %collective-permute-start.8) | collective-permute-done | bytes 458784 | tf_op jit(solution)/shard_map/ppermute | solution.py:100
  36.8 3.7 %collective-permute-done.6 = bf16[64,3584]{1,0:T(8,128)(2,1)S(1)} collective-permute-done((bf16[64,3584]{1,0:T(8,128)(2,1)S(1)}, bf16[64,3584]{1,0:T(8,128)(2,1)S(1)}, u32[]{:S(2)}, u32[]{:S(2)}) %collective-permute-start.6) | collective-permute-done | bytes 458784 | tf_op jit(solution)/shard_map/ppermute | solution.py:100
  41.2 2.8 %fusion.97 = f32[192,1152]{1,0:T(8,128)S(1)} fusion(bf16[192,3584]{1,0:T(8,128)(2,1)S(1)} %bitcast.159, bf16[1152,3584]{1,0:T(8,128)(2,1)S(1)} %bitcast.150), kind=kOutput, calls=%fused_computation.244 | convolution fusion | flops 1585446912 | bytes 10518528 | tf_op jit(solution)/shard_map/dot_general | solution.py:133
  44.0 1.6 %multiply_reduce_fusion.1 = (f32[256]{0:T(256)S(1)}, f32[256]{0:T(256)S(1)}) fusion(f32[512,1152]{1,0:T(8,128)} %get-tuple-element.268, f32[192,1152]{1,0:T(8,128)S(1)} %fusion.97, f32[64,1152]{1,0:T(8,128)S(1)} %fusion.96), kind=kLoop, calls=%fused_computation.44 | loop fusion | flops 1179136 | bytes 2361344 | tf_op jit(solution)/shard_map/reduce_sum | solution.py:171
  45.9 2.6 %fusion.95 = (f32[256]{0:T(256)S(1)}, f32[256,1152]{1,0:T(8,128)S(1)}) fusion(bf16[256,3584]{1,0:T(8,128)(2,1)S(1)} %collective-permute-done.9, bf16[1152,3584]{1,0:T(8,128)(2,1)S(1)} %bitcast.150), kind=kOutput, calls=%fused_computation.242 | convolution fusion | flops 2114223872 | bytes 11273216 | tf_op jit(solution)/shard_map/dot_general | solution.py:133
  48.5 1.7 %exponential_reduce_fusion = (f32[256]{0:T(256)S(1)}, f32[256]{0:T(256)S(1)}) fusion(f32[256,1152]{1,0:T(8,128)S(1)} %get-tuple-element.225, f32[256]{0:T(256)S(1)} %get-tuple-element.224, f32[512,1152]{1,0:T(8,128)} %get-tuple-element.268), kind=kLoop, calls=%fused_computation.43 | loop fusion | flops 1179136 | bytes 2362368 | tf_op jit(solution)/shard_map/reduce_sum | solution.py:171
  51.3 0.8 collective-permute-done.10
  52.6 1.5 %collective-permute-start.11 = (f32[3,512]{1,0:T(4,128)S(1)}, f32[3,512]{1,0:T(4,128)S(1)}, u32[]{:S(2)}, u32[]{:S(2)}) collective-permute-start(f32[3,512]{1,0:T(4,128)S(1)} %get-tuple-element.219), channel_id=1, source_target_pairs={{0,2},{1,3},{2,4},{3,5},{4,6},{5,7},{6,0},{7,1},{8,10},{9,11},{10,... | collective-permute-start | bytes 18440 | tf_op jit(solution)/shard_map/ppermute | solution.py:100
  54.0 1.8 %collective-permute-start.13 = (f32[3,512]{1,0:T(4,128)S(1)}, f32[3,512]{1,0:T(4,128)S(1)}, u32[]{:S(2)}, u32[]{:S(2)}) collective-permute-start(f32[3,512]{1,0:T(4,128)S(1)} %get-tuple-element.219), channel_id=1, source_target_pairs={{0,6},{1,7},{2,0},{3,1},{4,2},{5,3},{6,4},{7,5},{8,14},{9,15},{10,... | collective-permute-start | bytes 18440 | tf_op jit(solution)/shard_map/ppermute | solution.py:100
  55.8 1.7 %collective-permute-done.12 = f32[3,512]{1,0:T(4,128)S(1)} collective-permute-done((f32[3,512]{1,0:T(4,128)S(1)}, f32[3,512]{1,0:T(4,128)S(1)}, u32[]{:S(2)}, u32[]{:S(2)}) %collective-permute-start.12) | collective-permute-done | bytes 6176 | tf_op jit(solution)/shard_map/ppermute | solution.py:100
  57.8 2.1 %collective-permute-start.15 = (f32[3,512]{1,0:T(4,128)S(1)}, f32[3,512]{1,0:T(4,128)S(1)}, u32[]{:S(2)}, u32[]{:S(2)}) collective-permute-start(f32[3,512]{1,0:T(4,128)S(1)} %get-tuple-element.217), channel_id=1, source_target_pairs={{0,16},{1,17},{2,18},{3,19},{4,20},{5,21},{6,22},{7,23},{8,24},{9,... | collective-permute-start | bytes 18440 | tf_op jit(solution)/shard_map/ppermute | solution.py:100
  60.6 2.6 %collective-permute-start.16 = (f32[3,512]{1,0:T(4,128)S(1)}, f32[3,512]{1,0:T(4,128)S(1)}, u32[]{:S(2)}, u32[]{:S(2)}) collective-permute-start(f32[3,512]{1,0:T(4,128)S(1)} %get-tuple-element.217), channel_id=1, source_target_pairs={{0,24},{1,25},{2,26},{3,27},{4,28},{5,29},{6,30},{7,31},{8,0},{9,1... | collective-permute-start | bytes 18440 | tf_op jit(solution)/shard_map/ppermute | solution.py:100
  63.1 1.6 %collective-permute-done.14 = f32[3,512]{1,0:T(4,128)S(1)} collective-permute-done((f32[3,512]{1,0:T(4,128)S(1)}, f32[3,512]{1,0:T(4,128)S(1)}, u32[]{:S(2)}, u32[]{:S(2)}) %collective-permute-start.14) | collective-permute-done | bytes 6176 | tf_op jit(solution)/shard_map/ppermute | solution.py:100
  64.9 1.9 %collective-permute-start.18 = (f32[3,512]{1,0:T(4,128)S(1)}, f32[3,512]{1,0:T(4,128)S(1)}, u32[]{:S(2)}, u32[]{:S(2)}) collective-permute-start(f32[3,512]{1,0:T(4,128)S(1)} %get-tuple-element.215), channel_id=1, source_target_pairs={{0,64},{1,65},{2,66},{3,67},{4,68},{5,69},{6,70},{7,71},{8,72},{9,... | collective-permute-start | bytes 18440 | tf_op jit(solution)/shard_map/ppermute | solution.py:100
  66.8 1.4 %collective-permute-start.17 = (f32[3,512]{1,0:T(4,128)S(1)}, f32[3,512]{1,0:T(4,128)S(1)}, u32[]{:S(2)}, u32[]{:S(2)}) collective-permute-start(f32[3,512]{1,0:T(4,128)S(1)} %get-tuple-element.215), channel_id=1, source_target_pairs={{0,32},{1,33},{2,34},{3,35},{4,36},{5,37},{6,38},{7,39},{8,40},{9,... | collective-permute-start | bytes 18440 | tf_op jit(solution)/shard_map/ppermute | solution.py:100
  68.2 1.9 %collective-permute-start.19 = (f32[3,512]{1,0:T(4,128)S(1)}, f32[3,512]{1,0:T(4,128)S(1)}, u32[]{:S(2)}, u32[]{:S(2)}) collective-permute-start(f32[3,512]{1,0:T(4,128)S(1)} %get-tuple-element.215), channel_id=1, source_target_pairs={{0,96},{1,97},{2,98},{3,99},{4,100},{5,101},{6,102},{7,103},{8,104... | collective-permute-start | bytes 18440 | tf_op jit(solution)/shard_map/ppermute | solution.py:100
  70.1 1.5 %collective-permute-done.17 = f32[3,512]{1,0:T(4,128)S(1)} collective-permute-done((f32[3,512]{1,0:T(4,128)S(1)}, f32[3,512]{1,0:T(4,128)S(1)}, u32[]{:S(2)}, u32[]{:S(2)}) %collective-permute-start.17) | collective-permute-done | bytes 6176 | tf_op jit(solution)/shard_map/ppermute | solution.py:100
  72.6 1.6 %multiply_convert_fusion.1 = bf16[256,1152]{1,0:T(8,128)(2,1)S(1)} fusion(f32[256,1152]{1,0:T(8,128)S(1)} %get-tuple-element.225, f32[512,1152]{1,0:T(8,128)} %get-tuple-element.268, f32[256]{0:T(256)S(1)} %bitcast.219, f32[256]{0:T(256)S(1)} %bitcast.220), kind=kLoop, calls=%fused_computation.41 | loop fusion | flops 1474560 | bytes 2951168 | tf_op jit(solution)/shard_map/convert_element_type | solution.py:199
  74.2 2.6 %convolution_convert_fusion.1 = bf16[256,3584]{1,0:T(8,128)(2,1)S(1)} fusion(bf16[256,1152]{1,0:T(8,128)(2,1)S(1)} %multiply_convert_fusion.1, bf16[1152,3584]{1,0:T(8,128)(2,1)S(1)} %bitcast.150), kind=kOutput, calls=%fused_computation.29 | convolution fusion | flops 2114846720 | bytes 10682368 | tf_op jit(solution)/shard_map/dot_general | solution.py:205
  77.1 1.6 %multiply_convert_fusion = bf16[256,1152]{1,0:T(8,128)(2,1)S(1)} fusion(f32[256,1152]{1,0:T(8,128)S(1)} %get-tuple-element.106, f32[512,1152]{1,0:T(8,128)} %get-tuple-element.268, f32[256]{0:T(256)S(1)} %bitcast.218, f32[256]{0:T(256)S(1)} %bitcast.217), kind=kLoop, calls=%fused_computation.40 | loop fusion | flops 1474560 | bytes 2951168 | tf_op jit(solution)/shard_map/convert_element_type | solution.py:199
  78.8 2.6 %fusion.98 = f32[256,3584]{1,0:T(8,128)S(1)} fusion(bf16[256,1152]{1,0:T(8,128)(2,1)S(1)} %multiply_convert_fusion, bf16[1152,3584]{1,0:T(8,128)(2,1)S(1)} %bitcast.150), kind=kOutput, calls=%fused_computation.245 | convolution fusion | flops 2113929216 | bytes 12517376 | tf_op jit(solution)/shard_map/dot_general | solution.py:209
  82.1 1.8 %collective-permute-start.21 = (bf16[64,3584]{1,0:T(8,128)(2,1)S(1)}, bf16[64,3584]{1,0:T(8,128)(2,1)S(1)}, u32[]{:S(2)}, u32[]{:S(2)}) collective-permute-start(bf16[64,3584]{1,0:T(8,128)(2,1)S(1)} %get-tuple-element.201), channel_id=1, source_target_pairs={{0,2},{1,33},{2,4},{3,35},{4,6},{5,37},{6,0},{7,39},{8,10},{9,41},... | collective-permute-start | bytes 1376264 | tf_op jit(solution)/shard_map/ppermute | solution.py:100
  83.9 1.5 %collective-permute-start.23 = (bf16[64,3584]{1,0:T(8,128)(2,1)S(1)}, bf16[64,3584]{1,0:T(8,128)(2,1)S(1)}, u32[]{:S(2)}, u32[]{:S(2)}) collective-permute-start(bf16[64,3584]{1,0:T(8,128)(2,1)S(1)} %get-tuple-element.202), channel_id=1, source_target_pairs={{0,6},{1,97},{2,0},{3,99},{4,2},{5,101},{6,4},{7,103},{8,14},{9,10... | collective-permute-start | bytes 1376264 | tf_op jit(solution)/shard_map/ppermute | solution.py:100
  85.4 1.2 %collective-permute-start.22 = (bf16[64,3584]{1,0:T(8,128)(2,1)S(1)}, bf16[64,3584]{1,0:T(8,128)(2,1)S(1)}, u32[]{:S(2)}, u32[]{:S(2)}) collective-permute-start(bf16[64,3584]{1,0:T(8,128)(2,1)S(1)} %get-tuple-element.203), channel_id=1, source_target_pairs={{0,4},{1,65},{2,6},{3,67},{4,0},{5,69},{6,2},{7,71},{8,12},{9,73},... | collective-permute-start | bytes 1376264 | tf_op jit(solution)/shard_map/ppermute | solution.py:100
  86.6 6.7 %convolution_convert_fusion = bf16[1152,3584]{1,0:T(8,128)(2,1)} fusion(bf16[256,3584]{1,0:T(8,128)(2,1)S(1)} %collective-permute-done.9, bf16[256,3584]{1,0:T(8,128)(2,1)S(1)} %bitcast.152, bf16[256,1152]{1,0:T(8,128)(2,1)S(1)} %multiply_convert_fusion.1, bf16[256,1152]{1,0:T(8,128)(2,1)S(1)} %multiply_convert_fusion), kind=kOutput, calls=%fused_computation.28 | convolution fusion | flops 4241686528 | bytes 13107200 | tf_op jit(solution)/shard_map/dot_general | solution.py:214
  93.4 4.6 %collective-permute-done.22 = bf16[64,3584]{1,0:T(8,128)(2,1)S(1)} collective-permute-done((bf16[64,3584]{1,0:T(8,128)(2,1)S(1)}, bf16[64,3584]{1,0:T(8,128)(2,1)S(1)}, u32[]{:S(2)}, u32[]{:S(2)}) %collective-permute-start.22) | collective-permute-done | bytes 458784 | tf_op jit(solution)/shard_map/ppermute | solution.py:100
  99.2 2.6 %collective-permute-start.26 = (bf16[16,3584]{1,0:T(8,128)(2,1)S(1)}, bf16[16,3584]{1,0:T(8,128)(2,1)S(1)}, u32[]{:S(2)}, u32[]{:S(2)}) collective-permute-start(bf16[16,3584]{1,0:T(8,128)(2,1)S(1)} %get-tuple-element.207), channel_id=1, source_target_pairs={{0,96},{1,7},{2,98},{3,1},{4,100},{5,3},{6,102},{7,5},{8,104},{9,1... | collective-permute-start | bytes 344072 | tf_op jit(solution)/shard_map/ppermute | solution.py:100
  101.8 1.5 %collective-permute-start.25 = (bf16[16,3584]{1,0:T(8,128)(2,1)S(1)}, bf16[16,3584]{1,0:T(8,128)(2,1)S(1)}, u32[]{:S(2)}, u32[]{:S(2)}) collective-permute-start(bf16[16,3584]{1,0:T(8,128)(2,1)S(1)} %get-tuple-element.208), channel_id=1, source_target_pairs={{0,64},{1,5},{2,66},{3,7},{4,68},{5,1},{6,70},{7,3},{8,72},{9,13},... | collective-permute-start | bytes 344072 | tf_op jit(solution)/shard_map/ppermute | solution.py:100
  103.3 1.3 %collective-permute-done.24 = bf16[16,3584]{1,0:T(8,128)(2,1)S(1)} collective-permute-done((bf16[16,3584]{1,0:T(8,128)(2,1)S(1)}, bf16[16,3584]{1,0:T(8,128)(2,1)S(1)}, u32[]{:S(2)}, u32[]{:S(2)}) %collective-permute-start.24) | collective-permute-done | bytes 114720 | tf_op jit(solution)/shard_map/ppermute | solution.py:100
  104.5 3.5 %collective-permute-done.25 = bf16[16,3584]{1,0:T(8,128)(2,1)S(1)} collective-permute-done((bf16[16,3584]{1,0:T(8,128)(2,1)S(1)}, bf16[16,3584]{1,0:T(8,128)(2,1)S(1)}, u32[]{:S(2)}, u32[]{:S(2)}) %collective-permute-start.25) | collective-permute-done | bytes 114720 | tf_op jit(solution)/shard_map/ppermute | solution.py:100
  108.5 3.0 %collective-permute-start.29 = (bf16[4,3584]{1,0:T(4,128)(2,1)S(1)}, bf16[4,3584]{1,0:T(4,128)(2,1)S(1)}, u32[]{:S(2)}, u32[]{:S(2)}) collective-permute-start(bf16[4,3584]{1,0:T(4,128)(2,1)S(1)} %get-tuple-element.210), channel_id=1, source_target_pairs={{0,24},{1,25},{2,26},{3,27},{4,28},{5,29},{6,30},{7,31},{8,0},{9,1... | collective-permute-start | bytes 86024 | tf_op jit(solution)/shard_map/ppermute | solution.py:100
  111.5 1.4 %collective-permute-start.28 = (bf16[4,3584]{1,0:T(4,128)(2,1)S(1)}, bf16[4,3584]{1,0:T(4,128)(2,1)S(1)}, u32[]{:S(2)}, u32[]{:S(2)}) collective-permute-start(bf16[4,3584]{1,0:T(4,128)(2,1)S(1)} %get-tuple-element.211), channel_id=1, source_target_pairs={{0,16},{1,17},{2,18},{3,19},{4,20},{5,21},{6,22},{7,23},{8,24},{9,... | collective-permute-start | bytes 86024 | tf_op jit(solution)/shard_map/ppermute | solution.py:100
  113.5 3.4 %collective-permute-done.28 = bf16[4,3584]{1,0:T(4,128)(2,1)S(1)} collective-permute-done((bf16[4,3584]{1,0:T(4,128)(2,1)S(1)}, bf16[4,3584]{1,0:T(4,128)(2,1)S(1)}, u32[]{:S(2)}, u32[]{:S(2)}) %collective-permute-start.28) | collective-permute-done | bytes 28704 | tf_op jit(solution)/shard_map/ppermute | solution.py:100
  (106 shorter events, 10.7 us)
Async XLA Ops:
  0.6 8.9 %copy-start.1 = (bf16[4,3584]{1,0:T(4,128)(2,1)S(1)}, bf16[4,3584]{1,0:T(4,128)(2,1)}, u32[]{:S(2)}) copy-start(bf16[4,3584]{1,0:T(4,128)(2,1)} %param.8) | copy-start | bytes 86020
  0.6 15.2 %copy-start = (f32[512,64]{0,1:T(8,128)S(1)}, f32[512,64]{0,1:T(8,128)}, u32[]{:S(2)}) copy-start(f32[512,64]{0,1:T(8,128)} %param.11) | copy-start | bytes 393220
  0.6 7.6 %collective-permute-start = (bf16[4,3584]{1,0:T(4,128)(2,1)}, bf16[4,3584]{1,0:T(4,128)(2,1)S(1)}, u32[]{:S(2)}, u32[]{:S(2)}) collective-permute-start(bf16[4,3584]{1,0:T(4,128)(2,1)} %param.8), channel_id=1, source_target_pairs={{0,8},{1,9},{2,10},{3,11},{4,12},{5,13},{6,14},{7,15},{8,16},{9,17... | collective-permute-start | bytes 86024 | tf_op jit(solution)/shard_map/ppermute | solution.py:100
  2.4 5.8 %collective-permute-start.2 = (bf16[4,3584]{1,0:T(4,128)(2,1)}, bf16[4,3584]{1,0:T(4,128)(2,1)S(1)}, u32[]{:S(2)}, u32[]{:S(2)}) collective-permute-start(bf16[4,3584]{1,0:T(4,128)(2,1)} %param.8), channel_id=1, source_target_pairs={{0,24},{1,25},{2,26},{3,27},{4,28},{5,29},{6,30},{7,31},{8,0},{9,1... | collective-permute-start | bytes 86024 | tf_op jit(solution)/shard_map/ppermute | solution.py:100
  4.0 5.6 %collective-permute-start.1 = (bf16[4,3584]{1,0:T(4,128)(2,1)}, bf16[4,3584]{1,0:T(4,128)(2,1)S(1)}, u32[]{:S(2)}, u32[]{:S(2)}) collective-permute-start(bf16[4,3584]{1,0:T(4,128)(2,1)} %param.8), channel_id=1, source_target_pairs={{0,16},{1,17},{2,18},{3,19},{4,20},{5,21},{6,22},{7,23},{8,24},{9,... | collective-permute-start | bytes 86024 | tf_op jit(solution)/shard_map/ppermute | solution.py:100
  9.7 12.0 %collective-permute-start.5 = (bf16[16,3584]{1,0:T(8,128)(2,1)S(1)}, bf16[16,3584]{1,0:T(8,128)(2,1)S(1)}, u32[]{:S(2)}, u32[]{:S(2)}) collective-permute-start(bf16[16,3584]{1,0:T(8,128)(2,1)S(1)} %reshape.485), channel_id=1, source_target_pairs={{0,96},{1,7},{2,98},{3,1},{4,100},{5,3},{6,102},{7,5},{8,104},{9,1... | collective-permute-start | bytes 344072 | tf_op jit(solution)/shard_map/ppermute | solution.py:100
  12.6 9.1 %collective-permute-start.4 = (bf16[16,3584]{1,0:T(8,128)(2,1)S(1)}, bf16[16,3584]{1,0:T(8,128)(2,1)S(1)}, u32[]{:S(2)}, u32[]{:S(2)}) collective-permute-start(bf16[16,3584]{1,0:T(8,128)(2,1)S(1)} %reshape.485), channel_id=1, source_target_pairs={{0,64},{1,5},{2,66},{3,7},{4,68},{5,1},{6,70},{7,3},{8,72},{9,13},... | collective-permute-start | bytes 344072 | tf_op jit(solution)/shard_map/ppermute | solution.py:100
  13.4 8.3 %collective-permute-start.3 = (bf16[16,3584]{1,0:T(8,128)(2,1)S(1)}, bf16[16,3584]{1,0:T(8,128)(2,1)S(1)}, u32[]{:S(2)}, u32[]{:S(2)}) collective-permute-start(bf16[16,3584]{1,0:T(8,128)(2,1)S(1)} %reshape.485), channel_id=1, source_target_pairs={{0,32},{1,3},{2,34},{3,5},{4,36},{5,7},{6,38},{7,1},{8,40},{9,11},... | collective-permute-start | bytes 344072 | tf_op jit(solution)/shard_map/ppermute | solution.py:100
  21.7 19.4 %slice-start = ((s8[8257536]{0:T(1024)(128)(4,1)}), s8[4194304]{0:T(1024)(128)(4,1)S(1)}, s32[]{:S(2)}) async-start(s8[8257536]{0:T(1024)(128)(4,1)} %bitcast.149), calls=%async_computation | async-start | bytes 8388608
  21.8 19.4 %slice-start.1 = ((s8[8257536]{0:T(1024)(128)(4,1)}), s8[4063232]{0:T(1024)(128)(4,1)S(1)}, s32[]{:S(2)}) async-start(s8[8257536]{0:T(1024)(128)(4,1)} %bitcast.149), calls=%async_computation.1 | async-start | bytes 8126464
  21.8 15.0 %collective-permute-start.8 = (bf16[64,3584]{1,0:T(8,128)(2,1)S(1)}, bf16[64,3584]{1,0:T(8,128)(2,1)S(1)}, u32[]{:S(2)}, u32[]{:S(2)}) collective-permute-start(bf16[64,3584]{1,0:T(8,128)(2,1)S(1)} %bitcast.153), channel_id=1, source_target_pairs={{0,6},{1,97},{2,0},{3,99},{4,2},{5,101},{6,4},{7,103},{8,14},{9,10... | collective-permute-start | bytes 1376264 | tf_op jit(solution)/shard_map/ppermute | solution.py:100
  25.9 10.9 %collective-permute-start.7 = (bf16[64,3584]{1,0:T(8,128)(2,1)S(1)}, bf16[64,3584]{1,0:T(8,128)(2,1)S(1)}, u32[]{:S(2)}, u32[]{:S(2)}) collective-permute-start(bf16[64,3584]{1,0:T(8,128)(2,1)S(1)} %bitcast.154), channel_id=1, source_target_pairs={{0,4},{1,65},{2,6},{3,67},{4,0},{5,69},{6,2},{7,71},{8,12},{9,73},... | collective-permute-start | bytes 1376264 | tf_op jit(solution)/shard_map/ppermute | solution.py:100
  25.9 14.6 %collective-permute-start.6 = (bf16[64,3584]{1,0:T(8,128)(2,1)S(1)}, bf16[64,3584]{1,0:T(8,128)(2,1)S(1)}, u32[]{:S(2)}, u32[]{:S(2)}) collective-permute-start(bf16[64,3584]{1,0:T(8,128)(2,1)S(1)} %bitcast.155), channel_id=1, source_target_pairs={{0,2},{1,33},{2,4},{3,35},{4,6},{5,37},{6,0},{7,39},{8,10},{9,41},... | collective-permute-start | bytes 1376264 | tf_op jit(solution)/shard_map/ppermute | solution.py:100
  40.7 5.1 %collective-permute-start.9 = (bf16[256,3584]{1,0:T(8,128)(2,1)S(1)}, bf16[256,3584]{1,0:T(8,128)(2,1)S(1)}, u32[]{:S(2)}, u32[]{:S(2)}) collective-permute-start(bf16[256,3584]{1,0:T(8,128)(2,1)S(1)} %bitcast.151), channel_id=1, source_target_pairs={{0,1},{1,0},{2,3},{3,2},{4,5},{5,4},{6,7},{7,6},{8,9},{9,8},{10,11... | collective-permute-start | bytes 5505032 | tf_op jit(solution)/shard_map/ppermute | solution.py:162
  50.8 1.3 %collective-permute-start.10 = (f32[3,512]{1,0:T(4,128)S(1)}, f32[3,512]{1,0:T(4,128)S(1)}, u32[]{:S(2)}, u32[]{:S(2)}) collective-permute-start(f32[3,512]{1,0:T(4,128)S(1)} %fusion.10), channel_id=1, source_target_pairs={{0,1},{1,0},{2,3},{3,2},{4,5},{5,4},{6,7},{7,6},{8,9},{9,8},{10,11... | collective-permute-start | bytes 18440 | tf_op jit(solution)/shard_map/ppermute | solution.py:100
  52.2 5.3 %collective-permute-start.12 = (f32[3,512]{1,0:T(4,128)S(1)}, f32[3,512]{1,0:T(4,128)S(1)}, u32[]{:S(2)}, u32[]{:S(2)}) collective-permute-start(f32[3,512]{1,0:T(4,128)S(1)} %get-tuple-element.219), channel_id=1, source_target_pairs={{0,4},{1,5},{2,6},{3,7},{4,0},{5,1},{6,2},{7,3},{8,12},{9,13},{10,... | collective-permute-start | bytes 18440 | tf_op jit(solution)/shard_map/ppermute | solution.py:100
  52.6 5.0 %collective-permute-start.11 = (f32[3,512]{1,0:T(4,128)S(1)}, f32[3,512]{1,0:T(4,128)S(1)}, u32[]{:S(2)}, u32[]{:S(2)}) collective-permute-start(f32[3,512]{1,0:T(4,128)S(1)} %get-tuple-element.219), channel_id=1, source_target_pairs={{0,2},{1,3},{2,4},{3,5},{4,6},{5,7},{6,0},{7,1},{8,10},{9,11},{10,... | collective-permute-start | bytes 18440 | tf_op jit(solution)/shard_map/ppermute | solution.py:100
  54.0 3.7 %collective-permute-start.13 = (f32[3,512]{1,0:T(4,128)S(1)}, f32[3,512]{1,0:T(4,128)S(1)}, u32[]{:S(2)}, u32[]{:S(2)}) collective-permute-start(f32[3,512]{1,0:T(4,128)S(1)} %get-tuple-element.219), channel_id=1, source_target_pairs={{0,6},{1,7},{2,0},{3,1},{4,2},{5,3},{6,4},{7,5},{8,14},{9,15},{10,... | collective-permute-start | bytes 18440 | tf_op jit(solution)/shard_map/ppermute | solution.py:100
  57.8 5.3 %collective-permute-start.15 = (f32[3,512]{1,0:T(4,128)S(1)}, f32[3,512]{1,0:T(4,128)S(1)}, u32[]{:S(2)}, u32[]{:S(2)}) collective-permute-start(f32[3,512]{1,0:T(4,128)S(1)} %get-tuple-element.217), channel_id=1, source_target_pairs={{0,16},{1,17},{2,18},{3,19},{4,20},{5,21},{6,22},{7,23},{8,24},{9,... | collective-permute-start | bytes 18440 | tf_op jit(solution)/shard_map/ppermute | solution.py:100
  59.9 4.9 %collective-permute-start.14 = (f32[3,512]{1,0:T(4,128)S(1)}, f32[3,512]{1,0:T(4,128)S(1)}, u32[]{:S(2)}, u32[]{:S(2)}) collective-permute-start(f32[3,512]{1,0:T(4,128)S(1)} %get-tuple-element.217), channel_id=1, source_target_pairs={{0,8},{1,9},{2,10},{3,11},{4,12},{5,13},{6,14},{7,15},{8,16},{9,17... | collective-permute-start | bytes 18440 | tf_op jit(solution)/shard_map/ppermute | solution.py:100
  60.6 4.2 %collective-permute-start.16 = (f32[3,512]{1,0:T(4,128)S(1)}, f32[3,512]{1,0:T(4,128)S(1)}, u32[]{:S(2)}, u32[]{:S(2)}) collective-permute-start(f32[3,512]{1,0:T(4,128)S(1)} %get-tuple-element.217), channel_id=1, source_target_pairs={{0,24},{1,25},{2,26},{3,27},{4,28},{5,29},{6,30},{7,31},{8,0},{9,1... | collective-permute-start | bytes 18440 | tf_op jit(solution)/shard_map/ppermute | solution.py:100
  64.9 5.2 %collective-permute-start.18 = (f32[3,512]{1,0:T(4,128)S(1)}, f32[3,512]{1,0:T(4,128)S(1)}, u32[]{:S(2)}, u32[]{:S(2)}) collective-permute-start(f32[3,512]{1,0:T(4,128)S(1)} %get-tuple-element.215), channel_id=1, source_target_pairs={{0,64},{1,65},{2,66},{3,67},{4,68},{5,69},{6,70},{7,71},{8,72},{9,... | collective-permute-start | bytes 18440 | tf_op jit(solution)/shard_map/ppermute | solution.py:100
  66.8 4.9 %collective-permute-start.17 = (f32[3,512]{1,0:T(4,128)S(1)}, f32[3,512]{1,0:T(4,128)S(1)}, u32[]{:S(2)}, u32[]{:S(2)}) collective-permute-start(f32[3,512]{1,0:T(4,128)S(1)} %get-tuple-element.215), channel_id=1, source_target_pairs={{0,32},{1,33},{2,34},{3,35},{4,36},{5,37},{6,38},{7,39},{8,40},{9,... | collective-permute-start | bytes 18440 | tf_op jit(solution)/shard_map/ppermute | solution.py:100
  68.2 3.7 %collective-permute-start.19 = (f32[3,512]{1,0:T(4,128)S(1)}, f32[3,512]{1,0:T(4,128)S(1)}, u32[]{:S(2)}, u32[]{:S(2)}) collective-permute-start(f32[3,512]{1,0:T(4,128)S(1)} %get-tuple-element.215), channel_id=1, source_target_pairs={{0,96},{1,97},{2,98},{3,99},{4,100},{5,101},{6,102},{7,103},{8,104... | collective-permute-start | bytes 18440 | tf_op jit(solution)/shard_map/ppermute | solution.py:100
  76.8 4.5 %collective-permute-start.20 = (bf16[256,3584]{1,0:T(8,128)(2,1)S(1)}, bf16[256,3584]{1,0:T(8,128)(2,1)S(1)}, u32[]{:S(2)}, u32[]{:S(2)}) collective-permute-start(bf16[256,3584]{1,0:T(8,128)(2,1)S(1)} %convolution_convert_fusion.1), channel_id=1, source_target_pairs={{0,1},{1,0},{2,3},{3,2},{4,5},{5,4},{6,7},{7,6},{8,9},{9,8},{10,11... | collective-permute-start | bytes 5505032 | tf_op jit(solution)/shard_map/ppermute | solution.py:206
  82.1 11.2 %collective-permute-start.21 = (bf16[64,3584]{1,0:T(8,128)(2,1)S(1)}, bf16[64,3584]{1,0:T(8,128)(2,1)S(1)}, u32[]{:S(2)}, u32[]{:S(2)}) collective-permute-start(bf16[64,3584]{1,0:T(8,128)(2,1)S(1)} %get-tuple-element.201), channel_id=1, source_target_pairs={{0,2},{1,33},{2,4},{3,35},{4,6},{5,37},{6,0},{7,39},{8,10},{9,41},... | collective-permute-start | bytes 1376264 | tf_op jit(solution)/shard_map/ppermute | solution.py:100
  83.9 9.5 %collective-permute-start.23 = (bf16[64,3584]{1,0:T(8,128)(2,1)S(1)}, bf16[64,3584]{1,0:T(8,128)(2,1)S(1)}, u32[]{:S(2)}, u32[]{:S(2)}) collective-permute-start(bf16[64,3584]{1,0:T(8,128)(2,1)S(1)} %get-tuple-element.202), channel_id=1, source_target_pairs={{0,6},{1,97},{2,0},{3,99},{4,2},{5,101},{6,4},{7,103},{8,14},{9,10... | collective-permute-start | bytes 1376264 | tf_op jit(solution)/shard_map/ppermute | solution.py:100
  85.4 12.6 %collective-permute-start.22 = (bf16[64,3584]{1,0:T(8,128)(2,1)S(1)}, bf16[64,3584]{1,0:T(8,128)(2,1)S(1)}, u32[]{:S(2)}, u32[]{:S(2)}) collective-permute-start(bf16[64,3584]{1,0:T(8,128)(2,1)S(1)} %get-tuple-element.203), channel_id=1, source_target_pairs={{0,4},{1,65},{2,6},{3,67},{4,0},{5,69},{6,2},{7,71},{8,12},{9,73},... | collective-permute-start | bytes 1376264 | tf_op jit(solution)/shard_map/ppermute | solution.py:100
  98.4 6.1 %collective-permute-start.24 = (bf16[16,3584]{1,0:T(8,128)(2,1)S(1)}, bf16[16,3584]{1,0:T(8,128)(2,1)S(1)}, u32[]{:S(2)}, u32[]{:S(2)}) collective-permute-start(bf16[16,3584]{1,0:T(8,128)(2,1)S(1)} %get-tuple-element.206), channel_id=1, source_target_pairs={{0,32},{1,3},{2,34},{3,5},{4,36},{5,7},{6,38},{7,1},{8,40},{9,11},... | collective-permute-start | bytes 344072 | tf_op jit(solution)/shard_map/ppermute | solution.py:100
  99.2 5.3 %collective-permute-start.26 = (bf16[16,3584]{1,0:T(8,128)(2,1)S(1)}, bf16[16,3584]{1,0:T(8,128)(2,1)S(1)}, u32[]{:S(2)}, u32[]{:S(2)}) collective-permute-start(bf16[16,3584]{1,0:T(8,128)(2,1)S(1)} %get-tuple-element.207), channel_id=1, source_target_pairs={{0,96},{1,7},{2,98},{3,1},{4,100},{5,3},{6,102},{7,5},{8,104},{9,1... | collective-permute-start | bytes 344072 | tf_op jit(solution)/shard_map/ppermute | solution.py:100
  101.8 6.3 %collective-permute-start.25 = (bf16[16,3584]{1,0:T(8,128)(2,1)S(1)}, bf16[16,3584]{1,0:T(8,128)(2,1)S(1)}, u32[]{:S(2)}, u32[]{:S(2)}) collective-permute-start(bf16[16,3584]{1,0:T(8,128)(2,1)S(1)} %get-tuple-element.208), channel_id=1, source_target_pairs={{0,64},{1,5},{2,66},{3,7},{4,68},{5,1},{6,70},{7,3},{8,72},{9,13},... | collective-permute-start | bytes 344072 | tf_op jit(solution)/shard_map/ppermute | solution.py:100
  108.2 5.3 %collective-permute-start.27 = (bf16[4,3584]{1,0:T(4,128)(2,1)S(1)}, bf16[4,3584]{1,0:T(4,128)(2,1)S(1)}, u32[]{:S(2)}, u32[]{:S(2)}) collective-permute-start(bf16[4,3584]{1,0:T(4,128)(2,1)S(1)} %get-tuple-element.209), channel_id=1, source_target_pairs={{0,8},{1,9},{2,10},{3,11},{4,12},{5,13},{6,14},{7,15},{8,16},{9,17... | collective-permute-start | bytes 86024 | tf_op jit(solution)/shard_map/ppermute | solution.py:100
  108.5 5.0 %collective-permute-start.29 = (bf16[4,3584]{1,0:T(4,128)(2,1)S(1)}, bf16[4,3584]{1,0:T(4,128)(2,1)S(1)}, u32[]{:S(2)}, u32[]{:S(2)}) collective-permute-start(bf16[4,3584]{1,0:T(4,128)(2,1)S(1)} %get-tuple-element.210), channel_id=1, source_target_pairs={{0,24},{1,25},{2,26},{3,27},{4,28},{5,29},{6,30},{7,31},{8,0},{9,1... | collective-permute-start | bytes 86024 | tf_op jit(solution)/shard_map/ppermute | solution.py:100
  111.5 5.4 %collective-permute-start.28 = (bf16[4,3584]{1,0:T(4,128)(2,1)S(1)}, bf16[4,3584]{1,0:T(4,128)(2,1)S(1)}, u32[]{:S(2)}, u32[]{:S(2)}) collective-permute-start(bf16[4,3584]{1,0:T(4,128)(2,1)S(1)} %get-tuple-element.211), channel_id=1, source_target_pairs={{0,16},{1,17},{2,18},{3,19},{4,20},{5,21},{6,22},{7,23},{8,24},{9,... | collective-permute-start | bytes 86024 | tf_op jit(solution)/shard_map/ppermute | solution.py:100

commit v12 on v10

--- a/solution.py
+++ b/solution.py
@@ -81,7 +81,9 @@
     for d in range(n_dev):
         x, y, z, c = device_coords(d, voc_n)
         axis = ring_axis(stage, c)
-        if axis == "c":
+        if axis == "v":
+            z, c = divmod((z * 2 + c + shift) % voc_n, 2)
+        elif axis == "c":
             c = c ^ 1
         elif axis == "x":
             x = (x + shift) % RING
@@ -94,7 +96,7 @@
 
 
 def exchange(block_for, stage, n_dev, voc_n):
-    n = 2 if stage == "c" else RING
+    n = {"c": 2, "v": voc_n}.get(stage, RING)
     got = [block_for(0)]
     for shift in range(1, n):
         got.append(lax.ppermute(block_for(shift), AXES, stage_pairs(stage, shift, n_dev, voc_n)))
@@ -178,7 +180,7 @@
 
     place = (rows[:, None] == jnp.arange(rows.shape[0], dtype=jnp.int32)[None, :]).astype(jnp.float32)
     stats = jnp.dot(stats, place, precision=lax.Precision.HIGHEST)
-    for stage in ("c", "z", "y", "x"):
+    for stage in ("v", "y", "x"):
         got = exchange(lambda s: stats, stage, n_dev, voc_n)
         peak = jnp.max(got[:, 0], axis=0)
         summed = jnp.sum(got[:, 1] * jnp.exp(got[:, 0] - peak[None]), axis=0)

time: 117 us -> 122 us (1.043)
  waiting for transfers between devices: 28.4 us -> 31.6 us
  starting transfers between devices: 44.2 us -> 45.5 us
    ppermute x28 -> x31, waiting for transfers between devices: 27.7 us -> 31 us  [exchange(): lax.ppermute(block_for(shift), AXES, stage_pairs(stage, shift, n_dev, voc...]
    ppermute x28 -> x31, starting transfers between devices: 43.6 us -> 44.9 us  [exchange(): lax.ppermute(block_for(shift), AXES, stage_pairs(stage, shift, n_dev, voc...]
  transfers between devices with their start and end apart: 30 -> 33, of which waited for: 14 -> 13; matrix products, arithmetic and copies ran while one was open for 25% -> 24% of each run, Pallas kernels for 0% -> 0%
where the time goes in v12:
time: 122 us; the launch traced here: 121 us
  starting transfers between devices  45.5 us (37%)
  waiting for transfers between devices  31.6 us (26%)
  matrix products  24.4 us (20%)
  other arithmetic  13.6 us (11%)
  local copies, waits for them, and re-layouts  4.53 us (4%)
  between operations  1.73 us (1%)
    ppermute x31, starting transfers between devices, exchange(): lax.ppermute(block_for(shift), AXES, stage_pairs(stage, shift, n_dev, voc...  44.9 us
    ppermute x31, waiting for transfers between devices, exchange(): lax.ppermute(block_for(shift), AXES, stage_pairs(stage, shift, n_dev, voc...  31 us
    dot_general x3, matrix products, half_logits(): lax.dot_general(rows_block, head_weight, (((1,), (1,)), ((), ())), prefer...  11.4 us
    dot_general x1, matrix products, per_device(): lax.dot_general(grad, every, (((0,), (0,)), ((), ())), preferred_element_...  6.72 us
    add x1, other arithmetic, compact_target(): target + jnp.where(slot_local[:, j:j + 1] == columns, slot_probs[:, j:j +...  3.57 us
    convert_element_type x2, other arithmetic, half_grad(): (loss_scale * (total_h[:, None] * jnp.exp(logits - lse_h[:, None]) - tgt)...  3.27 us
    dot_general x1, matrix products, per_device(): jnp.dot(grad_other, head_weight, preferred_element_type=jnp.float32)  2.6 us
    dot_general x1, matrix products, per_device(): acc = jnp.dot(grad_own, head_weight, preferred_element_type=jnp.float32)  2.59 us
  transfers between devices with their start and end apart: 33, of which 13 were waited for; matrix products, arithmetic and copies ran while one was open for 24% of the time, Pallas kernels for 0%

profile of v12, /device:TPU:0, one launch (start us, length us, event | category | flops | bytes accessed | tf_op | source)
XLA Modules:
  0.0 121.4 jit_solution(8650576363845516483)
XLA Ops:
  0.6 1.7 %collective-permute-start = (bf16[4,3584]{1,0:T(4,128)(2,1)}, bf16[4,3584]{1,0:T(4,128)(2,1)S(1)}, u32[]{:S(2)}, u32[]{:S(2)}) collective-permute-start(bf16[4,3584]{1,0:T(4,128)(2,1)} %param.8), channel_id=1, source_target_pairs={{0,8},{1,9},{2,10},{3,11},{4,12},{5,13},{6,14},{7,15},{8,16},{9,17... | collective-permute-start | bytes 86024 | tf_op jit(solution)/shard_map/ppermute | solution.py:102
  2.4 1.6 %collective-permute-start.2 = (bf16[4,3584]{1,0:T(4,128)(2,1)}, bf16[4,3584]{1,0:T(4,128)(2,1)S(1)}, u32[]{:S(2)}, u32[]{:S(2)}) collective-permute-start(bf16[4,3584]{1,0:T(4,128)(2,1)} %param.8), channel_id=1, source_target_pairs={{0,24},{1,25},{2,26},{3,27},{4,28},{5,29},{6,30},{7,31},{8,0},{9,1... | collective-permute-start | bytes 86024 | tf_op jit(solution)/shard_map/ppermute | solution.py:102
  4.0 2.1 %collective-permute-start.1 = (bf16[4,3584]{1,0:T(4,128)(2,1)}, bf16[4,3584]{1,0:T(4,128)(2,1)S(1)}, u32[]{:S(2)}, u32[]{:S(2)}) collective-permute-start(bf16[4,3584]{1,0:T(4,128)(2,1)} %param.8), channel_id=1, source_target_pairs={{0,16},{1,17},{2,18},{3,19},{4,20},{5,21},{6,22},{7,23},{8,24},{9,... | collective-permute-start | bytes 86024 | tf_op jit(solution)/shard_map/ppermute | solution.py:102
  6.1 1.0 copy.40
  7.2 1.0 gather_fusion.2
  8.2 1.3 %collective-permute-done.1 = bf16[4,3584]{1,0:T(4,128)(2,1)S(1)} collective-permute-done((bf16[4,3584]{1,0:T(4,128)(2,1)}, bf16[4,3584]{1,0:T(4,128)(2,1)S(1)}, u32[]{:S(2)}, u32[]{:S(2)}) %collective-permute-start.1) | collective-permute-done | bytes 28704 | tf_op jit(solution)/shard_map/ppermute | solution.py:102
  9.7 2.9 %collective-permute-start.5 = (bf16[16,3584]{1,0:T(8,128)(2,1)S(1)}, bf16[16,3584]{1,0:T(8,128)(2,1)S(1)}, u32[]{:S(2)}, u32[]{:S(2)}) collective-permute-start(bf16[16,3584]{1,0:T(8,128)(2,1)S(1)} %reshape.484), channel_id=1, source_target_pairs={{0,96},{1,7},{2,98},{3,1},{4,100},{5,3},{6,102},{7,5},{8,104},{9,1... | collective-permute-start | bytes 344072 | tf_op jit(solution)/shard_map/ppermute | solution.py:102
  12.6 0.8 collective-permute-start.4
  13.4 0.9 collective-permute-start.3
  15.8 5.8 %conditional.1 = (f32[512,1152]{1,0:T(8,128)}) conditional(s32[]{:T(128)} %convert_element_type.48, (s32[512,64]{1,0:T(8,128)S(1)}, pred[512]{0:T(512)(128)(4,1)S(1)}, f32[512,64]{0,1:T(8,128)S(1)}, s32[512,1]{0,1:T(1,128)S(1)}) %tuple.103, (s32[512,64]{1,0:T(8,128)S(1)}, pred[512]{0:T(512)(128)(4,1)S(1)}, f32[512,64]{0,1:T(8,128)S(1)}, ...), branch_computations={%region_3.7_spmd, %region_7.11_spmd} | conditional | flops 17916928 | bytes 5218828 | solution.py:44
  16.6 1.0 gather_fusion
  18.1 3.6 %select_add_fusion = f32[512,1152]{1,0:T(8,128)} fusion(f32[512]{0:T(512)S(1)} %bitcast.188, s32[512]{0:T(512)S(1)} %bitcast.180, f32[512]{0:T(512)S(1)} %bitcast.189, s32[512]{0:T(512)S(1)} %bitcast.181, f32[512]{0:T(512)S(1)} %bitcast.190, s32[512]{0:T(512)S(1)} %bitcast.182, f32[512]{0:T(512)S(1)} %bitcast.191, s32[512]{0:T(512)S(1)} %bitcast.183, ...), kind=kLoop, calls=%fused_computation.4 | loop fusion | flops 13565952 | bytes 2392064 | tf_op jit(solution)/shard_map/cond/branch_0_fun/add | solution.py:37
  21.8 4.1 %collective-permute-start.8 = (bf16[64,3584]{1,0:T(8,128)(2,1)S(1)}, bf16[64,3584]{1,0:T(8,128)(2,1)S(1)}, u32[]{:S(2)}, u32[]{:S(2)}) collective-permute-start(bf16[64,3584]{1,0:T(8,128)(2,1)S(1)} %bitcast.146), channel_id=1, source_target_pairs={{0,6},{1,97},{2,0},{3,99},{4,2},{5,101},{6,4},{7,103},{8,14},{9,10... | collective-permute-start | bytes 1376264 | tf_op jit(solution)/shard_map/ppermute | solution.py:102
  25.9 1.3 %collective-permute-start.6 = (bf16[64,3584]{1,0:T(8,128)(2,1)S(1)}, bf16[64,3584]{1,0:T(8,128)(2,1)S(1)}, u32[]{:S(2)}, u32[]{:S(2)}) collective-permute-start(bf16[64,3584]{1,0:T(8,128)(2,1)S(1)} %bitcast.148), channel_id=1, source_target_pairs={{0,2},{1,33},{2,4},{3,35},{4,6},{5,37},{6,0},{7,39},{8,10},{9,41},... | collective-permute-start | bytes 1376264 | tf_op jit(solution)/shard_map/ppermute | solution.py:102
  27.2 5.9 %fusion.90 = f32[64,1152]{1,0:T(8,128)S(1)} fusion(bf16[64,3584]{1,0:T(8,128)(2,1)S(1)} %bitcast.149, bf16[1152,3584]{1,0:T(8,128)(2,1)} %param.9), kind=kOutput, calls=%fused_computation.238 | convolution fusion | flops 528482304 | bytes 9011200 | tf_op jit(solution)/shard_map/dot_general | solution.py:135
  33.1 3.7 %collective-permute-done.8 = bf16[64,3584]{1,0:T(8,128)(2,1)S(1)} collective-permute-done((bf16[64,3584]{1,0:T(8,128)(2,1)S(1)}, bf16[64,3584]{1,0:T(8,128)(2,1)S(1)}, u32[]{:S(2)}, u32[]{:S(2)}) %collective-permute-start.8) | collective-permute-done | bytes 458784 | tf_op jit(solution)/shard_map/ppermute | solution.py:102
  36.8 3.7 %collective-permute-done.6 = bf16[64,3584]{1,0:T(8,128)(2,1)S(1)} collective-permute-done((bf16[64,3584]{1,0:T(8,128)(2,1)S(1)}, bf16[64,3584]{1,0:T(8,128)(2,1)S(1)}, u32[]{:S(2)}, u32[]{:S(2)}) %collective-permute-start.6) | collective-permute-done | bytes 458784 | tf_op jit(solution)/shard_map/ppermute | solution.py:102
  41.2 2.8 %fusion.91 = f32[192,1152]{1,0:T(8,128)S(1)} fusion(bf16[192,3584]{1,0:T(8,128)(2,1)S(1)} %bitcast.152, bf16[1152,3584]{1,0:T(8,128)(2,1)S(1)} %bitcast.143), kind=kOutput, calls=%fused_computation.239 | convolution fusion | flops 1585446912 | bytes 10518528 | tf_op jit(solution)/shard_map/dot_general | solution.py:135
  44.8 2.7 %fusion.89 = (f32[256]{0:T(256)S(1)}, f32[256,1152]{1,0:T(8,128)S(1)}) fusion(bf16[256,3584]{1,0:T(8,128)(2,1)S(1)} %collective-permute-done.9, bf16[1152,3584]{1,0:T(8,128)(2,1)S(1)} %bitcast.143), kind=kOutput, calls=%fused_computation.237 | convolution fusion | flops 2114223872 | bytes 11273216 | tf_op jit(solution)/shard_map/dot_general | solution.py:135
  47.5 2.3 %multiply_reduce_fusion.1 = (f32[256]{0:T(256)S(1)}, f32[256]{0:T(256)S(1)}, f32[256]{0:T(256)S(1)}, f32[256]{0:T(256)S(1)}) fusion(f32[512,1152]{1,0:T(8,128)} %get-tuple-element.258, f32[192,1152]{1,0:T(8,128)S(1)} %fusion.91, f32[64,1152]{1,0:T(8,128)S(1)} %fusion.90, f32[256,1152]{1,0:T(8,128)S(1)} %get-tuple-element.213, f32[256]{0:T(256)S(1)} %get-tuple-element.212, ...), kind=kLoop, calls=%fused_computation.43 | loop fusion | flops 2653184 | bytes 4724736 | tf_op jit(solution)/shard_map/reduce_sum | solution.py:175
  50.4 0.9 collective-permute-start.15
  51.3 1.0 collective-permute-start.14
  52.4 4.1 %collective-permute-start.13 = (f32[3,512]{1,0:T(4,128)S(1)}, f32[3,512]{1,0:T(4,128)S(1)}, u32[]{:S(2)}, u32[]{:S(2)}) collective-permute-start(f32[3,512]{1,0:T(4,128)S(1)} %get-tuple-element.215), channel_id=1, source_target_pairs={{0,4},{1,5},{2,6},{3,7},{4,0},{5,1},{6,2},{7,3},{8,12},{9,13},{10,... | collective-permute-start | bytes 18440 | tf_op jit(solution)/shard_map/ppermute | solution.py:102
  56.5 4.8 %collective-permute-done.11 = f32[3,512]{1,0:T(4,128)S(1)} collective-permute-done((f32[3,512]{1,0:T(4,128)S(1)}, f32[3,512]{1,0:T(4,128)S(1)}, u32[]{:S(2)}, u32[]{:S(2)}) %collective-permute-start.11) | collective-permute-done | bytes 6176 | tf_op jit(solution)/shard_map/ppermute | solution.py:102
  61.5 1.3 %collective-permute-done.16 = f32[3,512]{1,0:T(4,128)S(1)} collective-permute-done((f32[3,512]{1,0:T(4,128)S(1)}, f32[3,512]{1,0:T(4,128)S(1)}, u32[]{:S(2)}, u32[]{:S(2)}) %collective-permute-start.16) | collective-permute-done | bytes 6176 | tf_op jit(solution)/shard_map/ppermute | solution.py:102
  62.9 2.1 %collective-permute-start.18 = (f32[3,512]{1,0:T(4,128)S(1)}, f32[3,512]{1,0:T(4,128)S(1)}, u32[]{:S(2)}, u32[]{:S(2)}) collective-permute-start(f32[3,512]{1,0:T(4,128)S(1)} %get-tuple-element.207), channel_id=1, source_target_pairs={{0,16},{1,17},{2,18},{3,19},{4,20},{5,21},{6,22},{7,23},{8,24},{9,... | collective-permute-start | bytes 18440 | tf_op jit(solution)/shard_map/ppermute | solution.py:102
  65.6 2.6 %collective-permute-start.19 = (f32[3,512]{1,0:T(4,128)S(1)}, f32[3,512]{1,0:T(4,128)S(1)}, u32[]{:S(2)}, u32[]{:S(2)}) collective-permute-start(f32[3,512]{1,0:T(4,128)S(1)} %get-tuple-element.207), channel_id=1, source_target_pairs={{0,24},{1,25},{2,26},{3,27},{4,28},{5,29},{6,30},{7,31},{8,0},{9,1... | collective-permute-start | bytes 18440 | tf_op jit(solution)/shard_map/ppermute | solution.py:102
  68.2 1.6 %collective-permute-done.17 = f32[3,512]{1,0:T(4,128)S(1)} collective-permute-done((f32[3,512]{1,0:T(4,128)S(1)}, f32[3,512]{1,0:T(4,128)S(1)}, u32[]{:S(2)}, u32[]{:S(2)}) %collective-permute-start.17) | collective-permute-done | bytes 6176 | tf_op jit(solution)/shard_map/ppermute | solution.py:102
  69.9 1.9 %collective-permute-start.21 = (f32[3,512]{1,0:T(4,128)S(1)}, f32[3,512]{1,0:T(4,128)S(1)}, u32[]{:S(2)}, u32[]{:S(2)}) collective-permute-start(f32[3,512]{1,0:T(4,128)S(1)} %get-tuple-element.205), channel_id=1, source_target_pairs={{0,64},{1,65},{2,66},{3,67},{4,68},{5,69},{6,70},{7,71},{8,72},{9,... | collective-permute-start | bytes 18440 | tf_op jit(solution)/shard_map/ppermute | solution.py:102
  71.8 1.4 %collective-permute-start.20 = (f32[3,512]{1,0:T(4,128)S(1)}, f32[3,512]{1,0:T(4,128)S(1)}, u32[]{:S(2)}, u32[]{:S(2)}) collective-permute-start(f32[3,512]{1,0:T(4,128)S(1)} %get-tuple-element.205), channel_id=1, source_target_pairs={{0,32},{1,33},{2,34},{3,35},{4,36},{5,37},{6,38},{7,39},{8,40},{9,... | collective-permute-start | bytes 18440 | tf_op jit(solution)/shard_map/ppermute | solution.py:102
  73.2 1.9 %collective-permute-start.22 = (f32[3,512]{1,0:T(4,128)S(1)}, f32[3,512]{1,0:T(4,128)S(1)}, u32[]{:S(2)}, u32[]{:S(2)}) collective-permute-start(f32[3,512]{1,0:T(4,128)S(1)} %get-tuple-element.205), channel_id=1, source_target_pairs={{0,96},{1,97},{2,98},{3,99},{4,100},{5,101},{6,102},{7,103},{8,104... | collective-permute-start | bytes 18440 | tf_op jit(solution)/shard_map/ppermute | solution.py:102
  75.2 1.5 %collective-permute-done.20 = f32[3,512]{1,0:T(4,128)S(1)} collective-permute-done((f32[3,512]{1,0:T(4,128)S(1)}, f32[3,512]{1,0:T(4,128)S(1)}, u32[]{:S(2)}, u32[]{:S(2)}) %collective-permute-start.20) | collective-permute-done | bytes 6176 | tf_op jit(solution)/shard_map/ppermute | solution.py:102
  77.6 1.6 %multiply_convert_fusion.1 = bf16[256,1152]{1,0:T(8,128)(2,1)S(1)} fusion(f32[256,1152]{1,0:T(8,128)S(1)} %get-tuple-element.213, f32[512,1152]{1,0:T(8,128)} %get-tuple-element.258, f32[256]{0:T(256)S(1)} %bitcast.205, f32[256]{0:T(256)S(1)} %bitcast.206), kind=kLoop, calls=%fused_computation.41 | loop fusion | flops 1474560 | bytes 2951168 | tf_op jit(solution)/shard_map/convert_element_type | solution.py:201
  79.3 2.6 %convolution_convert_fusion.1 = bf16[256,3584]{1,0:T(8,128)(2,1)S(1)} fusion(bf16[256,1152]{1,0:T(8,128)(2,1)S(1)} %multiply_convert_fusion.1, bf16[1152,3584]{1,0:T(8,128)(2,1)S(1)} %bitcast.143), kind=kOutput, calls=%fused_computation.29 | convolution fusion | flops 2114846720 | bytes 10682368 | tf_op jit(solution)/shard_map/dot_general | solution.py:207
  82.2 1.6 %multiply_convert_fusion = bf16[256,1152]{1,0:T(8,128)(2,1)S(1)} fusion(f32[256,1152]{1,0:T(8,128)S(1)} %get-tuple-element.98, f32[512,1152]{1,0:T(8,128)} %get-tuple-element.258, f32[256]{0:T(256)S(1)} %bitcast.204, f32[256]{0:T(256)S(1)} %bitcast.203), kind=kLoop, calls=%fused_computation.40 | loop fusion | flops 1474560 | bytes 2951168 | tf_op jit(solution)/shard_map/convert_element_type | solution.py:201
  83.8 2.6 %fusion.92 = f32[256,3584]{1,0:T(8,128)S(1)} fusion(bf16[256,1152]{1,0:T(8,128)(2,1)S(1)} %multiply_convert_fusion, bf16[1152,3584]{1,0:T(8,128)(2,1)S(1)} %bitcast.143), kind=kOutput, calls=%fused_computation.240 | convolution fusion | flops 2113929216 | bytes 12517376 | tf_op jit(solution)/shard_map/dot_general | solution.py:211
  87.2 0.7 collective-permute-start.24
  87.8 2.6 %collective-permute-start.26 = (bf16[64,3584]{1,0:T(8,128)(2,1)S(1)}, bf16[64,3584]{1,0:T(8,128)(2,1)S(1)}, u32[]{:S(2)}, u32[]{:S(2)}) collective-permute-start(bf16[64,3584]{1,0:T(8,128)(2,1)S(1)} %get-tuple-element.192), channel_id=1, source_target_pairs={{0,6},{1,97},{2,0},{3,99},{4,2},{5,101},{6,4},{7,103},{8,14},{9,10... | collective-permute-start | bytes 1376264 | tf_op jit(solution)/shard_map/ppermute | solution.py:102
  90.5 6.7 %convolution_convert_fusion = bf16[1152,3584]{1,0:T(8,128)(2,1)} fusion(bf16[256,3584]{1,0:T(8,128)(2,1)S(1)} %collective-permute-done.9, bf16[256,3584]{1,0:T(8,128)(2,1)S(1)} %bitcast.145, bf16[256,1152]{1,0:T(8,128)(2,1)S(1)} %multiply_convert_fusion.1, bf16[256,1152]{1,0:T(8,128)(2,1)S(1)} %multiply_convert_fusion), kind=kOutput, calls=%fused_computation.28 | convolution fusion | flops 4241686528 | bytes 13107200 | tf_op jit(solution)/shard_map/dot_general | solution.py:215
  97.2 4.6 %collective-permute-done.24 = bf16[64,3584]{1,0:T(8,128)(2,1)S(1)} collective-permute-done((bf16[64,3584]{1,0:T(8,128)(2,1)S(1)}, bf16[64,3584]{1,0:T(8,128)(2,1)S(1)}, u32[]{:S(2)}, u32[]{:S(2)}) %collective-permute-start.24) | collective-permute-done | bytes 458784 | tf_op jit(solution)/shard_map/ppermute | solution.py:102
  102.3 0.7 collective-permute-start.27
  103.0 2.6 %collective-permute-start.29 = (bf16[16,3584]{1,0:T(8,128)(2,1)S(1)}, bf16[16,3584]{1,0:T(8,128)(2,1)S(1)}, u32[]{:S(2)}, u32[]{:S(2)}) collective-permute-start(bf16[16,3584]{1,0:T(8,128)(2,1)S(1)} %get-tuple-element.197), channel_id=1, source_target_pairs={{0,96},{1,7},{2,98},{3,1},{4,100},{5,3},{6,102},{7,5},{8,104},{9,1... | collective-permute-start | bytes 344072 | tf_op jit(solution)/shard_map/ppermute | solution.py:102
  105.6 1.5 %collective-permute-start.28 = (bf16[16,3584]{1,0:T(8,128)(2,1)S(1)}, bf16[16,3584]{1,0:T(8,128)(2,1)S(1)}, u32[]{:S(2)}, u32[]{:S(2)}) collective-permute-start(bf16[16,3584]{1,0:T(8,128)(2,1)S(1)} %get-tuple-element.198), channel_id=1, source_target_pairs={{0,64},{1,5},{2,66},{3,7},{4,68},{5,1},{6,70},{7,3},{8,72},{9,13},... | collective-permute-start | bytes 344072 | tf_op jit(solution)/shard_map/ppermute | solution.py:102
  107.1 1.2 %collective-permute-done.27 = bf16[16,3584]{1,0:T(8,128)(2,1)S(1)} collective-permute-done((bf16[16,3584]{1,0:T(8,128)(2,1)S(1)}, bf16[16,3584]{1,0:T(8,128)(2,1)S(1)}, u32[]{:S(2)}, u32[]{:S(2)}) %collective-permute-start.27) | collective-permute-done | bytes 114720 | tf_op jit(solution)/shard_map/ppermute | solution.py:102
  108.4 3.5 %collective-permute-done.28 = bf16[16,3584]{1,0:T(8,128)(2,1)S(1)} collective-permute-done((bf16[16,3584]{1,0:T(8,128)(2,1)S(1)}, bf16[16,3584]{1,0:T(8,128)(2,1)S(1)}, u32[]{:S(2)}, u32[]{:S(2)}) %collective-permute-start.28) | collective-permute-done | bytes 114720 | tf_op jit(solution)/shard_map/ppermute | solution.py:102
  112.4 3.0 %collective-permute-start.32 = (bf16[4,3584]{1,0:T(4,128)(2,1)S(1)}, bf16[4,3584]{1,0:T(4,128)(2,1)S(1)}, u32[]{:S(2)}, u32[]{:S(2)}) collective-permute-start(bf16[4,3584]{1,0:T(4,128)(2,1)S(1)} %get-tuple-element.200), channel_id=1, source_target_pairs={{0,24},{1,25},{2,26},{3,27},{4,28},{5,29},{6,30},{7,31},{8,0},{9,1... | collective-permute-start | bytes 86024 | tf_op jit(solution)/shard_map/ppermute | solution.py:102
  115.4 1.4 %collective-permute-start.31 = (bf16[4,3584]{1,0:T(4,128)(2,1)S(1)}, bf16[4,3584]{1,0:T(4,128)(2,1)S(1)}, u32[]{:S(2)}, u32[]{:S(2)}) collective-permute-start(bf16[4,3584]{1,0:T(4,128)(2,1)S(1)} %get-tuple-element.201), channel_id=1, source_target_pairs={{0,16},{1,17},{2,18},{3,19},{4,20},{5,21},{6,22},{7,23},{8,24},{9,... | collective-permute-start | bytes 86024 | tf_op jit(solution)/shard_map/ppermute | solution.py:102
  117.4 3.4 %collective-permute-done.31 = bf16[4,3584]{1,0:T(4,128)(2,1)S(1)} collective-permute-done((bf16[4,3584]{1,0:T(4,128)(2,1)S(1)}, bf16[4,3584]{1,0:T(4,128)(2,1)S(1)}, u32[]{:S(2)}, u32[]{:S(2)}) %collective-permute-start.31) | collective-permute-done | bytes 28704 | tf_op jit(solution)/shard_map/ppermute | solution.py:102
  (110 shorter events, 9.5 us)
Async XLA Ops:
  0.6 8.9 %copy-start.1 = (bf16[4,3584]{1,0:T(4,128)(2,1)S(1)}, bf16[4,3584]{1,0:T(4,128)(2,1)}, u32[]{:S(2)}) copy-start(bf16[4,3584]{1,0:T(4,128)(2,1)} %param.8) | copy-start | bytes 86020
  0.6 15.2 %copy-start = (f32[512,64]{0,1:T(8,128)S(1)}, f32[512,64]{0,1:T(8,128)}, u32[]{:S(2)}) copy-start(f32[512,64]{0,1:T(8,128)} %param.11) | copy-start | bytes 393220
  0.6 7.6 %collective-permute-start = (bf16[4,3584]{1,0:T(4,128)(2,1)}, bf16[4,3584]{1,0:T(4,128)(2,1)S(1)}, u32[]{:S(2)}, u32[]{:S(2)}) collective-permute-start(bf16[4,3584]{1,0:T(4,128)(2,1)} %param.8), channel_id=1, source_target_pairs={{0,8},{1,9},{2,10},{3,11},{4,12},{5,13},{6,14},{7,15},{8,16},{9,17... | collective-permute-start | bytes 86024 | tf_op jit(solution)/shard_map/ppermute | solution.py:102
  2.4 5.8 %collective-permute-start.2 = (bf16[4,3584]{1,0:T(4,128)(2,1)}, bf16[4,3584]{1,0:T(4,128)(2,1)S(1)}, u32[]{:S(2)}, u32[]{:S(2)}) collective-permute-start(bf16[4,3584]{1,0:T(4,128)(2,1)} %param.8), channel_id=1, source_target_pairs={{0,24},{1,25},{2,26},{3,27},{4,28},{5,29},{6,30},{7,31},{8,0},{9,1... | collective-permute-start | bytes 86024 | tf_op jit(solution)/shard_map/ppermute | solution.py:102
  4.0 5.6 %collective-permute-start.1 = (bf16[4,3584]{1,0:T(4,128)(2,1)}, bf16[4,3584]{1,0:T(4,128)(2,1)S(1)}, u32[]{:S(2)}, u32[]{:S(2)}) collective-permute-start(bf16[4,3584]{1,0:T(4,128)(2,1)} %param.8), channel_id=1, source_target_pairs={{0,16},{1,17},{2,18},{3,19},{4,20},{5,21},{6,22},{7,23},{8,24},{9,... | collective-permute-start | bytes 86024 | tf_op jit(solution)/shard_map/ppermute | solution.py:102
  9.7 12.0 %collective-permute-start.5 = (bf16[16,3584]{1,0:T(8,128)(2,1)S(1)}, bf16[16,3584]{1,0:T(8,128)(2,1)S(1)}, u32[]{:S(2)}, u32[]{:S(2)}) collective-permute-start(bf16[16,3584]{1,0:T(8,128)(2,1)S(1)} %reshape.484), channel_id=1, source_target_pairs={{0,96},{1,7},{2,98},{3,1},{4,100},{5,3},{6,102},{7,5},{8,104},{9,1... | collective-permute-start | bytes 344072 | tf_op jit(solution)/shard_map/ppermute | solution.py:102
  12.6 9.1 %collective-permute-start.4 = (bf16[16,3584]{1,0:T(8,128)(2,1)S(1)}, bf16[16,3584]{1,0:T(8,128)(2,1)S(1)}, u32[]{:S(2)}, u32[]{:S(2)}) collective-permute-start(bf16[16,3584]{1,0:T(8,128)(2,1)S(1)} %reshape.484), channel_id=1, source_target_pairs={{0,64},{1,5},{2,66},{3,7},{4,68},{5,1},{6,70},{7,3},{8,72},{9,13},... | collective-permute-start | bytes 344072 | tf_op jit(solution)/shard_map/ppermute | solution.py:102
  13.4 8.3 %collective-permute-start.3 = (bf16[16,3584]{1,0:T(8,128)(2,1)S(1)}, bf16[16,3584]{1,0:T(8,128)(2,1)S(1)}, u32[]{:S(2)}, u32[]{:S(2)}) collective-permute-start(bf16[16,3584]{1,0:T(8,128)(2,1)S(1)} %reshape.484), channel_id=1, source_target_pairs={{0,32},{1,3},{2,34},{3,5},{4,36},{5,7},{6,38},{7,1},{8,40},{9,11},... | collective-permute-start | bytes 344072 | tf_op jit(solution)/shard_map/ppermute | solution.py:102
  21.7 19.4 %slice-start = ((s8[8257536]{0:T(1024)(128)(4,1)}), s8[4194304]{0:T(1024)(128)(4,1)S(1)}, s32[]{:S(2)}) async-start(s8[8257536]{0:T(1024)(128)(4,1)} %bitcast.142), calls=%async_computation | async-start | bytes 8388608
  21.8 19.4 %slice-start.1 = ((s8[8257536]{0:T(1024)(128)(4,1)}), s8[4063232]{0:T(1024)(128)(4,1)S(1)}, s32[]{:S(2)}) async-start(s8[8257536]{0:T(1024)(128)(4,1)} %bitcast.142), calls=%async_computation.1 | async-start | bytes 8126464
  21.8 15.0 %collective-permute-start.8 = (bf16[64,3584]{1,0:T(8,128)(2,1)S(1)}, bf16[64,3584]{1,0:T(8,128)(2,1)S(1)}, u32[]{:S(2)}, u32[]{:S(2)}) collective-permute-start(bf16[64,3584]{1,0:T(8,128)(2,1)S(1)} %bitcast.146), channel_id=1, source_target_pairs={{0,6},{1,97},{2,0},{3,99},{4,2},{5,101},{6,4},{7,103},{8,14},{9,10... | collective-permute-start | bytes 1376264 | tf_op jit(solution)/shard_map/ppermute | solution.py:102
  25.9 10.9 %collective-permute-start.7 = (bf16[64,3584]{1,0:T(8,128)(2,1)S(1)}, bf16[64,3584]{1,0:T(8,128)(2,1)S(1)}, u32[]{:S(2)}, u32[]{:S(2)}) collective-permute-start(bf16[64,3584]{1,0:T(8,128)(2,1)S(1)} %bitcast.147), channel_id=1, source_target_pairs={{0,4},{1,65},{2,6},{3,67},{4,0},{5,69},{6,2},{7,71},{8,12},{9,73},... | collective-permute-start | bytes 1376264 | tf_op jit(solution)/shard_map/ppermute | solution.py:102
  25.9 14.6 %collective-permute-start.6 = (bf16[64,3584]{1,0:T(8,128)(2,1)S(1)}, bf16[64,3584]{1,0:T(8,128)(2,1)S(1)}, u32[]{:S(2)}, u32[]{:S(2)}) collective-permute-start(bf16[64,3584]{1,0:T(8,128)(2,1)S(1)} %bitcast.148), channel_id=1, source_target_pairs={{0,2},{1,33},{2,4},{3,35},{4,6},{5,37},{6,0},{7,39},{8,10},{9,41},... | collective-permute-start | bytes 1376264 | tf_op jit(solution)/shard_map/ppermute | solution.py:102
  40.7 4.0 %collective-permute-start.9 = (bf16[256,3584]{1,0:T(8,128)(2,1)S(1)}, bf16[256,3584]{1,0:T(8,128)(2,1)S(1)}, u32[]{:S(2)}, u32[]{:S(2)}) collective-permute-start(bf16[256,3584]{1,0:T(8,128)(2,1)S(1)} %bitcast.144), channel_id=1, source_target_pairs={{0,1},{1,0},{2,3},{3,2},{4,5},{5,4},{6,7},{7,6},{8,9},{9,8},{10,11... | collective-permute-start | bytes 5505032 | tf_op jit(solution)/shard_map/ppermute | solution.py:164
  50.3 6.2 %collective-permute-start.10 = (f32[3,512]{1,0:T(4,128)S(1)}, f32[3,512]{1,0:T(4,128)S(1)}, u32[]{:S(2)}, u32[]{:S(2)}) collective-permute-start(f32[3,512]{1,0:T(4,128)S(1)} %get-tuple-element.215), channel_id=1, source_target_pairs={{0,1},{1,2},{2,3},{3,4},{4,5},{5,6},{6,7},{7,0},{8,9},{9,10},{10,1... | collective-permute-start | bytes 18440 | tf_op jit(solution)/shard_map/ppermute | solution.py:102
  50.4 11.0 %collective-permute-start.15 = (f32[3,512]{1,0:T(4,128)S(1)}, f32[3,512]{1,0:T(4,128)S(1)}, u32[]{:S(2)}, u32[]{:S(2)}) collective-permute-start(f32[3,512]{1,0:T(4,128)S(1)} %get-tuple-element.215), channel_id=1, source_target_pairs={{0,6},{1,7},{2,0},{3,1},{4,2},{5,3},{6,4},{7,5},{8,14},{9,15},{10,... | collective-permute-start | bytes 18440 | tf_op jit(solution)/shard_map/ppermute | solution.py:102
  51.3 10.1 %collective-permute-start.14 = (f32[3,512]{1,0:T(4,128)S(1)}, f32[3,512]{1,0:T(4,128)S(1)}, u32[]{:S(2)}, u32[]{:S(2)}) collective-permute-start(f32[3,512]{1,0:T(4,128)S(1)} %get-tuple-element.215), channel_id=1, source_target_pairs={{0,5},{1,6},{2,7},{3,0},{4,1},{5,2},{6,3},{7,4},{8,13},{9,14},{10,... | collective-permute-start | bytes 18440 | tf_op jit(solution)/shard_map/ppermute | solution.py:102
  52.4 9.0 %collective-permute-start.13 = (f32[3,512]{1,0:T(4,128)S(1)}, f32[3,512]{1,0:T(4,128)S(1)}, u32[]{:S(2)}, u32[]{:S(2)}) collective-permute-start(f32[3,512]{1,0:T(4,128)S(1)} %get-tuple-element.215), channel_id=1, source_target_pairs={{0,4},{1,5},{2,6},{3,7},{4,0},{5,1},{6,2},{7,3},{8,12},{9,13},{10,... | collective-permute-start | bytes 18440 | tf_op jit(solution)/shard_map/ppermute | solution.py:102
  56.5 4.9 %collective-permute-start.12 = (f32[3,512]{1,0:T(4,128)S(1)}, f32[3,512]{1,0:T(4,128)S(1)}, u32[]{:S(2)}, u32[]{:S(2)}) collective-permute-start(f32[3,512]{1,0:T(4,128)S(1)} %get-tuple-element.215), channel_id=1, source_target_pairs={{0,3},{1,4},{2,5},{3,6},{4,7},{5,0},{6,1},{7,2},{8,11},{9,12},{10,... | collective-permute-start | bytes 18440 | tf_op jit(solution)/shard_map/ppermute | solution.py:102
  56.5 4.9 %collective-permute-start.11 = (f32[3,512]{1,0:T(4,128)S(1)}, f32[3,512]{1,0:T(4,128)S(1)}, u32[]{:S(2)}, u32[]{:S(2)}) collective-permute-start(f32[3,512]{1,0:T(4,128)S(1)} %get-tuple-element.215), channel_id=1, source_target_pairs={{0,2},{1,3},{2,4},{3,5},{4,6},{5,7},{6,0},{7,1},{8,10},{9,11},{10,... | collective-permute-start | bytes 18440 | tf_op jit(solution)/shard_map/ppermute | solution.py:102
  61.4 1.4 %collective-permute-start.16 = (f32[3,512]{1,0:T(4,128)S(1)}, f32[3,512]{1,0:T(4,128)S(1)}, u32[]{:S(2)}, u32[]{:S(2)}) collective-permute-start(f32[3,512]{1,0:T(4,128)S(1)} %get-tuple-element.215), channel_id=1, source_target_pairs={{0,7},{1,0},{2,1},{3,2},{4,3},{5,4},{6,5},{7,6},{8,15},{9,8},{10,9... | collective-permute-start | bytes 18440 | tf_op jit(solution)/shard_map/ppermute | solution.py:102
  62.9 5.3 %collective-permute-start.18 = (f32[3,512]{1,0:T(4,128)S(1)}, f32[3,512]{1,0:T(4,128)S(1)}, u32[]{:S(2)}, u32[]{:S(2)}) collective-permute-start(f32[3,512]{1,0:T(4,128)S(1)} %get-tuple-element.207), channel_id=1, source_target_pairs={{0,16},{1,17},{2,18},{3,19},{4,20},{5,21},{6,22},{7,23},{8,24},{9,... | collective-permute-start | bytes 18440 | tf_op jit(solution)/shard_map/ppermute | solution.py:102
  64.9 4.9 %collective-permute-start.17 = (f32[3,512]{1,0:T(4,128)S(1)}, f32[3,512]{1,0:T(4,128)S(1)}, u32[]{:S(2)}, u32[]{:S(2)}) collective-permute-start(f32[3,512]{1,0:T(4,128)S(1)} %get-tuple-element.207), channel_id=1, source_target_pairs={{0,8},{1,9},{2,10},{3,11},{4,12},{5,13},{6,14},{7,15},{8,16},{9,17... | collective-permute-start | bytes 18440 | tf_op jit(solution)/shard_map/ppermute | solution.py:102
  65.6 4.2 %collective-permute-start.19 = (f32[3,512]{1,0:T(4,128)S(1)}, f32[3,512]{1,0:T(4,128)S(1)}, u32[]{:S(2)}, u32[]{:S(2)}) collective-permute-start(f32[3,512]{1,0:T(4,128)S(1)} %get-tuple-element.207), channel_id=1, source_target_pairs={{0,24},{1,25},{2,26},{3,27},{4,28},{5,29},{6,30},{7,31},{8,0},{9,1... | collective-permute-start | bytes 18440 | tf_op jit(solution)/shard_map/ppermute | solution.py:102
  69.9 5.2 %collective-permute-start.21 = (f32[3,512]{1,0:T(4,128)S(1)}, f32[3,512]{1,0:T(4,128)S(1)}, u32[]{:S(2)}, u32[]{:S(2)}) collective-permute-start(f32[3,512]{1,0:T(4,128)S(1)} %get-tuple-element.205), channel_id=1, source_target_pairs={{0,64},{1,65},{2,66},{3,67},{4,68},{5,69},{6,70},{7,71},{8,72},{9,... | collective-permute-start | bytes 18440 | tf_op jit(solution)/shard_map/ppermute | solution.py:102
  71.8 4.9 %collective-permute-start.20 = (f32[3,512]{1,0:T(4,128)S(1)}, f32[3,512]{1,0:T(4,128)S(1)}, u32[]{:S(2)}, u32[]{:S(2)}) collective-permute-start(f32[3,512]{1,0:T(4,128)S(1)} %get-tuple-element.205), channel_id=1, source_target_pairs={{0,32},{1,33},{2,34},{3,35},{4,36},{5,37},{6,38},{7,39},{8,40},{9,... | collective-permute-start | bytes 18440 | tf_op jit(solution)/shard_map/ppermute | solution.py:102
  73.2 3.7 %collective-permute-start.22 = (f32[3,512]{1,0:T(4,128)S(1)}, f32[3,512]{1,0:T(4,128)S(1)}, u32[]{:S(2)}, u32[]{:S(2)}) collective-permute-start(f32[3,512]{1,0:T(4,128)S(1)} %get-tuple-element.205), channel_id=1, source_target_pairs={{0,96},{1,97},{2,98},{3,99},{4,100},{5,101},{6,102},{7,103},{8,104... | collective-permute-start | bytes 18440 | tf_op jit(solution)/shard_map/ppermute | solution.py:102
  81.9 4.5 %collective-permute-start.23 = (bf16[256,3584]{1,0:T(8,128)(2,1)S(1)}, bf16[256,3584]{1,0:T(8,128)(2,1)S(1)}, u32[]{:S(2)}, u32[]{:S(2)}) collective-permute-start(bf16[256,3584]{1,0:T(8,128)(2,1)S(1)} %convolution_convert_fusion.1), channel_id=1, source_target_pairs={{0,1},{1,0},{2,3},{3,2},{4,5},{5,4},{6,7},{7,6},{8,9},{9,8},{10,11... | collective-permute-start | bytes 5505032 | tf_op jit(solution)/shard_map/ppermute | solution.py:208
  87.2 14.7 %collective-permute-start.24 = (bf16[64,3584]{1,0:T(8,128)(2,1)S(1)}, bf16[64,3584]{1,0:T(8,128)(2,1)S(1)}, u32[]{:S(2)}, u32[]{:S(2)}) collective-permute-start(bf16[64,3584]{1,0:T(8,128)(2,1)S(1)} %get-tuple-element.191), channel_id=1, source_target_pairs={{0,2},{1,33},{2,4},{3,35},{4,6},{5,37},{6,0},{7,39},{8,10},{9,41},... | collective-permute-start | bytes 1376264 | tf_op jit(solution)/shard_map/ppermute | solution.py:102
  87.8 14.0 %collective-permute-start.26 = (bf16[64,3584]{1,0:T(8,128)(2,1)S(1)}, bf16[64,3584]{1,0:T(8,128)(2,1)S(1)}, u32[]{:S(2)}, u32[]{:S(2)}) collective-permute-start(bf16[64,3584]{1,0:T(8,128)(2,1)S(1)} %get-tuple-element.192), channel_id=1, source_target_pairs={{0,6},{1,97},{2,0},{3,99},{4,2},{5,101},{6,4},{7,103},{8,14},{9,10... | collective-permute-start | bytes 1376264 | tf_op jit(solution)/shard_map/ppermute | solution.py:102
  90.5 11.4 %collective-permute-start.25 = (bf16[64,3584]{1,0:T(8,128)(2,1)S(1)}, bf16[64,3584]{1,0:T(8,128)(2,1)S(1)}, u32[]{:S(2)}, u32[]{:S(2)}) collective-permute-start(bf16[64,3584]{1,0:T(8,128)(2,1)S(1)} %get-tuple-element.193), channel_id=1, source_target_pairs={{0,4},{1,65},{2,6},{3,67},{4,0},{5,69},{6,2},{7,71},{8,12},{9,73},... | collective-permute-start | bytes 1376264 | tf_op jit(solution)/shard_map/ppermute | solution.py:102
  102.3 6.1 %collective-permute-start.27 = (bf16[16,3584]{1,0:T(8,128)(2,1)S(1)}, bf16[16,3584]{1,0:T(8,128)(2,1)S(1)}, u32[]{:S(2)}, u32[]{:S(2)}) collective-permute-start(bf16[16,3584]{1,0:T(8,128)(2,1)S(1)} %get-tuple-element.196), channel_id=1, source_target_pairs={{0,32},{1,3},{2,34},{3,5},{4,36},{5,7},{6,38},{7,1},{8,40},{9,11},... | collective-permute-start | bytes 344072 | tf_op jit(solution)/shard_map/ppermute | solution.py:102
  103.0 5.3 %collective-permute-start.29 = (bf16[16,3584]{1,0:T(8,128)(2,1)S(1)}, bf16[16,3584]{1,0:T(8,128)(2,1)S(1)}, u32[]{:S(2)}, u32[]{:S(2)}) collective-permute-start(bf16[16,3584]{1,0:T(8,128)(2,1)S(1)} %get-tuple-element.197), channel_id=1, source_target_pairs={{0,96},{1,7},{2,98},{3,1},{4,100},{5,3},{6,102},{7,5},{8,104},{9,1... | collective-permute-start | bytes 344072 | tf_op jit(solution)/shard_map/ppermute | solution.py:102
  105.6 6.3 %collective-permute-start.28 = (bf16[16,3584]{1,0:T(8,128)(2,1)S(1)}, bf16[16,3584]{1,0:T(8,128)(2,1)S(1)}, u32[]{:S(2)}, u32[]{:S(2)}) collective-permute-start(bf16[16,3584]{1,0:T(8,128)(2,1)S(1)} %get-tuple-element.198), channel_id=1, source_target_pairs={{0,64},{1,5},{2,66},{3,7},{4,68},{5,1},{6,70},{7,3},{8,72},{9,13},... | collective-permute-start | bytes 344072 | tf_op jit(solution)/shard_map/ppermute | solution.py:102
  112.0 5.3 %collective-permute-start.30 = (bf16[4,3584]{1,0:T(4,128)(2,1)S(1)}, bf16[4,3584]{1,0:T(4,128)(2,1)S(1)}, u32[]{:S(2)}, u32[]{:S(2)}) collective-permute-start(bf16[4,3584]{1,0:T(4,128)(2,1)S(1)} %get-tuple-element.199), channel_id=1, source_target_pairs={{0,8},{1,9},{2,10},{3,11},{4,12},{5,13},{6,14},{7,15},{8,16},{9,17... | collective-permute-start | bytes 86024 | tf_op jit(solution)/shard_map/ppermute | solution.py:102
  112.4 5.0 %collective-permute-start.32 = (bf16[4,3584]{1,0:T(4,128)(2,1)S(1)}, bf16[4,3584]{1,0:T(4,128)(2,1)S(1)}, u32[]{:S(2)}, u32[]{:S(2)}) collective-permute-start(bf16[4,3584]{1,0:T(4,128)(2,1)S(1)} %get-tuple-element.200), channel_id=1, source_target_pairs={{0,24},{1,25},{2,26},{3,27},{4,28},{5,29},{6,30},{7,31},{8,0},{9,1... | collective-permute-start | bytes 86024 | tf_op jit(solution)/shard_map/ppermute | solution.py:102
  115.4 5.4 %collective-permute-start.31 = (bf16[4,3584]{1,0:T(4,128)(2,1)S(1)}, bf16[4,3584]{1,0:T(4,128)(2,1)S(1)}, u32[]{:S(2)}, u32[]{:S(2)}) collective-permute-start(bf16[4,3584]{1,0:T(4,128)(2,1)S(1)} %get-tuple-element.201), channel_id=1, source_target_pairs={{0,16},{1,17},{2,18},{3,19},{4,20},{5,21},{6,22},{7,23},{8,24},{9,... | collective-permute-start | bytes 86024 | tf_op jit(solution)/shard_map/ppermute | solution.py:102

commit v13 on v12

--- a/solution.py
+++ b/solution.py
@@ -81,8 +81,9 @@
     for d in range(n_dev):
         x, y, z, c = device_coords(d, voc_n)
         axis = ring_axis(stage, c)
-        if axis == "v":
-            z, c = divmod((z * 2 + c + shift) % voc_n, 2)
+        if axis in ("x1", "x2", "y1", "y2", "z1", "z2"):
+            bit = int(axis[1])
+            x, y, z = (x ^ bit, y, z) if axis[0] == "x" else (x, y ^ bit, z) if axis[0] == "y" else (x, y, z ^ bit)
         elif axis == "c":
             c = c ^ 1
         elif axis == "x":
@@ -96,7 +97,7 @@
 
 
 def exchange(block_for, stage, n_dev, voc_n):
-    n = {"c": 2, "v": voc_n}.get(stage, RING)
+    n = 2 if (stage == "c" or stage[0] in "xyz" and stage[1:] in ("1", "2")) else RING
     got = [block_for(0)]
     for shift in range(1, n):
         got.append(lax.ppermute(block_for(shift), AXES, stage_pairs(stage, shift, n_dev, voc_n)))
@@ -180,7 +181,7 @@
 
     place = (rows[:, None] == jnp.arange(rows.shape[0], dtype=jnp.int32)[None, :]).astype(jnp.float32)
     stats = jnp.dot(stats, place, precision=lax.Precision.HIGHEST)
-    for stage in ("v", "y", "x"):
+    for stage in ("c", "z1", "z2", "y1", "y2", "x1", "x2"):
         got = exchange(lambda s: stats, stage, n_dev, voc_n)
         peak = jnp.max(got[:, 0], axis=0)
         summed = jnp.sum(got[:, 1] * jnp.exp(got[:, 0] - peak[None]), axis=0)

time: 122 us -> 123 us (level)
  waiting for transfers between devices: 31.6 us -> 44.5 us
  starting transfers between devices: 45.5 us -> 34.1 us
    ppermute x31 -> x25, waiting for transfers between devices: 31 us -> 43.9 us  [exchange(): lax.ppermute(block_for(shift), AXES, stage_pairs(stage, shift, n_dev, voc...]
    ppermute x31 -> x25, starting transfers between devices: 44.9 us -> 33.8 us  [exchange(): lax.ppermute(block_for(shift), AXES, stage_pairs(stage, shift, n_dev, voc...]
  transfers between devices with their start and end apart: 33 -> 27, of which waited for: 13 -> 17; matrix products, arithmetic and copies ran while one was open for 24% -> 24% of each run, Pallas kernels for 0% -> 0%
where the time goes in v13:
time: 123 us
  waiting for transfers between devices  44.5 us (36%)
  starting transfers between devices  34.1 us (28%)
  matrix products  24.4 us (20%)
  other arithmetic  13.8 us (11%)
  local copies, waits for them, and re-layouts  4.49 us (4%)
  between operations  1.7 us (1%)
    ppermute x25, waiting for transfers between devices, exchange(): lax.ppermute(block_for(shift), AXES, stage_pairs(stage, shift, n_dev, voc...  43.9 us
    ppermute x25, starting transfers between devices, exchange(): lax.ppermute(block_for(shift), AXES, stage_pairs(stage, shift, n_dev, voc...  33.8 us
    dot_general x3, matrix products, half_logits(): lax.dot_general(rows_block, head_weight, (((1,), (1,)), ((), ())), prefer...  11.4 us
    dot_general x1, matrix products, per_device(): lax.dot_general(grad, every, (((0,), (0,)), ((), ())), preferred_element_...  6.72 us
    add x1, other arithmetic, compact_target(): target + jnp.where(slot_local[:, j:j + 1] == columns, slot_probs[:, j:j +...  3.57 us
    convert_element_type x2, other arithmetic, half_grad(): (loss_scale * (total_h[:, None] * jnp.exp(logits - lse_h[:, None]) - tgt)...  3.27 us
    dot_general x1, matrix products, per_device(): jnp.dot(grad_other, head_weight, preferred_element_type=jnp.float32)  2.6 us
    dot_general x1, matrix products, per_device(): acc = jnp.dot(grad_own, head_weight, preferred_element_type=jnp.float32)  2.59 us
  transfers between devices with their start and end apart: 27, of which 17 were waited for; matrix products, arithmetic and copies ran while one was open for 24% of the time, Pallas kernels for 0%

profile of v13, /device:TPU:0, one launch (start us, length us, event | category | flops | bytes accessed | tf_op | source)
XLA Modules:
  0.0 123.2 jit_solution(13746046000307808672)
XLA Ops:
  0.6 1.7 %collective-permute-start = (bf16[4,3584]{1,0:T(4,128)(2,1)}, bf16[4,3584]{1,0:T(4,128)(2,1)S(1)}, u32[]{:S(2)}, u32[]{:S(2)}) collective-permute-start(bf16[4,3584]{1,0:T(4,128)(2,1)} %param.8), channel_id=1, source_target_pairs={{0,8},{1,9},{2,10},{3,11},{4,12},{5,13},{6,14},{7,15},{8,16},{9,17... | collective-permute-start | bytes 86024 | tf_op jit(solution)/shard_map/ppermute | solution.py:103
  2.4 1.6 %collective-permute-start.2 = (bf16[4,3584]{1,0:T(4,128)(2,1)}, bf16[4,3584]{1,0:T(4,128)(2,1)S(1)}, u32[]{:S(2)}, u32[]{:S(2)}) collective-permute-start(bf16[4,3584]{1,0:T(4,128)(2,1)} %param.8), channel_id=1, source_target_pairs={{0,24},{1,25},{2,26},{3,27},{4,28},{5,29},{6,30},{7,31},{8,0},{9,1... | collective-permute-start | bytes 86024 | tf_op jit(solution)/shard_map/ppermute | solution.py:103
  4.0 2.1 %collective-permute-start.1 = (bf16[4,3584]{1,0:T(4,128)(2,1)}, bf16[4,3584]{1,0:T(4,128)(2,1)S(1)}, u32[]{:S(2)}, u32[]{:S(2)}) collective-permute-start(bf16[4,3584]{1,0:T(4,128)(2,1)} %param.8), channel_id=1, source_target_pairs={{0,16},{1,17},{2,18},{3,19},{4,20},{5,21},{6,22},{7,23},{8,24},{9,... | collective-permute-start | bytes 86024 | tf_op jit(solution)/shard_map/ppermute | solution.py:103
  6.1 1.0 copy.48
  7.2 1.0 gather_fusion.2
  8.2 1.3 %collective-permute-done.1 = bf16[4,3584]{1,0:T(4,128)(2,1)S(1)} collective-permute-done((bf16[4,3584]{1,0:T(4,128)(2,1)}, bf16[4,3584]{1,0:T(4,128)(2,1)S(1)}, u32[]{:S(2)}, u32[]{:S(2)}) %collective-permute-start.1) | collective-permute-done | bytes 28704 | tf_op jit(solution)/shard_map/ppermute | solution.py:103
  9.7 2.9 %collective-permute-start.5 = (bf16[16,3584]{1,0:T(8,128)(2,1)S(1)}, bf16[16,3584]{1,0:T(8,128)(2,1)S(1)}, u32[]{:S(2)}, u32[]{:S(2)}) collective-permute-start(bf16[16,3584]{1,0:T(8,128)(2,1)S(1)} %reshape.488), channel_id=1, source_target_pairs={{0,96},{1,7},{2,98},{3,1},{4,100},{5,3},{6,102},{7,5},{8,104},{9,1... | collective-permute-start | bytes 344072 | tf_op jit(solution)/shard_map/ppermute | solution.py:103
  12.6 0.8 collective-permute-start.4
  13.4 0.9 collective-permute-start.3
  14.5 0.6 compare_reduce_fusion
  15.8 5.8 %conditional.1 = (f32[512,1152]{1,0:T(8,128)}) conditional(s32[]{:T(128)} %convert_element_type.48, (s32[512,64]{1,0:T(8,128)S(1)}, pred[512]{0:T(512)(128)(4,1)S(1)}, f32[512,64]{0,1:T(8,128)S(1)}, s32[512,1]{0,1:T(1,128)S(1)}) %tuple.116, (s32[512,64]{1,0:T(8,128)S(1)}, pred[512]{0:T(512)(128)(4,1)S(1)}, f32[512,64]{0,1:T(8,128)S(1)}, ...), branch_computations={%region_3.7_spmd, %region_7.11_spmd} | conditional | flops 17916928 | bytes 5218828 | solution.py:44
  16.6 1.0 gather_fusion
  18.1 3.6 %select_add_fusion = f32[512,1152]{1,0:T(8,128)} fusion(f32[512]{0:T(512)S(1)} %bitcast.234, s32[512]{0:T(512)S(1)} %bitcast.225, f32[512]{0:T(512)S(1)} %bitcast.235, s32[512]{0:T(512)S(1)} %bitcast.226, f32[512]{0:T(512)S(1)} %bitcast.236, s32[512]{0:T(512)S(1)} %bitcast.227, f32[512]{0:T(512)S(1)} %bitcast.237, s32[512]{0:T(512)S(1)} %bitcast.228, ...), kind=kLoop, calls=%fused_computation.4 | loop fusion | flops 13565952 | bytes 2392064 | tf_op jit(solution)/shard_map/cond/branch_0_fun/add | solution.py:37
  21.8 4.1 %collective-permute-start.8 = (bf16[64,3584]{1,0:T(8,128)(2,1)S(1)}, bf16[64,3584]{1,0:T(8,128)(2,1)S(1)}, u32[]{:S(2)}, u32[]{:S(2)}) collective-permute-start(bf16[64,3584]{1,0:T(8,128)(2,1)S(1)} %bitcast.188), channel_id=1, source_target_pairs={{0,6},{1,97},{2,0},{3,99},{4,2},{5,101},{6,4},{7,103},{8,14},{9,10... | collective-permute-start | bytes 1376264 | tf_op jit(solution)/shard_map/ppermute | solution.py:103
  25.9 1.3 %collective-permute-start.6 = (bf16[64,3584]{1,0:T(8,128)(2,1)S(1)}, bf16[64,3584]{1,0:T(8,128)(2,1)S(1)}, u32[]{:S(2)}, u32[]{:S(2)}) collective-permute-start(bf16[64,3584]{1,0:T(8,128)(2,1)S(1)} %bitcast.190), channel_id=1, source_target_pairs={{0,2},{1,33},{2,4},{3,35},{4,6},{5,37},{6,0},{7,39},{8,10},{9,41},... | collective-permute-start | bytes 1376264 | tf_op jit(solution)/shard_map/ppermute | solution.py:103
  27.2 5.9 %fusion.139 = f32[64,1152]{1,0:T(8,128)S(1)} fusion(bf16[64,3584]{1,0:T(8,128)(2,1)S(1)} %bitcast.191, bf16[1152,3584]{1,0:T(8,128)(2,1)} %param.9), kind=kOutput, calls=%fused_computation.304 | convolution fusion | flops 528482304 | bytes 9011200 | tf_op jit(solution)/shard_map/dot_general | solution.py:136
  33.1 3.7 %collective-permute-done.8 = bf16[64,3584]{1,0:T(8,128)(2,1)S(1)} collective-permute-done((bf16[64,3584]{1,0:T(8,128)(2,1)S(1)}, bf16[64,3584]{1,0:T(8,128)(2,1)S(1)}, u32[]{:S(2)}, u32[]{:S(2)}) %collective-permute-start.8) | collective-permute-done | bytes 458784 | tf_op jit(solution)/shard_map/ppermute | solution.py:103
  36.8 3.7 %collective-permute-done.6 = bf16[64,3584]{1,0:T(8,128)(2,1)S(1)} collective-permute-done((bf16[64,3584]{1,0:T(8,128)(2,1)S(1)}, bf16[64,3584]{1,0:T(8,128)(2,1)S(1)}, u32[]{:S(2)}, u32[]{:S(2)}) %collective-permute-start.6) | collective-permute-done | bytes 458784 | tf_op jit(solution)/shard_map/ppermute | solution.py:103
  41.2 2.8 %fusion.140 = f32[192,1152]{1,0:T(8,128)S(1)} fusion(bf16[192,3584]{1,0:T(8,128)(2,1)S(1)} %bitcast.194, bf16[1152,3584]{1,0:T(8,128)(2,1)S(1)} %bitcast.185), kind=kOutput, calls=%fused_computation.305 | convolution fusion | flops 1585446912 | bytes 10518528 | tf_op jit(solution)/shard_map/dot_general | solution.py:136
  44.2 0.6 collective-permute-done.9
  44.8 2.7 %fusion.138 = (f32[256]{0:T(256)S(1)}, f32[256,1152]{1,0:T(8,128)S(1)}) fusion(bf16[256,3584]{1,0:T(8,128)(2,1)S(1)} %collective-permute-done.9, bf16[1152,3584]{1,0:T(8,128)(2,1)S(1)} %bitcast.185), kind=kOutput, calls=%fused_computation.303 | convolution fusion | flops 2114223872 | bytes 11273216 | tf_op jit(solution)/shard_map/dot_general | solution.py:136
  47.5 2.3 %multiply_reduce_fusion.1 = (f32[256]{0:T(256)S(1)}, f32[256]{0:T(256)S(1)}, f32[256]{0:T(256)S(1)}, f32[256]{0:T(256)S(1)}) fusion(f32[512,1152]{1,0:T(8,128)} %get-tuple-element.278, f32[192,1152]{1,0:T(8,128)S(1)} %fusion.140, f32[64,1152]{1,0:T(8,128)S(1)} %fusion.139, f32[256,1152]{1,0:T(8,128)S(1)} %get-tuple-element.235, ...), kind=kLoop, calls=%fused_computation.43 | loop fusion | flops 2653184 | bytes 4724736 | tf_op jit(solution)/shard_map/reduce_sum | solution.py:176
  50.4 1.0 collective-permute-done.10
  51.7 3.6 %collective-permute-done.11 = f32[3,512]{1,0:T(4,128)S(1)} collective-permute-done((f32[3,512]{1,0:T(4,128)S(1)}, f32[3,512]{1,0:T(4,128)S(1)}, u32[]{:S(2)}, u32[]{:S(2)}) %collective-permute-start.11) | collective-permute-done | bytes 6176 | tf_op jit(solution)/shard_map/ppermute | solution.py:103
  55.8 4.8 %collective-permute-done.12 = f32[3,512]{1,0:T(4,128)S(1)} collective-permute-done((f32[3,512]{1,0:T(4,128)S(1)}, f32[3,512]{1,0:T(4,128)S(1)}, u32[]{:S(2)}, u32[]{:S(2)}) %collective-permute-start.12) | collective-permute-done | bytes 6176 | tf_op jit(solution)/shard_map/ppermute | solution.py:103
  61.1 3.3 %collective-permute-done.13 = f32[3,512]{1,0:T(4,128)S(1)} collective-permute-done((f32[3,512]{1,0:T(4,128)S(1)}, f32[3,512]{1,0:T(4,128)S(1)}, u32[]{:S(2)}, u32[]{:S(2)}) %collective-permute-start.13) | collective-permute-done | bytes 6176 | tf_op jit(solution)/shard_map/ppermute | solution.py:103
  64.5 2.1 %collective-permute-start.14 = (f32[3,512]{1,0:T(4,128)S(1)}, f32[3,512]{1,0:T(4,128)S(1)}, u32[]{:S(2)}, u32[]{:S(2)}) collective-permute-start(f32[3,512]{1,0:T(4,128)S(1)} %get-tuple-element.223), channel_id=1, source_target_pairs={{0,16},{1,17},{2,18},{3,19},{4,20},{5,21},{6,22},{7,23},{8,24},{9,... | collective-permute-start | bytes 18440 | tf_op jit(solution)/shard_map/ppermute | solution.py:103
  66.6 3.1 %collective-permute-done.14 = f32[3,512]{1,0:T(4,128)S(1)} collective-permute-done((f32[3,512]{1,0:T(4,128)S(1)}, f32[3,512]{1,0:T(4,128)S(1)}, u32[]{:S(2)}, u32[]{:S(2)}) %collective-permute-start.14) | collective-permute-done | bytes 6176 | tf_op jit(solution)/shard_map/ppermute | solution.py:103
  69.8 1.9 %collective-permute-start.15 = (f32[3,512]{1,0:T(4,128)S(1)}, f32[3,512]{1,0:T(4,128)S(1)}, u32[]{:S(2)}, u32[]{:S(2)}) collective-permute-start(f32[3,512]{1,0:T(4,128)S(1)} %get-tuple-element.221), channel_id=1, source_target_pairs={{0,32},{1,33},{2,34},{3,35},{4,36},{5,37},{6,38},{7,39},{8,40},{9,... | collective-permute-start | bytes 18440 | tf_op jit(solution)/shard_map/ppermute | solution.py:103
  71.7 1.8 %collective-permute-done.15 = f32[3,512]{1,0:T(4,128)S(1)} collective-permute-done((f32[3,512]{1,0:T(4,128)S(1)}, f32[3,512]{1,0:T(4,128)S(1)}, u32[]{:S(2)}, u32[]{:S(2)}) %collective-permute-start.15) | collective-permute-done | bytes 6176 | tf_op jit(solution)/shard_map/ppermute | solution.py:103
  73.6 1.9 %collective-permute-start.16 = (f32[3,512]{1,0:T(4,128)S(1)}, f32[3,512]{1,0:T(4,128)S(1)}, u32[]{:S(2)}, u32[]{:S(2)}) collective-permute-start(f32[3,512]{1,0:T(4,128)S(1)} %get-tuple-element.219), channel_id=1, source_target_pairs={{0,64},{1,65},{2,66},{3,67},{4,68},{5,69},{6,70},{7,71},{8,72},{9,... | collective-permute-start | bytes 18440 | tf_op jit(solution)/shard_map/ppermute | solution.py:103
  75.6 3.2 %collective-permute-done.16 = f32[3,512]{1,0:T(4,128)S(1)} collective-permute-done((f32[3,512]{1,0:T(4,128)S(1)}, f32[3,512]{1,0:T(4,128)S(1)}, u32[]{:S(2)}, u32[]{:S(2)}) %collective-permute-start.16) | collective-permute-done | bytes 6176 | tf_op jit(solution)/shard_map/ppermute | solution.py:103
  79.0 0.6 fusion.9
  79.6 1.6 %multiply_convert_fusion.1 = bf16[256,1152]{1,0:T(8,128)(2,1)S(1)} fusion(f32[256,1152]{1,0:T(8,128)S(1)} %get-tuple-element.235, f32[512,1152]{1,0:T(8,128)} %get-tuple-element.278, f32[256]{0:T(256)S(1)} %bitcast.257, f32[256]{0:T(256)S(1)} %bitcast.258), kind=kLoop, calls=%fused_computation.41 | loop fusion | flops 1474560 | bytes 2951168 | tf_op jit(solution)/shard_map/convert_element_type | solution.py:202
  81.2 2.6 %convolution_convert_fusion.1 = bf16[256,3584]{1,0:T(8,128)(2,1)S(1)} fusion(bf16[256,1152]{1,0:T(8,128)(2,1)S(1)} %multiply_convert_fusion.1, bf16[1152,3584]{1,0:T(8,128)(2,1)S(1)} %bitcast.185), kind=kOutput, calls=%fused_computation.29 | convolution fusion | flops 2114846720 | bytes 10682368 | tf_op jit(solution)/shard_map/dot_general | solution.py:208
  84.0 1.6 %multiply_convert_fusion = bf16[256,1152]{1,0:T(8,128)(2,1)S(1)} fusion(f32[256,1152]{1,0:T(8,128)S(1)} %get-tuple-element.98, f32[512,1152]{1,0:T(8,128)} %get-tuple-element.278, f32[256]{0:T(256)S(1)} %bitcast.256, f32[256]{0:T(256)S(1)} %bitcast.255), kind=kLoop, calls=%fused_computation.40 | loop fusion | flops 1474560 | bytes 2951168 | tf_op jit(solution)/shard_map/convert_element_type | solution.py:202
  85.6 2.6 %fusion.141 = f32[256,3584]{1,0:T(8,128)S(1)} fusion(bf16[256,1152]{1,0:T(8,128)(2,1)S(1)} %multiply_convert_fusion, bf16[1152,3584]{1,0:T(8,128)(2,1)S(1)} %bitcast.185), kind=kOutput, calls=%fused_computation.306 | convolution fusion | flops 2113929216 | bytes 12517376 | tf_op jit(solution)/shard_map/dot_general | solution.py:212
  89.0 3.2 %collective-permute-start.20 = (bf16[64,3584]{1,0:T(8,128)(2,1)S(1)}, bf16[64,3584]{1,0:T(8,128)(2,1)S(1)}, u32[]{:S(2)}, u32[]{:S(2)}) collective-permute-start(bf16[64,3584]{1,0:T(8,128)(2,1)S(1)} %get-tuple-element.200), channel_id=1, source_target_pairs={{0,6},{1,97},{2,0},{3,99},{4,2},{5,101},{6,4},{7,103},{8,14},{9,10... | collective-permute-start | bytes 1376264 | tf_op jit(solution)/shard_map/ppermute | solution.py:103
  92.2 6.7 %convolution_convert_fusion = bf16[1152,3584]{1,0:T(8,128)(2,1)} fusion(bf16[256,3584]{1,0:T(8,128)(2,1)S(1)} %collective-permute-done.9, bf16[256,3584]{1,0:T(8,128)(2,1)S(1)} %bitcast.187, bf16[256,1152]{1,0:T(8,128)(2,1)S(1)} %multiply_convert_fusion.1, bf16[256,1152]{1,0:T(8,128)(2,1)S(1)} %multiply_convert_fusion), kind=kOutput, calls=%fused_computation.28 | convolution fusion | flops 4241686528 | bytes 13107200 | tf_op jit(solution)/shard_map/dot_general | solution.py:216
  99.0 4.6 %collective-permute-done.18 = bf16[64,3584]{1,0:T(8,128)(2,1)S(1)} collective-permute-done((bf16[64,3584]{1,0:T(8,128)(2,1)S(1)}, bf16[64,3584]{1,0:T(8,128)(2,1)S(1)}, u32[]{:S(2)}, u32[]{:S(2)}) %collective-permute-start.18) | collective-permute-done | bytes 458784 | tf_op jit(solution)/shard_map/ppermute | solution.py:103
  104.1 1.9 %collective-permute-start.21 = (bf16[16,3584]{1,0:T(8,128)(2,1)S(1)}, bf16[16,3584]{1,0:T(8,128)(2,1)S(1)}, u32[]{:S(2)}, u32[]{:S(2)}) collective-permute-start(bf16[16,3584]{1,0:T(8,128)(2,1)S(1)} %get-tuple-element.204), channel_id=1, source_target_pairs={{0,32},{1,3},{2,34},{3,5},{4,36},{5,7},{6,38},{7,1},{8,40},{9,11},... | collective-permute-start | bytes 344072 | tf_op jit(solution)/shard_map/ppermute | solution.py:103
  105.9 1.4 %collective-permute-start.23 = (bf16[16,3584]{1,0:T(8,128)(2,1)S(1)}, bf16[16,3584]{1,0:T(8,128)(2,1)S(1)}, u32[]{:S(2)}, u32[]{:S(2)}) collective-permute-start(bf16[16,3584]{1,0:T(8,128)(2,1)S(1)} %get-tuple-element.205), channel_id=1, source_target_pairs={{0,96},{1,7},{2,98},{3,1},{4,100},{5,3},{6,102},{7,5},{8,104},{9,1... | collective-permute-start | bytes 344072 | tf_op jit(solution)/shard_map/ppermute | solution.py:103
  107.4 0.7 collective-permute-start.22
  108.1 2.1 %collective-permute-done.21 = bf16[16,3584]{1,0:T(8,128)(2,1)S(1)} collective-permute-done((bf16[16,3584]{1,0:T(8,128)(2,1)S(1)}, bf16[16,3584]{1,0:T(8,128)(2,1)S(1)}, u32[]{:S(2)}, u32[]{:S(2)}) %collective-permute-start.21) | collective-permute-done | bytes 114720 | tf_op jit(solution)/shard_map/ppermute | solution.py:103
  110.7 2.9 %collective-permute-done.22 = bf16[16,3584]{1,0:T(8,128)(2,1)S(1)} collective-permute-done((bf16[16,3584]{1,0:T(8,128)(2,1)S(1)}, bf16[16,3584]{1,0:T(8,128)(2,1)S(1)}, u32[]{:S(2)}, u32[]{:S(2)}) %collective-permute-start.22) | collective-permute-done | bytes 114720 | tf_op jit(solution)/shard_map/ppermute | solution.py:103
  114.2 2.9 %collective-permute-start.26 = (bf16[4,3584]{1,0:T(4,128)(2,1)S(1)}, bf16[4,3584]{1,0:T(4,128)(2,1)S(1)}, u32[]{:S(2)}, u32[]{:S(2)}) collective-permute-start(bf16[4,3584]{1,0:T(4,128)(2,1)S(1)} %get-tuple-element.208), channel_id=1, source_target_pairs={{0,24},{1,25},{2,26},{3,27},{4,28},{5,29},{6,30},{7,31},{8,0},{9,1... | collective-permute-start | bytes 86024 | tf_op jit(solution)/shard_map/ppermute | solution.py:103
  117.1 0.8 collective-permute-start.25
  119.0 3.4 %collective-permute-done.25 = bf16[4,3584]{1,0:T(4,128)(2,1)S(1)} collective-permute-done((bf16[4,3584]{1,0:T(4,128)(2,1)S(1)}, bf16[4,3584]{1,0:T(4,128)(2,1)S(1)}, u32[]{:S(2)}, u32[]{:S(2)}) %collective-permute-start.25) | collective-permute-done | bytes 28704 | tf_op jit(solution)/shard_map/ppermute | solution.py:103
  (105 shorter events, 9.0 us)
Async XLA Ops:
  0.6 8.9 %copy-start.1 = (bf16[4,3584]{1,0:T(4,128)(2,1)S(1)}, bf16[4,3584]{1,0:T(4,128)(2,1)}, u32[]{:S(2)}) copy-start(bf16[4,3584]{1,0:T(4,128)(2,1)} %param.8) | copy-start | bytes 86020
  0.6 15.2 %copy-start = (f32[512,64]{0,1:T(8,128)S(1)}, f32[512,64]{0,1:T(8,128)}, u32[]{:S(2)}) copy-start(f32[512,64]{0,1:T(8,128)} %param.11) | copy-start | bytes 393220
  0.6 7.6 %collective-permute-start = (bf16[4,3584]{1,0:T(4,128)(2,1)}, bf16[4,3584]{1,0:T(4,128)(2,1)S(1)}, u32[]{:S(2)}, u32[]{:S(2)}) collective-permute-start(bf16[4,3584]{1,0:T(4,128)(2,1)} %param.8), channel_id=1, source_target_pairs={{0,8},{1,9},{2,10},{3,11},{4,12},{5,13},{6,14},{7,15},{8,16},{9,17... | collective-permute-start | bytes 86024 | tf_op jit(solution)/shard_map/ppermute | solution.py:103
  2.4 5.8 %collective-permute-start.2 = (bf16[4,3584]{1,0:T(4,128)(2,1)}, bf16[4,3584]{1,0:T(4,128)(2,1)S(1)}, u32[]{:S(2)}, u32[]{:S(2)}) collective-permute-start(bf16[4,3584]{1,0:T(4,128)(2,1)} %param.8), channel_id=1, source_target_pairs={{0,24},{1,25},{2,26},{3,27},{4,28},{5,29},{6,30},{7,31},{8,0},{9,1... | collective-permute-start | bytes 86024 | tf_op jit(solution)/shard_map/ppermute | solution.py:103
  4.0 5.6 %collective-permute-start.1 = (bf16[4,3584]{1,0:T(4,128)(2,1)}, bf16[4,3584]{1,0:T(4,128)(2,1)S(1)}, u32[]{:S(2)}, u32[]{:S(2)}) collective-permute-start(bf16[4,3584]{1,0:T(4,128)(2,1)} %param.8), channel_id=1, source_target_pairs={{0,16},{1,17},{2,18},{3,19},{4,20},{5,21},{6,22},{7,23},{8,24},{9,... | collective-permute-start | bytes 86024 | tf_op jit(solution)/shard_map/ppermute | solution.py:103
  9.7 12.0 %collective-permute-start.5 = (bf16[16,3584]{1,0:T(8,128)(2,1)S(1)}, bf16[16,3584]{1,0:T(8,128)(2,1)S(1)}, u32[]{:S(2)}, u32[]{:S(2)}) collective-permute-start(bf16[16,3584]{1,0:T(8,128)(2,1)S(1)} %reshape.488), channel_id=1, source_target_pairs={{0,96},{1,7},{2,98},{3,1},{4,100},{5,3},{6,102},{7,5},{8,104},{9,1... | collective-permute-start | bytes 344072 | tf_op jit(solution)/shard_map/ppermute | solution.py:103
  12.6 9.1 %collective-permute-start.4 = (bf16[16,3584]{1,0:T(8,128)(2,1)S(1)}, bf16[16,3584]{1,0:T(8,128)(2,1)S(1)}, u32[]{:S(2)}, u32[]{:S(2)}) collective-permute-start(bf16[16,3584]{1,0:T(8,128)(2,1)S(1)} %reshape.488), channel_id=1, source_target_pairs={{0,64},{1,5},{2,66},{3,7},{4,68},{5,1},{6,70},{7,3},{8,72},{9,13},... | collective-permute-start | bytes 344072 | tf_op jit(solution)/shard_map/ppermute | solution.py:103
  13.4 8.3 %collective-permute-start.3 = (bf16[16,3584]{1,0:T(8,128)(2,1)S(1)}, bf16[16,3584]{1,0:T(8,128)(2,1)S(1)}, u32[]{:S(2)}, u32[]{:S(2)}) collective-permute-start(bf16[16,3584]{1,0:T(8,128)(2,1)S(1)} %reshape.488), channel_id=1, source_target_pairs={{0,32},{1,3},{2,34},{3,5},{4,36},{5,7},{6,38},{7,1},{8,40},{9,11},... | collective-permute-start | bytes 344072 | tf_op jit(solution)/shard_map/ppermute | solution.py:103
  21.7 19.4 %slice-start = ((s8[8257536]{0:T(1024)(128)(4,1)}), s8[4194304]{0:T(1024)(128)(4,1)S(1)}, s32[]{:S(2)}) async-start(s8[8257536]{0:T(1024)(128)(4,1)} %bitcast.184), calls=%async_computation | async-start | bytes 8388608
  21.8 19.4 %slice-start.1 = ((s8[8257536]{0:T(1024)(128)(4,1)}), s8[4063232]{0:T(1024)(128)(4,1)S(1)}, s32[]{:S(2)}) async-start(s8[8257536]{0:T(1024)(128)(4,1)} %bitcast.184), calls=%async_computation.1 | async-start | bytes 8126464
  21.8 15.0 %collective-permute-start.8 = (bf16[64,3584]{1,0:T(8,128)(2,1)S(1)}, bf16[64,3584]{1,0:T(8,128)(2,1)S(1)}, u32[]{:S(2)}, u32[]{:S(2)}) collective-permute-start(bf16[64,3584]{1,0:T(8,128)(2,1)S(1)} %bitcast.188), channel_id=1, source_target_pairs={{0,6},{1,97},{2,0},{3,99},{4,2},{5,101},{6,4},{7,103},{8,14},{9,10... | collective-permute-start | bytes 1376264 | tf_op jit(solution)/shard_map/ppermute | solution.py:103
  25.9 10.9 %collective-permute-start.7 = (bf16[64,3584]{1,0:T(8,128)(2,1)S(1)}, bf16[64,3584]{1,0:T(8,128)(2,1)S(1)}, u32[]{:S(2)}, u32[]{:S(2)}) collective-permute-start(bf16[64,3584]{1,0:T(8,128)(2,1)S(1)} %bitcast.189), channel_id=1, source_target_pairs={{0,4},{1,65},{2,6},{3,67},{4,0},{5,69},{6,2},{7,71},{8,12},{9,73},... | collective-permute-start | bytes 1376264 | tf_op jit(solution)/shard_map/ppermute | solution.py:103
  25.9 14.6 %collective-permute-start.6 = (bf16[64,3584]{1,0:T(8,128)(2,1)S(1)}, bf16[64,3584]{1,0:T(8,128)(2,1)S(1)}, u32[]{:S(2)}, u32[]{:S(2)}) collective-permute-start(bf16[64,3584]{1,0:T(8,128)(2,1)S(1)} %bitcast.190), channel_id=1, source_target_pairs={{0,2},{1,33},{2,4},{3,35},{4,6},{5,37},{6,0},{7,39},{8,10},{9,41},... | collective-permute-start | bytes 1376264 | tf_op jit(solution)/shard_map/ppermute | solution.py:103
  40.7 4.0 %collective-permute-start.9 = (bf16[256,3584]{1,0:T(8,128)(2,1)S(1)}, bf16[256,3584]{1,0:T(8,128)(2,1)S(1)}, u32[]{:S(2)}, u32[]{:S(2)}) collective-permute-start(bf16[256,3584]{1,0:T(8,128)(2,1)S(1)} %bitcast.186), channel_id=1, source_target_pairs={{0,1},{1,0},{2,3},{3,2},{4,5},{5,4},{6,7},{7,6},{8,9},{9,8},{10,11... | collective-permute-start | bytes 5505032 | tf_op jit(solution)/shard_map/ppermute | solution.py:165
  50.3 1.2 collective-permute-start.10
  51.5 3.7 %collective-permute-start.11 = (f32[3,512]{1,0:T(4,128)S(1)}, f32[3,512]{1,0:T(4,128)S(1)}, u32[]{:S(2)}, u32[]{:S(2)}) collective-permute-start(f32[3,512]{1,0:T(4,128)S(1)} %get-tuple-element.229), channel_id=1, source_target_pairs={{0,2},{1,3},{2,0},{3,1},{4,6},{5,7},{6,4},{7,5},{8,10},{9,11},{10,... | collective-permute-start | bytes 18440 | tf_op jit(solution)/shard_map/ppermute | solution.py:103
  55.4 5.2 %collective-permute-start.12 = (f32[3,512]{1,0:T(4,128)S(1)}, f32[3,512]{1,0:T(4,128)S(1)}, u32[]{:S(2)}, u32[]{:S(2)}) collective-permute-start(f32[3,512]{1,0:T(4,128)S(1)} %get-tuple-element.227), channel_id=1, source_target_pairs={{0,4},{1,5},{2,6},{3,7},{4,0},{5,1},{6,2},{7,3},{8,12},{9,13},{10,... | collective-permute-start | bytes 18440 | tf_op jit(solution)/shard_map/ppermute | solution.py:103
  60.7 3.7 %collective-permute-start.13 = (f32[3,512]{1,0:T(4,128)S(1)}, f32[3,512]{1,0:T(4,128)S(1)}, u32[]{:S(2)}, u32[]{:S(2)}) collective-permute-start(f32[3,512]{1,0:T(4,128)S(1)} %get-tuple-element.225), channel_id=1, source_target_pairs={{0,8},{1,9},{2,10},{3,11},{4,12},{5,13},{6,14},{7,15},{8,0},{9,1},... | collective-permute-start | bytes 18440 | tf_op jit(solution)/shard_map/ppermute | solution.py:103
  64.5 5.2 %collective-permute-start.14 = (f32[3,512]{1,0:T(4,128)S(1)}, f32[3,512]{1,0:T(4,128)S(1)}, u32[]{:S(2)}, u32[]{:S(2)}) collective-permute-start(f32[3,512]{1,0:T(4,128)S(1)} %get-tuple-element.223), channel_id=1, source_target_pairs={{0,16},{1,17},{2,18},{3,19},{4,20},{5,21},{6,22},{7,23},{8,24},{9,... | collective-permute-start | bytes 18440 | tf_op jit(solution)/shard_map/ppermute | solution.py:103
  69.8 3.7 %collective-permute-start.15 = (f32[3,512]{1,0:T(4,128)S(1)}, f32[3,512]{1,0:T(4,128)S(1)}, u32[]{:S(2)}, u32[]{:S(2)}) collective-permute-start(f32[3,512]{1,0:T(4,128)S(1)} %get-tuple-element.221), channel_id=1, source_target_pairs={{0,32},{1,33},{2,34},{3,35},{4,36},{5,37},{6,38},{7,39},{8,40},{9,... | collective-permute-start | bytes 18440 | tf_op jit(solution)/shard_map/ppermute | solution.py:103
  73.6 5.2 %collective-permute-start.16 = (f32[3,512]{1,0:T(4,128)S(1)}, f32[3,512]{1,0:T(4,128)S(1)}, u32[]{:S(2)}, u32[]{:S(2)}) collective-permute-start(f32[3,512]{1,0:T(4,128)S(1)} %get-tuple-element.219), channel_id=1, source_target_pairs={{0,64},{1,65},{2,66},{3,67},{4,68},{5,69},{6,70},{7,71},{8,72},{9,... | collective-permute-start | bytes 18440 | tf_op jit(solution)/shard_map/ppermute | solution.py:103
  83.9 4.3 %collective-permute-start.17 = (bf16[256,3584]{1,0:T(8,128)(2,1)S(1)}, bf16[256,3584]{1,0:T(8,128)(2,1)S(1)}, u32[]{:S(2)}, u32[]{:S(2)}) collective-permute-start(bf16[256,3584]{1,0:T(8,128)(2,1)S(1)} %convolution_convert_fusion.1), channel_id=1, source_target_pairs={{0,1},{1,0},{2,3},{3,2},{4,5},{5,4},{6,7},{7,6},{8,9},{9,8},{10,11... | collective-permute-start | bytes 5505032 | tf_op jit(solution)/shard_map/ppermute | solution.py:209
  88.9 14.7 %collective-permute-start.18 = (bf16[64,3584]{1,0:T(8,128)(2,1)S(1)}, bf16[64,3584]{1,0:T(8,128)(2,1)S(1)}, u32[]{:S(2)}, u32[]{:S(2)}) collective-permute-start(bf16[64,3584]{1,0:T(8,128)(2,1)S(1)} %get-tuple-element.199), channel_id=1, source_target_pairs={{0,2},{1,33},{2,4},{3,35},{4,6},{5,37},{6,0},{7,39},{8,10},{9,41},... | collective-permute-start | bytes 1376264 | tf_op jit(solution)/shard_map/ppermute | solution.py:103
  89.0 14.6 %collective-permute-start.20 = (bf16[64,3584]{1,0:T(8,128)(2,1)S(1)}, bf16[64,3584]{1,0:T(8,128)(2,1)S(1)}, u32[]{:S(2)}, u32[]{:S(2)}) collective-permute-start(bf16[64,3584]{1,0:T(8,128)(2,1)S(1)} %get-tuple-element.200), channel_id=1, source_target_pairs={{0,6},{1,97},{2,0},{3,99},{4,2},{5,101},{6,4},{7,103},{8,14},{9,10... | collective-permute-start | bytes 1376264 | tf_op jit(solution)/shard_map/ppermute | solution.py:103
  92.2 11.4 %collective-permute-start.19 = (bf16[64,3584]{1,0:T(8,128)(2,1)S(1)}, bf16[64,3584]{1,0:T(8,128)(2,1)S(1)}, u32[]{:S(2)}, u32[]{:S(2)}) collective-permute-start(bf16[64,3584]{1,0:T(8,128)(2,1)S(1)} %get-tuple-element.201), channel_id=1, source_target_pairs={{0,4},{1,65},{2,6},{3,67},{4,0},{5,69},{6,2},{7,71},{8,12},{9,73},... | collective-permute-start | bytes 1376264 | tf_op jit(solution)/shard_map/ppermute | solution.py:103
  104.1 6.1 %collective-permute-start.21 = (bf16[16,3584]{1,0:T(8,128)(2,1)S(1)}, bf16[16,3584]{1,0:T(8,128)(2,1)S(1)}, u32[]{:S(2)}, u32[]{:S(2)}) collective-permute-start(bf16[16,3584]{1,0:T(8,128)(2,1)S(1)} %get-tuple-element.204), channel_id=1, source_target_pairs={{0,32},{1,3},{2,34},{3,5},{4,36},{5,7},{6,38},{7,1},{8,40},{9,11},... | collective-permute-start | bytes 344072 | tf_op jit(solution)/shard_map/ppermute | solution.py:103
  105.9 4.8 %collective-permute-start.23 = (bf16[16,3584]{1,0:T(8,128)(2,1)S(1)}, bf16[16,3584]{1,0:T(8,128)(2,1)S(1)}, u32[]{:S(2)}, u32[]{:S(2)}) collective-permute-start(bf16[16,3584]{1,0:T(8,128)(2,1)S(1)} %get-tuple-element.205), channel_id=1, source_target_pairs={{0,96},{1,7},{2,98},{3,1},{4,100},{5,3},{6,102},{7,5},{8,104},{9,1... | collective-permute-start | bytes 344072 | tf_op jit(solution)/shard_map/ppermute | solution.py:103
  107.4 6.3 %collective-permute-start.22 = (bf16[16,3584]{1,0:T(8,128)(2,1)S(1)}, bf16[16,3584]{1,0:T(8,128)(2,1)S(1)}, u32[]{:S(2)}, u32[]{:S(2)}) collective-permute-start(bf16[16,3584]{1,0:T(8,128)(2,1)S(1)} %get-tuple-element.206), channel_id=1, source_target_pairs={{0,64},{1,5},{2,66},{3,7},{4,68},{5,1},{6,70},{7,3},{8,72},{9,13},... | collective-permute-start | bytes 344072 | tf_op jit(solution)/shard_map/ppermute | solution.py:103
  113.8 5.2 %collective-permute-start.24 = (bf16[4,3584]{1,0:T(4,128)(2,1)S(1)}, bf16[4,3584]{1,0:T(4,128)(2,1)S(1)}, u32[]{:S(2)}, u32[]{:S(2)}) collective-permute-start(bf16[4,3584]{1,0:T(4,128)(2,1)S(1)} %get-tuple-element.207), channel_id=1, source_target_pairs={{0,8},{1,9},{2,10},{3,11},{4,12},{5,13},{6,14},{7,15},{8,16},{9,17... | collective-permute-start | bytes 86024 | tf_op jit(solution)/shard_map/ppermute | solution.py:103
  114.2 4.8 %collective-permute-start.26 = (bf16[4,3584]{1,0:T(4,128)(2,1)S(1)}, bf16[4,3584]{1,0:T(4,128)(2,1)S(1)}, u32[]{:S(2)}, u32[]{:S(2)}) collective-permute-start(bf16[4,3584]{1,0:T(4,128)(2,1)S(1)} %get-tuple-element.208), channel_id=1, source_target_pairs={{0,24},{1,25},{2,26},{3,27},{4,28},{5,29},{6,30},{7,31},{8,0},{9,1... | collective-permute-start | bytes 86024 | tf_op jit(solution)/shard_map/ppermute | solution.py:103
  117.1 5.4 %collective-permute-start.25 = (bf16[4,3584]{1,0:T(4,128)(2,1)S(1)}, bf16[4,3584]{1,0:T(4,128)(2,1)S(1)}, u32[]{:S(2)}, u32[]{:S(2)}) collective-permute-start(bf16[4,3584]{1,0:T(4,128)(2,1)S(1)} %get-tuple-element.209), channel_id=1, source_target_pairs={{0,16},{1,17},{2,18},{3,19},{4,20},{5,21},{6,22},{7,23},{8,24},{9,... | collective-permute-start | bytes 86024 | tf_op jit(solution)/shard_map/ppermute | solution.py:103

commit v14 on v10

--- a/solution.py
+++ b/solution.py
@@ -148,16 +148,15 @@
     logprob_arr = jnp.take(teacher_logprob, rows, axis=0)
     local = index_arr - offset
     probs_arr = jnp.exp(logprob_arr)
-    target = teacher_target(local, probs_arr, voc_dev)
 
     own = hidden_rows
     for stage in ("r1", "r2"):
         own = exchange(lambda s: own, stage, n_dev, voc_n).reshape(-1, width)
-        if stage == "r2":
-            own, target = lax.optimization_barrier((own, target))
+    own, local, probs_arr = lax.optimization_barrier((own, local, probs_arr))
     got = exchange(lambda s: own, "r3", n_dev, voc_n)
+    target = teacher_target(local, probs_arr, voc_dev)
     first_logits = half_logits(own, head_weight)
-    got, first_logits = lax.optimization_barrier((got, first_logits))
+    got, target, first_logits = lax.optimization_barrier((got, target, first_logits))
     own = got.reshape(-1, width)
     other = lax.ppermute(own, AXES, stage_pairs("c", 1, n_dev, voc_n))
     logits_own = jnp.concatenate(

time: 117 us -> 118 us (level)
  matrix products: 24.4 us -> 27.9 us
  waiting for transfers between devices: 28.4 us -> 25.4 us
    dot_general x3, matrix products: 11.4 us -> 14.9 us  [half_logits(): lax.dot_general(rows_block, head_weight, (((1,), (1,)), ((), ())), prefer...]
    ppermute x28, waiting for transfers between devices: 27.7 us -> 25.4 us  [exchange(): lax.ppermute(block_for(shift), AXES, stage_pairs(stage, shift, n_dev, voc...]
  transfers between devices with their start and end apart: 30 -> 30, of which waited for: 14 -> 16; matrix products, arithmetic and copies ran while one was open for 25% -> 28% of each run, Pallas kernels for 0% -> 0%
where the time goes in v14:
time: 118 us
  starting transfers between devices  44.5 us (38%)
  matrix products  27.9 us (24%)
  waiting for transfers between devices  25.4 us (22%)
  other arithmetic  13.8 us (12%)
  local copies, waits for them, and re-layouts  4.51 us (4%)
  between operations  1.77 us (2%)
    ppermute x28, starting transfers between devices, exchange(): lax.ppermute(block_for(shift), AXES, stage_pairs(stage, shift, n_dev, voc...  43.9 us
    ppermute x28, waiting for transfers between devices, exchange(): lax.ppermute(block_for(shift), AXES, stage_pairs(stage, shift, n_dev, voc...  25.4 us
    dot_general x3, matrix products, half_logits(): lax.dot_general(rows_block, head_weight, (((1,), (1,)), ((), ())), prefer...  14.9 us
    dot_general x1, matrix products, per_device(): lax.dot_general(grad, every, (((0,), (0,)), ((), ())), preferred_element_...  6.72 us
    add x1, other arithmetic, compact_target(): target + jnp.where(slot_local[:, j:j + 1] == columns, slot_probs[:, j:j +...  3.57 us
    convert_element_type x2, other arithmetic, half_grad(): (loss_scale * (total_h[:, None] * jnp.exp(logits - lse_h[:, None]) - tgt)...  3.27 us
    dot_general x1, matrix products, per_device(): jnp.dot(grad_other, head_weight, preferred_element_type=jnp.float32)  2.6 us
    dot_general x1, matrix products, per_device(): acc = jnp.dot(grad_own, head_weight, preferred_element_type=jnp.float32)  2.59 us
  transfers between devices with their start and end apart: 30, of which 16 were waited for; matrix products, arithmetic and copies ran while one was open for 28% of the time, Pallas kernels for 0%

profile of v14, /device:TPU:0, one launch (start us, length us, event | category | flops | bytes accessed | tf_op | source)
XLA Modules:
  0.0 117.9 jit_solution(11346597694044152689)
XLA Ops:
  0.6 1.7 %collective-permute-start = (bf16[4,3584]{1,0:T(4,128)(2,1)}, bf16[4,3584]{1,0:T(4,128)(2,1)S(1)}, u32[]{:S(2)}, u32[]{:S(2)}) collective-permute-start(bf16[4,3584]{1,0:T(4,128)(2,1)} %param.8), channel_id=1, source_target_pairs={{0,8},{1,9},{2,10},{3,11},{4,12},{5,13},{6,14},{7,15},{8,16},{9,17... | collective-permute-start | bytes 86024 | tf_op jit(solution)/shard_map/ppermute | solution.py:100
  2.4 1.6 %collective-permute-start.2 = (bf16[4,3584]{1,0:T(4,128)(2,1)}, bf16[4,3584]{1,0:T(4,128)(2,1)S(1)}, u32[]{:S(2)}, u32[]{:S(2)}) collective-permute-start(bf16[4,3584]{1,0:T(4,128)(2,1)} %param.8), channel_id=1, source_target_pairs={{0,24},{1,25},{2,26},{3,27},{4,28},{5,29},{6,30},{7,31},{8,0},{9,1... | collective-permute-start | bytes 86024 | tf_op jit(solution)/shard_map/ppermute | solution.py:100
  3.9 2.1 %collective-permute-start.1 = (bf16[4,3584]{1,0:T(4,128)(2,1)}, bf16[4,3584]{1,0:T(4,128)(2,1)S(1)}, u32[]{:S(2)}, u32[]{:S(2)}) collective-permute-start(bf16[4,3584]{1,0:T(4,128)(2,1)} %param.8), channel_id=1, source_target_pairs={{0,16},{1,17},{2,18},{3,19},{4,20},{5,21},{6,22},{7,23},{8,24},{9,... | collective-permute-start | bytes 86024 | tf_op jit(solution)/shard_map/ppermute | solution.py:100
  6.1 1.0 copy.28
  7.2 1.0 gather_fusion.1
  8.5 1.0 gather_fusion
  9.7 2.9 %collective-permute-start.5 = (bf16[16,3584]{1,0:T(8,128)(2,1)S(1)}, bf16[16,3584]{1,0:T(8,128)(2,1)S(1)}, u32[]{:S(2)}, u32[]{:S(2)}) collective-permute-start(bf16[16,3584]{1,0:T(8,128)(2,1)S(1)} %reshape.478), channel_id=1, source_target_pairs={{0,96},{1,7},{2,98},{3,1},{4,100},{5,3},{6,102},{7,5},{8,104},{9,1... | collective-permute-start | bytes 344072 | tf_op jit(solution)/shard_map/ppermute | solution.py:100
  13.4 0.9 collective-permute-start.3
  15.0 4.0 %collective-permute-done.4 = bf16[16,3584]{1,0:T(8,128)(2,1)S(1)} collective-permute-done((bf16[16,3584]{1,0:T(8,128)(2,1)S(1)}, bf16[16,3584]{1,0:T(8,128)(2,1)S(1)}, u32[]{:S(2)}, u32[]{:S(2)}) %collective-permute-start.4) | collective-permute-done | bytes 114720 | tf_op jit(solution)/shard_map/ppermute | solution.py:100
  19.0 1.2 collective-permute-done.3
  20.2 4.1 %collective-permute-start.8 = (bf16[64,3584]{1,0:T(8,128)(2,1)S(1)}, bf16[64,3584]{1,0:T(8,128)(2,1)S(1)}, u32[]{:S(2)}, u32[]{:S(2)}) collective-permute-start(bf16[64,3584]{1,0:T(8,128)(2,1)S(1)} %bitcast.151), channel_id=1, source_target_pairs={{0,6},{1,97},{2,0},{3,99},{4,2},{5,101},{6,4},{7,103},{8,14},{9,10... | collective-permute-start | bytes 1376264 | tf_op jit(solution)/shard_map/ppermute | solution.py:100
  24.3 1.3 %collective-permute-start.6 = (bf16[64,3584]{1,0:T(8,128)(2,1)S(1)}, bf16[64,3584]{1,0:T(8,128)(2,1)S(1)}, u32[]{:S(2)}, u32[]{:S(2)}) collective-permute-start(bf16[64,3584]{1,0:T(8,128)(2,1)S(1)} %bitcast.153), channel_id=1, source_target_pairs={{0,2},{1,33},{2,4},{3,35},{4,6},{5,37},{6,0},{7,39},{8,10},{9,41},... | collective-permute-start | bytes 1376264 | tf_op jit(solution)/shard_map/ppermute | solution.py:100
  27.0 4.6 %conditional.1 = (f32[512,1152]{1,0:T(8,128)}) conditional(s32[]{:T(128)} %convert_element_type.47, (s32[512,64]{1,0:T(8,128)S(1)}, f32[512,64]{1,0:T(8,128)S(1)}) %tuple.24, (s32[512,64]{1,0:T(8,128)S(1)}, f32[512,64]{1,0:T(8,128)S(1)}) %tuple.24), branch_computations={%region_3.7_spmd, %region_7.11_spmd} | conditional | flops 17883136 | bytes 4423692 | solution.py:44
  28.0 3.6 %select_add_fusion = f32[512,1152]{1,0:T(8,128)} fusion(f32[512]{0:T(512)S(1)} %bitcast.191, s32[512]{0:T(512)S(1)} %bitcast.183, f32[512]{0:T(512)S(1)} %bitcast.192, s32[512]{0:T(512)S(1)} %bitcast.184, f32[512]{0:T(512)S(1)} %bitcast.193, s32[512]{0:T(512)S(1)} %bitcast.185, f32[512]{0:T(512)S(1)} %bitcast.194, s32[512]{0:T(512)S(1)} %bitcast.186, ...), kind=kLoop, calls=%fused_computation.3 | loop fusion | flops 13565952 | bytes 2392064 | tf_op jit(solution)/shard_map/cond/branch_0_fun/add | solution.py:37
  31.6 5.9 %fusion.96 = f32[64,1152]{1,0:T(8,128)S(1)} fusion(bf16[64,3584]{1,0:T(8,128)(2,1)S(1)} %bitcast.154, bf16[1152,3584]{1,0:T(8,128)(2,1)} %param.9), kind=kOutput, calls=%fused_computation.239 | convolution fusion | flops 528482304 | bytes 9011200 | tf_op jit(solution)/shard_map/dot_general | solution.py:133
  37.5 1.3 %collective-permute-done.6 = bf16[64,3584]{1,0:T(8,128)(2,1)S(1)} collective-permute-done((bf16[64,3584]{1,0:T(8,128)(2,1)S(1)}, bf16[64,3584]{1,0:T(8,128)(2,1)S(1)}, u32[]{:S(2)}, u32[]{:S(2)}) %collective-permute-start.6) | collective-permute-done | bytes 458784 | tf_op jit(solution)/shard_map/ppermute | solution.py:100
  39.6 6.3 %fusion.97 = f32[192,1152]{1,0:T(8,128)S(1)} fusion(bf16[192,3584]{1,0:T(8,128)(2,1)S(1)} %bitcast.158, bf16[1152,3584]{1,0:T(8,128)(2,1)} %param.9), kind=kOutput, calls=%fused_computation.240 | convolution fusion | flops 1585446912 | bytes 10518528 | tf_op jit(solution)/shard_map/dot_general | solution.py:133
  46.1 2.6 %fusion.95 = (f32[256]{0:T(256)S(1)}, f32[256,1152]{1,0:T(8,128)S(1)}) fusion(bf16[256,3584]{1,0:T(8,128)(2,1)S(1)} %collective-permute-done.9, bf16[1152,3584]{1,0:T(8,128)(2,1)S(1)} %bitcast.148), kind=kOutput, calls=%fused_computation.238 | convolution fusion | flops 2114223872 | bytes 11273216 | tf_op jit(solution)/shard_map/dot_general | solution.py:133
  48.7 2.4 %multiply_reduce_fusion.1 = (f32[256]{0:T(256)S(1)}, f32[256]{0:T(256)S(1)}, f32[256]{0:T(256)S(1)}, f32[256]{0:T(256)S(1)}) fusion(f32[512,1152]{1,0:T(8,128)} %get-tuple-element.196, f32[192,1152]{1,0:T(8,128)S(1)} %fusion.97, f32[64,1152]{1,0:T(8,128)S(1)} %fusion.96, f32[256,1152]{1,0:T(8,128)S(1)} %get-tuple-element.153, f32[256]{0:T(256)S(1)} %get-tuple-element.152, ...), kind=kLoop, calls=%fused_computation.38 | loop fusion | flops 2653184 | bytes 4724736 | tf_op jit(solution)/shard_map/reduce_sum | solution.py:172
  52.1 0.8 collective-permute-done.10
  53.0 1.0 collective-permute-start.12
  54.0 0.8 collective-permute-start.11
  54.9 2.4 %collective-permute-start.13 = (f32[3,512]{1,0:T(4,128)S(1)}, f32[3,512]{1,0:T(4,128)S(1)}, u32[]{:S(2)}, u32[]{:S(2)}) collective-permute-start(f32[3,512]{1,0:T(4,128)S(1)} %get-tuple-element.147), channel_id=1, source_target_pairs={{0,6},{1,7},{2,0},{3,1},{4,2},{5,3},{6,4},{7,5},{8,14},{9,15},{10,... | collective-permute-start | bytes 18440 | tf_op jit(solution)/shard_map/ppermute | solution.py:100
  57.3 1.0 collective-permute-done.12
  59.0 2.1 %collective-permute-start.15 = (f32[3,512]{1,0:T(4,128)S(1)}, f32[3,512]{1,0:T(4,128)S(1)}, u32[]{:S(2)}, u32[]{:S(2)}) collective-permute-start(f32[3,512]{1,0:T(4,128)S(1)} %get-tuple-element.145), channel_id=1, source_target_pairs={{0,16},{1,17},{2,18},{3,19},{4,20},{5,21},{6,22},{7,23},{8,24},{9,... | collective-permute-start | bytes 18440 | tf_op jit(solution)/shard_map/ppermute | solution.py:100
  61.8 2.6 %collective-permute-start.16 = (f32[3,512]{1,0:T(4,128)S(1)}, f32[3,512]{1,0:T(4,128)S(1)}, u32[]{:S(2)}, u32[]{:S(2)}) collective-permute-start(f32[3,512]{1,0:T(4,128)S(1)} %get-tuple-element.145), channel_id=1, source_target_pairs={{0,24},{1,25},{2,26},{3,27},{4,28},{5,29},{6,30},{7,31},{8,0},{9,1... | collective-permute-start | bytes 18440 | tf_op jit(solution)/shard_map/ppermute | solution.py:100
  64.4 1.6 %collective-permute-done.14 = f32[3,512]{1,0:T(4,128)S(1)} collective-permute-done((f32[3,512]{1,0:T(4,128)S(1)}, f32[3,512]{1,0:T(4,128)S(1)}, u32[]{:S(2)}, u32[]{:S(2)}) %collective-permute-start.14) | collective-permute-done | bytes 6176 | tf_op jit(solution)/shard_map/ppermute | solution.py:100
  66.1 0.9 collective-permute-start.18
  67.6 2.6 %collective-permute-start.19 = (f32[3,512]{1,0:T(4,128)S(1)}, f32[3,512]{1,0:T(4,128)S(1)}, u32[]{:S(2)}, u32[]{:S(2)}) collective-permute-start(f32[3,512]{1,0:T(4,128)S(1)} %get-tuple-element.143), channel_id=1, source_target_pairs={{0,96},{1,97},{2,98},{3,99},{4,100},{5,101},{6,102},{7,103},{8,104... | collective-permute-start | bytes 18440 | tf_op jit(solution)/shard_map/ppermute | solution.py:100
  70.3 1.1 collective-permute-done.18
  72.6 1.6 %multiply_convert_fusion.1 = bf16[256,1152]{1,0:T(8,128)(2,1)S(1)} fusion(f32[256,1152]{1,0:T(8,128)S(1)} %get-tuple-element.153, f32[512,1152]{1,0:T(8,128)} %get-tuple-element.196, f32[256]{0:T(256)S(1)} %bitcast.215, f32[256]{0:T(256)S(1)} %bitcast.216), kind=kLoop, calls=%fused_computation.36 | loop fusion | flops 1474560 | bytes 2951168 | tf_op jit(solution)/shard_map/convert_element_type | solution.py:198
  74.3 2.6 %convolution_convert_fusion.1 = bf16[256,3584]{1,0:T(8,128)(2,1)S(1)} fusion(bf16[256,1152]{1,0:T(8,128)(2,1)S(1)} %multiply_convert_fusion.1, bf16[1152,3584]{1,0:T(8,128)(2,1)S(1)} %bitcast.148), kind=kOutput, calls=%fused_computation.24 | convolution fusion | flops 2114846720 | bytes 10682368 | tf_op jit(solution)/shard_map/dot_general | solution.py:204
  77.2 1.6 %multiply_convert_fusion = bf16[256,1152]{1,0:T(8,128)(2,1)S(1)} fusion(f32[256,1152]{1,0:T(8,128)S(1)} %get-tuple-element.62, f32[512,1152]{1,0:T(8,128)} %get-tuple-element.196, f32[256]{0:T(256)S(1)} %bitcast.214, f32[256]{0:T(256)S(1)} %bitcast.213), kind=kLoop, calls=%fused_computation.35 | loop fusion | flops 1474560 | bytes 2951168 | tf_op jit(solution)/shard_map/convert_element_type | solution.py:198
  78.8 2.6 %fusion.98 = f32[256,3584]{1,0:T(8,128)S(1)} fusion(bf16[256,1152]{1,0:T(8,128)(2,1)S(1)} %multiply_convert_fusion, bf16[1152,3584]{1,0:T(8,128)(2,1)S(1)} %bitcast.148), kind=kOutput, calls=%fused_computation.241 | convolution fusion | flops 2113929216 | bytes 12517376 | tf_op jit(solution)/shard_map/dot_general | solution.py:208
  82.2 1.4 %collective-permute-start.21 = (bf16[64,3584]{1,0:T(8,128)(2,1)S(1)}, bf16[64,3584]{1,0:T(8,128)(2,1)S(1)}, u32[]{:S(2)}, u32[]{:S(2)}) collective-permute-start(bf16[64,3584]{1,0:T(8,128)(2,1)S(1)} %get-tuple-element.129), channel_id=1, source_target_pairs={{0,2},{1,33},{2,4},{3,35},{4,6},{5,37},{6,0},{7,39},{8,10},{9,41},... | collective-permute-start | bytes 1376264 | tf_op jit(solution)/shard_map/ppermute | solution.py:100
  83.5 2.0 %collective-permute-start.23 = (bf16[64,3584]{1,0:T(8,128)(2,1)S(1)}, bf16[64,3584]{1,0:T(8,128)(2,1)S(1)}, u32[]{:S(2)}, u32[]{:S(2)}) collective-permute-start(bf16[64,3584]{1,0:T(8,128)(2,1)S(1)} %get-tuple-element.130), channel_id=1, source_target_pairs={{0,6},{1,97},{2,0},{3,99},{4,2},{5,101},{6,4},{7,103},{8,14},{9,10... | collective-permute-start | bytes 1376264 | tf_op jit(solution)/shard_map/ppermute | solution.py:100
  85.5 1.6 %collective-permute-start.22 = (bf16[64,3584]{1,0:T(8,128)(2,1)S(1)}, bf16[64,3584]{1,0:T(8,128)(2,1)S(1)}, u32[]{:S(2)}, u32[]{:S(2)}) collective-permute-start(bf16[64,3584]{1,0:T(8,128)(2,1)S(1)} %get-tuple-element.131), channel_id=1, source_target_pairs={{0,4},{1,65},{2,6},{3,67},{4,0},{5,69},{6,2},{7,71},{8,12},{9,73},... | collective-permute-start | bytes 1376264 | tf_op jit(solution)/shard_map/ppermute | solution.py:100
  87.1 6.7 %convolution_convert_fusion = bf16[1152,3584]{1,0:T(8,128)(2,1)} fusion(bf16[256,3584]{1,0:T(8,128)(2,1)S(1)} %collective-permute-done.9, bf16[256,3584]{1,0:T(8,128)(2,1)S(1)} %bitcast.150, bf16[256,1152]{1,0:T(8,128)(2,1)S(1)} %multiply_convert_fusion.1, bf16[256,1152]{1,0:T(8,128)(2,1)S(1)} %multiply_convert_fusion), kind=kOutput, calls=%fused_computation.23 | convolution fusion | flops 4241686528 | bytes 13107200 | tf_op jit(solution)/shard_map/dot_general | solution.py:212
  93.9 2.6 %collective-permute-done.23 = bf16[64,3584]{1,0:T(8,128)(2,1)S(1)} collective-permute-done((bf16[64,3584]{1,0:T(8,128)(2,1)S(1)}, bf16[64,3584]{1,0:T(8,128)(2,1)S(1)}, u32[]{:S(2)}, u32[]{:S(2)}) %collective-permute-start.23) | collective-permute-done | bytes 458784 | tf_op jit(solution)/shard_map/ppermute | solution.py:100
  96.5 1.8 %collective-permute-done.22 = bf16[64,3584]{1,0:T(8,128)(2,1)S(1)} collective-permute-done((bf16[64,3584]{1,0:T(8,128)(2,1)S(1)}, bf16[64,3584]{1,0:T(8,128)(2,1)S(1)}, u32[]{:S(2)}, u32[]{:S(2)}) %collective-permute-start.22) | collective-permute-done | bytes 458784 | tf_op jit(solution)/shard_map/ppermute | solution.py:100
  98.7 1.5 %collective-permute-start.24 = (bf16[16,3584]{1,0:T(8,128)(2,1)S(1)}, bf16[16,3584]{1,0:T(8,128)(2,1)S(1)}, u32[]{:S(2)}, u32[]{:S(2)}) collective-permute-start(bf16[16,3584]{1,0:T(8,128)(2,1)S(1)} %get-tuple-element.134), channel_id=1, source_target_pairs={{0,32},{1,3},{2,34},{3,5},{4,36},{5,7},{6,38},{7,1},{8,40},{9,11},... | collective-permute-start | bytes 344072 | tf_op jit(solution)/shard_map/ppermute | solution.py:100
  100.3 1.8 %collective-permute-start.26 = (bf16[16,3584]{1,0:T(8,128)(2,1)S(1)}, bf16[16,3584]{1,0:T(8,128)(2,1)S(1)}, u32[]{:S(2)}, u32[]{:S(2)}) collective-permute-start(bf16[16,3584]{1,0:T(8,128)(2,1)S(1)} %get-tuple-element.135), channel_id=1, source_target_pairs={{0,96},{1,7},{2,98},{3,1},{4,100},{5,3},{6,102},{7,5},{8,104},{9,1... | collective-permute-start | bytes 344072 | tf_op jit(solution)/shard_map/ppermute | solution.py:100
  102.1 1.4 %collective-permute-start.25 = (bf16[16,3584]{1,0:T(8,128)(2,1)S(1)}, bf16[16,3584]{1,0:T(8,128)(2,1)S(1)}, u32[]{:S(2)}, u32[]{:S(2)}) collective-permute-start(bf16[16,3584]{1,0:T(8,128)(2,1)S(1)} %get-tuple-element.136), channel_id=1, source_target_pairs={{0,64},{1,5},{2,66},{3,7},{4,68},{5,1},{6,70},{7,3},{8,72},{9,13},... | collective-permute-start | bytes 344072 | tf_op jit(solution)/shard_map/ppermute | solution.py:100
  103.5 1.3 %collective-permute-done.24 = bf16[16,3584]{1,0:T(8,128)(2,1)S(1)} collective-permute-done((bf16[16,3584]{1,0:T(8,128)(2,1)S(1)}, bf16[16,3584]{1,0:T(8,128)(2,1)S(1)}, u32[]{:S(2)}, u32[]{:S(2)}) %collective-permute-start.24) | collective-permute-done | bytes 114720 | tf_op jit(solution)/shard_map/ppermute | solution.py:100
  105.0 3.3 %collective-permute-done.25 = bf16[16,3584]{1,0:T(8,128)(2,1)S(1)} collective-permute-done((bf16[16,3584]{1,0:T(8,128)(2,1)S(1)}, bf16[16,3584]{1,0:T(8,128)(2,1)S(1)}, u32[]{:S(2)}, u32[]{:S(2)}) %collective-permute-start.25) | collective-permute-done | bytes 114720 | tf_op jit(solution)/shard_map/ppermute | solution.py:100
  108.9 3.0 %collective-permute-start.29 = (bf16[4,3584]{1,0:T(4,128)(2,1)S(1)}, bf16[4,3584]{1,0:T(4,128)(2,1)S(1)}, u32[]{:S(2)}, u32[]{:S(2)}) collective-permute-start(bf16[4,3584]{1,0:T(4,128)(2,1)S(1)} %get-tuple-element.138), channel_id=1, source_target_pairs={{0,24},{1,25},{2,26},{3,27},{4,28},{5,29},{6,30},{7,31},{8,0},{9,1... | collective-permute-start | bytes 86024 | tf_op jit(solution)/shard_map/ppermute | solution.py:100
  111.9 1.4 %collective-permute-start.28 = (bf16[4,3584]{1,0:T(4,128)(2,1)S(1)}, bf16[4,3584]{1,0:T(4,128)(2,1)S(1)}, u32[]{:S(2)}, u32[]{:S(2)}) collective-permute-start(bf16[4,3584]{1,0:T(4,128)(2,1)S(1)} %get-tuple-element.139), channel_id=1, source_target_pairs={{0,16},{1,17},{2,18},{3,19},{4,20},{5,21},{6,22},{7,23},{8,24},{9,... | collective-permute-start | bytes 86024 | tf_op jit(solution)/shard_map/ppermute | solution.py:100
  113.8 3.4 %collective-permute-done.28 = bf16[4,3584]{1,0:T(4,128)(2,1)S(1)} collective-permute-done((bf16[4,3584]{1,0:T(4,128)(2,1)S(1)}, bf16[4,3584]{1,0:T(4,128)(2,1)S(1)}, u32[]{:S(2)}, u32[]{:S(2)}) %collective-permute-start.28) | collective-permute-done | bytes 28704 | tf_op jit(solution)/shard_map/ppermute | solution.py:100
  (107 shorter events, 12.7 us)
Async XLA Ops:
  0.6 7.7 %copy-start.1 = (s32[512,64]{0,1:T(8,128)S(1)}, s32[512,64]{0,1:T(8,128)}, u32[]{:S(2)}) copy-start(s32[512,64]{0,1:T(8,128)} %param.10) | copy-start | bytes 393220
  0.6 8.9 %collective-permute-start = (bf16[4,3584]{1,0:T(4,128)(2,1)}, bf16[4,3584]{1,0:T(4,128)(2,1)S(1)}, u32[]{:S(2)}, u32[]{:S(2)}) collective-permute-start(bf16[4,3584]{1,0:T(4,128)(2,1)} %param.8), channel_id=1, source_target_pairs={{0,8},{1,9},{2,10},{3,11},{4,12},{5,13},{6,14},{7,15},{8,16},{9,17... | collective-permute-start | bytes 86024 | tf_op jit(solution)/shard_map/ppermute | solution.py:100
  2.4 7.2 %collective-permute-start.2 = (bf16[4,3584]{1,0:T(4,128)(2,1)}, bf16[4,3584]{1,0:T(4,128)(2,1)S(1)}, u32[]{:S(2)}, u32[]{:S(2)}) collective-permute-start(bf16[4,3584]{1,0:T(4,128)(2,1)} %param.8), channel_id=1, source_target_pairs={{0,24},{1,25},{2,26},{3,27},{4,28},{5,29},{6,30},{7,31},{8,0},{9,1... | collective-permute-start | bytes 86024 | tf_op jit(solution)/shard_map/ppermute | solution.py:100
  3.9 5.6 %collective-permute-start.1 = (bf16[4,3584]{1,0:T(4,128)(2,1)}, bf16[4,3584]{1,0:T(4,128)(2,1)S(1)}, u32[]{:S(2)}, u32[]{:S(2)}) collective-permute-start(bf16[4,3584]{1,0:T(4,128)(2,1)} %param.8), channel_id=1, source_target_pairs={{0,16},{1,17},{2,18},{3,19},{4,20},{5,21},{6,22},{7,23},{8,24},{9,... | collective-permute-start | bytes 86024 | tf_op jit(solution)/shard_map/ppermute | solution.py:100
  7.1 2.4 %copy-start.2 = (bf16[4,3584]{1,0:T(4,128)(2,1)S(1)}, bf16[4,3584]{1,0:T(4,128)(2,1)}, u32[]{:S(2)}) copy-start(bf16[4,3584]{1,0:T(4,128)(2,1)} %param.8) | copy-start | bytes 86020
  9.7 5.3 %collective-permute-start.5 = (bf16[16,3584]{1,0:T(8,128)(2,1)S(1)}, bf16[16,3584]{1,0:T(8,128)(2,1)S(1)}, u32[]{:S(2)}, u32[]{:S(2)}) collective-permute-start(bf16[16,3584]{1,0:T(8,128)(2,1)S(1)} %reshape.478), channel_id=1, source_target_pairs={{0,96},{1,7},{2,98},{3,1},{4,100},{5,3},{6,102},{7,5},{8,104},{9,1... | collective-permute-start | bytes 344072 | tf_op jit(solution)/shard_map/ppermute | solution.py:100
  12.6 6.4 %collective-permute-start.4 = (bf16[16,3584]{1,0:T(8,128)(2,1)S(1)}, bf16[16,3584]{1,0:T(8,128)(2,1)S(1)}, u32[]{:S(2)}, u32[]{:S(2)}) collective-permute-start(bf16[16,3584]{1,0:T(8,128)(2,1)S(1)} %reshape.478), channel_id=1, source_target_pairs={{0,64},{1,5},{2,66},{3,7},{4,68},{5,1},{6,70},{7,3},{8,72},{9,13},... | collective-permute-start | bytes 344072 | tf_op jit(solution)/shard_map/ppermute | solution.py:100
  13.4 6.7 %collective-permute-start.3 = (bf16[16,3584]{1,0:T(8,128)(2,1)S(1)}, bf16[16,3584]{1,0:T(8,128)(2,1)S(1)}, u32[]{:S(2)}, u32[]{:S(2)}) collective-permute-start(bf16[16,3584]{1,0:T(8,128)(2,1)S(1)} %reshape.478), channel_id=1, source_target_pairs={{0,32},{1,3},{2,34},{3,5},{4,36},{5,7},{6,38},{7,1},{8,40},{9,11},... | collective-permute-start | bytes 344072 | tf_op jit(solution)/shard_map/ppermute | solution.py:100
  20.2 17.4 %collective-permute-start.8 = (bf16[64,3584]{1,0:T(8,128)(2,1)S(1)}, bf16[64,3584]{1,0:T(8,128)(2,1)S(1)}, u32[]{:S(2)}, u32[]{:S(2)}) collective-permute-start(bf16[64,3584]{1,0:T(8,128)(2,1)S(1)} %bitcast.151), channel_id=1, source_target_pairs={{0,6},{1,97},{2,0},{3,99},{4,2},{5,101},{6,4},{7,103},{8,14},{9,10... | collective-permute-start | bytes 1376264 | tf_op jit(solution)/shard_map/ppermute | solution.py:100
  24.3 13.3 %collective-permute-start.7 = (bf16[64,3584]{1,0:T(8,128)(2,1)S(1)}, bf16[64,3584]{1,0:T(8,128)(2,1)S(1)}, u32[]{:S(2)}, u32[]{:S(2)}) collective-permute-start(bf16[64,3584]{1,0:T(8,128)(2,1)S(1)} %bitcast.152), channel_id=1, source_target_pairs={{0,4},{1,65},{2,6},{3,67},{4,0},{5,69},{6,2},{7,71},{8,12},{9,73},... | collective-permute-start | bytes 1376264 | tf_op jit(solution)/shard_map/ppermute | solution.py:100
  24.3 14.6 %collective-permute-start.6 = (bf16[64,3584]{1,0:T(8,128)(2,1)S(1)}, bf16[64,3584]{1,0:T(8,128)(2,1)S(1)}, u32[]{:S(2)}, u32[]{:S(2)}) collective-permute-start(bf16[64,3584]{1,0:T(8,128)(2,1)S(1)} %bitcast.153), channel_id=1, source_target_pairs={{0,2},{1,33},{2,4},{3,35},{4,6},{5,37},{6,0},{7,39},{8,10},{9,41},... | collective-permute-start | bytes 1376264 | tf_op jit(solution)/shard_map/ppermute | solution.py:100
  39.1 6.9 %collective-permute-start.9 = (bf16[256,3584]{1,0:T(8,128)(2,1)S(1)}, bf16[256,3584]{1,0:T(8,128)(2,1)S(1)}, u32[]{:S(2)}, u32[]{:S(2)}) collective-permute-start(bf16[256,3584]{1,0:T(8,128)(2,1)S(1)} %bitcast.149), channel_id=1, source_target_pairs={{0,1},{1,0},{2,3},{3,2},{4,5},{5,4},{6,7},{7,6},{8,9},{9,8},{10,11... | collective-permute-start | bytes 5505032 | tf_op jit(solution)/shard_map/ppermute | solution.py:161
  39.4 6.6 %slice-start = ((s8[8257536]{0:T(1024)(128)(4,1)}), s8[4194304]{0:T(1024)(128)(4,1)S(1)}, s32[]{:S(2)}) async-start(s8[8257536]{0:T(1024)(128)(4,1)} %bitcast.147), calls=%async_computation | async-start | bytes 8388608
  39.5 6.5 %slice-start.1 = ((s8[8257536]{0:T(1024)(128)(4,1)}), s8[4063232]{0:T(1024)(128)(4,1)S(1)}, s32[]{:S(2)}) async-start(s8[8257536]{0:T(1024)(128)(4,1)} %bitcast.147), calls=%async_computation.1 | async-start | bytes 8126464
  48.7 21.5 %copy-start = (f32[512,64]{0,1:T(8,128)S(1)}, f32[512,64]{0,1:T(8,128)}, u32[]{:S(2)}) copy-start(f32[512,64]{0,1:T(8,128)} %param.11) | copy-start | bytes 393220
  51.6 1.3 %collective-permute-start.10 = (f32[3,512]{1,0:T(4,128)S(1)}, f32[3,512]{1,0:T(4,128)S(1)}, u32[]{:S(2)}, u32[]{:S(2)}) collective-permute-start(f32[3,512]{1,0:T(4,128)S(1)} %fusion.10), channel_id=1, source_target_pairs={{0,1},{1,0},{2,3},{3,2},{4,5},{5,4},{6,7},{7,6},{8,9},{9,8},{10,11... | collective-permute-start | bytes 18440 | tf_op jit(solution)/shard_map/ppermute | solution.py:100
  53.0 5.2 %collective-permute-start.12 = (f32[3,512]{1,0:T(4,128)S(1)}, f32[3,512]{1,0:T(4,128)S(1)}, u32[]{:S(2)}, u32[]{:S(2)}) collective-permute-start(f32[3,512]{1,0:T(4,128)S(1)} %get-tuple-element.147), channel_id=1, source_target_pairs={{0,4},{1,5},{2,6},{3,7},{4,0},{5,1},{6,2},{7,3},{8,12},{9,13},{10,... | collective-permute-start | bytes 18440 | tf_op jit(solution)/shard_map/ppermute | solution.py:100
  54.0 4.9 %collective-permute-start.11 = (f32[3,512]{1,0:T(4,128)S(1)}, f32[3,512]{1,0:T(4,128)S(1)}, u32[]{:S(2)}, u32[]{:S(2)}) collective-permute-start(f32[3,512]{1,0:T(4,128)S(1)} %get-tuple-element.147), channel_id=1, source_target_pairs={{0,2},{1,3},{2,4},{3,5},{4,6},{5,7},{6,0},{7,1},{8,10},{9,11},{10,... | collective-permute-start | bytes 18440 | tf_op jit(solution)/shard_map/ppermute | solution.py:100
  54.9 4.1 %collective-permute-start.13 = (f32[3,512]{1,0:T(4,128)S(1)}, f32[3,512]{1,0:T(4,128)S(1)}, u32[]{:S(2)}, u32[]{:S(2)}) collective-permute-start(f32[3,512]{1,0:T(4,128)S(1)} %get-tuple-element.147), channel_id=1, source_target_pairs={{0,6},{1,7},{2,0},{3,1},{4,2},{5,3},{6,4},{7,5},{8,14},{9,15},{10,... | collective-permute-start | bytes 18440 | tf_op jit(solution)/shard_map/ppermute | solution.py:100
  59.0 5.3 %collective-permute-start.15 = (f32[3,512]{1,0:T(4,128)S(1)}, f32[3,512]{1,0:T(4,128)S(1)}, u32[]{:S(2)}, u32[]{:S(2)}) collective-permute-start(f32[3,512]{1,0:T(4,128)S(1)} %get-tuple-element.145), channel_id=1, source_target_pairs={{0,16},{1,17},{2,18},{3,19},{4,20},{5,21},{6,22},{7,23},{8,24},{9,... | collective-permute-start | bytes 18440 | tf_op jit(solution)/shard_map/ppermute | solution.py:100
  61.1 4.9 %collective-permute-start.14 = (f32[3,512]{1,0:T(4,128)S(1)}, f32[3,512]{1,0:T(4,128)S(1)}, u32[]{:S(2)}, u32[]{:S(2)}) collective-permute-start(f32[3,512]{1,0:T(4,128)S(1)} %get-tuple-element.145), channel_id=1, source_target_pairs={{0,8},{1,9},{2,10},{3,11},{4,12},{5,13},{6,14},{7,15},{8,16},{9,17... | collective-permute-start | bytes 18440 | tf_op jit(solution)/shard_map/ppermute | solution.py:100
  61.8 4.2 %collective-permute-start.16 = (f32[3,512]{1,0:T(4,128)S(1)}, f32[3,512]{1,0:T(4,128)S(1)}, u32[]{:S(2)}, u32[]{:S(2)}) collective-permute-start(f32[3,512]{1,0:T(4,128)S(1)} %get-tuple-element.145), channel_id=1, source_target_pairs={{0,24},{1,25},{2,26},{3,27},{4,28},{5,29},{6,30},{7,31},{8,0},{9,1... | collective-permute-start | bytes 18440 | tf_op jit(solution)/shard_map/ppermute | solution.py:100
  66.1 5.2 %collective-permute-start.18 = (f32[3,512]{1,0:T(4,128)S(1)}, f32[3,512]{1,0:T(4,128)S(1)}, u32[]{:S(2)}, u32[]{:S(2)}) collective-permute-start(f32[3,512]{1,0:T(4,128)S(1)} %get-tuple-element.143), channel_id=1, source_target_pairs={{0,64},{1,65},{2,66},{3,67},{4,68},{5,69},{6,70},{7,71},{8,72},{9,... | collective-permute-start | bytes 18440 | tf_op jit(solution)/shard_map/ppermute | solution.py:100
  67.0 4.9 %collective-permute-start.17 = (f32[3,512]{1,0:T(4,128)S(1)}, f32[3,512]{1,0:T(4,128)S(1)}, u32[]{:S(2)}, u32[]{:S(2)}) collective-permute-start(f32[3,512]{1,0:T(4,128)S(1)} %get-tuple-element.143), channel_id=1, source_target_pairs={{0,32},{1,33},{2,34},{3,35},{4,36},{5,37},{6,38},{7,39},{8,40},{9,... | collective-permute-start | bytes 18440 | tf_op jit(solution)/shard_map/ppermute | solution.py:100
  67.6 4.2 %collective-permute-start.19 = (f32[3,512]{1,0:T(4,128)S(1)}, f32[3,512]{1,0:T(4,128)S(1)}, u32[]{:S(2)}, u32[]{:S(2)}) collective-permute-start(f32[3,512]{1,0:T(4,128)S(1)} %get-tuple-element.143), channel_id=1, source_target_pairs={{0,96},{1,97},{2,98},{3,99},{4,100},{5,101},{6,102},{7,103},{8,104... | collective-permute-start | bytes 18440 | tf_op jit(solution)/shard_map/ppermute | solution.py:100
  76.9 4.5 %collective-permute-start.20 = (bf16[256,3584]{1,0:T(8,128)(2,1)S(1)}, bf16[256,3584]{1,0:T(8,128)(2,1)S(1)}, u32[]{:S(2)}, u32[]{:S(2)}) collective-permute-start(bf16[256,3584]{1,0:T(8,128)(2,1)S(1)} %convolution_convert_fusion.1), channel_id=1, source_target_pairs={{0,1},{1,0},{2,3},{3,2},{4,5},{5,4},{6,7},{7,6},{8,9},{9,8},{10,11... | collective-permute-start | bytes 5505032 | tf_op jit(solution)/shard_map/ppermute | solution.py:205
  82.2 11.7 %collective-permute-start.21 = (bf16[64,3584]{1,0:T(8,128)(2,1)S(1)}, bf16[64,3584]{1,0:T(8,128)(2,1)S(1)}, u32[]{:S(2)}, u32[]{:S(2)}) collective-permute-start(bf16[64,3584]{1,0:T(8,128)(2,1)S(1)} %get-tuple-element.129), channel_id=1, source_target_pairs={{0,2},{1,33},{2,4},{3,35},{4,6},{5,37},{6,0},{7,39},{8,10},{9,41},... | collective-permute-start | bytes 1376264 | tf_op jit(solution)/shard_map/ppermute | solution.py:100
  83.5 12.9 %collective-permute-start.23 = (bf16[64,3584]{1,0:T(8,128)(2,1)S(1)}, bf16[64,3584]{1,0:T(8,128)(2,1)S(1)}, u32[]{:S(2)}, u32[]{:S(2)}) collective-permute-start(bf16[64,3584]{1,0:T(8,128)(2,1)S(1)} %get-tuple-element.130), channel_id=1, source_target_pairs={{0,6},{1,97},{2,0},{3,99},{4,2},{5,101},{6,4},{7,103},{8,14},{9,10... | collective-permute-start | bytes 1376264 | tf_op jit(solution)/shard_map/ppermute | solution.py:100
  85.5 12.7 %collective-permute-start.22 = (bf16[64,3584]{1,0:T(8,128)(2,1)S(1)}, bf16[64,3584]{1,0:T(8,128)(2,1)S(1)}, u32[]{:S(2)}, u32[]{:S(2)}) collective-permute-start(bf16[64,3584]{1,0:T(8,128)(2,1)S(1)} %get-tuple-element.131), channel_id=1, source_target_pairs={{0,4},{1,65},{2,6},{3,67},{4,0},{5,69},{6,2},{7,71},{8,12},{9,73},... | collective-permute-start | bytes 1376264 | tf_op jit(solution)/shard_map/ppermute | solution.py:100
  98.7 6.1 %collective-permute-start.24 = (bf16[16,3584]{1,0:T(8,128)(2,1)S(1)}, bf16[16,3584]{1,0:T(8,128)(2,1)S(1)}, u32[]{:S(2)}, u32[]{:S(2)}) collective-permute-start(bf16[16,3584]{1,0:T(8,128)(2,1)S(1)} %get-tuple-element.134), channel_id=1, source_target_pairs={{0,32},{1,3},{2,34},{3,5},{4,36},{5,7},{6,38},{7,1},{8,40},{9,11},... | collective-permute-start | bytes 344072 | tf_op jit(solution)/shard_map/ppermute | solution.py:100
  100.3 4.8 %collective-permute-start.26 = (bf16[16,3584]{1,0:T(8,128)(2,1)S(1)}, bf16[16,3584]{1,0:T(8,128)(2,1)S(1)}, u32[]{:S(2)}, u32[]{:S(2)}) collective-permute-start(bf16[16,3584]{1,0:T(8,128)(2,1)S(1)} %get-tuple-element.135), channel_id=1, source_target_pairs={{0,96},{1,7},{2,98},{3,1},{4,100},{5,3},{6,102},{7,5},{8,104},{9,1... | collective-permute-start | bytes 344072 | tf_op jit(solution)/shard_map/ppermute | solution.py:100
  102.1 6.3 %collective-permute-start.25 = (bf16[16,3584]{1,0:T(8,128)(2,1)S(1)}, bf16[16,3584]{1,0:T(8,128)(2,1)S(1)}, u32[]{:S(2)}, u32[]{:S(2)}) collective-permute-start(bf16[16,3584]{1,0:T(8,128)(2,1)S(1)} %get-tuple-element.136), channel_id=1, source_target_pairs={{0,64},{1,5},{2,66},{3,7},{4,68},{5,1},{6,70},{7,3},{8,72},{9,13},... | collective-permute-start | bytes 344072 | tf_op jit(solution)/shard_map/ppermute | solution.py:100
  108.5 5.3 %collective-permute-start.27 = (bf16[4,3584]{1,0:T(4,128)(2,1)S(1)}, bf16[4,3584]{1,0:T(4,128)(2,1)S(1)}, u32[]{:S(2)}, u32[]{:S(2)}) collective-permute-start(bf16[4,3584]{1,0:T(4,128)(2,1)S(1)} %get-tuple-element.137), channel_id=1, source_target_pairs={{0,8},{1,9},{2,10},{3,11},{4,12},{5,13},{6,14},{7,15},{8,16},{9,17... | collective-permute-start | bytes 86024 | tf_op jit(solution)/shard_map/ppermute | solution.py:100
  108.9 5.0 %collective-permute-start.29 = (bf16[4,3584]{1,0:T(4,128)(2,1)S(1)}, bf16[4,3584]{1,0:T(4,128)(2,1)S(1)}, u32[]{:S(2)}, u32[]{:S(2)}) collective-permute-start(bf16[4,3584]{1,0:T(4,128)(2,1)S(1)} %get-tuple-element.138), channel_id=1, source_target_pairs={{0,24},{1,25},{2,26},{3,27},{4,28},{5,29},{6,30},{7,31},{8,0},{9,1... | collective-permute-start | bytes 86024 | tf_op jit(solution)/shard_map/ppermute | solution.py:100
  111.9 5.4 %collective-permute-start.28 = (bf16[4,3584]{1,0:T(4,128)(2,1)S(1)}, bf16[4,3584]{1,0:T(4,128)(2,1)S(1)}, u32[]{:S(2)}, u32[]{:S(2)}) collective-permute-start(bf16[4,3584]{1,0:T(4,128)(2,1)S(1)} %get-tuple-element.139), channel_id=1, source_target_pairs={{0,16},{1,17},{2,18},{3,19},{4,20},{5,21},{6,22},{7,23},{8,24},{9,... | collective-permute-start | bytes 86024 | tf_op jit(solution)/shard_map/ppermute | solution.py:100
